TPU v7x, 1024 devices: a whole 8x8x8 slice. The times are simulated.
1024 devices in a mesh: row: 32 (over y_hi, z), col: 32 (over y_lo, x, core).
Axes of the slice: x: 8, y: 8 (y_hi: 4, y_lo: 2; y = y_hi * 2 + y_lo), z: 8, core: 2. Of those that a mesh axis runs over, the one named last changes fastest.
Arguments:
- object_planes: float32 [2, 8192, 8192], P(None, 'row', 'col'), may hold values from -4 to 4
- probe_modes: float32 [2, 3, 256, 256], replicated, may hold values from -1 to 1
- positions: int32 [32, 32, 1, 2], P('row', 'col'), may hold values from -64 to 64
- amplitudes: float32 [32, 32, 1, 256, 256], P('row', 'col'), may hold values from 0.2 to 4
Outputs:
- object_next: float32 [2, 8192, 8192], P(None, 'row', 'col')
Inputs may be any that keep to these rules, and one draw needn't show every extreme that they name: positions[i, j, t] holds the row offset then the column offset of pattern t of tile (i, j); its window may reach up to 64 pixels into the neighbouring tiles.
All inputs are finite; a program needn't handle non-finite values.
Results may differ from a plain program's by a relative error of at most 0.004.
Values sent between devices are 32-bit elements; how exact they have to be, the bound alone decides.
No kernel may reach another device: no remote copies, remote signals or barrier semaphores. Data moves between devices by JAX's collectives and lax.ppermute only.
A program may use at most 32 MiB of HBM per device.

v0:
```python
import math

import jax
import jax.numpy as jnp
from jax import lax
from jax.sharding import PartitionSpec as P

W = 256
M = 64
ITERS = 2


AMPLITUDE_FLOOR = 0.5
EPSILON = 1e-06


def with_halo(block, sides, width):
    for axis, dim in sides:
        count = lax.axis_size(axis)
        forward = [(i, i + 1) for i in range(count - 1)]
        backward = [(target, source) for source, target in forward]
        low = lax.ppermute(
            lax.slice_in_dim(block, block.shape[dim] - width, None, axis=dim), axis, forward
        )
        high = lax.ppermute(lax.slice_in_dim(block, 0, width, axis=dim), axis, backward)
        block = jnp.concatenate([low, block, high], axis=dim)
    return block


def tables(length):
    counter = jnp.arange(length, dtype=jnp.int32)
    product = counter[:, None] * counter[None, :] % length
    phases = product.astype(jnp.float32) * (2.0 * math.pi / length)
    factor = 1.0 / math.sqrt(length)
    return (
        (jnp.cos(phases) * factor).astype(jnp.bfloat16),
        (-jnp.sin(phases) * factor).astype(jnp.bfloat16),
    )


def operators(table_re, table_im):
    left_side = jnp.stack(
        [jnp.stack([table_re, -table_im], 1), jnp.stack([table_im, table_re], 1)], 0
    )
    right_side = jnp.stack(
        [jnp.stack([table_re, table_im], 1), jnp.stack([-table_im, table_re], 1)], 0
    )
    return (left_side, right_side)


def transform(waves, left_side, right_side):
    half_done = jnp.einsum(
        "puqr,qkrc->pkuc", left_side, waves, preferred_element_type=jnp.float32
    ).astype(jnp.bfloat16)
    return jnp.einsum("qkrc,qcpv->pkrv", half_done, right_side, preferred_element_type=jnp.float32)


def pattern_gradient(windows, measured, probe_re, probe_im, forward, inverse):
    obj_re = windows[:, 0][:, None]
    obj_im = windows[:, 1][:, None]
    exit_re = obj_re * probe_re[None] - obj_im * probe_im[None]
    exit_im = obj_re * probe_im[None] + obj_im * probe_re[None]
    exit_waves = jnp.stack([exit_re, exit_im])
    flat_shape = (2, -1) + exit_waves.shape[3:]
    spectrum = transform(
        exit_waves.reshape(flat_shape).astype(jnp.bfloat16), forward[0], forward[1]
    ).reshape(exit_waves.shape)
    modulus = jnp.sqrt(jnp.sum(spectrum * spectrum, axis=(0, 2)))
    scaling = measured / jnp.maximum(modulus, AMPLITUDE_FLOOR)
    corrected = (spectrum * scaling[None, :, None]).astype(jnp.bfloat16).reshape(flat_shape)
    revised = transform(corrected, inverse[0], inverse[1]).reshape(exit_waves.shape)
    residue = revised - exit_waves
    grad_re = jnp.sum(probe_re[None] * residue[0] + probe_im[None] * residue[1], axis=1)
    grad_im = jnp.sum(probe_re[None] * residue[1] - probe_im[None] * residue[0], axis=1)
    return jnp.stack([grad_re, grad_im], axis=1)


def placed(piece, row_to, col_to, rows_all, cols_all):
    return jnp.pad(
        piece,
        (
            (0, 0),
            (row_to, rows_all - row_to - piece.shape[1]),
            (col_to, cols_all - col_to - piece.shape[2]),
        ),
    )


def fold_margins(gathered, tile_size):
    extent = gathered.shape[1]
    strips = jnp.concatenate([gathered[:, :, :M], gathered[:, :, tile_size + M :]], axis=2)
    across = with_halo(strips, (("col", 2),), M)
    inner = (
        gathered[:, :, M : tile_size + M]
        + placed(across[:, :, :M], 0, 0, extent, tile_size)
        + placed(across[:, :, 3 * M :], 0, tile_size - M, extent, tile_size)
    )
    bands = jnp.concatenate([inner[:, :M], inner[:, tile_size + M :]], axis=1)
    downward = with_halo(bands, (("row", 1),), M)
    return (
        inner[:, M : tile_size + M]
        + placed(downward[:, :M], 0, 0, tile_size, tile_size)
        + placed(downward[:, 3 * M :], tile_size - M, 0, tile_size, tile_size)
    )


def widen(current):
    return with_halo(current, (("row", 1), ("col", 2)), M)


def on_device(object_planes, probe_modes, positions, amplitudes):
    table_re, table_im = tables(W)
    forward = operators(table_re, table_im)
    inverse = operators(table_re, -table_im)
    probe_re = probe_modes[0]
    probe_im = probe_modes[1]
    peak_power = jnp.max(jnp.sum(probe_modes * probe_modes, axis=(0, 1))) + EPSILON
    offsets = positions.reshape(-1, 2)
    measured = amplitudes.reshape(-1, W, W)
    tile_size = object_planes.shape[1]
    anchor_zero = jnp.zeros((), jnp.int32)
    current = object_planes
    extended = widen(current)
    for update in range(ITERS):
        corners = [(anchor_zero, offsets[0, 0] + M, offsets[0, 1] + M)]
        windows = jnp.stack([lax.dynamic_slice(extended, corner, (2, W, W)) for corner in corners])
        changes = pattern_gradient(windows, measured, probe_re, probe_im, forward, inverse)
        gathered = jnp.zeros_like(extended)
        gathered = lax.dynamic_update_slice(gathered, changes[0], corners[0])
        if update + 1 < ITERS:
            current = (
                extended[:, M : M + tile_size, M : M + tile_size]
                + fold_margins(gathered, tile_size) / peak_power
            )
            extended = widen(current)
        else:
            current = (
                extended[:, M : M + tile_size, M : M + tile_size]
                + fold_margins(gathered, tile_size) / peak_power
            )
    return current


def solution(mesh):
    in_specs = (
        P(None, "row", "col"),
        P(),
        P("row", "col", None, None),
        P("row", "col", None, None, None),
    )
    out_specs = P(None, "row", "col")
    return jax.shard_map(
        on_device, mesh=mesh, in_specs=in_specs, out_specs=out_specs, check_vma=False
    )
```

profile of v0, /device:TPU:87, one launch (start us, length us, event | category | flops | bytes accessed | tf_op | source)
XLA Modules:
  0.0 173.5 jit_solution(2652917314862205239)
XLA Ops:
  0.0 1.0 fusion.65
  1.0 4.9 %collective-permute-start = (f32[2,64,256]{2,1,0:T(8,128)S(1)}, f32[2,64,256]{2,1,0:T(8,128)S(1)}, u32[]{:S(2)}, u32[]{:S(2)}) collective-permute-start(f32[2,64,256]{2,1,0:T(8,128)S(1)} %get-tuple-element.42), channel_id=1, source_target_pairs={{0,32},{32,64},{64,96},{96,128},{128,160},{160,192},{192,224},{224... | collective-permute-start | bytes 393224 | tf_op jit(solution)/shard_map/ppermute | solution.py:22
  5.9 14.5 %collective-permute-start.1 = (f32[2,64,256]{2,1,0:T(8,128)S(1)}, f32[2,64,256]{2,1,0:T(8,128)S(1)}, u32[]{:S(2)}, u32[]{:S(2)}) collective-permute-start(f32[2,64,256]{2,1,0:T(8,128)S(1)} %get-tuple-element.41), channel_id=1, source_target_pairs={{32,0},{64,32},{96,64},{128,96},{160,128},{192,160},{224,192},{256... | collective-permute-start | bytes 393224 | tf_op jit(solution)/shard_map/ppermute | solution.py:25
  20.4 1.0 fusion.54
  21.4 1.0 multiply_convert_fusion
  23.4 2.4 %fusion.57 = (f32[1,3,256,256]{3,2,1,0:T(8,128)S(1)}, f32[1,3,256,256]{3,2,1,0:T(8,128)}) fusion(f32[2,3,256,256]{3,2,1,0:T(8,128)} %param.5), kind=kLoop, calls=%fused_computation.111 | loop fusion | bytes 3145728 | tf_op jit(solution)/shard_map/slice | solution.py:115
  27.2 1.0 fusion.63
  28.2 5.2 %collective-permute-start.2 = (f32[2,384,64]{2,1,0:T(8,128)}, f32[2,384,64]{2,1,0:T(8,128)}, u32[]{:S(2)}, u32[]{:S(2)}) collective-permute-start(f32[2,384,64]{2,1,0:T(8,128)} %get-tuple-element.34), channel_id=1, source_target_pairs={{0,1},{1,2},{2,3},{3,4},{4,5},{5,6},{6,7},{7,8},{8,9},{9,10},{10,1... | collective-permute-start | bytes 589832 | tf_op jit(solution)/shard_map/ppermute | solution.py:22
  33.3 1.9 %collective-permute-start.3 = (f32[2,384,64]{2,1,0:T(8,128)}, f32[2,384,64]{2,1,0:T(8,128)}, u32[]{:S(2)}, u32[]{:S(2)}) collective-permute-start(f32[2,384,64]{2,1,0:T(8,128)} %get-tuple-element.33), channel_id=1, source_target_pairs={{1,0},{2,1},{3,2},{4,3},{5,4},{6,5},{7,6},{8,7},{9,8},{10,9},{11,1... | collective-permute-start | bytes 589832 | tf_op jit(solution)/shard_map/ppermute | solution.py:25
  38.6 1.4 copy.106
  40.0 1.1 copy.52
  41.1 2.2 %maximum_bitcast_fusion.4 = (bf16[2,256,2,256,1]{3,1,2,0,4:T(8,128)(2,1)}, bf16[2,256,2,256,1]{3,1,2,0,4:T(8,128)(2,1)}) fusion(bf16[1,256,2,256]{3,1,2,0:T(8,128)(2,1)} %get-tuple-element.48, bf16[1,256,2,256]{3,1,2,0:T(8,128)(2,1)} %get-tuple-element.43, bf16[1,256,2,256]{3,1,2,0:T(8,128)(2,1)S(1)} %get-tuple-element.44, ...), kind=kLoop, calls=%fused_computation.67 | loop fusion | flops 524288 | bytes 2097152 | tf_op jit(solution)/shard_map/stack | solution.py:45
  44.0 1.5 fusion.31
  45.8 1.6 convert_bitcast_fusion.3
  47.4 4.3 %fusion.2 = (f32[256,256]{0,1:T(8,128)}, f32[2,256,3,256,1]{3,1,4,2,0:T(8,128)}) fusion(bf16[1,1,3,256,256]{3,4,0,2,1:T(8,128)(2,1)} %get-tuple-element.19, bf16[1,1,3,256,256]{3,4,0,2,1:T(8,128)(2,1)} %get-tuple-element.13, bf16[1,256,2,256]{3,1,2,0:T(8,128)(2,1)} %get-tuple-element.48, bf16[1,256,2,256]{3,1,2,0:T(8,128)(2,1)S(1)} %copy-done.6, ...), kind=kOutput, calls=%fused_computation.11 | convolution fusion | flops 809041920 | bytes 3670016 | tf_op jit(solution)/shard_map/qkrc,qcpv->pkrv/dot_general | solution.py:55
  51.7 1.0 fusion.50
  52.7 4.2 %maximum_subtract_fusion = f32[2,3,256,256]{2,3,1,0:T(8,128)} fusion(f32[1,3,256,256]{2,3,1,0:T(8,128)} %get-tuple-element.20, f32[1,3,256,256]{2,3,1,0:T(8,128)} %get-tuple-element.14, bf16[2,256,2,256,1]{3,1,2,0,4:T(8,128)(2,1)} %get-tuple-element.55, bf16[1,256,2,256]{3,1,2,0:T(8,128)(2,1)S(1)} %get-tuple-element.44, ...), kind=kOutput, calls=%fused_computation | convolution fusion | flops 808321024 | bytes 6029312 | tf_op jit(solution)/shard_map/qkrc,qcpv->pkrv/dot_general | solution.py:55
  56.9 1.7 add_reduce_fusion.1
  58.6 1.0 copy.56
  59.7 7.3 %dynamic_update_slice.6 = f32[2,384,384]{2,1,0:T(8,128)S(1)} dynamic-update-slice(f32[2,384,384]{2,1,0:T(8,128)S(1)} %broadcast.187.clone, f32[2,256,256]{2,1,0:T(8,128)} %copy.56, s32[]{:T(128)} %constant.30.clone.1, s32[]{:T(128)S(6)} %select_n.50, s32[]{:T(128)S(6)} %select_n.51) | dynamic-update-slice | bytes 1048580 | tf_op jit(solution)/shard_map/dynamic_update_slice | solution.py:129
  67.2 4.7 %collective-permute-start.4 = (f32[2,384,64]{2,1,0:T(8,128)S(1)}, f32[2,384,64]{2,1,0:T(8,128)S(1)}, u32[]{:S(2)}, u32[]{:S(2)}) collective-permute-start(f32[2,384,64]{2,1,0:T(8,128)S(1)} %get-tuple-element.25), channel_id=1, source_target_pairs={{0,1},{1,2},{2,3},{3,4},{4,5},{5,6},{6,7},{7,8},{8,9},{9,10},{10,1... | collective-permute-start | bytes 589832 | tf_op jit(solution)/shard_map/ppermute | solution.py:22
  71.9 1.9 %collective-permute-start.5 = (f32[2,384,64]{2,1,0:T(8,128)S(1)}, f32[2,384,64]{2,1,0:T(8,128)S(1)}, u32[]{:S(2)}, u32[]{:S(2)}) collective-permute-start(f32[2,384,64]{2,1,0:T(8,128)S(1)} %get-tuple-element.26), channel_id=1, source_target_pairs={{1,0},{2,1},{3,2},{4,3},{5,4},{6,5},{7,6},{8,7},{9,8},{10,9},{11,1... | collective-permute-start | bytes 589832 | tf_op jit(solution)/shard_map/ppermute | solution.py:25
  73.8 2.8 %collective-permute-done.4 = f32[2,384,64]{2,1,0:T(8,128)S(1)} collective-permute-done((f32[2,384,64]{2,1,0:T(8,128)S(1)}, f32[2,384,64]{2,1,0:T(8,128)S(1)}, u32[]{:S(2)}, u32[]{:S(2)}) %collective-permute-start.4) | collective-permute-done | bytes 196640 | tf_op jit(solution)/shard_map/ppermute | solution.py:22
  76.6 5.6 %collective-permute-done.5 = f32[2,384,64]{2,1,0:T(8,128)S(1)} collective-permute-done((f32[2,384,64]{2,1,0:T(8,128)S(1)}, f32[2,384,64]{2,1,0:T(8,128)S(1)}, u32[]{:S(2)}, u32[]{:S(2)}) %collective-permute-start.5) | collective-permute-done | bytes 196640 | tf_op jit(solution)/shard_map/ppermute | solution.py:25
  82.2 1.3 fusion.13
  84.4 1.9 %collective-permute-start.6 = (f32[2,64,256]{2,1,0:T(8,128)S(1)}, f32[2,64,256]{2,1,0:T(8,128)S(1)}, u32[]{:S(2)}, u32[]{:S(2)}) collective-permute-start(f32[2,64,256]{2,1,0:T(8,128)S(1)} %get-tuple-element.31), channel_id=1, source_target_pairs={{0,32},{32,64},{64,96},{96,128},{128,160},{160,192},{192,224},{224... | collective-permute-start | bytes 393224 | tf_op jit(solution)/shard_map/ppermute | solution.py:22
  86.4 7.6 %collective-permute-start.7 = (f32[2,64,256]{2,1,0:T(8,128)S(1)}, f32[2,64,256]{2,1,0:T(8,128)S(1)}, u32[]{:S(2)}, u32[]{:S(2)}) collective-permute-start(f32[2,64,256]{2,1,0:T(8,128)S(1)} %get-tuple-element.32), channel_id=1, source_target_pairs={{32,0},{64,32},{96,64},{128,96},{160,128},{192,160},{224,192},{256... | collective-permute-start | bytes 393224 | tf_op jit(solution)/shard_map/ppermute | solution.py:25
  96.0 1.1 fusion.37
  97.2 1.9 %collective-permute-start.8 = (f32[2,64,256]{2,1,0:T(8,128)S(1)}, f32[2,64,256]{2,1,0:T(8,128)S(1)}, u32[]{:S(2)}, u32[]{:S(2)}) collective-permute-start(f32[2,64,256]{2,1,0:T(8,128)S(1)} %get-tuple-element.37), channel_id=1, source_target_pairs={{0,32},{32,64},{64,96},{96,128},{128,160},{160,192},{192,224},{224... | collective-permute-start | bytes 393224 | tf_op jit(solution)/shard_map/ppermute | solution.py:22
  99.1 8.0 %collective-permute-start.9 = (f32[2,64,256]{2,1,0:T(8,128)S(1)}, f32[2,64,256]{2,1,0:T(8,128)S(1)}, u32[]{:S(2)}, u32[]{:S(2)}) collective-permute-start(f32[2,64,256]{2,1,0:T(8,128)S(1)} %get-tuple-element.38), channel_id=1, source_target_pairs={{32,0},{64,32},{96,64},{128,96},{160,128},{192,160},{224,192},{256... | collective-permute-start | bytes 393224 | tf_op jit(solution)/shard_map/ppermute | solution.py:25
  107.1 2.5 %collective-permute-done.8 = f32[2,64,256]{2,1,0:T(8,128)S(1)} collective-permute-done((f32[2,64,256]{2,1,0:T(8,128)S(1)}, f32[2,64,256]{2,1,0:T(8,128)S(1)}, u32[]{:S(2)}, u32[]{:S(2)}) %collective-permute-start.8) | collective-permute-done | bytes 131104 | tf_op jit(solution)/shard_map/ppermute | solution.py:22
  110.6 4.1 %collective-permute-start.10 = (f32[2,384,64]{2,1,0:T(8,128)S(1)}, f32[2,384,64]{2,1,0:T(8,128)S(1)}, u32[]{:S(2)}, u32[]{:S(2)}) collective-permute-start(f32[2,384,64]{2,1,0:T(8,128)S(1)} %get-tuple-element.30), channel_id=1, source_target_pairs={{0,1},{1,2},{2,3},{3,4},{4,5},{5,6},{6,7},{7,8},{8,9},{9,10},{10,1... | collective-permute-start | bytes 589832 | tf_op jit(solution)/shard_map/ppermute | solution.py:22
  114.7 2.1 %collective-permute-start.11 = (f32[2,384,64]{2,1,0:T(8,128)S(1)}, f32[2,384,64]{2,1,0:T(8,128)S(1)}, u32[]{:S(2)}, u32[]{:S(2)}) collective-permute-start(f32[2,384,64]{2,1,0:T(8,128)S(1)} %get-tuple-element.29), channel_id=1, source_target_pairs={{1,0},{2,1},{3,2},{4,3},{5,4},{6,5},{7,6},{8,7},{9,8},{10,9},{11,1... | collective-permute-start | bytes 589832 | tf_op jit(solution)/shard_map/ppermute | solution.py:25
  116.9 2.6 %collective-permute-done.10 = f32[2,384,64]{2,1,0:T(8,128)S(1)} collective-permute-done((f32[2,384,64]{2,1,0:T(8,128)S(1)}, f32[2,384,64]{2,1,0:T(8,128)S(1)}, u32[]{:S(2)}, u32[]{:S(2)}) %collective-permute-start.10) | collective-permute-done | bytes 196640 | tf_op jit(solution)/shard_map/ppermute | solution.py:22
  119.4 5.6 %collective-permute-done.11 = f32[2,384,64]{2,1,0:T(8,128)S(1)} collective-permute-done((f32[2,384,64]{2,1,0:T(8,128)S(1)}, f32[2,384,64]{2,1,0:T(8,128)S(1)}, u32[]{:S(2)}, u32[]{:S(2)}) %collective-permute-start.11) | collective-permute-done | bytes 196640 | tf_op jit(solution)/shard_map/ppermute | solution.py:25
  126.0 1.6 convert_bitcast_fusion.1
  127.7 4.2 %fusion = (f32[256,256]{0,1:T(8,128)}, f32[2,256,3,256,1]{3,1,4,2,0:T(8,128)}) fusion(bf16[1,256,2,256]{3,1,2,0:T(8,128)(2,1)S(1)} %copy-done.8, bf16[1,256,2,256]{3,1,2,0:T(8,128)(2,1)S(1)} %copy-done.7, bf16[2,256,2,256,1]{3,1,2,0,4:T(8,128)(2,1)} %get-tuple-element.56, bf16[1,1,3,256,256]{3,4,2,1,0:T(8,128)(2,1)} %get-tuple-element.17, ...), kind=kOutput, calls=%fused_computation.5 | convolution fusion | flops 807862272 | bytes 3670016 | tf_op jit(solution)/shard_map/qkrc,qcpv->pkrv/dot_general | solution.py:55
  131.9 1.0 fusion.49
  133.0 4.2 %maximum_subtract_fusion.1 = f32[2,3,256,256]{2,3,1,0:T(8,128)} fusion(f32[1,3,256,256]{2,3,1,0:T(8,128)} %get-tuple-element.18, f32[1,3,256,256]{2,3,1,0:T(8,128)} %get-tuple-element.10, bf16[2,256,2,256,1]{3,1,2,0,4:T(8,128)(2,1)} %get-tuple-element.55, bf16[1,256,2,256]{3,1,2,0:T(8,128)(2,1)S(1)} %copy-done.3, bf16[1,256,2,256]{3,1,2,0:T(8,128)(2,1)S(1)} %copy-done.5, ...), kind=kOutput, calls=%fused_computation.1 | convolution fusion | flops 808321024 | bytes 6029312 | tf_op jit(solution)/shard_map/qkrc,qcpv->pkrv/dot_general | solution.py:55
  137.1 1.7 add_reduce_fusion
  139.2 7.4 %dynamic_update_slice.7 = f32[2,384,384]{2,1,0:T(8,128)S(1)} dynamic-update-slice(f32[2,384,384]{2,1,0:T(8,128)S(1)} %broadcast.187, f32[2,256,256]{2,1,0:T(8,128)S(1)} %copy.66, s32[]{:T(128)} %constant.30.clone.1, s32[]{:T(128)S(6)} %select_n.50, s32[]{:T(128)S(6)} %select_n.51) | dynamic-update-slice | bytes 1048580 | tf_op jit(solution)/shard_map/dynamic_update_slice | solution.py:129
  146.7 2.4 %collective-permute-start.12 = (f32[2,384,64]{2,1,0:T(8,128)S(1)}, f32[2,384,64]{2,1,0:T(8,128)S(1)}, u32[]{:S(2)}, u32[]{:S(2)}) collective-permute-start(f32[2,384,64]{2,1,0:T(8,128)S(1)} %get-tuple-element.23), channel_id=1, source_target_pairs={{0,1},{1,2},{2,3},{3,4},{4,5},{5,6},{6,7},{7,8},{8,9},{9,10},{10,1... | collective-permute-start | bytes 589832 | tf_op jit(solution)/shard_map/ppermute | solution.py:22
  149.0 2.0 %collective-permute-start.13 = (f32[2,384,64]{2,1,0:T(8,128)S(1)}, f32[2,384,64]{2,1,0:T(8,128)S(1)}, u32[]{:S(2)}, u32[]{:S(2)}) collective-permute-start(f32[2,384,64]{2,1,0:T(8,128)S(1)} %get-tuple-element.24), channel_id=1, source_target_pairs={{1,0},{2,1},{3,2},{4,3},{5,4},{6,5},{7,6},{8,7},{9,8},{10,9},{11,1... | collective-permute-start | bytes 589832 | tf_op jit(solution)/shard_map/ppermute | solution.py:25
  151.0 2.7 %collective-permute-done.12 = f32[2,384,64]{2,1,0:T(8,128)S(1)} collective-permute-done((f32[2,384,64]{2,1,0:T(8,128)S(1)}, f32[2,384,64]{2,1,0:T(8,128)S(1)}, u32[]{:S(2)}, u32[]{:S(2)}) %collective-permute-start.12) | collective-permute-done | bytes 196640 | tf_op jit(solution)/shard_map/ppermute | solution.py:22
  153.7 5.6 %collective-permute-done.13 = f32[2,384,64]{2,1,0:T(8,128)S(1)} collective-permute-done((f32[2,384,64]{2,1,0:T(8,128)S(1)}, f32[2,384,64]{2,1,0:T(8,128)S(1)}, u32[]{:S(2)}, u32[]{:S(2)}) %collective-permute-start.13) | collective-permute-done | bytes 196640 | tf_op jit(solution)/shard_map/ppermute | solution.py:25
  159.8 1.9 %collective-permute-start.14 = (f32[2,64,256]{2,1,0:T(8,128)S(1)}, f32[2,64,256]{2,1,0:T(8,128)S(1)}, u32[]{:S(2)}, u32[]{:S(2)}) collective-permute-start(f32[2,64,256]{2,1,0:T(8,128)S(1)} %get-tuple-element.27), channel_id=1, source_target_pairs={{0,32},{32,64},{64,96},{96,128},{128,160},{160,192},{192,224},{224... | collective-permute-start | bytes 393224 | tf_op jit(solution)/shard_map/ppermute | solution.py:22
  161.7 7.9 %collective-permute-start.15 = (f32[2,64,256]{2,1,0:T(8,128)S(1)}, f32[2,64,256]{2,1,0:T(8,128)S(1)}, u32[]{:S(2)}, u32[]{:S(2)}) collective-permute-start(f32[2,64,256]{2,1,0:T(8,128)S(1)} %get-tuple-element.28), channel_id=1, source_target_pairs={{32,0},{64,32},{96,64},{128,96},{160,128},{192,160},{224,192},{256... | collective-permute-start | bytes 393224 | tf_op jit(solution)/shard_map/ppermute | solution.py:25
  169.6 2.1 %collective-permute-done.14 = f32[2,64,256]{2,1,0:T(8,128)S(1)} collective-permute-done((f32[2,64,256]{2,1,0:T(8,128)S(1)}, f32[2,64,256]{2,1,0:T(8,128)S(1)}, u32[]{:S(2)}, u32[]{:S(2)}) %collective-permute-start.14) | collective-permute-done | bytes 131104 | tf_op jit(solution)/shard_map/ppermute | solution.py:22
  (58 shorter events, 11.5 us)
Async XLA Ops:
  1.0 25.8 %collective-permute-start = (f32[2,64,256]{2,1,0:T(8,128)S(1)}, f32[2,64,256]{2,1,0:T(8,128)S(1)}, u32[]{:S(2)}, u32[]{:S(2)}) collective-permute-start(f32[2,64,256]{2,1,0:T(8,128)S(1)} %get-tuple-element.42), channel_id=1, source_target_pairs={{0,32},{32,64},{64,96},{96,128},{128,160},{160,192},{192,224},{224... | collective-permute-start | bytes 393224 | tf_op jit(solution)/shard_map/ppermute | solution.py:22
  5.9 21.2 %collective-permute-start.1 = (f32[2,64,256]{2,1,0:T(8,128)S(1)}, f32[2,64,256]{2,1,0:T(8,128)S(1)}, u32[]{:S(2)}, u32[]{:S(2)}) collective-permute-start(f32[2,64,256]{2,1,0:T(8,128)S(1)} %get-tuple-element.41), channel_id=1, source_target_pairs={{32,0},{64,32},{96,64},{128,96},{160,128},{192,160},{224,192},{256... | collective-permute-start | bytes 393224 | tf_op jit(solution)/shard_map/ppermute | solution.py:25
  25.8 1.3 copy-start.1
  26.7 26.0 %copy-start.2 = (bf16[1,256,2,256]{3,1,2,0:T(8,128)(2,1)}, bf16[1,256,2,256]{3,1,2,0:T(8,128)(2,1)S(1)}, u32[]{:S(2)}) copy-start(bf16[1,256,2,256]{3,1,2,0:T(8,128)(2,1)S(1)} %get-tuple-element.44) | copy-start | bytes 786436
  26.7 8.5 %copy-start.9 = (s32[1,1,1,2]{3,2,1,0:T(1,128)S(1)}, s32[1,1,1,2]{3,2,1,0:T(1,128)}, u32[]{:S(2)}) copy-start(s32[1,1,1,2]{3,2,1,0:T(1,128)} %param.6) | copy-start | bytes 28
  28.2 15.1 %collective-permute-start.2 = (f32[2,384,64]{2,1,0:T(8,128)}, f32[2,384,64]{2,1,0:T(8,128)}, u32[]{:S(2)}, u32[]{:S(2)}) collective-permute-start(f32[2,384,64]{2,1,0:T(8,128)} %get-tuple-element.34), channel_id=1, source_target_pairs={{0,1},{1,2},{2,3},{3,4},{4,5},{5,6},{6,7},{7,8},{8,9},{9,10},{10,1... | collective-permute-start | bytes 589832 | tf_op jit(solution)/shard_map/ppermute | solution.py:22
  33.3 10.6 %collective-permute-start.3 = (f32[2,384,64]{2,1,0:T(8,128)}, f32[2,384,64]{2,1,0:T(8,128)}, u32[]{:S(2)}, u32[]{:S(2)}) collective-permute-start(f32[2,384,64]{2,1,0:T(8,128)} %get-tuple-element.33), channel_id=1, source_target_pairs={{1,0},{2,1},{3,2},{4,3},{5,4},{6,5},{7,6},{8,7},{9,8},{10,9},{11,1... | collective-permute-start | bytes 589832 | tf_op jit(solution)/shard_map/ppermute | solution.py:25
  45.7 1.6 copy-start.6
  47.4 5.3 %copy-start.4 = (bf16[1,256,2,256]{3,1,2,0:T(8,128)(2,1)S(1)}, bf16[1,256,2,256]{3,1,2,0:T(8,128)(2,1)}, u32[]{:S(2)}) copy-start(bf16[1,256,2,256]{3,1,2,0:T(8,128)(2,1)} %get-tuple-element.47) | copy-start | bytes 786436
  67.1 26.8 %copy-start = (f32[2,3,256,256]{3,2,1,0:T(8,128)S(1)}, f32[2,3,256,256]{3,2,1,0:T(8,128)}, u32[]{:S(2)}) copy-start(f32[2,3,256,256]{3,2,1,0:T(8,128)} %param.5) | copy-start | bytes 4718596
  67.2 9.4 %collective-permute-start.4 = (f32[2,384,64]{2,1,0:T(8,128)S(1)}, f32[2,384,64]{2,1,0:T(8,128)S(1)}, u32[]{:S(2)}, u32[]{:S(2)}) collective-permute-start(f32[2,384,64]{2,1,0:T(8,128)S(1)} %get-tuple-element.25), channel_id=1, source_target_pairs={{0,1},{1,2},{2,3},{3,4},{4,5},{5,6},{6,7},{7,8},{8,9},{9,10},{10,1... | collective-permute-start | bytes 589832 | tf_op jit(solution)/shard_map/ppermute | solution.py:22
  71.9 10.3 %collective-permute-start.5 = (f32[2,384,64]{2,1,0:T(8,128)S(1)}, f32[2,384,64]{2,1,0:T(8,128)S(1)}, u32[]{:S(2)}, u32[]{:S(2)}) collective-permute-start(f32[2,384,64]{2,1,0:T(8,128)S(1)} %get-tuple-element.26), channel_id=1, source_target_pairs={{1,0},{2,1},{3,2},{4,3},{5,4},{6,5},{7,6},{8,7},{9,8},{10,9},{11,1... | collective-permute-start | bytes 589832 | tf_op jit(solution)/shard_map/ppermute | solution.py:25
  84.4 11.3 %collective-permute-start.6 = (f32[2,64,256]{2,1,0:T(8,128)S(1)}, f32[2,64,256]{2,1,0:T(8,128)S(1)}, u32[]{:S(2)}, u32[]{:S(2)}) collective-permute-start(f32[2,64,256]{2,1,0:T(8,128)S(1)} %get-tuple-element.31), channel_id=1, source_target_pairs={{0,32},{32,64},{64,96},{96,128},{128,160},{160,192},{192,224},{224... | collective-permute-start | bytes 393224 | tf_op jit(solution)/shard_map/ppermute | solution.py:22
  86.4 9.6 %collective-permute-start.7 = (f32[2,64,256]{2,1,0:T(8,128)S(1)}, f32[2,64,256]{2,1,0:T(8,128)S(1)}, u32[]{:S(2)}, u32[]{:S(2)}) collective-permute-start(f32[2,64,256]{2,1,0:T(8,128)S(1)} %get-tuple-element.32), channel_id=1, source_target_pairs={{32,0},{64,32},{96,64},{128,96},{160,128},{192,160},{224,192},{256... | collective-permute-start | bytes 393224 | tf_op jit(solution)/shard_map/ppermute | solution.py:25
  97.2 12.4 %collective-permute-start.8 = (f32[2,64,256]{2,1,0:T(8,128)S(1)}, f32[2,64,256]{2,1,0:T(8,128)S(1)}, u32[]{:S(2)}, u32[]{:S(2)}) collective-permute-start(f32[2,64,256]{2,1,0:T(8,128)S(1)} %get-tuple-element.37), channel_id=1, source_target_pairs={{0,32},{32,64},{64,96},{96,128},{128,160},{160,192},{192,224},{224... | collective-permute-start | bytes 393224 | tf_op jit(solution)/shard_map/ppermute | solution.py:22
  99.1 11.3 %collective-permute-start.9 = (f32[2,64,256]{2,1,0:T(8,128)S(1)}, f32[2,64,256]{2,1,0:T(8,128)S(1)}, u32[]{:S(2)}, u32[]{:S(2)}) collective-permute-start(f32[2,64,256]{2,1,0:T(8,128)S(1)} %get-tuple-element.38), channel_id=1, source_target_pairs={{32,0},{64,32},{96,64},{128,96},{160,128},{192,160},{224,192},{256... | collective-permute-start | bytes 393224 | tf_op jit(solution)/shard_map/ppermute | solution.py:25
  110.6 8.8 %collective-permute-start.10 = (f32[2,384,64]{2,1,0:T(8,128)S(1)}, f32[2,384,64]{2,1,0:T(8,128)S(1)}, u32[]{:S(2)}, u32[]{:S(2)}) collective-permute-start(f32[2,384,64]{2,1,0:T(8,128)S(1)} %get-tuple-element.30), channel_id=1, source_target_pairs={{0,1},{1,2},{2,3},{3,4},{4,5},{5,6},{6,7},{7,8},{8,9},{9,10},{10,1... | collective-permute-start | bytes 589832 | tf_op jit(solution)/shard_map/ppermute | solution.py:22
  114.7 10.3 %collective-permute-start.11 = (f32[2,384,64]{2,1,0:T(8,128)S(1)}, f32[2,384,64]{2,1,0:T(8,128)S(1)}, u32[]{:S(2)}, u32[]{:S(2)}) collective-permute-start(f32[2,384,64]{2,1,0:T(8,128)S(1)} %get-tuple-element.29), channel_id=1, source_target_pairs={{1,0},{2,1},{3,2},{4,3},{5,4},{6,5},{7,6},{8,7},{9,8},{10,9},{11,1... | collective-permute-start | bytes 589832 | tf_op jit(solution)/shard_map/ppermute | solution.py:25
  126.0 1.6 copy-start.7
  126.0 1.6 copy-start.8
  127.6 5.3 %copy-start.3 = (bf16[1,256,2,256]{3,1,2,0:T(8,128)(2,1)S(1)}, bf16[1,256,2,256]{3,1,2,0:T(8,128)(2,1)}, u32[]{:S(2)}) copy-start(bf16[1,256,2,256]{3,1,2,0:T(8,128)(2,1)} %copy-done.2) | copy-start | bytes 786436
  127.6 5.3 %copy-start.5 = (bf16[1,256,2,256]{3,1,2,0:T(8,128)(2,1)S(1)}, bf16[1,256,2,256]{3,1,2,0:T(8,128)(2,1)}, u32[]{:S(2)}) copy-start(bf16[1,256,2,256]{3,1,2,0:T(8,128)(2,1)} %get-tuple-element.47) | copy-start | bytes 786436
  146.7 7.1 %collective-permute-start.12 = (f32[2,384,64]{2,1,0:T(8,128)S(1)}, f32[2,384,64]{2,1,0:T(8,128)S(1)}, u32[]{:S(2)}, u32[]{:S(2)}) collective-permute-start(f32[2,384,64]{2,1,0:T(8,128)S(1)} %get-tuple-element.23), channel_id=1, source_target_pairs={{0,1},{1,2},{2,3},{3,4},{4,5},{5,6},{6,7},{7,8},{8,9},{9,10},{10,1... | collective-permute-start | bytes 589832 | tf_op jit(solution)/shard_map/ppermute | solution.py:22
  149.0 10.3 %collective-permute-start.13 = (f32[2,384,64]{2,1,0:T(8,128)S(1)}, f32[2,384,64]{2,1,0:T(8,128)S(1)}, u32[]{:S(2)}, u32[]{:S(2)}) collective-permute-start(f32[2,384,64]{2,1,0:T(8,128)S(1)} %get-tuple-element.24), channel_id=1, source_target_pairs={{1,0},{2,1},{3,2},{4,3},{5,4},{6,5},{7,6},{8,7},{9,8},{10,9},{11,1... | collective-permute-start | bytes 589832 | tf_op jit(solution)/shard_map/ppermute | solution.py:25
  159.8 11.9 %collective-permute-start.14 = (f32[2,64,256]{2,1,0:T(8,128)S(1)}, f32[2,64,256]{2,1,0:T(8,128)S(1)}, u32[]{:S(2)}, u32[]{:S(2)}) collective-permute-start(f32[2,64,256]{2,1,0:T(8,128)S(1)} %get-tuple-element.27), channel_id=1, source_target_pairs={{0,32},{32,64},{64,96},{96,128},{128,160},{160,192},{192,224},{224... | collective-permute-start | bytes 393224 | tf_op jit(solution)/shard_map/ppermute | solution.py:22
  161.7 10.9 %collective-permute-start.15 = (f32[2,64,256]{2,1,0:T(8,128)S(1)}, f32[2,64,256]{2,1,0:T(8,128)S(1)}, u32[]{:S(2)}, u32[]{:S(2)}) collective-permute-start(f32[2,64,256]{2,1,0:T(8,128)S(1)} %get-tuple-element.28), channel_id=1, source_target_pairs={{32,0},{64,32},{96,64},{128,96},{160,128},{192,160},{224,192},{256... | collective-permute-start | bytes 393224 | tf_op jit(solution)/shard_map/ppermute | solution.py:25
where the time goes:
time: 175 us; the launch traced here: 173 us
  starting transfers between devices  72.9 us (42%)
  waiting for transfers between devices  32.5 us (19%)
  local copies, waits for them, and re-layouts  26.3 us (15%)
  other arithmetic  21.4 us (12%)
  matrix products  16.9 us (10%)
  between operations  3.55 us (2%)
    ppermute x8, starting transfers between devices, with_halo(): lax.ppermute(lax.slice_in_dim(block, 0, width, axis=dim), axis, backward)  45.9 us
    ppermute x8, starting transfers between devices, with_halo(): lax.ppermute(lax.slice_in_dim(block, block.shape[dim] - width, None, axis...  27 us
    ppermute x8, waiting for transfers between devices, with_halo(): lax.ppermute(lax.slice_in_dim(block, 0, width, axis=dim), axis, backward)  19.6 us
    dot_general x4, matrix products, transform(): jnp.einsum('qkrc,qcpv->pkrv', half_done, right_side, preferred_element_ty...  16.9 us
    dynamic_update_slice x2, local copies, waits for them, and re-layouts, on_device(): gathered = lax.dynamic_update_slice(gathered, changes[0], corners[0])  14.6 us
    ppermute x8, waiting for transfers between devices, with_halo(): lax.ppermute(lax.slice_in_dim(block, block.shape[dim] - width, None, axis...  12.9 us
  transfers between devices with their start and end apart: 16, of which 13 were waited for; matrix products, arithmetic and copies ran while one was open for 7% of the time, Pallas kernels for 0%

commit v1 on v0

--- a/solution.py
+++ b/solution.py
@@ -13,18 +13,7 @@
 AMPLITUDE_FLOOR = 0.5
 EPSILON = 1e-06
 
-
-def with_halo(block, sides, width):
-    for axis, dim in sides:
-        count = lax.axis_size(axis)
-        forward = [(i, i + 1) for i in range(count - 1)]
-        backward = [(target, source) for source, target in forward]
-        low = lax.ppermute(
-            lax.slice_in_dim(block, block.shape[dim] - width, None, axis=dim), axis, forward
-        )
-        high = lax.ppermute(lax.slice_in_dim(block, 0, width, axis=dim), axis, backward)
-        block = jnp.concatenate([low, block, high], axis=dim)
-    return block
+OFFSETS = [(a, b) for a in (-1, 0, 1) for b in (-1, 0, 1)]
 
 
 def tables(length):
@@ -75,37 +64,54 @@
     return jnp.stack([grad_re, grad_im], axis=1)
 
 
-def placed(piece, row_to, col_to, rows_all, cols_all):
-    return jnp.pad(
-        piece,
-        (
-            (0, 0),
-            (row_to, rows_all - row_to - piece.shape[1]),
-            (col_to, cols_all - col_to - piece.shape[2]),
-        ),
-    )
+def from_neighbor(x, a, b, rows, cols):
+    if b == 0:
+        pairs = [(r, r - a) for r in range(rows) if 0 <= r - a < rows]
+        return lax.ppermute(x, "row", pairs)
+    if a == 0:
+        pairs = [(c, c - b) for c in range(cols) if 0 <= c - b < cols]
+        return lax.ppermute(x, "col", pairs)
+    pairs = [
+        (r * cols + c, (r - a) * cols + (c - b))
+        for r in range(rows)
+        for c in range(cols)
+        if 0 <= r - a < rows and 0 <= c - b < cols
+    ]
+    return lax.ppermute(x, ("row", "col"), pairs)
 
 
-def fold_margins(gathered, tile_size):
-    extent = gathered.shape[1]
-    strips = jnp.concatenate([gathered[:, :, :M], gathered[:, :, tile_size + M :]], axis=2)
-    across = with_halo(strips, (("col", 2),), M)
-    inner = (
-        gathered[:, :, M : tile_size + M]
-        + placed(across[:, :, :M], 0, 0, extent, tile_size)
-        + placed(across[:, :, 3 * M :], 0, tile_size - M, extent, tile_size)
-    )
-    bands = jnp.concatenate([inner[:, :M], inner[:, tile_size + M :]], axis=1)
-    downward = with_halo(bands, (("row", 1),), M)
-    return (
-        inner[:, M : tile_size + M]
-        + placed(downward[:, :M], 0, 0, tile_size, tile_size)
-        + placed(downward[:, 3 * M :], tile_size - M, 0, tile_size, tile_size)
-    )
+def overlap(a, step, src_origin, src_size, dst_origin, dst_size):
+    low = max(a * step + src_origin, dst_origin)
+    high = min(a * step + src_origin + src_size, dst_origin + dst_size)
+    shift = a * step + src_origin
+    return (low - shift, high - shift), (low - dst_origin, high - dst_origin)
 
 
-def widen(current):
-    return with_halo(current, (("row", 1), ("col", 2)), M)
+def neighbor_sum(frame, step, src_origin, dst_origin, dst_size):
+    rows = lax.axis_size("row")
+    cols = lax.axis_size("col")
+    src_size = frame.shape[1]
+    total = None
+    for a, b in OFFSETS:
+        (r0, r1), (p0, p1) = overlap(a, step, src_origin, src_size, dst_origin, dst_size)
+        (c0, c1), (q0, q1) = overlap(b, step, src_origin, src_size, dst_origin, dst_size)
+        piece = frame[:, r0:r1, c0:c1]
+        if (a, b) != (0, 0):
+            piece = from_neighbor(piece, a, b, rows, cols)
+        piece = jnp.pad(piece, ((0, 0), (p0, dst_size - p1), (q0, dst_size - q1)))
+        total = piece if total is None else total + piece
+    return total
+
+
+def inside_mask(extent, tile_size):
+    rows = lax.axis_size("row")
+    cols = lax.axis_size("col")
+    i = lax.axis_index("row")
+    j = lax.axis_index("col")
+    pixel = jnp.arange(extent, dtype=jnp.int32)
+    row_ok = ((pixel >= M) | (i > 0)) & ((pixel < tile_size + M) | (i < rows - 1))
+    col_ok = ((pixel >= M) | (j > 0)) & ((pixel < tile_size + M) | (j < cols - 1))
+    return row_ok[:, None] & col_ok[None, :]
 
 
 def on_device(object_planes, probe_modes, positions, amplitudes):
@@ -118,26 +124,24 @@
     offsets = positions.reshape(-1, 2)
     measured = amplitudes.reshape(-1, W, W)
     tile_size = object_planes.shape[1]
-    anchor_zero = jnp.zeros((), jnp.int32)
-    current = object_planes
-    extended = widen(current)
+    extent = tile_size + 2 * M
+    place = extent - W
+    zero = jnp.zeros((), jnp.int32)
+    corner = (zero, offsets[0, 0] + M, offsets[0, 1] + M)
+    spread = (zero, place - M - offsets[0, 0], place - M - offsets[0, 1])
+    extended = neighbor_sum(object_planes, tile_size, M, 0, extent)
     for update in range(ITERS):
-        corners = [(anchor_zero, offsets[0, 0] + M, offsets[0, 1] + M)]
-        windows = jnp.stack([lax.dynamic_slice(extended, corner, (2, W, W)) for corner in corners])
-        changes = pattern_gradient(windows, measured, probe_re, probe_im, forward, inverse)
-        gathered = jnp.zeros_like(extended)
-        gathered = lax.dynamic_update_slice(gathered, changes[0], corners[0])
+        windows = lax.dynamic_slice(extended, corner, (2, W, W))[None]
+        change = pattern_gradient(windows, measured, probe_re, probe_im, forward, inverse)[0]
+        padded = jnp.pad(change, ((0, 0), (place, place), (place, place)))
+        gathered = lax.dynamic_slice(padded, spread, (2, extent, extent))
         if update + 1 < ITERS:
-            current = (
-                extended[:, M : M + tile_size, M : M + tile_size]
-                + fold_margins(gathered, tile_size) / peak_power
-            )
-            extended = widen(current)
+            total = neighbor_sum(gathered, tile_size, 0, 0, extent)
+            mask = inside_mask(extent, tile_size)
+            extended = jnp.where(mask[None], extended + total / peak_power, 0.0)
         else:
-            current = (
-                extended[:, M : M + tile_size, M : M + tile_size]
-                + fold_margins(gathered, tile_size) / peak_power
-            )
+            total = neighbor_sum(gathered, tile_size, 0, M, tile_size)
+            current = extended[:, M : M + tile_size, M : M + tile_size] + total / peak_power
     return current
 
 

time: 175 us -> 201 us (1.15)
  the two profiles are of different devices: /device:TPU:87 before, /device:TPU:80 now
where the time goes in v1:
time: 201 us; the launch traced here: 200 us
  starting transfers between devices  109 us (54%)
  waiting for transfers between devices  33.8 us (17%)
  other arithmetic  18.2 us (9%)
  local copies, waits for them, and re-layouts  17 us (8%)
  matrix products  15.2 us (8%)
  between operations  6.42 us (3%)
    ppermute x12, starting transfers between devices, from_neighbor(): return lax.ppermute(x, ('row', 'col'), pairs)  60.1 us
    ppermute x12, waiting for transfers between devices, from_neighbor(): return lax.ppermute(x, ('row', 'col'), pairs)  33.8 us
    ppermute x6, starting transfers between devices, from_neighbor(): return lax.ppermute(x, 'row', pairs)  25.9 us
    ppermute x6, starting transfers between devices, from_neighbor(): return lax.ppermute(x, 'col', pairs)  23.1 us
    dot_general x4, matrix products, transform(): jnp.einsum('qkrc,qcpv->pkrv', half_done, right_side, preferred_element_ty...  15.2 us
    slice x9, local copies, waits for them, and re-layouts, neighbor_sum(): piece = frame[:, r0:r1, c0:c1]  6.49 us
    unnamed x52, local copies, waits for them, and re-layouts  4.72 us
  transfers between devices with their start and end apart: 24, of which 6 were waited for; matrix products, arithmetic and copies ran while one was open for 6% of the time, Pallas kernels for 0%

profile of v1, /device:TPU:80, one launch (start us, length us, event | category | flops | bytes accessed | tf_op | source)
XLA Modules:
  0.0 199.7 jit_solution(17011388360062620287)
XLA Ops:
  0.0 1.4 copy.55
  2.0 4.6 %collective-permute-start = (f32[2,64,64]{1,2,0:T(8,128)S(1)}, f32[2,64,64]{1,2,0:T(8,128)S(1)}, u32[]{:S(2)}, u32[]{:S(2)}) collective-permute-start(f32[2,64,64]{1,2,0:T(8,128)S(1)} %get-tuple-element.43), channel_id=1, source_target_pairs={{0,33},{1,34},{2,35},{3,36},{4,37},{5,38},{6,39},{7,40},{8,41},{9,... | collective-permute-start | bytes 98312 | tf_op jit(solution)/shard_map/ppermute | solution.py:80
  6.6 8.5 %collective-permute-start.2 = (f32[2,64,64]{1,2,0:T(8,128)S(1)}, f32[2,64,64]{1,2,0:T(8,128)S(1)}, u32[]{:S(2)}, u32[]{:S(2)}) collective-permute-start(f32[2,64,64]{1,2,0:T(8,128)S(1)} %get-tuple-element.46), channel_id=1, source_target_pairs={{1,32},{2,33},{3,34},{4,35},{5,36},{6,37},{7,38},{8,39},{9,40},{10... | collective-permute-start | bytes 98312 | tf_op jit(solution)/shard_map/ppermute | solution.py:80
  15.1 8.0 %collective-permute-start.5 = (f32[2,64,64]{1,2,0:T(8,128)S(1)}, f32[2,64,64]{1,2,0:T(8,128)S(1)}, u32[]{:S(2)}, u32[]{:S(2)}) collective-permute-start(f32[2,64,64]{1,2,0:T(8,128)S(1)} %get-tuple-element.45), channel_id=1, source_target_pairs={{32,1},{33,2},{34,3},{35,4},{36,5},{37,6},{38,7},{39,8},{40,9},{41... | collective-permute-start | bytes 98312 | tf_op jit(solution)/shard_map/ppermute | solution.py:80
  24.0 1.9 collective-permute-start.1
  25.9 8.1 %collective-permute-start.6 = (f32[2,64,256]{1,2,0:T(8,128)}, f32[2,64,256]{1,2,0:T(8,128)S(1)}, u32[]{:S(2)}, u32[]{:S(2)}) collective-permute-start(f32[2,64,256]{1,2,0:T(8,128)} %get-tuple-element.48), channel_id=1, source_target_pairs={{32,0},{64,32},{96,64},{128,96},{160,128},{192,160},{224,192},{256... | collective-permute-start | bytes 393224 | tf_op jit(solution)/shard_map/ppermute | solution.py:70
  37.8 1.1 fusion.62
  39.0 3.0 %collective-permute-start.3 = (f32[2,256,64]{1,2,0:T(8,128)}, f32[2,256,64]{1,2,0:T(8,128)S(1)}, u32[]{:S(2)}, u32[]{:S(2)}) collective-permute-start(f32[2,256,64]{1,2,0:T(8,128)} %get-tuple-element.49), channel_id=1, source_target_pairs={{0,1},{1,2},{2,3},{3,4},{4,5},{5,6},{6,7},{7,8},{8,9},{9,10},{10,1... | collective-permute-start | bytes 393224 | tf_op jit(solution)/shard_map/ppermute | solution.py:73
  42.0 4.8 %collective-permute-start.4 = (f32[2,256,64]{1,2,0:T(8,128)}, f32[2,256,64]{1,2,0:T(8,128)}, u32[]{:S(2)}, u32[]{:S(2)}) collective-permute-start(f32[2,256,64]{1,2,0:T(8,128)} %get-tuple-element.50), channel_id=1, source_target_pairs={{1,0},{2,1},{3,2},{4,3},{5,4},{6,5},{7,6},{8,7},{9,8},{10,9},{11,1... | collective-permute-start | bytes 393224 | tf_op jit(solution)/shard_map/ppermute | solution.py:73
  46.8 1.1 maximum_bitcast_fusion.4
  48.0 2.1 %collective-permute-start.7 = (f32[2,64,64]{1,2,0:T(8,128)}, f32[2,64,64]{1,2,0:T(8,128)}, u32[]{:S(2)}, u32[]{:S(2)}) collective-permute-start(f32[2,64,64]{1,2,0:T(8,128)} %get-tuple-element.44), channel_id=1, source_target_pairs={{33,0},{34,1},{35,2},{36,3},{37,4},{38,5},{39,6},{40,7},{41,8},{42... | collective-permute-start | bytes 98312 | tf_op jit(solution)/shard_map/ppermute | solution.py:80
  56.2 1.1 copy.72
  57.4 1.6 pad_add_fusion
  60.3 1.1 copy.67
  61.4 1.6 convert_bitcast_fusion.3
  63.0 4.3 %fusion.2 = (f32[256,256]{0,1:T(8,128)}, f32[2,256,3,256,1]{3,1,4,2,0:T(8,128)}) fusion(bf16[1,1,3,256,256]{3,4,0,2,1:T(8,128)(2,1)} %get-tuple-element.19, bf16[1,1,3,256,256]{3,4,0,2,1:T(8,128)(2,1)} %get-tuple-element.13, bf16[1,256,2,256]{3,1,2,0:T(8,128)(2,1)S(1)} %copy-done.16, bf16[1,256,2,256]{3,1,2,0:T(8,128)(2,1)S(1)} %copy-done.13, ...), kind=kOutput, calls=%fused_computation.29 | convolution fusion | flops 809041920 | bytes 3670016 | tf_op jit(solution)/shard_map/qkrc,qcpv->pkrv/dot_general | solution.py:44
  67.3 1.0 fusion.49
  68.4 4.2 %maximum_subtract_fusion = f32[2,3,256,256]{2,3,1,0:T(8,128)} fusion(f32[1,3,256,256]{2,3,1,0:T(8,128)} %get-tuple-element.20, f32[1,3,256,256]{2,3,1,0:T(8,128)} %get-tuple-element.14, bf16[2,256,2,256,1]{3,1,2,0,4:T(8,128)(2,1)} %get-tuple-element.63, bf16[1,256,2,256]{3,1,2,0:T(8,128)(2,1)S(1)} %copy-done.8, bf16[1,256,2,256]{3,1,2,0:T(8,128)(2,1)S(1)} %copy-done.11, ...), kind=kOutput, calls=%fused_computation.18 | convolution fusion | flops 808321024 | bytes 6029312 | tf_op jit(solution)/shard_map/qkrc,qcpv->pkrv/dot_general | solution.py:44
  72.6 1.7 add_reduce_fusion.1
  74.3 1.3 pad_dynamic-slice_fusion.4
  75.6 2.1 %collective-permute-start.11 = (f32[2,384,128]{1,2,0:T(8,128)}, f32[2,384,128]{1,2,0:T(8,128)}, u32[]{:S(2)}, u32[]{:S(2)}) collective-permute-start(f32[2,384,128]{1,2,0:T(8,128)} %get-tuple-element.39), channel_id=1, source_target_pairs={{0,1},{1,2},{2,3},{3,4},{4,5},{5,6},{6,7},{7,8},{8,9},{9,10},{10,1... | collective-permute-start | bytes 1179656 | tf_op jit(solution)/shard_map/ppermute | solution.py:73
  77.7 5.6 %collective-permute-start.12 = (f32[2,384,128]{1,2,0:T(8,128)}, f32[2,384,128]{1,2,0:T(8,128)}, u32[]{:S(2)}, u32[]{:S(2)}) collective-permute-start(f32[2,384,128]{1,2,0:T(8,128)} %get-tuple-element.40), channel_id=1, source_target_pairs={{1,0},{2,1},{3,2},{4,3},{5,4},{6,5},{7,6},{8,7},{9,8},{10,9},{11,1... | collective-permute-start | bytes 1179656 | tf_op jit(solution)/shard_map/ppermute | solution.py:73
  84.3 2.7 %collective-permute-start.10 = (f32[2,128,128]{1,2,0:T(8,128)S(1)}, f32[2,128,128]{1,2,0:T(8,128)S(1)}, u32[]{:S(2)}, u32[]{:S(2)}) collective-permute-start(f32[2,128,128]{1,2,0:T(8,128)S(1)} %get-tuple-element.36), channel_id=1, source_target_pairs={{1,32},{2,33},{3,34},{4,35},{5,36},{6,37},{7,38},{8,39},{9,40},{10... | collective-permute-start | bytes 393224 | tf_op jit(solution)/shard_map/ppermute | solution.py:80
  87.0 7.2 %collective-permute-start.13 = (f32[2,128,128]{1,2,0:T(8,128)S(1)}, f32[2,128,128]{1,2,0:T(8,128)S(1)}, u32[]{:S(2)}, u32[]{:S(2)}) collective-permute-start(f32[2,128,128]{1,2,0:T(8,128)S(1)} %get-tuple-element.35), channel_id=1, source_target_pairs={{32,1},{33,2},{34,3},{35,4},{36,5},{37,6},{38,7},{39,8},{40,9},{41... | collective-permute-start | bytes 393224 | tf_op jit(solution)/shard_map/ppermute | solution.py:80
  94.2 1.2 pad_dynamic-slice_fusion.6
  95.5 1.9 collective-permute-start.14
  97.4 3.9 %collective-permute-start.9 = (f32[2,128,384]{1,2,0:T(8,128)}, f32[2,128,384]{1,2,0:T(8,128)}, u32[]{:S(2)}, u32[]{:S(2)}) collective-permute-start(f32[2,128,384]{1,2,0:T(8,128)} %get-tuple-element.37), channel_id=1, source_target_pairs={{0,32},{32,64},{64,96},{96,128},{128,160},{160,192},{192,224},{224... | collective-permute-start | bytes 1179656 | tf_op jit(solution)/shard_map/ppermute | solution.py:70
  102.0 15.0 %collective-permute-start.15 = (f32[2,128,128]{1,2,0:T(8,128)}, f32[2,128,128]{1,2,0:T(8,128)}, u32[]{:S(2)}, u32[]{:S(2)}) collective-permute-start(f32[2,128,128]{1,2,0:T(8,128)} %get-tuple-element.34), channel_id=1, source_target_pairs={{33,0},{34,1},{35,2},{36,3},{37,4},{38,5},{39,6},{40,7},{41,8},{42... | collective-permute-start | bytes 393224 | tf_op jit(solution)/shard_map/ppermute | solution.py:80
  118.7 1.2 collective-permute-done.15
  119.9 2.1 %collective-permute-start.8 = (f32[2,128,128]{1,2,0:T(8,128)}, f32[2,128,128]{1,2,0:T(8,128)S(1)}, u32[]{:S(2)}, u32[]{:S(2)}) collective-permute-start(f32[2,128,128]{1,2,0:T(8,128)} %get-tuple-element.33), channel_id=1, source_target_pairs={{0,33},{1,34},{2,35},{3,36},{4,37},{5,38},{6,39},{7,40},{8,41},{9,... | collective-permute-start | bytes 393224 | tf_op jit(solution)/shard_map/ppermute | solution.py:80
  122.1 12.8 %collective-permute-done.8 = f32[2,128,128]{1,2,0:T(8,128)S(1)} collective-permute-done((f32[2,128,128]{1,2,0:T(8,128)}, f32[2,128,128]{1,2,0:T(8,128)S(1)}, u32[]{:S(2)}, u32[]{:S(2)}) %collective-permute-start.8) | collective-permute-done | bytes 131104 | tf_op jit(solution)/shard_map/ppermute | solution.py:80
  134.9 2.7 %fusion.15 = f32[2,384,384]{1,2,0:T(8,128)S(1)} fusion(f32[2,128,128]{1,2,0:T(8,128)} %collective-permute-done.15, f32[2,128,384]{1,2,0:T(8,128)} %collective-permute-done.14, f32[2,128,128]{1,2,0:T(8,128)} %copy-done.22, f32[2,384,128]{1,2,0:T(8,128)} %collective-permute-done.12, s32[]{:T(128)S(6)} %select_n.60, s32[]{:T(128)S(6)} %select_n.61, ...), kind=kLoop, calls=%fused_computation.45 | loop fusion | flops 5603328 | bytes 5128204 | tf_op jit(solution)/shard_map/jit(_where)/select_n | solution.py:141
  139.4 1.6 convert_bitcast_fusion.1
  141.0 3.5 %fusion = (f32[256,256]{0,1:T(8,128)S(1)}, f32[2,256,3,256,1]{3,1,4,2,0:T(8,128)}) fusion(bf16[1,256,2,256]{3,1,2,0:T(8,128)(2,1)S(1)} %copy-done.17, bf16[1,256,2,256]{3,1,2,0:T(8,128)(2,1)S(1)} %copy-done.14, bf16[2,256,2,256,1]{3,1,2,0,4:T(8,128)(2,1)} %get-tuple-element.64, bf16[1,1,3,256,256]{3,4,2,1,0:T(8,128)(2,1)} %get-tuple-element.17, ...), kind=kOutput, calls=%fused_computation.23 | convolution fusion | flops 807862272 | bytes 3670016 | tf_op jit(solution)/shard_map/qkrc,qcpv->pkrv/dot_general | solution.py:44
  145.4 3.2 %maximum_subtract_fusion.1 = f32[2,3,256,256]{2,3,1,0:T(8,128)S(1)} fusion(f32[1,3,256,256]{2,3,1,0:T(8,128)} %get-tuple-element.18, f32[1,3,256,256]{2,3,1,0:T(8,128)} %get-tuple-element.10, bf16[2,256,2,256,1]{3,1,2,0,4:T(8,128)(2,1)} %get-tuple-element.63, bf16[1,256,2,256]{3,1,2,0:T(8,128)(2,1)S(1)} %copy-done.9, ...), kind=kOutput, calls=%fused_computation.19 | convolution fusion | flops 808321024 | bytes 6029312 | tf_op jit(solution)/shard_map/qkrc,qcpv->pkrv/dot_general | solution.py:44
  149.2 1.9 collective-permute-start.17
  151.1 8.1 %collective-permute-start.22 = (f32[2,64,256]{1,2,0:T(8,128)S(1)}, f32[2,64,256]{1,2,0:T(8,128)S(1)}, u32[]{:S(2)}, u32[]{:S(2)}) collective-permute-start(f32[2,64,256]{1,2,0:T(8,128)S(1)} %get-tuple-element.28), channel_id=1, source_target_pairs={{32,0},{64,32},{96,64},{128,96},{160,128},{192,160},{224,192},{256... | collective-permute-start | bytes 393224 | tf_op jit(solution)/shard_map/ppermute | solution.py:70
  159.5 1.9 collective-permute-start.16
  161.6 1.9 collective-permute-start.19
  163.5 5.8 %collective-permute-start.20 = (f32[2,256,64]{1,2,0:T(8,128)S(1)}, f32[2,256,64]{1,2,0:T(8,128)S(1)}, u32[]{:S(2)}, u32[]{:S(2)}) collective-permute-start(f32[2,256,64]{1,2,0:T(8,128)S(1)} %get-tuple-element.30), channel_id=1, source_target_pairs={{1,0},{2,1},{3,2},{4,3},{5,4},{6,5},{7,6},{8,7},{9,8},{10,9},{11,1... | collective-permute-start | bytes 393224 | tf_op jit(solution)/shard_map/ppermute | solution.py:73
  169.3 3.4 %collective-permute-done.16 = f32[2,64,64]{1,2,0:T(8,128)S(1)} collective-permute-done((f32[2,64,64]{1,2,0:T(8,128)S(1)}, f32[2,64,64]{1,2,0:T(8,128)S(1)}, u32[]{:S(2)}, u32[]{:S(2)}) %collective-permute-start.16) | collective-permute-done | bytes 32800 | tf_op jit(solution)/shard_map/ppermute | solution.py:80
  172.7 1.9 collective-permute-start.18
  174.6 7.9 %collective-permute-done.18 = f32[2,64,64]{1,2,0:T(8,128)S(1)} collective-permute-done((f32[2,64,64]{1,2,0:T(8,128)S(1)}, f32[2,64,64]{1,2,0:T(8,128)S(1)}, u32[]{:S(2)}, u32[]{:S(2)}) %collective-permute-start.18) | collective-permute-done | bytes 32800 | tf_op jit(solution)/shard_map/ppermute | solution.py:80
  182.4 1.9 collective-permute-start.21
  184.4 6.7 %collective-permute-done.21 = f32[2,64,64]{1,2,0:T(8,128)S(1)} collective-permute-done((f32[2,64,64]{1,2,0:T(8,128)S(1)}, f32[2,64,64]{1,2,0:T(8,128)S(1)}, u32[]{:S(2)}, u32[]{:S(2)}) %collective-permute-start.21) | collective-permute-done | bytes 32800 | tf_op jit(solution)/shard_map/ppermute | solution.py:80
  191.0 4.2 %collective-permute-start.23 = (f32[2,64,64]{1,2,0:T(8,128)S(1)}, f32[2,64,64]{1,2,0:T(8,128)S(1)}, u32[]{:S(2)}, u32[]{:S(2)}) collective-permute-start(f32[2,64,64]{1,2,0:T(8,128)S(1)} %get-tuple-element.24), channel_id=1, source_target_pairs={{33,0},{34,1},{35,2},{36,3},{37,4},{38,5},{39,6},{40,7},{41,8},{42... | collective-permute-start | bytes 98312 | tf_op jit(solution)/shard_map/ppermute | solution.py:80
  195.2 1.9 collective-permute-done.23
  197.1 1.6 fusion.36
  (98 shorter events, 15.1 us)
Async XLA Ops:
  0.0 37.8 %copy-start = (f32[2,3,256,256]{3,2,1,0:T(8,128)S(1)}, f32[2,3,256,256]{3,2,1,0:T(8,128)}, u32[]{:S(2)}) copy-start(f32[2,3,256,256]{3,2,1,0:T(8,128)} %param.5) | copy-start | bytes 4718596
  2.0 36.9 %collective-permute-start = (f32[2,64,64]{1,2,0:T(8,128)S(1)}, f32[2,64,64]{1,2,0:T(8,128)S(1)}, u32[]{:S(2)}, u32[]{:S(2)}) collective-permute-start(f32[2,64,64]{1,2,0:T(8,128)S(1)} %get-tuple-element.43), channel_id=1, source_target_pairs={{0,33},{1,34},{2,35},{3,36},{4,37},{5,38},{6,39},{7,40},{8,41},{9,... | collective-permute-start | bytes 98312 | tf_op jit(solution)/shard_map/ppermute | solution.py:80
  6.6 35.4 %collective-permute-start.2 = (f32[2,64,64]{1,2,0:T(8,128)S(1)}, f32[2,64,64]{1,2,0:T(8,128)S(1)}, u32[]{:S(2)}, u32[]{:S(2)}) collective-permute-start(f32[2,64,64]{1,2,0:T(8,128)S(1)} %get-tuple-element.46), channel_id=1, source_target_pairs={{1,32},{2,33},{3,34},{4,35},{5,36},{6,37},{7,38},{8,39},{9,40},{10... | collective-permute-start | bytes 98312 | tf_op jit(solution)/shard_map/ppermute | solution.py:80
  15.1 32.8 %collective-permute-start.5 = (f32[2,64,64]{1,2,0:T(8,128)S(1)}, f32[2,64,64]{1,2,0:T(8,128)S(1)}, u32[]{:S(2)}, u32[]{:S(2)}) collective-permute-start(f32[2,64,64]{1,2,0:T(8,128)S(1)} %get-tuple-element.45), channel_id=1, source_target_pairs={{32,1},{33,2},{34,3},{35,4},{36,5},{37,6},{38,7},{39,8},{40,9},{41... | collective-permute-start | bytes 98312 | tf_op jit(solution)/shard_map/ppermute | solution.py:80
  24.0 33.3 %collective-permute-start.1 = (f32[2,64,256]{1,2,0:T(8,128)}, f32[2,64,256]{1,2,0:T(8,128)S(1)}, u32[]{:S(2)}, u32[]{:S(2)}) collective-permute-start(f32[2,64,256]{1,2,0:T(8,128)} %get-tuple-element.47), channel_id=1, source_target_pairs={{0,32},{32,64},{64,96},{96,128},{128,160},{160,192},{192,224},{224... | collective-permute-start | bytes 393224 | tf_op jit(solution)/shard_map/ppermute | solution.py:70
  25.9 31.4 %collective-permute-start.6 = (f32[2,64,256]{1,2,0:T(8,128)}, f32[2,64,256]{1,2,0:T(8,128)S(1)}, u32[]{:S(2)}, u32[]{:S(2)}) collective-permute-start(f32[2,64,256]{1,2,0:T(8,128)} %get-tuple-element.48), channel_id=1, source_target_pairs={{32,0},{64,32},{96,64},{128,96},{160,128},{192,160},{224,192},{256... | collective-permute-start | bytes 393224 | tf_op jit(solution)/shard_map/ppermute | solution.py:70
  38.8 11.2 %copy-start.23 = (s32[1,1,1,2]{3,2,1,0:T(1,128)S(1)}, s32[1,1,1,2]{3,2,1,0:T(1,128)}, u32[]{:S(2)}) copy-start(s32[1,1,1,2]{3,2,1,0:T(1,128)} %param.6) | copy-start | bytes 28
  38.8 16.8 %copy-start.3 = (f32[1,3,256,256]{3,2,1,0:T(8,128)S(1)}, f32[1,3,256,256]{3,2,1,0:T(8,128)}, u32[]{:S(2)}) copy-start(f32[1,3,256,256]{3,2,1,0:T(8,128)} %get-tuple-element.21) | copy-start | bytes 2359300
  38.9 7.9 %copy-start.7 = (bf16[1,256,2,256]{3,1,2,0:T(8,128)(2,1)}, bf16[1,256,2,256]{3,1,2,0:T(8,128)(2,1)S(1)}, u32[]{:S(2)}) copy-start(bf16[1,256,2,256]{3,1,2,0:T(8,128)(2,1)S(1)} %get-tuple-element.52) | copy-start | bytes 786436
  38.9 9.0 %copy-start.10 = (bf16[1,256,2,256]{3,1,2,0:T(8,128)(2,1)}, bf16[1,256,2,256]{3,1,2,0:T(8,128)(2,1)S(1)}, u32[]{:S(2)}) copy-start(bf16[1,256,2,256]{3,1,2,0:T(8,128)(2,1)S(1)} %get-tuple-element.55) | copy-start | bytes 786436
  38.9 9.0 %copy-start.12 = (bf16[1,256,2,256]{3,1,2,0:T(8,128)(2,1)}, bf16[1,256,2,256]{3,1,2,0:T(8,128)(2,1)S(1)}, u32[]{:S(2)}) copy-start(bf16[1,256,2,256]{3,1,2,0:T(8,128)(2,1)S(1)} %get-tuple-element.51) | copy-start | bytes 786436
  38.9 9.0 %copy-start.15 = (bf16[1,256,2,256]{3,1,2,0:T(8,128)(2,1)}, bf16[1,256,2,256]{3,1,2,0:T(8,128)(2,1)S(1)}, u32[]{:S(2)}) copy-start(bf16[1,256,2,256]{3,1,2,0:T(8,128)(2,1)S(1)} %get-tuple-element.56) | copy-start | bytes 786436
  39.0 11.1 %copy-start.18 = (f32[2,64,64]{1,2,0:T(8,128)}, f32[2,64,64]{1,2,0:T(8,128)S(1)}, u32[]{:S(2)}) copy-start(f32[2,64,64]{1,2,0:T(8,128)S(1)} %collective-permute-done) | copy-start | bytes 98308
  39.0 18.4 %collective-permute-start.3 = (f32[2,256,64]{1,2,0:T(8,128)}, f32[2,256,64]{1,2,0:T(8,128)S(1)}, u32[]{:S(2)}, u32[]{:S(2)}) collective-permute-start(f32[2,256,64]{1,2,0:T(8,128)} %get-tuple-element.49), channel_id=1, source_target_pairs={{0,1},{1,2},{2,3},{3,4},{4,5},{5,6},{6,7},{7,8},{8,9},{9,10},{10,1... | collective-permute-start | bytes 393224 | tf_op jit(solution)/shard_map/ppermute | solution.py:73
  42.0 8.0 %copy-start.19 = (f32[2,64,64]{1,2,0:T(8,128)}, f32[2,64,64]{1,2,0:T(8,128)S(1)}, u32[]{:S(2)}) copy-start(f32[2,64,64]{1,2,0:T(8,128)S(1)} %collective-permute-done.2) | copy-start | bytes 98308
  42.0 15.3 %collective-permute-start.4 = (f32[2,256,64]{1,2,0:T(8,128)}, f32[2,256,64]{1,2,0:T(8,128)}, u32[]{:S(2)}, u32[]{:S(2)}) collective-permute-start(f32[2,256,64]{1,2,0:T(8,128)} %get-tuple-element.50), channel_id=1, source_target_pairs={{1,0},{2,1},{3,2},{4,3},{5,4},{6,5},{7,6},{8,7},{9,8},{10,9},{11,1... | collective-permute-start | bytes 393224 | tf_op jit(solution)/shard_map/ppermute | solution.py:73
  47.9 2.8 %copy-start.20 = (f32[2,64,64]{1,2,0:T(8,128)}, f32[2,64,64]{1,2,0:T(8,128)S(1)}, u32[]{:S(2)}) copy-start(f32[2,64,64]{1,2,0:T(8,128)S(1)} %collective-permute-done.5) | copy-start | bytes 98308
  48.0 9.4 %collective-permute-start.7 = (f32[2,64,64]{1,2,0:T(8,128)}, f32[2,64,64]{1,2,0:T(8,128)}, u32[]{:S(2)}, u32[]{:S(2)}) collective-permute-start(f32[2,64,64]{1,2,0:T(8,128)} %get-tuple-element.44), channel_id=1, source_target_pairs={{33,0},{34,1},{35,2},{36,3},{37,4},{38,5},{39,6},{40,7},{41,8},{42... | collective-permute-start | bytes 98312 | tf_op jit(solution)/shard_map/ppermute | solution.py:80
  57.3 1.7 copy-start.4
  57.3 1.7 copy-start.6
  61.4 1.6 copy-start.13
  61.4 1.6 copy-start.16
  63.0 5.3 %copy-start.8 = (bf16[1,256,2,256]{3,1,2,0:T(8,128)(2,1)S(1)}, bf16[1,256,2,256]{3,1,2,0:T(8,128)(2,1)}, u32[]{:S(2)}) copy-start(bf16[1,256,2,256]{3,1,2,0:T(8,128)(2,1)} %copy-done.7) | copy-start | bytes 786436
  63.0 5.3 %copy-start.11 = (bf16[1,256,2,256]{3,1,2,0:T(8,128)(2,1)S(1)}, bf16[1,256,2,256]{3,1,2,0:T(8,128)(2,1)}, u32[]{:S(2)}) copy-start(bf16[1,256,2,256]{3,1,2,0:T(8,128)(2,1)} %copy-done.10) | copy-start | bytes 786436
  74.3 42.7 %copy-start.1 = (f32[2,3,256,256]{3,2,1,0:T(8,128)S(1)}, f32[2,3,256,256]{3,2,1,0:T(8,128)}, u32[]{:S(2)}) copy-start(f32[2,3,256,256]{3,2,1,0:T(8,128)} %param.5) | copy-start | bytes 4718596
  75.6 59.3 %collective-permute-start.11 = (f32[2,384,128]{1,2,0:T(8,128)}, f32[2,384,128]{1,2,0:T(8,128)}, u32[]{:S(2)}, u32[]{:S(2)}) collective-permute-start(f32[2,384,128]{1,2,0:T(8,128)} %get-tuple-element.39), channel_id=1, source_target_pairs={{0,1},{1,2},{2,3},{3,4},{4,5},{5,6},{6,7},{7,8},{8,9},{9,10},{10,1... | collective-permute-start | bytes 1179656 | tf_op jit(solution)/shard_map/ppermute | solution.py:73
  77.7 57.2 %collective-permute-start.12 = (f32[2,384,128]{1,2,0:T(8,128)}, f32[2,384,128]{1,2,0:T(8,128)}, u32[]{:S(2)}, u32[]{:S(2)}) collective-permute-start(f32[2,384,128]{1,2,0:T(8,128)} %get-tuple-element.40), channel_id=1, source_target_pairs={{1,0},{2,1},{3,2},{4,3},{5,4},{6,5},{7,6},{8,7},{9,8},{10,9},{11,1... | collective-permute-start | bytes 1179656 | tf_op jit(solution)/shard_map/ppermute | solution.py:73
  84.3 13.1 %collective-permute-start.10 = (f32[2,128,128]{1,2,0:T(8,128)S(1)}, f32[2,128,128]{1,2,0:T(8,128)S(1)}, u32[]{:S(2)}, u32[]{:S(2)}) collective-permute-start(f32[2,128,128]{1,2,0:T(8,128)S(1)} %get-tuple-element.36), channel_id=1, source_target_pairs={{1,32},{2,33},{3,34},{4,35},{5,36},{6,37},{7,38},{8,39},{9,40},{10... | collective-permute-start | bytes 393224 | tf_op jit(solution)/shard_map/ppermute | solution.py:80
  87.0 47.9 %copy-start.5 = (f32[2,64,256]{1,2,0:T(8,128)S(1)}, f32[2,64,256]{1,2,0:T(8,128)}, u32[]{:S(2)}) copy-start(f32[2,64,256]{1,2,0:T(8,128)} %copy-done.4) | copy-start | bytes 393220
  87.0 14.4 %collective-permute-start.13 = (f32[2,128,128]{1,2,0:T(8,128)S(1)}, f32[2,128,128]{1,2,0:T(8,128)S(1)}, u32[]{:S(2)}, u32[]{:S(2)}) collective-permute-start(f32[2,128,128]{1,2,0:T(8,128)S(1)} %get-tuple-element.35), channel_id=1, source_target_pairs={{32,1},{33,2},{34,3},{35,4},{36,5},{37,6},{38,7},{39,8},{40,9},{41... | collective-permute-start | bytes 393224 | tf_op jit(solution)/shard_map/ppermute | solution.py:80
  95.5 39.4 %collective-permute-start.14 = (f32[2,128,384]{1,2,0:T(8,128)}, f32[2,128,384]{1,2,0:T(8,128)}, u32[]{:S(2)}, u32[]{:S(2)}) collective-permute-start(f32[2,128,384]{1,2,0:T(8,128)} %get-tuple-element.38), channel_id=1, source_target_pairs={{32,0},{64,32},{96,64},{128,96},{160,128},{192,160},{224,192},{256... | collective-permute-start | bytes 1179656 | tf_op jit(solution)/shard_map/ppermute | solution.py:70
  97.4 4.0 %copy-start.21 = (f32[2,128,128]{1,2,0:T(8,128)}, f32[2,128,128]{1,2,0:T(8,128)S(1)}, u32[]{:S(2)}) copy-start(f32[2,128,128]{1,2,0:T(8,128)S(1)} %collective-permute-done.10) | copy-start | bytes 393220
  97.4 37.5 %collective-permute-start.9 = (f32[2,128,384]{1,2,0:T(8,128)}, f32[2,128,384]{1,2,0:T(8,128)}, u32[]{:S(2)}, u32[]{:S(2)}) collective-permute-start(f32[2,128,384]{1,2,0:T(8,128)} %get-tuple-element.37), channel_id=1, source_target_pairs={{0,32},{32,64},{64,96},{96,128},{128,160},{160,192},{192,224},{224... | collective-permute-start | bytes 1179656 | tf_op jit(solution)/shard_map/ppermute | solution.py:70
  101.3 0.7 copy-start.22
  102.0 17.9 %collective-permute-start.15 = (f32[2,128,128]{1,2,0:T(8,128)}, f32[2,128,128]{1,2,0:T(8,128)}, u32[]{:S(2)}, u32[]{:S(2)}) collective-permute-start(f32[2,128,128]{1,2,0:T(8,128)} %get-tuple-element.34), channel_id=1, source_target_pairs={{33,0},{34,1},{35,2},{36,3},{37,4},{38,5},{39,6},{40,7},{41,8},{42... | collective-permute-start | bytes 393224 | tf_op jit(solution)/shard_map/ppermute | solution.py:80
  119.9 15.0 %collective-permute-start.8 = (f32[2,128,128]{1,2,0:T(8,128)}, f32[2,128,128]{1,2,0:T(8,128)S(1)}, u32[]{:S(2)}, u32[]{:S(2)}) collective-permute-start(f32[2,128,128]{1,2,0:T(8,128)} %get-tuple-element.33), channel_id=1, source_target_pairs={{0,33},{1,34},{2,35},{3,36},{4,37},{5,38},{6,39},{7,40},{8,41},{9,... | collective-permute-start | bytes 393224 | tf_op jit(solution)/shard_map/ppermute | solution.py:80
  137.6 1.0 copy-start.2
  139.4 1.6 copy-start.14
  139.4 1.6 copy-start.17
  141.0 4.4 %copy-start.9 = (bf16[1,256,2,256]{3,1,2,0:T(8,128)(2,1)S(1)}, bf16[1,256,2,256]{3,1,2,0:T(8,128)(2,1)}, u32[]{:S(2)}) copy-start(bf16[1,256,2,256]{3,1,2,0:T(8,128)(2,1)} %copy-done.7) | copy-start | bytes 786436
  149.2 47.9 %collective-permute-start.17 = (f32[2,64,256]{1,2,0:T(8,128)S(1)}, f32[2,64,256]{1,2,0:T(8,128)S(1)}, u32[]{:S(2)}, u32[]{:S(2)}) collective-permute-start(f32[2,64,256]{1,2,0:T(8,128)S(1)} %get-tuple-element.27), channel_id=1, source_target_pairs={{0,32},{32,64},{64,96},{96,128},{128,160},{160,192},{192,224},{224... | collective-permute-start | bytes 393224 | tf_op jit(solution)/shard_map/ppermute | solution.py:70
  151.1 46.0 %collective-permute-start.22 = (f32[2,64,256]{1,2,0:T(8,128)S(1)}, f32[2,64,256]{1,2,0:T(8,128)S(1)}, u32[]{:S(2)}, u32[]{:S(2)}) collective-permute-start(f32[2,64,256]{1,2,0:T(8,128)S(1)} %get-tuple-element.28), channel_id=1, source_target_pairs={{32,0},{64,32},{96,64},{128,96},{160,128},{192,160},{224,192},{256... | collective-permute-start | bytes 393224 | tf_op jit(solution)/shard_map/ppermute | solution.py:70
  159.5 13.2 %collective-permute-start.16 = (f32[2,64,64]{1,2,0:T(8,128)S(1)}, f32[2,64,64]{1,2,0:T(8,128)S(1)}, u32[]{:S(2)}, u32[]{:S(2)}) collective-permute-start(f32[2,64,64]{1,2,0:T(8,128)S(1)} %get-tuple-element.23), channel_id=1, source_target_pairs={{0,33},{1,34},{2,35},{3,36},{4,37},{5,38},{6,39},{7,40},{8,41},{9,... | collective-permute-start | bytes 98312 | tf_op jit(solution)/shard_map/ppermute | solution.py:80
  161.6 35.5 %collective-permute-start.19 = (f32[2,256,64]{1,2,0:T(8,128)S(1)}, f32[2,256,64]{1,2,0:T(8,128)S(1)}, u32[]{:S(2)}, u32[]{:S(2)}) collective-permute-start(f32[2,256,64]{1,2,0:T(8,128)S(1)} %get-tuple-element.29), channel_id=1, source_target_pairs={{0,1},{1,2},{2,3},{3,4},{4,5},{5,6},{6,7},{7,8},{8,9},{9,10},{10,1... | collective-permute-start | bytes 393224 | tf_op jit(solution)/shard_map/ppermute | solution.py:73
  163.5 33.6 %collective-permute-start.20 = (f32[2,256,64]{1,2,0:T(8,128)S(1)}, f32[2,256,64]{1,2,0:T(8,128)S(1)}, u32[]{:S(2)}, u32[]{:S(2)}) collective-permute-start(f32[2,256,64]{1,2,0:T(8,128)S(1)} %get-tuple-element.30), channel_id=1, source_target_pairs={{1,0},{2,1},{3,2},{4,3},{5,4},{6,5},{7,6},{8,7},{9,8},{10,9},{11,1... | collective-permute-start | bytes 393224 | tf_op jit(solution)/shard_map/ppermute | solution.py:73
  172.7 9.8 %collective-permute-start.18 = (f32[2,64,64]{1,2,0:T(8,128)S(1)}, f32[2,64,64]{1,2,0:T(8,128)S(1)}, u32[]{:S(2)}, u32[]{:S(2)}) collective-permute-start(f32[2,64,64]{1,2,0:T(8,128)S(1)} %get-tuple-element.26), channel_id=1, source_target_pairs={{1,32},{2,33},{3,34},{4,35},{5,36},{6,37},{7,38},{8,39},{9,40},{10... | collective-permute-start | bytes 98312 | tf_op jit(solution)/shard_map/ppermute | solution.py:80
  182.4 8.6 %collective-permute-start.21 = (f32[2,64,64]{1,2,0:T(8,128)S(1)}, f32[2,64,64]{1,2,0:T(8,128)S(1)}, u32[]{:S(2)}, u32[]{:S(2)}) collective-permute-start(f32[2,64,64]{1,2,0:T(8,128)S(1)} %get-tuple-element.25), channel_id=1, source_target_pairs={{32,1},{33,2},{34,3},{35,4},{36,5},{37,6},{38,7},{39,8},{40,9},{41... | collective-permute-start | bytes 98312 | tf_op jit(solution)/shard_map/ppermute | solution.py:80
  191.0 6.1 %collective-permute-start.23 = (f32[2,64,64]{1,2,0:T(8,128)S(1)}, f32[2,64,64]{1,2,0:T(8,128)S(1)}, u32[]{:S(2)}, u32[]{:S(2)}) collective-permute-start(f32[2,64,64]{1,2,0:T(8,128)S(1)} %get-tuple-element.24), channel_id=1, source_target_pairs={{33,0},{34,1},{35,2},{36,3},{37,4},{38,5},{39,6},{40,7},{41,8},{42... | collective-permute-start | bytes 98312 | tf_op jit(solution)/shard_map/ppermute | solution.py:80

commit v2 on v1

--- a/solution.py
+++ b/solution.py
@@ -12,8 +12,6 @@
 
 AMPLITUDE_FLOOR = 0.5
 EPSILON = 1e-06
-
-OFFSETS = [(a, b) for a in (-1, 0, 1) for b in (-1, 0, 1)]
 
 
 def tables(length):
@@ -64,41 +62,25 @@
     return jnp.stack([grad_re, grad_im], axis=1)
 
 
-def from_neighbor(x, a, b, rows, cols):
-    if b == 0:
-        pairs = [(r, r - a) for r in range(rows) if 0 <= r - a < rows]
-        return lax.ppermute(x, "row", pairs)
-    if a == 0:
-        pairs = [(c, c - b) for c in range(cols) if 0 <= c - b < cols]
-        return lax.ppermute(x, "col", pairs)
-    pairs = [
-        (r * cols + c, (r - a) * cols + (c - b))
-        for r in range(rows)
-        for c in range(cols)
-        if 0 <= r - a < rows and 0 <= c - b < cols
-    ]
-    return lax.ppermute(x, ("row", "col"), pairs)
+def from_neighbor(x, axis, a):
+    count = lax.axis_size(axis)
+    pairs = [(r, r - a) for r in range(count) if 0 <= r - a < count]
+    return lax.ppermute(x, axis, pairs)
 
 
-def overlap(a, step, src_origin, src_size, dst_origin, dst_size):
-    low = max(a * step + src_origin, dst_origin)
-    high = min(a * step + src_origin + src_size, dst_origin + dst_size)
-    shift = a * step + src_origin
-    return (low - shift, high - shift), (low - dst_origin, high - dst_origin)
-
-
-def neighbor_sum(frame, step, src_origin, dst_origin, dst_size):
-    rows = lax.axis_size("row")
-    cols = lax.axis_size("col")
-    src_size = frame.shape[1]
+def neighbor_sum(frame, axis, dim, step, src_origin, dst_origin, dst_size):
+    src_size = frame.shape[dim]
     total = None
-    for a, b in OFFSETS:
-        (r0, r1), (p0, p1) = overlap(a, step, src_origin, src_size, dst_origin, dst_size)
-        (c0, c1), (q0, q1) = overlap(b, step, src_origin, src_size, dst_origin, dst_size)
-        piece = frame[:, r0:r1, c0:c1]
-        if (a, b) != (0, 0):
-            piece = from_neighbor(piece, a, b, rows, cols)
-        piece = jnp.pad(piece, ((0, 0), (p0, dst_size - p1), (q0, dst_size - q1)))
+    for a in (-1, 0, 1):
+        low = max(a * step + src_origin, dst_origin)
+        high = min(a * step + src_origin + src_size, dst_origin + dst_size)
+        shift = a * step + src_origin
+        piece = lax.slice_in_dim(frame, low - shift, high - shift, axis=dim)
+        if a != 0:
+            piece = from_neighbor(piece, axis, a)
+        widths = [(0, 0)] * frame.ndim
+        widths[dim] = (low - dst_origin, dst_origin + dst_size - high)
+        piece = jnp.pad(piece, widths)
         total = piece if total is None else total + piece
     return total
 
@@ -129,18 +111,21 @@
     zero = jnp.zeros((), jnp.int32)
     corner = (zero, offsets[0, 0] + M, offsets[0, 1] + M)
     spread = (zero, place - M - offsets[0, 0], place - M - offsets[0, 1])
-    extended = neighbor_sum(object_planes, tile_size, M, 0, extent)
+    extended = neighbor_sum(object_planes, "row", 1, tile_size, M, 0, extent)
+    extended = neighbor_sum(extended, "col", 2, tile_size, M, 0, extent)
     for update in range(ITERS):
         windows = lax.dynamic_slice(extended, corner, (2, W, W))[None]
         change = pattern_gradient(windows, measured, probe_re, probe_im, forward, inverse)[0]
         padded = jnp.pad(change, ((0, 0), (place, place), (place, place)))
         gathered = lax.dynamic_slice(padded, spread, (2, extent, extent))
         if update + 1 < ITERS:
-            total = neighbor_sum(gathered, tile_size, 0, 0, extent)
+            total = neighbor_sum(gathered, "col", 2, tile_size, 0, 0, extent)
+            total = neighbor_sum(total, "row", 1, tile_size, 0, 0, extent)
             mask = inside_mask(extent, tile_size)
             extended = jnp.where(mask[None], extended + total / peak_power, 0.0)
         else:
-            total = neighbor_sum(gathered, tile_size, 0, M, tile_size)
+            total = neighbor_sum(gathered, "col", 2, tile_size, 0, M, tile_size)
+            total = neighbor_sum(total, "row", 1, tile_size, 0, M, tile_size)
             current = extended[:, M : M + tile_size, M : M + tile_size] + total / peak_power
     return current
 

time: 201 us -> 149 us (0.74)
  the two profiles are of different devices: /device:TPU:80 before, /device:TPU:87 now
where the time goes in v2:
time: 149 us
  starting transfers between devices  59 us (40%)
  waiting for transfers between devices  35.1 us (24%)
  other arithmetic  20.9 us (14%)
  matrix products  15 us (10%)
  local copies, waits for them, and re-layouts  12.7 us (9%)
  between operations  5.75 us (4%)
    ppermute x12, starting transfers between devices, from_neighbor(): return lax.ppermute(x, axis, pairs)  59 us
    ppermute x12, waiting for transfers between devices, from_neighbor(): return lax.ppermute(x, axis, pairs)  35.1 us
    dot_general x4, matrix products, transform(): jnp.einsum('qkrc,qcpv->pkrv', half_done, right_side, preferred_element_ty...  15 us
    unnamed x36, local copies, waits for them, and re-layouts  4.04 us
    another operation x2, other arithmetic, operators(): jnp.stack([jnp.stack([table_re, table_im], 1), jnp.stack([-table_im, tabl...  3.18 us
    another operation x2, other arithmetic, pattern_gradient(): exit_waves = jnp.stack([exit_re, exit_im])  3.16 us
  transfers between devices with their start and end apart: 12, of which 8 were waited for; matrix products, arithmetic and copies ran while one was open for 8% of the time, Pallas kernels for 0%

profile of v2, /device:TPU:87, one launch (start us, length us, event | category | flops | bytes accessed | tf_op | source)
XLA Modules:
  0.0 148.5 jit_solution(15286269115020567376)
XLA Ops:
  0.0 1.4 copy.49
  1.5 4.9 %collective-permute-start = (f32[2,64,256]{1,2,0:T(8,128)S(1)}, f32[2,64,256]{1,2,0:T(8,128)S(1)}, u32[]{:S(2)}, u32[]{:S(2)}) collective-permute-start(f32[2,64,256]{1,2,0:T(8,128)S(1)} %get-tuple-element.37), channel_id=1, source_target_pairs={{0,32},{32,64},{64,96},{96,128},{128,160},{160,192},{192,224},{224... | collective-permute-start | bytes 393224 | tf_op jit(solution)/shard_map/ppermute | solution.py:68
  6.4 14.5 %collective-permute-start.1 = (f32[2,64,256]{1,2,0:T(8,128)S(1)}, f32[2,64,256]{1,2,0:T(8,128)S(1)}, u32[]{:S(2)}, u32[]{:S(2)}) collective-permute-start(f32[2,64,256]{1,2,0:T(8,128)S(1)} %get-tuple-element.38), channel_id=1, source_target_pairs={{32,0},{64,32},{96,64},{128,96},{160,128},{192,160},{224,192},{256... | collective-permute-start | bytes 393224 | tf_op jit(solution)/shard_map/ppermute | solution.py:68
  20.9 1.0 fusion.45
  21.9 1.0 multiply_convert_fusion
  22.9 1.0 multiply_convert_fusion.1
  23.9 1.3 fusion.54
  25.2 0.9 fusion.35
  26.1 4.8 %collective-permute-done = f32[2,64,256]{1,2,0:T(8,128)S(1)} collective-permute-done((f32[2,64,256]{1,2,0:T(8,128)S(1)}, f32[2,64,256]{1,2,0:T(8,128)S(1)}, u32[]{:S(2)}, u32[]{:S(2)}) %collective-permute-start) | collective-permute-done | bytes 131104 | tf_op jit(solution)/shard_map/ppermute | solution.py:68
  31.2 0.8 fusion.57
  32.0 4.7 %collective-permute-start.2 = (f32[2,384,64]{1,2,0:T(8,128)}, f32[2,384,64]{1,2,0:T(8,128)}, u32[]{:S(2)}, u32[]{:S(2)}) collective-permute-start(f32[2,384,64]{1,2,0:T(8,128)} %get-tuple-element.27), channel_id=1, source_target_pairs={{0,1},{1,2},{2,3},{3,4},{4,5},{5,6},{6,7},{7,8},{8,9},{9,10},{10,1... | collective-permute-start | bytes 589832 | tf_op jit(solution)/shard_map/ppermute | solution.py:68
  36.7 1.9 %collective-permute-start.3 = (f32[2,384,64]{1,2,0:T(8,128)}, f32[2,384,64]{1,2,0:T(8,128)}, u32[]{:S(2)}, u32[]{:S(2)}) collective-permute-start(f32[2,384,64]{1,2,0:T(8,128)} %get-tuple-element.28), channel_id=1, source_target_pairs={{1,0},{2,1},{3,2},{4,3},{5,4},{6,5},{7,6},{8,7},{9,8},{10,9},{11,1... | collective-permute-start | bytes 589832 | tf_op jit(solution)/shard_map/ppermute | solution.py:68
  44.6 1.1 copy.60
  45.7 2.2 %maximum_bitcast_fusion.4 = (bf16[2,256,2,256,1]{3,1,2,0,4:T(8,128)(2,1)}, bf16[2,256,2,256,1]{3,1,2,0,4:T(8,128)(2,1)}) fusion(bf16[1,256,2,256]{3,1,2,0:T(8,128)(2,1)} %get-tuple-element.44, bf16[1,256,2,256]{3,1,2,0:T(8,128)(2,1)} %get-tuple-element.39, bf16[1,256,2,256]{3,1,2,0:T(8,128)(2,1)S(1)} %get-tuple-element.40, ...), kind=kLoop, calls=%fused_computation.55 | loop fusion | flops 524288 | bytes 2097152 | tf_op jit(solution)/shard_map/stack | solution.py:32
  48.0 1.1 pad_add_fusion
  49.3 1.0 copy.53
  50.3 1.1 slice_bitcast_fusion.3
  51.6 1.6 %convert_bitcast_fusion.3 = (bf16[1,1,3,256,256]{3,4,0,2,1:T(8,128)(2,1)}, f32[1,3,256,256]{2,3,1,0:T(8,128)}, bf16[1,1,3,256,256]{3,4,0,2,1:T(8,128)(2,1)}, f32[1,3,256,256]{2,3,1,0:T(8,128)}) fusion(f32[1,3,256,256]{2,3,1,0:T(8,128)S(1)} %copy.114, f32[256,256]{0,1:T(8,128)S(1)} %copy.55, f32[1,3,256,256]{2,3,1,0:T(8,128)S(1)} %copy.113, ...), kind=kLoop, calls=%fused_computation.66 | loop fusion | flops 1572864 | bytes 4456448 | tf_op jit(solution)/shard_map/stack | solution.py:50
  53.2 4.3 %fusion.2 = (f32[256,256]{0,1:T(8,128)}, f32[2,256,3,256,1]{3,1,4,2,0:T(8,128)}) fusion(bf16[1,1,3,256,256]{3,4,0,2,1:T(8,128)(2,1)} %get-tuple-element.19, bf16[1,1,3,256,256]{3,4,0,2,1:T(8,128)(2,1)} %get-tuple-element.13, bf16[1,256,2,256]{3,1,2,0:T(8,128)(2,1)} %get-tuple-element.44, bf16[1,256,2,256]{3,1,2,0:T(8,128)(2,1)S(1)} %copy-done.11, ...), kind=kOutput, calls=%fused_computation.17 | convolution fusion | flops 809041920 | bytes 3670016 | tf_op jit(solution)/shard_map/qkrc,qcpv->pkrv/dot_general | solution.py:42
  57.5 1.0 fusion.41
  58.6 4.2 %maximum_subtract_fusion = f32[2,3,256,256]{2,3,1,0:T(8,128)} fusion(f32[1,3,256,256]{2,3,1,0:T(8,128)} %get-tuple-element.20, f32[1,3,256,256]{2,3,1,0:T(8,128)} %get-tuple-element.14, bf16[2,256,2,256,1]{3,1,2,0,4:T(8,128)(2,1)} %get-tuple-element.51, bf16[1,256,2,256]{3,1,2,0:T(8,128)(2,1)S(1)} %copy-done.8, bf16[1,256,2,256]{3,1,2,0:T(8,128)(2,1)S(1)} %copy-done.10, ...), kind=kOutput, calls=%fused_computation.6 | convolution fusion | flops 808321024 | bytes 6029312 | tf_op jit(solution)/shard_map/qkrc,qcpv->pkrv/dot_general | solution.py:42
  62.8 1.7 %add_reduce_fusion.1 = (f32[256,256]{0,1:T(8,128)S(1)}, f32[256,256]{0,1:T(8,128)S(1)}) fusion(f32[1,3,256,256]{2,3,1,0:T(8,128)S(1)} %copy.114, f32[1,3,256,256]{2,3,1,0:T(8,128)S(1)} %copy.113, f32[2,3,256,256]{2,3,1,0:T(8,128)} %maximum_subtract_fusion), kind=kLoop, calls=%fused_computation.47 | loop fusion | flops 1441792 | bytes 3670016 | tf_op jit(solution)/shard_map/reduce_sum | solution.py:60
  64.9 4.8 %collective-permute-start.4 = (f32[2,384,128]{1,2,0:T(8,128)S(1)}, f32[2,384,128]{1,2,0:T(8,128)S(1)}, u32[]{:S(2)}, u32[]{:S(2)}) collective-permute-start(f32[2,384,128]{1,2,0:T(8,128)S(1)} %get-tuple-element.33), channel_id=1, source_target_pairs={{0,1},{1,2},{2,3},{3,4},{4,5},{5,6},{6,7},{7,8},{8,9},{9,10},{10,1... | collective-permute-start | bytes 1179656 | tf_op jit(solution)/shard_map/ppermute | solution.py:68
  69.7 2.1 %collective-permute-start.5 = (f32[2,384,128]{1,2,0:T(8,128)S(1)}, f32[2,384,128]{1,2,0:T(8,128)S(1)}, u32[]{:S(2)}, u32[]{:S(2)}) collective-permute-start(f32[2,384,128]{1,2,0:T(8,128)S(1)} %get-tuple-element.34), channel_id=1, source_target_pairs={{1,0},{2,1},{3,2},{4,3},{5,4},{6,5},{7,6},{8,7},{9,8},{10,9},{11,1... | collective-permute-start | bytes 1179656 | tf_op jit(solution)/shard_map/ppermute | solution.py:68
  71.8 2.6 %collective-permute-done.4 = f32[2,384,128]{1,2,0:T(8,128)S(1)} collective-permute-done((f32[2,384,128]{1,2,0:T(8,128)S(1)}, f32[2,384,128]{1,2,0:T(8,128)S(1)}, u32[]{:S(2)}, u32[]{:S(2)}) %collective-permute-start.4) | collective-permute-done | bytes 393248 | tf_op jit(solution)/shard_map/ppermute | solution.py:68
  74.4 5.8 %collective-permute-done.5 = f32[2,384,128]{1,2,0:T(8,128)S(1)} collective-permute-done((f32[2,384,128]{1,2,0:T(8,128)S(1)}, f32[2,384,128]{1,2,0:T(8,128)S(1)}, u32[]{:S(2)}, u32[]{:S(2)}) %collective-permute-start.5) | collective-permute-done | bytes 393248 | tf_op jit(solution)/shard_map/ppermute | solution.py:68
  80.6 1.0 fusion.55
  81.6 1.9 %collective-permute-start.6 = (f32[2,128,384]{1,2,0:T(8,128)}, f32[2,128,384]{1,2,0:T(8,128)}, u32[]{:S(2)}, u32[]{:S(2)}) collective-permute-start(f32[2,128,384]{1,2,0:T(8,128)} %get-tuple-element.23), channel_id=1, source_target_pairs={{0,32},{32,64},{64,96},{96,128},{128,160},{160,192},{192,224},{224... | collective-permute-start | bytes 1179656 | tf_op jit(solution)/shard_map/ppermute | solution.py:68
  83.5 7.8 %collective-permute-start.7 = (f32[2,128,384]{1,2,0:T(8,128)}, f32[2,128,384]{1,2,0:T(8,128)}, u32[]{:S(2)}, u32[]{:S(2)}) collective-permute-start(f32[2,128,384]{1,2,0:T(8,128)} %get-tuple-element.24), channel_id=1, source_target_pairs={{32,0},{64,32},{96,64},{128,96},{160,128},{192,160},{224,192},{256... | collective-permute-start | bytes 1179656 | tf_op jit(solution)/shard_map/ppermute | solution.py:68
  91.3 0.8 multiply_reduce_fusion
  92.1 1.6 %reduce_max.9 = f32[]{:T(128)} reduce(f32[256,256]{1,0:T(8,128)} %multiply_reduce_fusion, f32[]{:T(128)} %constant.58.clone.1), dimensions={0,1}, to_apply=%region_4.5 | reduce | flops 65535 | bytes 262152 | tf_op jit(solution)/shard_map/reduce_max | solution.py:105
  94.4 6.8 %collective-permute-done.6 = f32[2,128,384]{1,2,0:T(8,128)} collective-permute-done((f32[2,128,384]{1,2,0:T(8,128)}, f32[2,128,384]{1,2,0:T(8,128)}, u32[]{:S(2)}, u32[]{:S(2)}) %collective-permute-start.6) | collective-permute-done | bytes 393248 | tf_op jit(solution)/shard_map/ppermute | solution.py:68
  101.3 1.4 add_select_fusion
  102.7 1.0 copy-done.2
  104.5 1.6 %convert_bitcast_fusion.1 = (bf16[1,1,3,256,256]{3,4,2,1,0:T(8,128)(2,1)}, f32[1,3,256,256]{2,3,1,0:T(8,128)}, bf16[1,1,3,256,256]{3,4,2,1,0:T(8,128)(2,1)}, f32[1,3,256,256]{2,3,1,0:T(8,128)}) fusion(f32[1,3,256,256]{2,3,1,0:T(8,128)S(1)} %copy.114, f32[256,256]{0,1:T(8,128)S(1)} %copy.66, f32[1,3,256,256]{2,3,1,0:T(8,128)S(1)} %copy.113, ...), kind=kLoop, calls=%fused_computation.64 | loop fusion | flops 1572864 | bytes 4456448 | tf_op jit(solution)/shard_map/stack | solution.py:50
  106.1 3.4 %fusion = (f32[256,256]{0,1:T(8,128)S(1)}, f32[2,256,3,256,1]{3,1,4,2,0:T(8,128)}) fusion(bf16[1,256,2,256]{3,1,2,0:T(8,128)(2,1)S(1)} %copy-done.13, bf16[1,256,2,256]{3,1,2,0:T(8,128)(2,1)S(1)} %copy-done.12, bf16[2,256,2,256,1]{3,1,2,0,4:T(8,128)(2,1)S(1)} %copy-done.14, bf16[1,1,3,256,256]{3,4,2,1,0:T(8,128)(2,1)} %get-tuple-element.17, ...), kind=kOutput, calls=%fused_computation.11 | convolution fusion | flops 807862272 | bytes 3670016 | tf_op jit(solution)/shard_map/qkrc,qcpv->pkrv/dot_general | solution.py:42
  109.4 0.8 fusion.40
  110.2 3.2 %maximum_subtract_fusion.1 = f32[2,3,256,256]{2,3,1,0:T(8,128)S(1)} fusion(f32[1,3,256,256]{2,3,1,0:T(8,128)} %get-tuple-element.18, f32[1,3,256,256]{2,3,1,0:T(8,128)} %get-tuple-element.10, bf16[2,256,2,256,1]{3,1,2,0,4:T(8,128)(2,1)} %get-tuple-element.51, bf16[1,256,2,256]{3,1,2,0:T(8,128)(2,1)S(1)} %copy-done.9, ...), kind=kOutput, calls=%fused_computation.7 | convolution fusion | flops 808321024 | bytes 6029312 | tf_op jit(solution)/shard_map/qkrc,qcpv->pkrv/dot_general | solution.py:42
  114.0 5.0 %collective-permute-start.8 = (f32[2,384,64]{1,2,0:T(8,128)S(1)}, f32[2,384,64]{1,2,0:T(8,128)S(1)}, u32[]{:S(2)}, u32[]{:S(2)}) collective-permute-start(f32[2,384,64]{1,2,0:T(8,128)S(1)} %get-tuple-element.29), channel_id=1, source_target_pairs={{0,1},{1,2},{2,3},{3,4},{4,5},{5,6},{6,7},{7,8},{8,9},{9,10},{10,1... | collective-permute-start | bytes 589832 | tf_op jit(solution)/shard_map/ppermute | solution.py:68
  119.0 1.9 %collective-permute-start.9 = (f32[2,384,64]{1,2,0:T(8,128)S(1)}, f32[2,384,64]{1,2,0:T(8,128)S(1)}, u32[]{:S(2)}, u32[]{:S(2)}) collective-permute-start(f32[2,384,64]{1,2,0:T(8,128)S(1)} %get-tuple-element.30), channel_id=1, source_target_pairs={{1,0},{2,1},{3,2},{4,3},{5,4},{6,5},{7,6},{8,7},{9,8},{10,9},{11,1... | collective-permute-start | bytes 589832 | tf_op jit(solution)/shard_map/ppermute | solution.py:68
  120.9 0.7 collective-permute-done.8
  121.6 5.6 %collective-permute-done.9 = f32[2,384,64]{1,2,0:T(8,128)S(1)} collective-permute-done((f32[2,384,64]{1,2,0:T(8,128)S(1)}, f32[2,384,64]{1,2,0:T(8,128)S(1)}, u32[]{:S(2)}, u32[]{:S(2)}) %collective-permute-start.9) | collective-permute-done | bytes 196640 | tf_op jit(solution)/shard_map/ppermute | solution.py:68
  127.6 1.9 %collective-permute-start.10 = (f32[2,64,256]{1,2,0:T(8,128)S(1)}, f32[2,64,256]{1,2,0:T(8,128)S(1)}, u32[]{:S(2)}, u32[]{:S(2)}) collective-permute-start(f32[2,64,256]{1,2,0:T(8,128)S(1)} %get-tuple-element.25), channel_id=1, source_target_pairs={{0,32},{32,64},{64,96},{96,128},{128,160},{160,192},{192,224},{224... | collective-permute-start | bytes 393224 | tf_op jit(solution)/shard_map/ppermute | solution.py:68
  129.6 7.6 %collective-permute-start.11 = (f32[2,64,256]{1,2,0:T(8,128)S(1)}, f32[2,64,256]{1,2,0:T(8,128)S(1)}, u32[]{:S(2)}, u32[]{:S(2)}) collective-permute-start(f32[2,64,256]{1,2,0:T(8,128)S(1)} %get-tuple-element.26), channel_id=1, source_target_pairs={{32,0},{64,32},{96,64},{128,96},{160,128},{192,160},{224,192},{256... | collective-permute-start | bytes 393224 | tf_op jit(solution)/shard_map/ppermute | solution.py:68
  137.1 5.0 %collective-permute-done.10 = f32[2,64,256]{1,2,0:T(8,128)S(1)} collective-permute-done((f32[2,64,256]{1,2,0:T(8,128)S(1)}, f32[2,64,256]{1,2,0:T(8,128)S(1)}, u32[]{:S(2)}, u32[]{:S(2)}) %collective-permute-start.10) | collective-permute-done | bytes 131104 | tf_op jit(solution)/shard_map/ppermute | solution.py:68
  142.1 3.9 %collective-permute-done.11 = f32[2,64,256]{1,2,0:T(8,128)S(1)} collective-permute-done((f32[2,64,256]{1,2,0:T(8,128)S(1)}, f32[2,64,256]{1,2,0:T(8,128)S(1)}, u32[]{:S(2)}, u32[]{:S(2)}) %collective-permute-start.11) | collective-permute-done | bytes 131104 | tf_op jit(solution)/shard_map/ppermute | solution.py:68
  146.0 1.5 %fusion.28 = f32[2,256,256]{1,2,0:T(8,128)S(1)} fusion(f32[2,384,256]{1,2,0:T(8,128)S(1)} %fusion.15, f32[2,384,384]{1,2,0:T(8,128)} %copy-done.2, f32[2,64,256]{1,2,0:T(8,128)S(1)} %collective-permute-done.11, f32[2,64,256]{1,2,0:T(8,128)S(1)} %collective-permute-done.10, f32[]{:T(128)S(6)} %add.192), kind=kLoop, calls=%fused_computation.54 | loop fusion | flops 524288 | bytes 1835012 | tf_op jit(solution)/shard_map/add | solution.py:129
  147.5 1.0 copy.74
  (58 shorter events, 4.8 us)
Async XLA Ops:
  0.0 23.9 %copy-start = (f32[2,3,256,256]{3,2,1,0:T(8,128)S(1)}, f32[2,3,256,256]{3,2,1,0:T(8,128)}, u32[]{:S(2)}) copy-start(f32[2,3,256,256]{3,2,1,0:T(8,128)} %param.5) | copy-start | bytes 4718596
  1.5 29.4 %collective-permute-start = (f32[2,64,256]{1,2,0:T(8,128)S(1)}, f32[2,64,256]{1,2,0:T(8,128)S(1)}, u32[]{:S(2)}, u32[]{:S(2)}) collective-permute-start(f32[2,64,256]{1,2,0:T(8,128)S(1)} %get-tuple-element.37), channel_id=1, source_target_pairs={{0,32},{32,64},{64,96},{96,128},{128,160},{160,192},{192,224},{224... | collective-permute-start | bytes 393224 | tf_op jit(solution)/shard_map/ppermute | solution.py:68
  6.4 24.5 %collective-permute-start.1 = (f32[2,64,256]{1,2,0:T(8,128)S(1)}, f32[2,64,256]{1,2,0:T(8,128)S(1)}, u32[]{:S(2)}, u32[]{:S(2)}) collective-permute-start(f32[2,64,256]{1,2,0:T(8,128)S(1)} %get-tuple-element.38), channel_id=1, source_target_pairs={{32,0},{64,32},{96,64},{128,96},{160,128},{192,160},{224,192},{256... | collective-permute-start | bytes 393224 | tf_op jit(solution)/shard_map/ppermute | solution.py:68
  26.1 19.6 %copy-start.7 = (bf16[1,256,2,256]{3,1,2,0:T(8,128)(2,1)}, bf16[1,256,2,256]{3,1,2,0:T(8,128)(2,1)S(1)}, u32[]{:S(2)}) copy-start(bf16[1,256,2,256]{3,1,2,0:T(8,128)(2,1)S(1)} %get-tuple-element.40) | copy-start | bytes 786436
  26.1 12.6 %copy-start.15 = (s32[1,1,1,2]{3,2,1,0:T(1,128)S(1)}, s32[1,1,1,2]{3,2,1,0:T(1,128)}, u32[]{:S(2)}) copy-start(s32[1,1,1,2]{3,2,1,0:T(1,128)} %param.6) | copy-start | bytes 28
  26.1 17.9 %copy-start.4 = (f32[1,3,256,256]{3,2,1,0:T(8,128)S(1)}, f32[1,3,256,256]{3,2,1,0:T(8,128)}, u32[]{:S(2)}) copy-start(f32[1,3,256,256]{3,2,1,0:T(8,128)} %get-tuple-element.21) | copy-start | bytes 2359300
  31.2 13.1 %copy-start.3 = (f32[1,3,256,256]{3,2,1,0:T(8,128)S(1)}, f32[1,3,256,256]{3,2,1,0:T(8,128)}, u32[]{:S(2)}) copy-start(f32[1,3,256,256]{3,2,1,0:T(8,128)} %get-tuple-element.22) | copy-start | bytes 2359300
  32.0 15.9 %collective-permute-start.2 = (f32[2,384,64]{1,2,0:T(8,128)}, f32[2,384,64]{1,2,0:T(8,128)}, u32[]{:S(2)}, u32[]{:S(2)}) collective-permute-start(f32[2,384,64]{1,2,0:T(8,128)} %get-tuple-element.27), channel_id=1, source_target_pairs={{0,1},{1,2},{2,3},{3,4},{4,5},{5,6},{6,7},{7,8},{8,9},{9,10},{10,1... | collective-permute-start | bytes 589832 | tf_op jit(solution)/shard_map/ppermute | solution.py:68
  36.7 11.2 %collective-permute-start.3 = (f32[2,384,64]{1,2,0:T(8,128)}, f32[2,384,64]{1,2,0:T(8,128)}, u32[]{:S(2)}, u32[]{:S(2)}) collective-permute-start(f32[2,384,64]{1,2,0:T(8,128)} %get-tuple-element.28), channel_id=1, source_target_pairs={{1,0},{2,1},{3,2},{4,3},{5,4},{6,5},{7,6},{8,7},{9,8},{10,9},{11,1... | collective-permute-start | bytes 589832 | tf_op jit(solution)/shard_map/ppermute | solution.py:68
  45.7 11.9 %copy-start.5 = (f32[1,1,1,256,256]{3,4,2,1,0:T(8,128)}, f32[1,1,1,256,256]{3,4,2,1,0:T(8,128)S(1)}, u32[]{:S(2)}) copy-start(f32[1,1,1,256,256]{3,4,2,1,0:T(8,128)S(1)} %copy.60) | copy-start | bytes 786436
  51.6 1.6 %copy-start.11 = (bf16[1,256,2,256]{3,1,2,0:T(8,128)(2,1)S(1)}, bf16[1,256,2,256]{3,1,2,0:T(8,128)(2,1)}, u32[]{:S(2)}) copy-start(bf16[1,256,2,256]{3,1,2,0:T(8,128)(2,1)} %get-tuple-element.39) | copy-start | bytes 786436
  53.2 5.4 %copy-start.8 = (bf16[1,256,2,256]{3,1,2,0:T(8,128)(2,1)S(1)}, bf16[1,256,2,256]{3,1,2,0:T(8,128)(2,1)}, u32[]{:S(2)}) copy-start(bf16[1,256,2,256]{3,1,2,0:T(8,128)(2,1)} %copy-done.7) | copy-start | bytes 786436
  53.2 5.4 %copy-start.10 = (bf16[1,256,2,256]{3,1,2,0:T(8,128)(2,1)S(1)}, bf16[1,256,2,256]{3,1,2,0:T(8,128)(2,1)}, u32[]{:S(2)}) copy-start(bf16[1,256,2,256]{3,1,2,0:T(8,128)(2,1)} %get-tuple-element.43) | copy-start | bytes 786436
  64.9 9.6 %collective-permute-start.4 = (f32[2,384,128]{1,2,0:T(8,128)S(1)}, f32[2,384,128]{1,2,0:T(8,128)S(1)}, u32[]{:S(2)}, u32[]{:S(2)}) collective-permute-start(f32[2,384,128]{1,2,0:T(8,128)S(1)} %get-tuple-element.33), channel_id=1, source_target_pairs={{0,1},{1,2},{2,3},{3,4},{4,5},{5,6},{6,7},{7,8},{8,9},{9,10},{10,1... | collective-permute-start | bytes 1179656 | tf_op jit(solution)/shard_map/ppermute | solution.py:68
  69.7 21.5 %copy-start.1 = (f32[2,3,256,256]{3,2,1,0:T(8,128)S(1)}, f32[2,3,256,256]{3,2,1,0:T(8,128)}, u32[]{:S(2)}) copy-start(f32[2,3,256,256]{3,2,1,0:T(8,128)} %param.5) | copy-start | bytes 4718596
  69.7 10.4 %collective-permute-start.5 = (f32[2,384,128]{1,2,0:T(8,128)S(1)}, f32[2,384,128]{1,2,0:T(8,128)S(1)}, u32[]{:S(2)}, u32[]{:S(2)}) collective-permute-start(f32[2,384,128]{1,2,0:T(8,128)S(1)} %get-tuple-element.34), channel_id=1, source_target_pairs={{1,0},{2,1},{3,2},{4,3},{5,4},{6,5},{7,6},{8,7},{9,8},{10,9},{11,1... | collective-permute-start | bytes 1179656 | tf_op jit(solution)/shard_map/ppermute | solution.py:68
  81.6 19.7 %collective-permute-start.6 = (f32[2,128,384]{1,2,0:T(8,128)}, f32[2,128,384]{1,2,0:T(8,128)}, u32[]{:S(2)}, u32[]{:S(2)}) collective-permute-start(f32[2,128,384]{1,2,0:T(8,128)} %get-tuple-element.23), channel_id=1, source_target_pairs={{0,32},{32,64},{64,96},{96,128},{128,160},{160,192},{192,224},{224... | collective-permute-start | bytes 1179656 | tf_op jit(solution)/shard_map/ppermute | solution.py:68
  83.5 17.8 %collective-permute-start.7 = (f32[2,128,384]{1,2,0:T(8,128)}, f32[2,128,384]{1,2,0:T(8,128)}, u32[]{:S(2)}, u32[]{:S(2)}) collective-permute-start(f32[2,128,384]{1,2,0:T(8,128)} %get-tuple-element.24), channel_id=1, source_target_pairs={{32,0},{64,32},{96,64},{128,96},{160,128},{192,160},{224,192},{256... | collective-permute-start | bytes 1179656 | tf_op jit(solution)/shard_map/ppermute | solution.py:68
  102.7 1.0 copy-start.2
  104.4 1.6 %copy-start.12 = (bf16[1,256,2,256]{3,1,2,0:T(8,128)(2,1)S(1)}, bf16[1,256,2,256]{3,1,2,0:T(8,128)(2,1)}, u32[]{:S(2)}) copy-start(bf16[1,256,2,256]{3,1,2,0:T(8,128)(2,1)} %get-tuple-element.39) | copy-start | bytes 786436
  104.5 1.6 %copy-start.13 = (bf16[1,256,2,256]{3,1,2,0:T(8,128)(2,1)S(1)}, bf16[1,256,2,256]{3,1,2,0:T(8,128)(2,1)}, u32[]{:S(2)}) copy-start(bf16[1,256,2,256]{3,1,2,0:T(8,128)(2,1)} %get-tuple-element.44) | copy-start | bytes 786436
  104.5 1.6 %copy-start.14 = (bf16[2,256,2,256,1]{3,1,2,0,4:T(8,128)(2,1)S(1)}, bf16[2,256,2,256,1]{3,1,2,0,4:T(8,128)(2,1)}, u32[]{:S(2)}) copy-start(bf16[2,256,2,256,1]{3,1,2,0,4:T(8,128)(2,1)} %get-tuple-element.52) | copy-start | bytes 1572868
  106.1 3.4 %copy-start.6 = (f32[1,1,1,256,256]{3,4,2,1,0:T(8,128)S(1)}, f32[1,1,1,256,256]{3,4,2,1,0:T(8,128)}, u32[]{:S(2)}) copy-start(f32[1,1,1,256,256]{3,4,2,1,0:T(8,128)} %copy-done.5) | copy-start | bytes 786436
  106.1 4.2 %copy-start.9 = (bf16[1,256,2,256]{3,1,2,0:T(8,128)(2,1)S(1)}, bf16[1,256,2,256]{3,1,2,0:T(8,128)(2,1)}, u32[]{:S(2)}) copy-start(bf16[1,256,2,256]{3,1,2,0:T(8,128)(2,1)} %copy-done.7) | copy-start | bytes 786436
  114.0 7.6 %collective-permute-start.8 = (f32[2,384,64]{1,2,0:T(8,128)S(1)}, f32[2,384,64]{1,2,0:T(8,128)S(1)}, u32[]{:S(2)}, u32[]{:S(2)}) collective-permute-start(f32[2,384,64]{1,2,0:T(8,128)S(1)} %get-tuple-element.29), channel_id=1, source_target_pairs={{0,1},{1,2},{2,3},{3,4},{4,5},{5,6},{6,7},{7,8},{8,9},{9,10},{10,1... | collective-permute-start | bytes 589832 | tf_op jit(solution)/shard_map/ppermute | solution.py:68
  119.0 8.2 %collective-permute-start.9 = (f32[2,384,64]{1,2,0:T(8,128)S(1)}, f32[2,384,64]{1,2,0:T(8,128)S(1)}, u32[]{:S(2)}, u32[]{:S(2)}) collective-permute-start(f32[2,384,64]{1,2,0:T(8,128)S(1)} %get-tuple-element.30), channel_id=1, source_target_pairs={{1,0},{2,1},{3,2},{4,3},{5,4},{6,5},{7,6},{8,7},{9,8},{10,9},{11,1... | collective-permute-start | bytes 589832 | tf_op jit(solution)/shard_map/ppermute | solution.py:68
  127.6 14.5 %collective-permute-start.10 = (f32[2,64,256]{1,2,0:T(8,128)S(1)}, f32[2,64,256]{1,2,0:T(8,128)S(1)}, u32[]{:S(2)}, u32[]{:S(2)}) collective-permute-start(f32[2,64,256]{1,2,0:T(8,128)S(1)} %get-tuple-element.25), channel_id=1, source_target_pairs={{0,32},{32,64},{64,96},{96,128},{128,160},{160,192},{192,224},{224... | collective-permute-start | bytes 393224 | tf_op jit(solution)/shard_map/ppermute | solution.py:68
  129.6 16.4 %collective-permute-start.11 = (f32[2,64,256]{1,2,0:T(8,128)S(1)}, f32[2,64,256]{1,2,0:T(8,128)S(1)}, u32[]{:S(2)}, u32[]{:S(2)}) collective-permute-start(f32[2,64,256]{1,2,0:T(8,128)S(1)} %get-tuple-element.26), channel_id=1, source_target_pairs={{32,0},{64,32},{96,64},{128,96},{160,128},{192,160},{224,192},{256... | collective-permute-start | bytes 393224 | tf_op jit(solution)/shard_map/ppermute | solution.py:68

commit v3 on v2

--- a/solution.py
+++ b/solution.py
@@ -3,6 +3,8 @@
 import jax
 import jax.numpy as jnp
 from jax import lax
+from jax.experimental import pallas as pl
+from jax.experimental.pallas import tpu as pltpu
 from jax.sharding import PartitionSpec as P
 
 W = 256
@@ -25,41 +27,68 @@
     )
 
 
-def operators(table_re, table_im):
-    left_side = jnp.stack(
-        [jnp.stack([table_re, -table_im], 1), jnp.stack([table_im, table_re], 1)], 0
-    )
-    right_side = jnp.stack(
-        [jnp.stack([table_re, table_im], 1), jnp.stack([-table_im, table_re], 1)], 0
-    )
-    return (left_side, right_side)
+INTERPRET = False
 
 
-def transform(waves, left_side, right_side):
-    half_done = jnp.einsum(
-        "puqr,qkrc->pkuc", left_side, waves, preferred_element_type=jnp.float32
-    ).astype(jnp.bfloat16)
-    return jnp.einsum("qkrc,qcpv->pkrv", half_done, right_side, preferred_element_type=jnp.float32)
+def gradient_kernel(window_ref, probe_ref, measured_ref, table_re_ref, table_im_ref, out_ref, spectrum_ref):
+    modes = probe_ref.shape[1]
+    table_re = table_re_ref[...]
+    table_im = table_im_ref[...]
+
+    def product(left, right):
+        return jnp.dot(left, right, preferred_element_type=jnp.float32)
+
+    def exit_wave(k):
+        obj_re = window_ref[0]
+        obj_im = window_ref[1]
+        probe_re = probe_ref[0, k]
+        probe_im = probe_ref[1, k]
+        return obj_re * probe_re - obj_im * probe_im, obj_re * probe_im + obj_im * probe_re
+
+    power = None
+    for k in range(modes):
+        exit_re, exit_im = exit_wave(k)
+        exit_re = exit_re.astype(jnp.bfloat16)
+        exit_im = exit_im.astype(jnp.bfloat16)
+        half_re = (product(table_re, exit_re) - product(table_im, exit_im)).astype(jnp.bfloat16)
+        half_im = (product(table_im, exit_re) + product(table_re, exit_im)).astype(jnp.bfloat16)
+        spec_re = product(half_re, table_re) - product(half_im, table_im)
+        spec_im = product(half_re, table_im) + product(half_im, table_re)
+        spectrum_ref[0, k] = spec_re
+        spectrum_ref[1, k] = spec_im
+        term = spec_re * spec_re + spec_im * spec_im
+        power = term if power is None else power + term
+    scaling = measured_ref[...] / jnp.maximum(jnp.sqrt(power), AMPLITUDE_FLOOR)
+    grad_re = None
+    grad_im = None
+    for k in range(modes):
+        fixed_re = (spectrum_ref[0, k] * scaling).astype(jnp.bfloat16)
+        fixed_im = (spectrum_ref[1, k] * scaling).astype(jnp.bfloat16)
+        back_re = (product(table_re, fixed_re) + product(table_im, fixed_im)).astype(jnp.bfloat16)
+        back_im = (product(table_re, fixed_im) - product(table_im, fixed_re)).astype(jnp.bfloat16)
+        revised_re = product(back_re, table_re) + product(back_im, table_im)
+        revised_im = product(back_im, table_re) - product(back_re, table_im)
+        exit_re, exit_im = exit_wave(k)
+        residue_re = revised_re - exit_re
+        residue_im = revised_im - exit_im
+        probe_re = probe_ref[0, k]
+        probe_im = probe_ref[1, k]
+        part_re = probe_re * residue_re + probe_im * residue_im
+        part_im = probe_re * residue_im - probe_im * residue_re
+        grad_re = part_re if grad_re is None else grad_re + part_re
+        grad_im = part_im if grad_im is None else grad_im + part_im
+    out_ref[0] = grad_re
+    out_ref[1] = grad_im
 
 
-def pattern_gradient(windows, measured, probe_re, probe_im, forward, inverse):
-    obj_re = windows[:, 0][:, None]
-    obj_im = windows[:, 1][:, None]
-    exit_re = obj_re * probe_re[None] - obj_im * probe_im[None]
-    exit_im = obj_re * probe_im[None] + obj_im * probe_re[None]
-    exit_waves = jnp.stack([exit_re, exit_im])
-    flat_shape = (2, -1) + exit_waves.shape[3:]
-    spectrum = transform(
-        exit_waves.reshape(flat_shape).astype(jnp.bfloat16), forward[0], forward[1]
-    ).reshape(exit_waves.shape)
-    modulus = jnp.sqrt(jnp.sum(spectrum * spectrum, axis=(0, 2)))
-    scaling = measured / jnp.maximum(modulus, AMPLITUDE_FLOOR)
-    corrected = (spectrum * scaling[None, :, None]).astype(jnp.bfloat16).reshape(flat_shape)
-    revised = transform(corrected, inverse[0], inverse[1]).reshape(exit_waves.shape)
-    residue = revised - exit_waves
-    grad_re = jnp.sum(probe_re[None] * residue[0] + probe_im[None] * residue[1], axis=1)
-    grad_im = jnp.sum(probe_re[None] * residue[1] - probe_im[None] * residue[0], axis=1)
-    return jnp.stack([grad_re, grad_im], axis=1)
+def pattern_gradient(window, measured, probe_modes, table_re, table_im):
+    _, modes, rows, cols = probe_modes.shape
+    return pl.pallas_call(
+        gradient_kernel,
+        out_shape=jax.ShapeDtypeStruct((2, rows, cols), jnp.float32),
+        scratch_shapes=[pltpu.VMEM((2, modes, rows, cols), jnp.float32)],
+        interpret=INTERPRET,
+    )(window, probe_modes, measured, table_re, table_im)
 
 
 def from_neighbor(x, axis, a):
@@ -98,10 +127,6 @@
 
 def on_device(object_planes, probe_modes, positions, amplitudes):
     table_re, table_im = tables(W)
-    forward = operators(table_re, table_im)
-    inverse = operators(table_re, -table_im)
-    probe_re = probe_modes[0]
-    probe_im = probe_modes[1]
     peak_power = jnp.max(jnp.sum(probe_modes * probe_modes, axis=(0, 1))) + EPSILON
     offsets = positions.reshape(-1, 2)
     measured = amplitudes.reshape(-1, W, W)
@@ -114,8 +139,8 @@
     extended = neighbor_sum(object_planes, "row", 1, tile_size, M, 0, extent)
     extended = neighbor_sum(extended, "col", 2, tile_size, M, 0, extent)
     for update in range(ITERS):
-        windows = lax.dynamic_slice(extended, corner, (2, W, W))[None]
-        change = pattern_gradient(windows, measured, probe_re, probe_im, forward, inverse)[0]
+        window = lax.dynamic_slice(extended, corner, (2, W, W))
+        change = pattern_gradient(window, measured[0], probe_modes, table_re, table_im)
         padded = jnp.pad(change, ((0, 0), (place, place), (place, place)))
         gathered = lax.dynamic_slice(padded, spread, (2, extent, extent))
         if update + 1 < ITERS:

time: 149 us -> 129 us (0.87)
  the two profiles are of different devices: /device:TPU:87 before, /device:TPU:71 now
where the time goes in v3:
time: 129 us; the launch traced here: 128 us
  starting transfers between devices  60.2 us (47%)
  waiting for transfers between devices  33.9 us (26%)
  Pallas kernels  10.5 us (8%)
  other arithmetic  8.88 us (7%)
  local copies, waits for them, and re-layouts  8.52 us (7%)
  between operations  6 us (5%)
    ppermute x12, starting transfers between devices, from_neighbor(): return lax.ppermute(x, axis, pairs)  60.2 us
    ppermute x12, waiting for transfers between devices, from_neighbor(): return lax.ppermute(x, axis, pairs)  33.9 us
    pallas_call x2, Pallas kernels, pattern_gradient(): pl.pallas_call(gradient_kernel, out_shape=jax.ShapeDtypeStruct((2, rows,...  10.5 us
    slice x6, local copies, waits for them, and re-layouts, neighbor_sum(): piece = lax.slice_in_dim(frame, low - shift, high - shift, axis=dim)  4.89 us
    add x4, other arithmetic, neighbor_sum(): total = piece if total is None else total + piece  3.4 us
  transfers between devices with their start and end apart: 12, of which 11 were waited for; matrix products, arithmetic and copies ran while one was open for 3% of the time, Pallas kernels for 0%

profile of v3, /device:TPU:71, one launch (start us, length us, event | category | flops | bytes accessed | tf_op | source)
XLA Modules:
  0.0 128.0 jit_solution(13297218489073393557)
XLA Ops:
  0.0 1.0 fusion.22
  1.0 4.9 %collective-permute-start = (f32[2,64,256]{2,1,0:T(8,128)S(1)}, f32[2,64,256]{2,1,0:T(8,128)S(1)}, u32[]{:S(2)}, u32[]{:S(2)}) collective-permute-start(f32[2,64,256]{2,1,0:T(8,128)S(1)} %get-tuple-element.15), channel_id=1, source_target_pairs={{0,32},{32,64},{64,96},{96,128},{128,160},{160,192},{192,224},{224... | collective-permute-start | bytes 393224 | tf_op jit(solution)/shard_map/ppermute | solution.py:97
  5.9 13.6 %collective-permute-start.1 = (f32[2,64,256]{2,1,0:T(8,128)S(1)}, f32[2,64,256]{2,1,0:T(8,128)S(1)}, u32[]{:S(2)}, u32[]{:S(2)}) collective-permute-start(f32[2,64,256]{2,1,0:T(8,128)S(1)} %get-tuple-element.16), channel_id=1, source_target_pairs={{32,0},{64,32},{96,64},{128,96},{160,128},{192,160},{224,192},{256... | collective-permute-start | bytes 393224 | tf_op jit(solution)/shard_map/ppermute | solution.py:97
  19.5 1.4 %collective-permute-done = f32[2,64,256]{2,1,0:T(8,128)S(1)} collective-permute-done((f32[2,64,256]{2,1,0:T(8,128)S(1)}, f32[2,64,256]{2,1,0:T(8,128)S(1)}, u32[]{:S(2)}, u32[]{:S(2)}) %collective-permute-start) | collective-permute-done | bytes 131104 | tf_op jit(solution)/shard_map/ppermute | solution.py:97
  20.9 1.8 %collective-permute-done.1 = f32[2,64,256]{2,1,0:T(8,128)S(1)} collective-permute-done((f32[2,64,256]{2,1,0:T(8,128)S(1)}, f32[2,64,256]{2,1,0:T(8,128)S(1)}, u32[]{:S(2)}, u32[]{:S(2)}) %collective-permute-start.1) | collective-permute-done | bytes 131104 | tf_op jit(solution)/shard_map/ppermute | solution.py:97
  22.7 1.1 pad_add_fusion.1
  23.8 0.0 copy-start.5
  23.8 0.2 fusion.21
  24.0 7.5 %collective-permute-start.2 = (f32[2,384,64]{2,1,0:T(8,128)S(1)}, f32[2,384,64]{2,1,0:T(8,128)S(1)}, u32[]{:S(2)}, u32[]{:S(2)}) collective-permute-start(f32[2,384,64]{2,1,0:T(8,128)S(1)} %get-tuple-element.9), channel_id=1, source_target_pairs={{0,1},{1,2},{2,3},{3,4},{4,5},{5,6},{6,7},{7,8},{8,9},{9,10},{10,1... | collective-permute-start | bytes 589832 | tf_op jit(solution)/shard_map/ppermute | solution.py:97
  31.5 1.9 %collective-permute-start.3 = (f32[2,384,64]{2,1,0:T(8,128)S(1)}, f32[2,384,64]{2,1,0:T(8,128)S(1)}, u32[]{:S(2)}, u32[]{:S(2)}) collective-permute-start(f32[2,384,64]{2,1,0:T(8,128)S(1)} %get-tuple-element.10), channel_id=1, source_target_pairs={{1,0},{2,1},{3,2},{4,3},{5,4},{6,5},{7,6},{8,7},{9,8},{10,9},{11,1... | collective-permute-start | bytes 589832 | tf_op jit(solution)/shard_map/ppermute | solution.py:97
  33.4 0.6 fusion.23
  39.1 1.8 %multiply_convert_fusion = (bf16[256,256]{1,0:T(8,128)(2,1)}, bf16[256,256]{1,0:T(8,128)(2,1)}) fusion(), kind=kLoop, calls=%fused_computation.25 | loop fusion | flops 1245184 | bytes 262144 | tf_op jit(solution)/shard_map/convert_element_type | solution.py:26
  40.9 0.0 collective-permute-done.2
  40.9 0.9 collective-permute-done.3
  41.8 0.5 pad_add_fusion
  42.3 0.3 copy-done.3
  42.6 1.0 constant_dynamic-slice_fusion.1.window_ref
  43.6 5.2 %shard_map.46 = f32[2,256,256]{2,1,0:T(8,128)} custom-call(f32[2,256,256]{2,1,0:T(8,128)} %constant_dynamic-slice_fusion.1.window_ref, f32[2,3,256,256]{3,2,1,0:T(8,128)} %probe_ref.3, f32[256,256]{1,0:T(8,128)} %bitcast.10, bf16[256,256]{1,0:T(8,128)(2,1)} %get-tuple-element.20.table_re_ref, bf16[256,256]{1,0:T(8,128)(2,1)} %get-tuple-element.19.table_im_ref), custom_call_target="tpu_custom_call" | custom-call | tf_op jit(solution)/shard_map/pallas_call | solution.py:86
  48.8 1.5 %pad_dynamic-slice_fusion.4 = (f32[2,384,128]{2,1,0:T(8,128)S(1)}, f32[2,384,128]{2,1,0:T(8,128)S(1)}) fusion(s32[]{:T(128)S(6)} %select_n.36, s32[]{:T(128)S(6)} %add.161, f32[2,256,256]{2,1,0:T(8,128)} %shard_map.46, s32[]{:T(128)S(6)} %select_n.37), kind=kLoop, calls=%fused_computation.4 | loop fusion | bytes 1310732 | tf_op jit(solution)/shard_map/slice | solution.py:107
  50.3 4.0 %collective-permute-start.4 = (f32[2,384,128]{2,1,0:T(8,128)S(1)}, f32[2,384,128]{2,1,0:T(8,128)S(1)}, u32[]{:S(2)}, u32[]{:S(2)}) collective-permute-start(f32[2,384,128]{2,1,0:T(8,128)S(1)} %get-tuple-element.13), channel_id=1, source_target_pairs={{0,1},{1,2},{2,3},{3,4},{4,5},{5,6},{6,7},{7,8},{8,9},{9,10},{10,1... | collective-permute-start | bytes 1179656 | tf_op jit(solution)/shard_map/ppermute | solution.py:97
  54.3 1.9 %collective-permute-start.5 = (f32[2,384,128]{2,1,0:T(8,128)S(1)}, f32[2,384,128]{2,1,0:T(8,128)S(1)}, u32[]{:S(2)}, u32[]{:S(2)}) collective-permute-start(f32[2,384,128]{2,1,0:T(8,128)S(1)} %get-tuple-element.14), channel_id=1, source_target_pairs={{1,0},{2,1},{3,2},{4,3},{5,4},{6,5},{7,6},{8,7},{9,8},{10,9},{11,1... | collective-permute-start | bytes 1179656 | tf_op jit(solution)/shard_map/ppermute | solution.py:97
  56.2 2.8 %collective-permute-done.4 = f32[2,384,128]{2,1,0:T(8,128)S(1)} collective-permute-done((f32[2,384,128]{2,1,0:T(8,128)S(1)}, f32[2,384,128]{2,1,0:T(8,128)S(1)}, u32[]{:S(2)}, u32[]{:S(2)}) %collective-permute-start.4) | collective-permute-done | bytes 393248 | tf_op jit(solution)/shard_map/ppermute | solution.py:97
  59.0 5.6 %collective-permute-done.5 = f32[2,384,128]{2,1,0:T(8,128)S(1)} collective-permute-done((f32[2,384,128]{2,1,0:T(8,128)S(1)}, f32[2,384,128]{2,1,0:T(8,128)S(1)}, u32[]{:S(2)}, u32[]{:S(2)}) %collective-permute-start.5) | collective-permute-done | bytes 393248 | tf_op jit(solution)/shard_map/ppermute | solution.py:97
  64.6 0.4 fusion.1
  65.0 0.0 copy-start
  65.0 0.8 fusion.19
  65.8 1.9 %collective-permute-start.6 = (f32[2,128,384]{2,1,0:T(8,128)}, f32[2,128,384]{2,1,0:T(8,128)S(1)}, u32[]{:S(2)}, u32[]{:S(2)}) collective-permute-start(f32[2,128,384]{2,1,0:T(8,128)} %get-tuple-element.5), channel_id=1, source_target_pairs={{0,32},{32,64},{64,96},{96,128},{128,160},{160,192},{192,224},{224... | collective-permute-start | bytes 1179656 | tf_op jit(solution)/shard_map/ppermute | solution.py:97
  67.7 8.3 %collective-permute-start.7 = (f32[2,128,384]{2,1,0:T(8,128)S(1)}, f32[2,128,384]{2,1,0:T(8,128)}, u32[]{:S(2)}, u32[]{:S(2)}) collective-permute-start(f32[2,128,384]{2,1,0:T(8,128)S(1)} %get-tuple-element.6), channel_id=1, source_target_pairs={{32,0},{64,32},{96,64},{128,96},{160,128},{192,160},{224,192},{256... | collective-permute-start | bytes 1179656 | tf_op jit(solution)/shard_map/ppermute | solution.py:97
  76.1 0.1 multiply_reduce_fusion
  76.2 0.7 reduce_max.9
  77.6 0.1 broadcast_and_fusion
  77.8 8.7 %collective-permute-done.6 = f32[2,128,384]{2,1,0:T(8,128)S(1)} collective-permute-done((f32[2,128,384]{2,1,0:T(8,128)}, f32[2,128,384]{2,1,0:T(8,128)S(1)}, u32[]{:S(2)}, u32[]{:S(2)}) %collective-permute-start.6) | collective-permute-done | bytes 393248 | tf_op jit(solution)/shard_map/ppermute | solution.py:97
  86.5 0.7 copy-done.4
  87.2 1.2 collective-permute-done.7
  88.4 1.7 %add_select_fusion = f32[2,384,384]{2,1,0:T(8,128)S(1)} fusion(f32[2,128,384]{2,1,0:T(8,128)} %collective-permute-done.7, f32[2,384,384]{2,1,0:T(8,128)S(1)} %fusion.1, f32[2,128,384]{2,1,0:T(8,128)} %copy-done.4, f32[]{:T(128)S(6)} %add.154, pred[384,384]{1,0:T(8,128)(4,1)S(1)} %broadcast_and_fusion, f32[2,384,64]{2,1,0:T(8,128)} %copy-done.3, ...), kind=kLoop, calls=%fused_computation.9 | loop fusion | flops 2064384 | bytes 4472836 | tf_op jit(solution)/shard_map/jit(_where)/select_n | solution.py:150
  90.1 1.0 constant_dynamic-slice_fusion.window_ref
  91.1 5.2 %shard_map.47 = f32[2,256,256]{2,1,0:T(8,128)} custom-call(f32[2,256,256]{2,1,0:T(8,128)} %constant_dynamic-slice_fusion.window_ref, f32[2,3,256,256]{3,2,1,0:T(8,128)} %probe_ref.3, f32[256,256]{1,0:T(8,128)} %bitcast.11, bf16[256,256]{1,0:T(8,128)(2,1)} %get-tuple-element.20.table_re_ref, bf16[256,256]{1,0:T(8,128)(2,1)} %get-tuple-element.19.table_im_ref), custom_call_target="tpu_custom_call" | custom-call | tf_op jit(solution)/shard_map/pallas_call | solution.py:86
  96.4 1.4 %pad_dynamic-slice_fusion.1 = (f32[2,384,64]{2,1,0:T(8,128)S(1)}, f32[2,384,64]{2,1,0:T(8,128)S(1)}) fusion(s32[]{:T(128)S(6)} %select_n.36, s32[]{:T(128)S(6)} %add.162, f32[2,256,256]{2,1,0:T(8,128)} %shard_map.47, s32[]{:T(128)S(6)} %select_n.37), kind=kLoop, calls=%fused_computation.1 | loop fusion | bytes 917516 | tf_op jit(solution)/shard_map/slice | solution.py:107
  97.8 3.9 %collective-permute-start.8 = (f32[2,384,64]{2,1,0:T(8,128)S(1)}, f32[2,384,64]{2,1,0:T(8,128)S(1)}, u32[]{:S(2)}, u32[]{:S(2)}) collective-permute-start(f32[2,384,64]{2,1,0:T(8,128)S(1)} %get-tuple-element.11), channel_id=1, source_target_pairs={{0,1},{1,2},{2,3},{3,4},{4,5},{5,6},{6,7},{7,8},{8,9},{9,10},{10,1... | collective-permute-start | bytes 589832 | tf_op jit(solution)/shard_map/ppermute | solution.py:97
  101.7 1.9 %collective-permute-start.9 = (f32[2,384,64]{2,1,0:T(8,128)S(1)}, f32[2,384,64]{2,1,0:T(8,128)}, u32[]{:S(2)}, u32[]{:S(2)}) collective-permute-start(f32[2,384,64]{2,1,0:T(8,128)S(1)} %get-tuple-element.12), channel_id=1, source_target_pairs={{1,0},{2,1},{3,2},{4,3},{5,4},{6,5},{7,6},{8,7},{9,8},{10,9},{11,1... | collective-permute-start | bytes 589832 | tf_op jit(solution)/shard_map/ppermute | solution.py:97
  103.6 2.8 %collective-permute-done.8 = f32[2,384,64]{2,1,0:T(8,128)S(1)} collective-permute-done((f32[2,384,64]{2,1,0:T(8,128)S(1)}, f32[2,384,64]{2,1,0:T(8,128)S(1)}, u32[]{:S(2)}, u32[]{:S(2)}) %collective-permute-start.8) | collective-permute-done | bytes 196640 | tf_op jit(solution)/shard_map/ppermute | solution.py:97
  106.4 5.7 %collective-permute-done.9 = f32[2,384,64]{2,1,0:T(8,128)} collective-permute-done((f32[2,384,64]{2,1,0:T(8,128)S(1)}, f32[2,384,64]{2,1,0:T(8,128)}, u32[]{:S(2)}, u32[]{:S(2)}) %collective-permute-start.9) | collective-permute-done | bytes 196640 | tf_op jit(solution)/shard_map/ppermute | solution.py:97
  112.1 1.4 %fusion.3 = f32[2,384,256]{2,1,0:T(8,128)S(1)} fusion(s32[]{:T(128)S(6)} %select_n.36, s32[]{:T(128)S(6)} %add.163, f32[2,256,256]{2,1,0:T(8,128)S(1)} %copy-done.1, f32[2,384,64]{2,1,0:T(8,128)} %collective-permute-done.9, f32[2,384,64]{2,1,0:T(8,128)S(1)} %collective-permute-done.8), kind=kLoop, calls=%fused_computation.12 | loop fusion | flops 393216 | bytes 1703944 | tf_op jit(solution)/shard_map/add | solution.py:113
  113.5 1.9 %collective-permute-start.10 = (f32[2,64,256]{2,1,0:T(8,128)S(1)}, f32[2,64,256]{2,1,0:T(8,128)S(1)}, u32[]{:S(2)}, u32[]{:S(2)}) collective-permute-start(f32[2,64,256]{2,1,0:T(8,128)S(1)} %get-tuple-element.7), channel_id=1, source_target_pairs={{0,32},{32,64},{64,96},{96,128},{128,160},{160,192},{192,224},{224... | collective-permute-start | bytes 393224 | tf_op jit(solution)/shard_map/ppermute | solution.py:97
  115.5 8.5 %collective-permute-start.11 = (f32[2,64,256]{2,1,0:T(8,128)S(1)}, f32[2,64,256]{2,1,0:T(8,128)S(1)}, u32[]{:S(2)}, u32[]{:S(2)}) collective-permute-start(f32[2,64,256]{2,1,0:T(8,128)S(1)} %get-tuple-element.8), channel_id=1, source_target_pairs={{32,0},{64,32},{96,64},{128,96},{160,128},{192,160},{224,192},{256... | collective-permute-start | bytes 393224 | tf_op jit(solution)/shard_map/ppermute | solution.py:97
  123.9 0.4 collective-permute-done.10
  124.3 2.6 %collective-permute-done.11 = f32[2,64,256]{2,1,0:T(8,128)S(1)} collective-permute-done((f32[2,64,256]{2,1,0:T(8,128)S(1)}, f32[2,64,256]{2,1,0:T(8,128)S(1)}, u32[]{:S(2)}, u32[]{:S(2)}) %collective-permute-start.11) | collective-permute-done | bytes 131104 | tf_op jit(solution)/shard_map/ppermute | solution.py:97
  127.0 1.0 fusion.6
  (10 shorter events, 0.0 us)
Async XLA Ops:
  1.0 19.9 %collective-permute-start = (f32[2,64,256]{2,1,0:T(8,128)S(1)}, f32[2,64,256]{2,1,0:T(8,128)S(1)}, u32[]{:S(2)}, u32[]{:S(2)}) collective-permute-start(f32[2,64,256]{2,1,0:T(8,128)S(1)} %get-tuple-element.15), channel_id=1, source_target_pairs={{0,32},{32,64},{64,96},{96,128},{128,160},{160,192},{192,224},{224... | collective-permute-start | bytes 393224 | tf_op jit(solution)/shard_map/ppermute | solution.py:97
  5.9 16.8 %collective-permute-start.1 = (f32[2,64,256]{2,1,0:T(8,128)S(1)}, f32[2,64,256]{2,1,0:T(8,128)S(1)}, u32[]{:S(2)}, u32[]{:S(2)}) collective-permute-start(f32[2,64,256]{2,1,0:T(8,128)S(1)} %get-tuple-element.16), channel_id=1, source_target_pairs={{32,0},{64,32},{96,64},{128,96},{160,128},{192,160},{224,192},{256... | collective-permute-start | bytes 393224 | tf_op jit(solution)/shard_map/ppermute | solution.py:97
  23.8 9.6 %copy-start.5 = (s32[1,1,1,2]{3,2,1,0:T(1,128)S(1)}, s32[1,1,1,2]{3,2,1,0:T(1,128)}, u32[]{:S(2)}) copy-start(s32[1,1,1,2]{3,2,1,0:T(1,128)} %param.6) | copy-start | bytes 28
  24.0 16.9 %collective-permute-start.2 = (f32[2,384,64]{2,1,0:T(8,128)S(1)}, f32[2,384,64]{2,1,0:T(8,128)S(1)}, u32[]{:S(2)}, u32[]{:S(2)}) collective-permute-start(f32[2,384,64]{2,1,0:T(8,128)S(1)} %get-tuple-element.9), channel_id=1, source_target_pairs={{0,1},{1,2},{2,3},{3,4},{4,5},{5,6},{6,7},{7,8},{8,9},{9,10},{10,1... | collective-permute-start | bytes 589832 | tf_op jit(solution)/shard_map/ppermute | solution.py:97
  31.5 10.3 %collective-permute-start.3 = (f32[2,384,64]{2,1,0:T(8,128)S(1)}, f32[2,384,64]{2,1,0:T(8,128)S(1)}, u32[]{:S(2)}, u32[]{:S(2)}) collective-permute-start(f32[2,384,64]{2,1,0:T(8,128)S(1)} %get-tuple-element.10), channel_id=1, source_target_pairs={{1,0},{2,1},{3,2},{4,3},{5,4},{6,5},{7,6},{8,7},{9,8},{10,9},{11,1... | collective-permute-start | bytes 589832 | tf_op jit(solution)/shard_map/ppermute | solution.py:97
  41.8 0.8 copy-start.3
  48.8 15.8 %copy-start.2 = (f32[2,256,256]{2,1,0:T(8,128)S(1)}, f32[2,256,256]{2,1,0:T(8,128)}, u32[]{:S(2)}) copy-start(f32[2,256,256]{2,1,0:T(8,128)} %shard_map.46) | copy-start | bytes 1572868
  50.3 8.7 %collective-permute-start.4 = (f32[2,384,128]{2,1,0:T(8,128)S(1)}, f32[2,384,128]{2,1,0:T(8,128)S(1)}, u32[]{:S(2)}, u32[]{:S(2)}) collective-permute-start(f32[2,384,128]{2,1,0:T(8,128)S(1)} %get-tuple-element.13), channel_id=1, source_target_pairs={{0,1},{1,2},{2,3},{3,4},{4,5},{5,6},{6,7},{7,8},{8,9},{9,10},{10,1... | collective-permute-start | bytes 1179656 | tf_op jit(solution)/shard_map/ppermute | solution.py:97
  54.3 10.3 %collective-permute-start.5 = (f32[2,384,128]{2,1,0:T(8,128)S(1)}, f32[2,384,128]{2,1,0:T(8,128)S(1)}, u32[]{:S(2)}, u32[]{:S(2)}) collective-permute-start(f32[2,384,128]{2,1,0:T(8,128)S(1)} %get-tuple-element.14), channel_id=1, source_target_pairs={{1,0},{2,1},{3,2},{4,3},{5,4},{6,5},{7,6},{8,7},{9,8},{10,9},{11,1... | collective-permute-start | bytes 1179656 | tf_op jit(solution)/shard_map/ppermute | solution.py:97
  65.0 11.0 %copy-start = (f32[2,3,256,256]{3,2,1,0:T(8,128)S(1)}, f32[2,3,256,256]{3,2,1,0:T(8,128)}, u32[]{:S(2)}) copy-start(f32[2,3,256,256]{3,2,1,0:T(8,128)} %probe_ref.3) | copy-start | bytes 4718596
  65.8 20.6 %collective-permute-start.6 = (f32[2,128,384]{2,1,0:T(8,128)}, f32[2,128,384]{2,1,0:T(8,128)S(1)}, u32[]{:S(2)}, u32[]{:S(2)}) collective-permute-start(f32[2,128,384]{2,1,0:T(8,128)} %get-tuple-element.5), channel_id=1, source_target_pairs={{0,32},{32,64},{64,96},{96,128},{128,160},{160,192},{192,224},{224... | collective-permute-start | bytes 1179656 | tf_op jit(solution)/shard_map/ppermute | solution.py:97
  67.7 20.6 %collective-permute-start.7 = (f32[2,128,384]{2,1,0:T(8,128)S(1)}, f32[2,128,384]{2,1,0:T(8,128)}, u32[]{:S(2)}, u32[]{:S(2)}) collective-permute-start(f32[2,128,384]{2,1,0:T(8,128)S(1)} %get-tuple-element.6), channel_id=1, source_target_pairs={{32,0},{64,32},{96,64},{128,96},{160,128},{192,160},{224,192},{256... | collective-permute-start | bytes 1179656 | tf_op jit(solution)/shard_map/ppermute | solution.py:97
  86.5 0.7 copy-start.4
  96.4 15.7 %copy-start.1 = (f32[2,256,256]{2,1,0:T(8,128)S(1)}, f32[2,256,256]{2,1,0:T(8,128)}, u32[]{:S(2)}) copy-start(f32[2,256,256]{2,1,0:T(8,128)} %shard_map.47) | copy-start | bytes 1572868
  97.8 8.6 %collective-permute-start.8 = (f32[2,384,64]{2,1,0:T(8,128)S(1)}, f32[2,384,64]{2,1,0:T(8,128)S(1)}, u32[]{:S(2)}, u32[]{:S(2)}) collective-permute-start(f32[2,384,64]{2,1,0:T(8,128)S(1)} %get-tuple-element.11), channel_id=1, source_target_pairs={{0,1},{1,2},{2,3},{3,4},{4,5},{5,6},{6,7},{7,8},{8,9},{9,10},{10,1... | collective-permute-start | bytes 589832 | tf_op jit(solution)/shard_map/ppermute | solution.py:97
  101.7 10.4 %collective-permute-start.9 = (f32[2,384,64]{2,1,0:T(8,128)S(1)}, f32[2,384,64]{2,1,0:T(8,128)}, u32[]{:S(2)}, u32[]{:S(2)}) collective-permute-start(f32[2,384,64]{2,1,0:T(8,128)S(1)} %get-tuple-element.12), channel_id=1, source_target_pairs={{1,0},{2,1},{3,2},{4,3},{5,4},{6,5},{7,6},{8,7},{9,8},{10,9},{11,1... | collective-permute-start | bytes 589832 | tf_op jit(solution)/shard_map/ppermute | solution.py:97
  113.5 10.8 %collective-permute-start.10 = (f32[2,64,256]{2,1,0:T(8,128)S(1)}, f32[2,64,256]{2,1,0:T(8,128)S(1)}, u32[]{:S(2)}, u32[]{:S(2)}) collective-permute-start(f32[2,64,256]{2,1,0:T(8,128)S(1)} %get-tuple-element.7), channel_id=1, source_target_pairs={{0,32},{32,64},{64,96},{96,128},{128,160},{160,192},{192,224},{224... | collective-permute-start | bytes 393224 | tf_op jit(solution)/shard_map/ppermute | solution.py:97
  115.5 11.5 %collective-permute-start.11 = (f32[2,64,256]{2,1,0:T(8,128)S(1)}, f32[2,64,256]{2,1,0:T(8,128)S(1)}, u32[]{:S(2)}, u32[]{:S(2)}) collective-permute-start(f32[2,64,256]{2,1,0:T(8,128)S(1)} %get-tuple-element.8), channel_id=1, source_target_pairs={{32,0},{64,32},{96,64},{128,96},{160,128},{192,160},{224,192},{256... | collective-permute-start | bytes 393224 | tf_op jit(solution)/shard_map/ppermute | solution.py:97

commit v4 on v3

--- a/solution.py
+++ b/solution.py
@@ -91,26 +91,38 @@
     )(window, probe_modes, measured, table_re, table_im)
 
 
-def from_neighbor(x, axis, a):
+def swap_with_neighbors(to_low, to_high, axis):
     count = lax.axis_size(axis)
-    pairs = [(r, r - a) for r in range(count) if 0 <= r - a < count]
-    return lax.ppermute(x, axis, pairs)
+    where = lax.axis_index(axis)
+    odd = where % 2 == 1
+    first = [[2 * k, 2 * k + 1] for k in range(count // 2)]
+    second = [[2 * k + 1, 2 * k + 2] for k in range(count // 2 - 1)] + [[0, count - 1]]
+    got = lax.all_gather(jnp.where(odd, to_low, to_high), axis, axis_index_groups=first)
+    partner_first = jnp.where(odd, got[0], got[1])
+    got = lax.all_gather(jnp.where(odd, to_high, to_low), axis, axis_index_groups=second)
+    second_pos = jnp.where(where == 0, 0, jnp.where(where == count - 1, 1, (where + 1) % 2))
+    partner_second = jnp.where(second_pos == 0, got[1], got[0])
+    from_low = jnp.where(odd, partner_first, partner_second)
+    from_high = jnp.where(odd, partner_second, partner_first)
+    from_low = jnp.where(where > 0, from_low, 0.0)
+    from_high = jnp.where(where < count - 1, from_high, 0.0)
+    return from_low, from_high
 
 
 def neighbor_sum(frame, axis, dim, step, src_origin, dst_origin, dst_size):
     src_size = frame.shape[dim]
-    total = None
+    pieces = {}
     for a in (-1, 0, 1):
         low = max(a * step + src_origin, dst_origin)
         high = min(a * step + src_origin + src_size, dst_origin + dst_size)
         shift = a * step + src_origin
-        piece = lax.slice_in_dim(frame, low - shift, high - shift, axis=dim)
-        if a != 0:
-            piece = from_neighbor(piece, axis, a)
         widths = [(0, 0)] * frame.ndim
         widths[dim] = (low - dst_origin, dst_origin + dst_size - high)
-        piece = jnp.pad(piece, widths)
-        total = piece if total is None else total + piece
+        pieces[a] = (lax.slice_in_dim(frame, low - shift, high - shift, axis=dim), widths)
+    from_low, from_high = swap_with_neighbors(pieces[1][0], pieces[-1][0], axis)
+    total = jnp.pad(pieces[0][0], pieces[0][1])
+    total = total + jnp.pad(from_low, pieces[-1][1])
+    total = total + jnp.pad(from_high, pieces[1][1])
     return total
 
 

time: 129 us -> 155 us (1.20)
  the two profiles are of different devices: /device:TPU:71 before, /device:TPU:23 now
where the time goes in v4:
time: 155 us
  blocking collectives  114 us (74%)
  other arithmetic  15.3 us (10%)
  Pallas kernels  10.5 us (7%)
  local copies, waits for them, and re-layouts  8.35 us (5%)
  between operations  5.99 us (4%)
    all_gather x6, blocking collectives, swap_with_neighbors(): lax.all_gather(jnp.where(odd, to_high, to_low), axis, axis_index_groups=s...  81 us
    all_gather x6, blocking collectives, swap_with_neighbors(): lax.all_gather(jnp.where(odd, to_low, to_high), axis, axis_index_groups=f...  33.4 us
    pallas_call x2, Pallas kernels, pattern_gradient(): pl.pallas_call(gradient_kernel, out_shape=jax.ShapeDtypeStruct((2, rows,...  10.5 us
    unnamed x20, local copies, waits for them, and re-layouts  5.02 us
    select_n x6, other arithmetic, swap_with_neighbors(): jnp.where(odd, to_high, to_low)  4.94 us

profile of v4, /device:TPU:23, one launch (start us, length us, event | category | flops | bytes accessed | tf_op | source)
XLA Modules:
  0.0 154.7 jit_solution(15359232159692790574)
XLA Ops:
  0.0 1.0 slice_select_fusion.14
  1.1 6.9 %all-gather = f32[4,64,256]{2,1,0:T(8,128)S(1)} all-gather(f32[2,64,256]{2,1,0:T(8,128)S(1)} %get-tuple-element.28), channel_id=2, replica_groups={{0,32},{64,96},{128,160},{192,224},{256,288},{320,352},{384,416},{448,4..., dimensions={0}, use_global_device_ids=true | all-gather | bytes 393216 | tf_op jit(solution)/shard_map/all_gather | solution.py:100
  7.9 23.1 %all-gather.1 = f32[4,64,256]{2,1,0:T(8,128)S(1)} all-gather(f32[2,64,256]{2,1,0:T(8,128)S(1)} %get-tuple-element.27), channel_id=3, replica_groups={{32,64},{96,128},{160,192},{224,256},{288,320},{352,384},{416,448},{480..., dimensions={0}, use_global_device_ids=true | all-gather | bytes 393216 | tf_op jit(solution)/shard_map/all_gather | solution.py:102
  31.2 0.2 slice_select_fusion.6
  31.4 0.1 copy.17
  31.5 3.1 %all-gather.2 = f32[4,384,64]{1,2,0:T(8,128)S(1)} all-gather(f32[2,384,64]{1,2,0:T(8,128)S(1)} %copy.17), channel_id=4, replica_groups={{0,1},{2,3},{4,5},{6,7},{8,9},{10,11},{12,13},{14,15},{16,17},{18,19},{..., dimensions={0}, use_global_device_ids=true | all-gather | bytes 589824 | tf_op jit(solution)/shard_map/all_gather | solution.py:100
  34.7 0.2 copy.29
  34.8 0.2 copy.30
  35.0 0.2 copy.20
  35.2 7.0 %all-gather.3 = f32[4,384,64]{1,2,0:T(8,128)S(1)} all-gather(f32[2,384,64]{1,2,0:T(8,128)S(1)} %copy.20), channel_id=5, replica_groups={{1,2},{3,4},{5,6},{7,8},{9,10},{11,12},{13,14},{15,16},{17,18},{19,20},..., dimensions={0}, use_global_device_ids=true | all-gather | bytes 589824 | tf_op jit(solution)/shard_map/all_gather | solution.py:102
  42.2 0.2 copy.31
  42.4 0.2 copy.32
  42.7 0.5 pad_add_fusion
  43.1 0.2 copy-done.5
  43.3 0.6 fusion.27
  46.5 1.0 constant_dynamic-slice_fusion.1.window_ref
  47.5 1.8 %multiply_convert_fusion = (bf16[256,256]{1,0:T(8,128)(2,1)}, bf16[256,256]{1,0:T(8,128)(2,1)}) fusion(), kind=kLoop, calls=%fused_computation.41 | loop fusion | flops 1245184 | bytes 262144 | tf_op jit(solution)/shard_map/convert_element_type | solution.py:26
  49.2 5.2 %shard_map.46 = f32[2,256,256]{2,1,0:T(8,128)} custom-call(f32[2,256,256]{2,1,0:T(8,128)} %constant_dynamic-slice_fusion.1.window_ref, f32[2,3,256,256]{3,2,1,0:T(8,128)} %probe_ref.3, f32[256,256]{1,0:T(8,128)} %bitcast.10, bf16[256,256]{1,0:T(8,128)(2,1)} %get-tuple-element.40.table_re_ref, bf16[256,256]{1,0:T(8,128)(2,1)} %get-tuple-element.39.table_im_ref), custom_call_target="tpu_custom_call" | custom-call | tf_op jit(solution)/shard_map/pallas_call | solution.py:86
  57.0 1.9 %fusion.13 = (f32[2,384,128]{2,1,0:T(8,128)S(1)}, f32[2,384,128]{2,1,0:T(8,128)S(1)}) fusion(s32[]{:T(128)S(6)} %select_n.437, s32[]{:T(128)S(6)} %select_n.438, f32[2,256,256]{2,1,0:T(8,128)} %shard_map.46, s32[]{:T(128)S(6)} %add.198, pred[]{:T(512)S(6)} %eq.59), kind=kLoop, calls=%fused_computation.46 | loop fusion | flops 196608 | bytes 1310733 | tf_op jit(solution)/shard_map/jit(_where)/select_n | solution.py:102
  58.9 2.4 %all-gather.4 = f32[4,384,128]{2,1,0:T(8,128)S(1)} all-gather(f32[2,384,128]{2,1,0:T(8,128)S(1)} %get-tuple-element.24), channel_id=6, replica_groups={{0,1},{2,3},{4,5},{6,7},{8,9},{10,11},{12,13},{14,15},{16,17},{18,19},{..., dimensions={0}, use_global_device_ids=true | all-gather | bytes 1179648 | tf_op jit(solution)/shard_map/all_gather | solution.py:100
  61.3 9.1 %all-gather.5 = f32[4,384,128]{2,1,0:T(8,128)S(1)} all-gather(f32[2,384,128]{2,1,0:T(8,128)S(1)} %get-tuple-element.23), channel_id=7, replica_groups={{1,2},{3,4},{5,6},{7,8},{9,10},{11,12},{13,14},{15,16},{17,18},{19,20},..., dimensions={0}, use_global_device_ids=true | all-gather | bytes 1179648 | tf_op jit(solution)/shard_map/all_gather | solution.py:102
  70.5 0.9 copy-done.2
  71.4 0.4 fusion.1
  71.9 10.9 %all-gather.6 = f32[4,128,384]{2,1,0:T(8,128)S(1)} all-gather(f32[2,128,384]{2,1,0:T(8,128)S(1)} %get-tuple-element.14), channel_id=8, replica_groups={{0,32},{64,96},{128,160},{192,224},{256,288},{320,352},{384,416},{448,4..., dimensions={0}, use_global_device_ids=true | all-gather | bytes 1179648 | tf_op jit(solution)/shard_map/all_gather | solution.py:100
  82.8 21.9 %all-gather.7 = f32[4,128,384]{2,1,0:T(8,128)S(1)} all-gather(f32[2,128,384]{2,1,0:T(8,128)S(1)} %get-tuple-element.13), channel_id=9, replica_groups={{32,64},{96,128},{160,192},{224,256},{288,320},{352,384},{416,448},{480..., dimensions={0}, use_global_device_ids=true | all-gather | bytes 1179648 | tf_op jit(solution)/shard_map/all_gather | solution.py:102
  104.8 0.8 broadcast_and_fusion
  105.6 0.6 copy-done
  106.2 0.8 multiply_reduce_fusion
  107.0 1.7 %reduce_max.9 = f32[]{:T(128)} reduce(f32[256,256]{1,0:T(8,128)} %multiply_reduce_fusion, f32[]{:T(128)} %constant.97.clone.1), dimensions={0,1}, to_apply=%region_1.2 | reduce | flops 65535 | bytes 262152 | tf_op jit(solution)/shard_map/reduce_max | solution.py:142
  109.4 1.4 add_select_fusion
  110.8 1.0 copy-done.3
  111.8 1.0 constant_dynamic-slice_fusion.window_ref
  112.8 5.3 %shard_map.47 = f32[2,256,256]{2,1,0:T(8,128)} custom-call(f32[2,256,256]{2,1,0:T(8,128)} %constant_dynamic-slice_fusion.window_ref, f32[2,3,256,256]{3,2,1,0:T(8,128)} %probe_ref.3, f32[256,256]{1,0:T(8,128)} %bitcast.11, bf16[256,256]{1,0:T(8,128)(2,1)} %get-tuple-element.40.table_re_ref, bf16[256,256]{1,0:T(8,128)(2,1)} %get-tuple-element.39.table_im_ref), custom_call_target="tpu_custom_call" | custom-call | tf_op jit(solution)/shard_map/pallas_call | solution.py:86
  118.1 1.7 %fusion.15 = (f32[2,384,64]{2,1,0:T(8,128)S(1)}, f32[2,384,64]{2,1,0:T(8,128)S(1)}) fusion(s32[]{:T(128)S(6)} %select_n.437, s32[]{:T(128)S(6)} %add.200, f32[2,256,256]{2,1,0:T(8,128)} %shard_map.47, s32[]{:T(128)S(6)} %select_n.438, pred[]{:T(512)S(6)} %eq.59), kind=kLoop, calls=%fused_computation.48 | loop fusion | flops 98304 | bytes 917517 | tf_op jit(solution)/shard_map/jit(_where)/select_n | solution.py:102
  119.8 0.1 copy.23
  120.0 4.6 %all-gather.8 = f32[4,384,64]{1,2,0:T(8,128)S(1)} all-gather(f32[2,384,64]{1,2,0:T(8,128)S(1)} %copy.23), channel_id=10, replica_groups={{0,1},{2,3},{4,5},{6,7},{8,9},{10,11},{12,13},{14,15},{16,17},{18,19},{..., dimensions={0}, use_global_device_ids=true | all-gather | bytes 589824 | tf_op jit(solution)/shard_map/all_gather | solution.py:100
  124.7 0.2 copy.33
  124.8 0.2 copy.34
  125.0 0.2 copy.26
  125.1 7.0 %all-gather.9 = f32[4,384,64]{1,2,0:T(8,128)S(1)} all-gather(f32[2,384,64]{1,2,0:T(8,128)S(1)} %copy.26), channel_id=11, replica_groups={{1,2},{3,4},{5,6},{7,8},{9,10},{11,12},{13,14},{15,16},{17,18},{19,20},..., dimensions={0}, use_global_device_ids=true | all-gather | bytes 589824 | tf_op jit(solution)/shard_map/all_gather | solution.py:102
  132.2 0.2 copy.35
  132.3 0.2 copy.36
  132.5 0.1 select_select_fusion.1
  132.6 0.9 copy-done.1
  133.5 0.4 fusion.3
  134.0 5.5 %all-gather.10 = f32[4,64,256]{2,1,0:T(8,128)S(1)} all-gather(f32[2,64,256]{2,1,0:T(8,128)S(1)} %get-tuple-element.16), channel_id=12, replica_groups={{0,32},{64,96},{128,160},{192,224},{256,288},{320,352},{384,416},{448,4..., dimensions={0}, use_global_device_ids=true | all-gather | bytes 393216 | tf_op jit(solution)/shard_map/all_gather | solution.py:100
  139.5 12.9 %all-gather.11 = f32[4,64,256]{2,1,0:T(8,128)S(1)} all-gather(f32[2,64,256]{2,1,0:T(8,128)S(1)} %get-tuple-element.15), channel_id=13, replica_groups={{32,64},{96,128},{160,192},{224,256},{288,320},{352,384},{416,448},{480..., dimensions={0}, use_global_device_ids=true | all-gather | bytes 393216 | tf_op jit(solution)/shard_map/all_gather | solution.py:102
  152.5 2.1 %fusion.6 = f32[2,256,256]{2,1,0:T(8,128)} fusion(f32[2,384,256]{2,1,0:T(8,128)S(1)} %fusion.3, f32[2,384,384]{2,1,0:T(8,128)} %copy-done.3, f32[2,64,256]{2,1,0:T(8,128)S(1)} %get-tuple-element.20, f32[2,64,256]{2,1,0:T(8,128)S(1)} %get-tuple-element.19, f32[]{:T(128)S(6)} %add.191), kind=kLoop, calls=%fused_computation.17 | loop fusion | flops 524288 | bytes 1835012 | tf_op jit(solution)/shard_map/add | solution.py:166
  (20 shorter events, 0.6 us)
Async XLA Ops:
  0.0 31.1 %copy-start.4 = (f32[2,256,256]{2,1,0:T(8,128)S(1)}, f32[2,256,256]{2,1,0:T(8,128)}, u32[]{:S(2)}) copy-start(f32[2,256,256]{2,1,0:T(8,128)} %param.4) | copy-start | bytes 1572868
  42.6 0.7 copy-start.5
  70.4 1.0 copy-start.2
  104.7 1.5 copy-start
  110.8 1.1 copy-start.3
  132.5 1.0 copy-start.1

commit v5 on v3

--- a/solution.py
+++ b/solution.py
@@ -30,13 +30,30 @@
 INTERPRET = False
 
 
-def gradient_kernel(window_ref, probe_ref, measured_ref, table_re_ref, table_im_ref, out_ref, spectrum_ref):
+def operators(table_re, table_im):
+    left_side = jnp.concatenate(
+        [jnp.concatenate([table_re, -table_im], 1), jnp.concatenate([table_im, table_re], 1)], 0
+    )
+    right_side = jnp.concatenate(
+        [jnp.concatenate([table_re, table_im], 1), jnp.concatenate([-table_im, table_re], 1)], 0
+    )
+    return left_side, right_side
+
+
+def gradient_kernel(window_ref, probe_ref, measured_ref, fwd_left_ref, fwd_right_ref,
+                    inv_left_ref, inv_right_ref, out_ref, spectrum_ref):
     modes = probe_ref.shape[1]
-    table_re = table_re_ref[...]
-    table_im = table_im_ref[...]
+    size = probe_ref.shape[3]
 
     def product(left, right):
         return jnp.dot(left, right, preferred_element_type=jnp.float32)
+
+    def stage(left_ref, right_ref, wave_re, wave_im):
+        stacked = jnp.concatenate([wave_re, wave_im], axis=0)
+        half = product(left_ref[...], stacked).astype(jnp.bfloat16)
+        side = jnp.concatenate([half[:size], half[size:]], axis=1)
+        done = product(side, right_ref[...])
+        return done[:, :size], done[:, size:]
 
     def exit_wave(k):
         obj_re = window_ref[0]
@@ -48,12 +65,9 @@
     power = None
     for k in range(modes):
         exit_re, exit_im = exit_wave(k)
-        exit_re = exit_re.astype(jnp.bfloat16)
-        exit_im = exit_im.astype(jnp.bfloat16)
-        half_re = (product(table_re, exit_re) - product(table_im, exit_im)).astype(jnp.bfloat16)
-        half_im = (product(table_im, exit_re) + product(table_re, exit_im)).astype(jnp.bfloat16)
-        spec_re = product(half_re, table_re) - product(half_im, table_im)
-        spec_im = product(half_re, table_im) + product(half_im, table_re)
+        spec_re, spec_im = stage(
+            fwd_left_ref, fwd_right_ref, exit_re.astype(jnp.bfloat16), exit_im.astype(jnp.bfloat16)
+        )
         spectrum_ref[0, k] = spec_re
         spectrum_ref[1, k] = spec_im
         term = spec_re * spec_re + spec_im * spec_im
@@ -64,10 +78,7 @@
     for k in range(modes):
         fixed_re = (spectrum_ref[0, k] * scaling).astype(jnp.bfloat16)
         fixed_im = (spectrum_ref[1, k] * scaling).astype(jnp.bfloat16)
-        back_re = (product(table_re, fixed_re) + product(table_im, fixed_im)).astype(jnp.bfloat16)
-        back_im = (product(table_re, fixed_im) - product(table_im, fixed_re)).astype(jnp.bfloat16)
-        revised_re = product(back_re, table_re) + product(back_im, table_im)
-        revised_im = product(back_im, table_re) - product(back_re, table_im)
+        revised_re, revised_im = stage(inv_left_ref, inv_right_ref, fixed_re, fixed_im)
         exit_re, exit_im = exit_wave(k)
         residue_re = revised_re - exit_re
         residue_im = revised_im - exit_im
@@ -81,14 +92,14 @@
     out_ref[1] = grad_im
 
 
-def pattern_gradient(window, measured, probe_modes, table_re, table_im):
+def pattern_gradient(window, measured, probe_modes, forward, inverse):
     _, modes, rows, cols = probe_modes.shape
     return pl.pallas_call(
         gradient_kernel,
         out_shape=jax.ShapeDtypeStruct((2, rows, cols), jnp.float32),
         scratch_shapes=[pltpu.VMEM((2, modes, rows, cols), jnp.float32)],
         interpret=INTERPRET,
-    )(window, probe_modes, measured, table_re, table_im)
+    )(window, probe_modes, measured, forward[0], forward[1], inverse[0], inverse[1])
 
 
 def from_neighbor(x, axis, a):
@@ -127,6 +138,8 @@
 
 def on_device(object_planes, probe_modes, positions, amplitudes):
     table_re, table_im = tables(W)
+    forward = operators(table_re, table_im)
+    inverse = operators(table_re, -table_im)
     peak_power = jnp.max(jnp.sum(probe_modes * probe_modes, axis=(0, 1))) + EPSILON
     offsets = positions.reshape(-1, 2)
     measured = amplitudes.reshape(-1, W, W)
@@ -140,7 +153,7 @@
     extended = neighbor_sum(extended, "col", 2, tile_size, M, 0, extent)
     for update in range(ITERS):
         window = lax.dynamic_slice(extended, corner, (2, W, W))
-        change = pattern_gradient(window, measured[0], probe_modes, table_re, table_im)
+        change = pattern_gradient(window, measured[0], probe_modes, forward, inverse)
         padded = jnp.pad(change, ((0, 0), (place, place), (place, place)))
         gathered = lax.dynamic_slice(padded, spread, (2, extent, extent))
         if update + 1 < ITERS:

time: 129 us -> 129 us (level)
  the two profiles are of different devices: /device:TPU:71 before, /device:TPU:87 now
where the time goes in v5:
time: 129 us; the launch traced here: 128 us
  starting transfers between devices  54.1 us (42%)
  waiting for transfers between devices  38.9 us (30%)
  Pallas kernels  11.8 us (9%)
  local copies, waits for them, and re-layouts  9.39 us (7%)
  other arithmetic  8.21 us (6%)
  between operations  5.9 us (5%)
    ppermute x12, starting transfers between devices, from_neighbor(): return lax.ppermute(x, axis, pairs)  54.1 us
    ppermute x12, waiting for transfers between devices, from_neighbor(): return lax.ppermute(x, axis, pairs)  38.9 us
    pallas_call x2, Pallas kernels, pattern_gradient(): pl.pallas_call(gradient_kernel, out_shape=jax.ShapeDtypeStruct((2, rows,...  11.8 us
    slice x6, local copies, waits for them, and re-layouts, neighbor_sum(): piece = lax.slice_in_dim(frame, low - shift, high - shift, axis=dim)  5.02 us
  transfers between devices with their start and end apart: 12, of which 9 were waited for; matrix products, arithmetic and copies ran while one was open for 4% of the time, Pallas kernels for 0%

profile of v5, /device:TPU:87, one launch (start us, length us, event | category | flops | bytes accessed | tf_op | source)
XLA Modules:
  0.0 128.3 jit_solution(4589030625271376808)
XLA Ops:
  0.0 1.0 fusion.25
  1.1 4.9 %collective-permute-start = (f32[2,64,256]{2,1,0:T(8,128)S(1)}, f32[2,64,256]{2,1,0:T(8,128)S(1)}, u32[]{:S(2)}, u32[]{:S(2)}) collective-permute-start(f32[2,64,256]{2,1,0:T(8,128)S(1)} %get-tuple-element.15), channel_id=1, source_target_pairs={{0,32},{32,64},{64,96},{96,128},{128,160},{160,192},{192,224},{224... | collective-permute-start | bytes 393224 | tf_op jit(solution)/shard_map/ppermute | solution.py:108
  6.0 14.5 %collective-permute-start.1 = (f32[2,64,256]{2,1,0:T(8,128)S(1)}, f32[2,64,256]{2,1,0:T(8,128)S(1)}, u32[]{:S(2)}, u32[]{:S(2)}) collective-permute-start(f32[2,64,256]{2,1,0:T(8,128)S(1)} %get-tuple-element.16), channel_id=1, source_target_pairs={{32,0},{64,32},{96,64},{128,96},{160,128},{192,160},{224,192},{256... | collective-permute-start | bytes 393224 | tf_op jit(solution)/shard_map/ppermute | solution.py:108
  20.5 1.3 %fusion.26 = (s32[1,1]{1,0:T(1,128)}, s32[1,1]{1,0:T(1,128)}) fusion(s32[1,2]{1,0:T(1,128)} %bitcast.12), kind=kLoop, calls=%fused_computation.51 | loop fusion | bytes 16 | tf_op jit(solution)/shard_map/slice | solution.py:150
  26.9 1.1 multiply_convert_fusion
  28.0 0.0 collective-permute-done
  28.0 0.0 collective-permute-done.1
  28.0 0.1 pad_add_fusion.1
  28.1 0.2 fusion.24
  28.2 5.2 %collective-permute-start.2 = (f32[2,384,64]{2,1,0:T(8,128)S(1)}, f32[2,384,64]{2,1,0:T(8,128)S(1)}, u32[]{:S(2)}, u32[]{:S(2)}) collective-permute-start(f32[2,384,64]{2,1,0:T(8,128)S(1)} %get-tuple-element.9), channel_id=1, source_target_pairs={{0,1},{1,2},{2,3},{3,4},{4,5},{5,6},{6,7},{7,8},{8,9},{9,10},{10,1... | collective-permute-start | bytes 589832 | tf_op jit(solution)/shard_map/ppermute | solution.py:108
  33.4 1.9 %collective-permute-start.3 = (f32[2,384,64]{2,1,0:T(8,128)S(1)}, f32[2,384,64]{2,1,0:T(8,128)S(1)}, u32[]{:S(2)}, u32[]{:S(2)}) collective-permute-start(f32[2,384,64]{2,1,0:T(8,128)S(1)} %get-tuple-element.10), channel_id=1, source_target_pairs={{1,0},{2,1},{3,2},{4,3},{5,4},{6,5},{7,6},{8,7},{9,8},{10,9},{11,1... | collective-permute-start | bytes 589832 | tf_op jit(solution)/shard_map/ppermute | solution.py:108
  35.4 1.0 fusion.15
  36.4 1.1 fusion.5
  37.4 0.7 collective-permute-done.2
  38.1 5.6 %collective-permute-done.3 = f32[2,384,64]{2,1,0:T(8,128)S(1)} collective-permute-done((f32[2,384,64]{2,1,0:T(8,128)S(1)}, f32[2,384,64]{2,1,0:T(8,128)S(1)}, u32[]{:S(2)}, u32[]{:S(2)}) %collective-permute-start.3) | collective-permute-done | bytes 196640 | tf_op jit(solution)/shard_map/ppermute | solution.py:108
  43.7 0.5 pad_add_fusion
  44.2 0.3 copy-done.3
  44.5 1.0 constant_dynamic-slice_fusion.1.window_ref
  45.5 5.9 %shard_map.46 = f32[2,256,256]{2,1,0:T(8,128)} custom-call(f32[2,256,256]{2,1,0:T(8,128)} %constant_dynamic-slice_fusion.1.window_ref, f32[2,3,256,256]{3,2,1,0:T(8,128)} %probe_ref.3, f32[256,256]{1,0:T(8,128)} %bitcast.10, bf16[512,512]{1,0:T(8,128)(2,1)} %get-tuple-element.18.fwd_left_ref.inv_right_ref, ...), custom_call_target="tpu_custom_call" | custom-call | tf_op jit(solution)/shard_map/pallas_call | solution.py:97
  51.4 1.5 %pad_dynamic-slice_fusion.4 = (f32[2,384,128]{2,1,0:T(8,128)S(1)}, f32[2,384,128]{2,1,0:T(8,128)S(1)}) fusion(s32[]{:T(128)S(6)} %select_n.44, s32[]{:T(128)S(6)} %add.169, f32[2,256,256]{2,1,0:T(8,128)} %shard_map.46, s32[]{:T(128)S(6)} %select_n.45), kind=kLoop, calls=%fused_computation.4 | loop fusion | bytes 1310732 | tf_op jit(solution)/shard_map/slice | solution.py:118
  52.9 1.9 %collective-permute-start.4 = (f32[2,384,128]{2,1,0:T(8,128)S(1)}, f32[2,384,128]{2,1,0:T(8,128)S(1)}, u32[]{:S(2)}, u32[]{:S(2)}) collective-permute-start(f32[2,384,128]{2,1,0:T(8,128)S(1)} %get-tuple-element.13), channel_id=1, source_target_pairs={{0,1},{1,2},{2,3},{3,4},{4,5},{5,6},{6,7},{7,8},{8,9},{9,10},{10,1... | collective-permute-start | bytes 1179656 | tf_op jit(solution)/shard_map/ppermute | solution.py:108
  54.8 2.4 %collective-permute-start.5 = (f32[2,384,128]{2,1,0:T(8,128)S(1)}, f32[2,384,128]{2,1,0:T(8,128)S(1)}, u32[]{:S(2)}, u32[]{:S(2)}) collective-permute-start(f32[2,384,128]{2,1,0:T(8,128)S(1)} %get-tuple-element.14), channel_id=1, source_target_pairs={{1,0},{2,1},{3,2},{4,3},{5,4},{6,5},{7,6},{8,7},{9,8},{10,9},{11,1... | collective-permute-start | bytes 1179656 | tf_op jit(solution)/shard_map/ppermute | solution.py:108
  57.2 2.3 %collective-permute-done.4 = f32[2,384,128]{2,1,0:T(8,128)S(1)} collective-permute-done((f32[2,384,128]{2,1,0:T(8,128)S(1)}, f32[2,384,128]{2,1,0:T(8,128)S(1)}, u32[]{:S(2)}, u32[]{:S(2)}) %collective-permute-start.4) | collective-permute-done | bytes 393248 | tf_op jit(solution)/shard_map/ppermute | solution.py:108
  59.5 5.6 %collective-permute-done.5 = f32[2,384,128]{2,1,0:T(8,128)S(1)} collective-permute-done((f32[2,384,128]{2,1,0:T(8,128)S(1)}, f32[2,384,128]{2,1,0:T(8,128)S(1)}, u32[]{:S(2)}, u32[]{:S(2)}) %collective-permute-start.5) | collective-permute-done | bytes 393248 | tf_op jit(solution)/shard_map/ppermute | solution.py:108
  65.1 0.4 fusion.1
  65.6 0.0 copy-start
  65.6 0.8 fusion.22
  66.4 1.9 %collective-permute-start.6 = (f32[2,128,384]{2,1,0:T(8,128)}, f32[2,128,384]{2,1,0:T(8,128)S(1)}, u32[]{:S(2)}, u32[]{:S(2)}) collective-permute-start(f32[2,128,384]{2,1,0:T(8,128)} %get-tuple-element.5), channel_id=1, source_target_pairs={{0,32},{32,64},{64,96},{96,128},{128,160},{160,192},{192,224},{224... | collective-permute-start | bytes 1179656 | tf_op jit(solution)/shard_map/ppermute | solution.py:108
  68.3 7.6 %collective-permute-start.7 = (f32[2,128,384]{2,1,0:T(8,128)S(1)}, f32[2,128,384]{2,1,0:T(8,128)}, u32[]{:S(2)}, u32[]{:S(2)}) collective-permute-start(f32[2,128,384]{2,1,0:T(8,128)S(1)} %get-tuple-element.6), channel_id=1, source_target_pairs={{32,0},{64,32},{96,64},{128,96},{160,128},{192,160},{224,192},{256... | collective-permute-start | bytes 1179656 | tf_op jit(solution)/shard_map/ppermute | solution.py:108
  75.9 0.1 multiply_reduce_fusion
  76.0 0.7 reduce_max.9
  77.3 0.1 broadcast_and_fusion
  77.4 10.9 %collective-permute-done.6 = f32[2,128,384]{2,1,0:T(8,128)S(1)} collective-permute-done((f32[2,128,384]{2,1,0:T(8,128)}, f32[2,128,384]{2,1,0:T(8,128)S(1)}, u32[]{:S(2)}, u32[]{:S(2)}) %collective-permute-start.6) | collective-permute-done | bytes 393248 | tf_op jit(solution)/shard_map/ppermute | solution.py:108
  88.3 0.7 copy-done.5
  89.1 1.7 %add_select_fusion = f32[2,384,384]{2,1,0:T(8,128)S(1)} fusion(f32[2,128,384]{2,1,0:T(8,128)} %collective-permute-done.7, f32[2,384,384]{2,1,0:T(8,128)S(1)} %fusion.1, f32[2,128,384]{2,1,0:T(8,128)} %copy-done.5, f32[]{:T(128)S(6)} %add.162, pred[384,384]{1,0:T(8,128)(4,1)S(1)} %broadcast_and_fusion, f32[2,384,64]{2,1,0:T(8,128)} %copy-done.3, ...), kind=kLoop, calls=%fused_computation.9 | loop fusion | flops 2064384 | bytes 4472836 | tf_op jit(solution)/shard_map/jit(_where)/select_n | solution.py:163
  90.8 1.0 constant_dynamic-slice_fusion.window_ref
  91.8 5.9 %shard_map.47 = f32[2,256,256]{2,1,0:T(8,128)} custom-call(f32[2,256,256]{2,1,0:T(8,128)} %constant_dynamic-slice_fusion.window_ref, f32[2,3,256,256]{3,2,1,0:T(8,128)} %probe_ref.3, f32[256,256]{1,0:T(8,128)} %bitcast.11, bf16[512,512]{1,0:T(8,128)(2,1)} %get-tuple-element.18.fwd_left_ref.inv_right_ref, ...), custom_call_target="tpu_custom_call" | custom-call | tf_op jit(solution)/shard_map/pallas_call | solution.py:97
  97.7 1.5 %pad_dynamic-slice_fusion.1 = (f32[2,384,64]{2,1,0:T(8,128)S(1)}, f32[2,384,64]{2,1,0:T(8,128)S(1)}) fusion(s32[]{:T(128)S(6)} %select_n.44, s32[]{:T(128)S(6)} %add.170, f32[2,256,256]{2,1,0:T(8,128)} %shard_map.47, s32[]{:T(128)S(6)} %select_n.45), kind=kLoop, calls=%fused_computation.1 | loop fusion | bytes 917516 | tf_op jit(solution)/shard_map/slice | solution.py:118
  99.2 2.4 %collective-permute-start.8 = (f32[2,384,64]{2,1,0:T(8,128)S(1)}, f32[2,384,64]{2,1,0:T(8,128)S(1)}, u32[]{:S(2)}, u32[]{:S(2)}) collective-permute-start(f32[2,384,64]{2,1,0:T(8,128)S(1)} %get-tuple-element.11), channel_id=1, source_target_pairs={{0,1},{1,2},{2,3},{3,4},{4,5},{5,6},{6,7},{7,8},{8,9},{9,10},{10,1... | collective-permute-start | bytes 589832 | tf_op jit(solution)/shard_map/ppermute | solution.py:108
  101.6 1.9 %collective-permute-start.9 = (f32[2,384,64]{2,1,0:T(8,128)S(1)}, f32[2,384,64]{2,1,0:T(8,128)S(1)}, u32[]{:S(2)}, u32[]{:S(2)}) collective-permute-start(f32[2,384,64]{2,1,0:T(8,128)S(1)} %get-tuple-element.12), channel_id=1, source_target_pairs={{1,0},{2,1},{3,2},{4,3},{5,4},{6,5},{7,6},{8,7},{9,8},{10,9},{11,1... | collective-permute-start | bytes 589832 | tf_op jit(solution)/shard_map/ppermute | solution.py:108
  103.6 2.7 %collective-permute-done.8 = f32[2,384,64]{2,1,0:T(8,128)S(1)} collective-permute-done((f32[2,384,64]{2,1,0:T(8,128)S(1)}, f32[2,384,64]{2,1,0:T(8,128)S(1)}, u32[]{:S(2)}, u32[]{:S(2)}) %collective-permute-start.8) | collective-permute-done | bytes 196640 | tf_op jit(solution)/shard_map/ppermute | solution.py:108
  106.3 5.6 %collective-permute-done.9 = f32[2,384,64]{2,1,0:T(8,128)S(1)} collective-permute-done((f32[2,384,64]{2,1,0:T(8,128)S(1)}, f32[2,384,64]{2,1,0:T(8,128)S(1)}, u32[]{:S(2)}, u32[]{:S(2)}) %collective-permute-start.9) | collective-permute-done | bytes 196640 | tf_op jit(solution)/shard_map/ppermute | solution.py:108
  111.9 0.4 fusion.3
  112.4 1.9 %collective-permute-start.10 = (f32[2,64,256]{2,1,0:T(8,128)S(1)}, f32[2,64,256]{2,1,0:T(8,128)S(1)}, u32[]{:S(2)}, u32[]{:S(2)}) collective-permute-start(f32[2,64,256]{2,1,0:T(8,128)S(1)} %get-tuple-element.7), channel_id=1, source_target_pairs={{0,32},{32,64},{64,96},{96,128},{128,160},{160,192},{192,224},{224... | collective-permute-start | bytes 393224 | tf_op jit(solution)/shard_map/ppermute | solution.py:108
  114.3 7.6 %collective-permute-start.11 = (f32[2,64,256]{2,1,0:T(8,128)S(1)}, f32[2,64,256]{2,1,0:T(8,128)S(1)}, u32[]{:S(2)}, u32[]{:S(2)}) collective-permute-start(f32[2,64,256]{2,1,0:T(8,128)S(1)} %get-tuple-element.8), channel_id=1, source_target_pairs={{32,0},{64,32},{96,64},{128,96},{160,128},{192,160},{224,192},{256... | collective-permute-start | bytes 393224 | tf_op jit(solution)/shard_map/ppermute | solution.py:108
  121.9 2.0 %collective-permute-done.10 = f32[2,64,256]{2,1,0:T(8,128)S(1)} collective-permute-done((f32[2,64,256]{2,1,0:T(8,128)S(1)}, f32[2,64,256]{2,1,0:T(8,128)S(1)}, u32[]{:S(2)}, u32[]{:S(2)}) %collective-permute-start.10) | collective-permute-done | bytes 131104 | tf_op jit(solution)/shard_map/ppermute | solution.py:108
  123.9 3.4 %collective-permute-done.11 = f32[2,64,256]{2,1,0:T(8,128)S(1)} collective-permute-done((f32[2,64,256]{2,1,0:T(8,128)S(1)}, f32[2,64,256]{2,1,0:T(8,128)S(1)}, u32[]{:S(2)}, u32[]{:S(2)}) %collective-permute-start.11) | collective-permute-done | bytes 131104 | tf_op jit(solution)/shard_map/ppermute | solution.py:108
  127.3 1.0 fusion.8
  (12 shorter events, 0.1 us)
Async XLA Ops:
  0.0 28.0 %copy-start.4 = (f32[2,256,256]{2,1,0:T(8,128)S(1)}, f32[2,256,256]{2,1,0:T(8,128)}, u32[]{:S(2)}) copy-start(f32[2,256,256]{2,1,0:T(8,128)} %param.4) | copy-start | bytes 1572868
  1.1 26.9 %collective-permute-start = (f32[2,64,256]{2,1,0:T(8,128)S(1)}, f32[2,64,256]{2,1,0:T(8,128)S(1)}, u32[]{:S(2)}, u32[]{:S(2)}) collective-permute-start(f32[2,64,256]{2,1,0:T(8,128)S(1)} %get-tuple-element.15), channel_id=1, source_target_pairs={{0,32},{32,64},{64,96},{96,128},{128,160},{160,192},{192,224},{224... | collective-permute-start | bytes 393224 | tf_op jit(solution)/shard_map/ppermute | solution.py:108
  6.0 22.0 %collective-permute-start.1 = (f32[2,64,256]{2,1,0:T(8,128)S(1)}, f32[2,64,256]{2,1,0:T(8,128)S(1)}, u32[]{:S(2)}, u32[]{:S(2)}) collective-permute-start(f32[2,64,256]{2,1,0:T(8,128)S(1)} %get-tuple-element.16), channel_id=1, source_target_pairs={{32,0},{64,32},{96,64},{128,96},{160,128},{192,160},{224,192},{256... | collective-permute-start | bytes 393224 | tf_op jit(solution)/shard_map/ppermute | solution.py:108
  28.2 9.9 %collective-permute-start.2 = (f32[2,384,64]{2,1,0:T(8,128)S(1)}, f32[2,384,64]{2,1,0:T(8,128)S(1)}, u32[]{:S(2)}, u32[]{:S(2)}) collective-permute-start(f32[2,384,64]{2,1,0:T(8,128)S(1)} %get-tuple-element.9), channel_id=1, source_target_pairs={{0,1},{1,2},{2,3},{3,4},{4,5},{5,6},{6,7},{7,8},{8,9},{9,10},{10,1... | collective-permute-start | bytes 589832 | tf_op jit(solution)/shard_map/ppermute | solution.py:108
  33.4 10.3 %collective-permute-start.3 = (f32[2,384,64]{2,1,0:T(8,128)S(1)}, f32[2,384,64]{2,1,0:T(8,128)S(1)}, u32[]{:S(2)}, u32[]{:S(2)}) collective-permute-start(f32[2,384,64]{2,1,0:T(8,128)S(1)} %get-tuple-element.10), channel_id=1, source_target_pairs={{1,0},{2,1},{3,2},{4,3},{5,4},{6,5},{7,6},{8,7},{9,8},{10,9},{11,1... | collective-permute-start | bytes 589832 | tf_op jit(solution)/shard_map/ppermute | solution.py:108
  43.7 0.8 copy-start.3
  51.4 13.7 %copy-start.2 = (f32[2,256,256]{2,1,0:T(8,128)S(1)}, f32[2,256,256]{2,1,0:T(8,128)}, u32[]{:S(2)}) copy-start(f32[2,256,256]{2,1,0:T(8,128)} %shard_map.46) | copy-start | bytes 1572868
  52.9 6.6 %collective-permute-start.4 = (f32[2,384,128]{2,1,0:T(8,128)S(1)}, f32[2,384,128]{2,1,0:T(8,128)S(1)}, u32[]{:S(2)}, u32[]{:S(2)}) collective-permute-start(f32[2,384,128]{2,1,0:T(8,128)S(1)} %get-tuple-element.13), channel_id=1, source_target_pairs={{0,1},{1,2},{2,3},{3,4},{4,5},{5,6},{6,7},{7,8},{8,9},{9,10},{10,1... | collective-permute-start | bytes 1179656 | tf_op jit(solution)/shard_map/ppermute | solution.py:108
  54.8 10.3 %collective-permute-start.5 = (f32[2,384,128]{2,1,0:T(8,128)S(1)}, f32[2,384,128]{2,1,0:T(8,128)S(1)}, u32[]{:S(2)}, u32[]{:S(2)}) collective-permute-start(f32[2,384,128]{2,1,0:T(8,128)S(1)} %get-tuple-element.14), channel_id=1, source_target_pairs={{1,0},{2,1},{3,2},{4,3},{5,4},{6,5},{7,6},{8,7},{9,8},{10,9},{11,1... | collective-permute-start | bytes 1179656 | tf_op jit(solution)/shard_map/ppermute | solution.py:108
  65.6 10.3 %copy-start = (f32[2,3,256,256]{3,2,1,0:T(8,128)S(1)}, f32[2,3,256,256]{3,2,1,0:T(8,128)}, u32[]{:S(2)}) copy-start(f32[2,3,256,256]{3,2,1,0:T(8,128)} %probe_ref.3) | copy-start | bytes 4718596
  66.4 21.9 %collective-permute-start.6 = (f32[2,128,384]{2,1,0:T(8,128)}, f32[2,128,384]{2,1,0:T(8,128)S(1)}, u32[]{:S(2)}, u32[]{:S(2)}) collective-permute-start(f32[2,128,384]{2,1,0:T(8,128)} %get-tuple-element.5), channel_id=1, source_target_pairs={{0,32},{32,64},{64,96},{96,128},{128,160},{160,192},{192,224},{224... | collective-permute-start | bytes 1179656 | tf_op jit(solution)/shard_map/ppermute | solution.py:108
  68.3 20.8 %collective-permute-start.7 = (f32[2,128,384]{2,1,0:T(8,128)S(1)}, f32[2,128,384]{2,1,0:T(8,128)}, u32[]{:S(2)}, u32[]{:S(2)}) collective-permute-start(f32[2,128,384]{2,1,0:T(8,128)S(1)} %get-tuple-element.6), channel_id=1, source_target_pairs={{32,0},{64,32},{96,64},{128,96},{160,128},{192,160},{224,192},{256... | collective-permute-start | bytes 1179656 | tf_op jit(solution)/shard_map/ppermute | solution.py:108
  88.3 0.7 copy-start.5
  97.7 14.2 %copy-start.1 = (f32[2,256,256]{2,1,0:T(8,128)S(1)}, f32[2,256,256]{2,1,0:T(8,128)}, u32[]{:S(2)}) copy-start(f32[2,256,256]{2,1,0:T(8,128)} %shard_map.47) | copy-start | bytes 1572868
  99.2 7.1 %collective-permute-start.8 = (f32[2,384,64]{2,1,0:T(8,128)S(1)}, f32[2,384,64]{2,1,0:T(8,128)S(1)}, u32[]{:S(2)}, u32[]{:S(2)}) collective-permute-start(f32[2,384,64]{2,1,0:T(8,128)S(1)} %get-tuple-element.11), channel_id=1, source_target_pairs={{0,1},{1,2},{2,3},{3,4},{4,5},{5,6},{6,7},{7,8},{8,9},{9,10},{10,1... | collective-permute-start | bytes 589832 | tf_op jit(solution)/shard_map/ppermute | solution.py:108
  101.6 10.3 %collective-permute-start.9 = (f32[2,384,64]{2,1,0:T(8,128)S(1)}, f32[2,384,64]{2,1,0:T(8,128)S(1)}, u32[]{:S(2)}, u32[]{:S(2)}) collective-permute-start(f32[2,384,64]{2,1,0:T(8,128)S(1)} %get-tuple-element.12), channel_id=1, source_target_pairs={{1,0},{2,1},{3,2},{4,3},{5,4},{6,5},{7,6},{8,7},{9,8},{10,9},{11,1... | collective-permute-start | bytes 589832 | tf_op jit(solution)/shard_map/ppermute | solution.py:108
  112.4 11.5 %collective-permute-start.10 = (f32[2,64,256]{2,1,0:T(8,128)S(1)}, f32[2,64,256]{2,1,0:T(8,128)S(1)}, u32[]{:S(2)}, u32[]{:S(2)}) collective-permute-start(f32[2,64,256]{2,1,0:T(8,128)S(1)} %get-tuple-element.7), channel_id=1, source_target_pairs={{0,32},{32,64},{64,96},{96,128},{128,160},{160,192},{192,224},{224... | collective-permute-start | bytes 393224 | tf_op jit(solution)/shard_map/ppermute | solution.py:108
  114.3 13.0 %collective-permute-start.11 = (f32[2,64,256]{2,1,0:T(8,128)S(1)}, f32[2,64,256]{2,1,0:T(8,128)S(1)}, u32[]{:S(2)}, u32[]{:S(2)}) collective-permute-start(f32[2,64,256]{2,1,0:T(8,128)S(1)} %get-tuple-element.8), channel_id=1, source_target_pairs={{32,0},{64,32},{96,64},{128,96},{160,128},{192,160},{224,192},{256... | collective-permute-start | bytes 393224 | tf_op jit(solution)/shard_map/ppermute | solution.py:108

commit v6 on v3

--- a/solution.py
+++ b/solution.py
@@ -114,6 +114,38 @@
     return total
 
 
+def rows_from_neighbors(change, offset, tile_size, extent):
+    reach = 2 * M
+    size = change.shape[1]
+    tag = jnp.broadcast_to(
+        jnp.stack([offset[0], offset[1]] + [offset[0]] * 6).astype(jnp.float32)[None, :, None],
+        (2, 8, change.shape[2]),
+    )
+    to_low = jnp.concatenate([change[:, :reach], tag], axis=1)
+    to_high = jnp.concatenate([change[:, size - reach :], tag], axis=1)
+    from_high = from_neighbor(to_low, "row", 1)
+    from_low = from_neighbor(to_high, "row", -1)
+    place = extent - W
+    total = None
+    for got, low_side in ((from_high, False), (from_low, True)):
+        strip = got[:, :reach]
+        row_at = got[0, reach, 0].astype(jnp.int32)
+        col_at = got[0, reach + 1, 0].astype(jnp.int32)
+        if low_side:
+            top = row_at + M + size - reach - tile_size
+            widths = (0, extent)
+        else:
+            top = row_at + M + tile_size
+            widths = (extent, 0)
+        padded = jnp.pad(strip, ((0, 0), widths, (place, place)))
+        start = widths[0] - top
+        piece = lax.dynamic_slice(
+            padded, (jnp.zeros((), jnp.int32), start, place - M - col_at), (2, extent, extent)
+        )
+        total = piece if total is None else total + piece
+    return total
+
+
 def inside_mask(extent, tile_size):
     rows = lax.axis_size("row")
     cols = lax.axis_size("col")
@@ -144,8 +176,8 @@
         padded = jnp.pad(change, ((0, 0), (place, place), (place, place)))
         gathered = lax.dynamic_slice(padded, spread, (2, extent, extent))
         if update + 1 < ITERS:
-            total = neighbor_sum(gathered, "col", 2, tile_size, 0, 0, extent)
-            total = neighbor_sum(total, "row", 1, tile_size, 0, 0, extent)
+            total = gathered + rows_from_neighbors(change, offsets[0], tile_size, extent)
+            total = neighbor_sum(total, "col", 2, tile_size, 0, 0, extent)
             mask = inside_mask(extent, tile_size)
             extended = jnp.where(mask[None], extended + total / peak_power, 0.0)
         else:

time: 129 us -> 126 us (0.977)
  the two profiles are of different devices: /device:TPU:71 before, /device:TPU:87 now
where the time goes in v6:
time: 126 us; the launch traced here: 125 us
  starting transfers between devices  54.4 us (43%)
  waiting for transfers between devices  25.9 us (21%)
  local copies, waits for them, and re-layouts  16 us (13%)
  Pallas kernels  10.5 us (8%)
  other arithmetic  9.38 us (7%)
  between operations  8.57 us (7%)
    ppermute x12, starting transfers between devices, from_neighbor(): return lax.ppermute(x, axis, pairs)  54.4 us
    ppermute x12, waiting for transfers between devices, from_neighbor(): return lax.ppermute(x, axis, pairs)  25.9 us
    pallas_call x2, Pallas kernels, pattern_gradient(): pl.pallas_call(gradient_kernel, out_shape=jax.ShapeDtypeStruct((2, rows,...  10.5 us
    another operation x1, local copies, waits for them, and re-layouts, rows_from_neighbors(): jnp.stack([offset[0], offset[1]] + [offset[0]] * 6).astype(jnp.float32)  5.19 us
    slice x5, local copies, waits for them, and re-layouts, neighbor_sum(): piece = lax.slice_in_dim(frame, low - shift, high - shift, axis=dim)  3.46 us
    select_n x1, other arithmetic, on_device(): extended = jnp.where(mask[None], extended + total / peak_power, 0.0)  2.58 us
  transfers between devices with their start and end apart: 12, of which 9 were waited for; matrix products, arithmetic and copies ran while one was open for 8% of the time, Pallas kernels for 0%

profile of v6, /device:TPU:87, one launch (start us, length us, event | category | flops | bytes accessed | tf_op | source)
XLA Modules:
  0.0 124.8 jit_solution(1354718073544965690)
XLA Ops:
  0.0 1.0 fusion.23
  1.0 4.9 %collective-permute-start = (f32[2,64,256]{2,1,0:T(8,128)S(1)}, f32[2,64,256]{2,1,0:T(8,128)S(1)}, u32[]{:S(2)}, u32[]{:S(2)}) collective-permute-start(f32[2,64,256]{2,1,0:T(8,128)S(1)} %get-tuple-element.15), channel_id=1, source_target_pairs={{0,32},{32,64},{64,96},{96,128},{128,160},{160,192},{192,224},{224... | collective-permute-start | bytes 393224 | tf_op jit(solution)/shard_map/ppermute | solution.py:97
  5.9 14.5 %collective-permute-start.1 = (f32[2,64,256]{2,1,0:T(8,128)S(1)}, f32[2,64,256]{2,1,0:T(8,128)S(1)}, u32[]{:S(2)}, u32[]{:S(2)}) collective-permute-start(f32[2,64,256]{2,1,0:T(8,128)S(1)} %get-tuple-element.16), channel_id=1, source_target_pairs={{32,0},{64,32},{96,64},{128,96},{160,128},{192,160},{224,192},{256... | collective-permute-start | bytes 393224 | tf_op jit(solution)/shard_map/ppermute | solution.py:97
  20.4 1.4 %fusion.27 = (s32[1,1]{1,0:T(1,128)}, s32[1,1]{1,0:T(1,128)}) fusion(s32[1,2]{1,0:T(1,128)} %bitcast.22), kind=kLoop, calls=%fused_computation.50 | loop fusion | bytes 16 | tf_op jit(solution)/shard_map/slice | solution.py:169
  24.3 0.4 collective-permute-done
  24.8 1.1 pad_add_fusion.1
  25.9 0.2 fusion.21
  26.0 4.8 %collective-permute-start.2 = (f32[2,384,64]{2,1,0:T(8,128)S(1)}, f32[2,384,64]{2,1,0:T(8,128)S(1)}, u32[]{:S(2)}, u32[]{:S(2)}) collective-permute-start(f32[2,384,64]{2,1,0:T(8,128)S(1)} %get-tuple-element.9), channel_id=1, source_target_pairs={{0,1},{1,2},{2,3},{3,4},{4,5},{5,6},{6,7},{7,8},{8,9},{9,10},{10,1... | collective-permute-start | bytes 589832 | tf_op jit(solution)/shard_map/ppermute | solution.py:97
  30.8 1.9 %collective-permute-start.3 = (f32[2,384,64]{2,1,0:T(8,128)S(1)}, f32[2,384,64]{2,1,0:T(8,128)S(1)}, u32[]{:S(2)}, u32[]{:S(2)}) collective-permute-start(f32[2,384,64]{2,1,0:T(8,128)S(1)} %get-tuple-element.10), channel_id=1, source_target_pairs={{1,0},{2,1},{3,2},{4,3},{5,4},{6,5},{7,6},{8,7},{9,8},{10,9},{11,1... | collective-permute-start | bytes 589832 | tf_op jit(solution)/shard_map/ppermute | solution.py:97
  32.7 0.7 fusion.26
  33.4 5.2 %stack.9 = s32[8]{0:T(128)S(1)} concatenate(s32[1]{0:T(128)} %bitcast.10, s32[1]{0:T(128)} %bitcast.11, s32[1]{0:T(128)} %bitcast.10, s32[1]{0:T(128)} %bitcast.10, s32[1]{0:T(128)} %bitcast.10, s32[1]{0:T(128)} %bitcast.10, s32[1]{0:T(128)} %bitcast.10, s32[1]{0:T(128)} %bitcast.10), dimensions={0} | concatenate | bytes 64 | tf_op jit(solution)/shard_map/stack | solution.py:121
  38.6 1.8 %multiply_convert_fusion = (bf16[256,256]{1,0:T(8,128)(2,1)}, bf16[256,256]{1,0:T(8,128)(2,1)}) fusion(), kind=kLoop, calls=%fused_computation.27 | loop fusion | flops 1245184 | bytes 262144 | tf_op jit(solution)/shard_map/convert_element_type | solution.py:26
  40.4 0.7 collective-permute-done.3
  41.1 0.5 pad_add_fusion
  41.6 0.3 copy-done.3
  41.9 1.0 constant_dynamic-slice_fusion.1.window_ref
  42.9 5.2 %shard_map.46 = f32[2,256,256]{2,1,0:T(8,128)} custom-call(f32[2,256,256]{2,1,0:T(8,128)} %constant_dynamic-slice_fusion.1.window_ref, f32[2,3,256,256]{3,2,1,0:T(8,128)} %probe_ref.3, f32[256,256]{1,0:T(8,128)} %bitcast.20, bf16[256,256]{1,0:T(8,128)(2,1)} %get-tuple-element.28.table_re_ref, bf16[256,256]{1,0:T(8,128)(2,1)} %get-tuple-element.27.table_im_ref), custom_call_target="tpu_custom_call" | custom-call | tf_op jit(solution)/shard_map/pallas_call | solution.py:86
  48.1 1.1 fusion.22
  49.2 0.1 pad_maximum_fusion.1
  49.3 2.1 %collective-permute-start.5 = (f32[2,136,256]{2,1,0:T(8,128)S(1)}, f32[2,136,256]{2,1,0:T(8,128)S(1)}, u32[]{:S(2)}, u32[]{:S(2)}) collective-permute-start(f32[2,136,256]{2,1,0:T(8,128)S(1)} %get-tuple-element.21), channel_id=1, source_target_pairs={{0,32},{32,64},{64,96},{96,128},{128,160},{160,192},{192,224},{224... | collective-permute-start | bytes 835592 | tf_op jit(solution)/shard_map/ppermute | solution.py:97
  51.4 7.6 %collective-permute-start.4 = (f32[2,136,256]{2,1,0:T(8,128)S(1)}, f32[2,136,256]{2,1,0:T(8,128)S(1)}, u32[]{:S(2)}, u32[]{:S(2)}) collective-permute-start(f32[2,136,256]{2,1,0:T(8,128)S(1)} %get-tuple-element.22), channel_id=1, source_target_pairs={{32,0},{64,32},{96,64},{128,96},{160,128},{192,160},{224,192},{256... | collective-permute-start | bytes 835592 | tf_op jit(solution)/shard_map/ppermute | solution.py:97
  61.5 6.1 %collective-permute-done.5 = f32[2,136,256]{2,1,0:T(8,128)S(1)} collective-permute-done((f32[2,136,256]{2,1,0:T(8,128)S(1)}, f32[2,136,256]{2,1,0:T(8,128)S(1)}, u32[]{:S(2)}, u32[]{:S(2)}) %collective-permute-start.5) | collective-permute-done | bytes 278560 | tf_op jit(solution)/shard_map/ppermute | solution.py:97
  67.6 0.6 fusion.24
  68.9 0.5 fusion.25
  71.4 1.0 fusion
  72.4 0.8 fusion.19
  73.2 3.0 %collective-permute-start.6 = (f32[2,384,128]{2,1,0:T(8,128)}, f32[2,384,128]{2,1,0:T(8,128)S(1)}, u32[]{:S(2)}, u32[]{:S(2)}) collective-permute-start(f32[2,384,128]{2,1,0:T(8,128)} %get-tuple-element.5), channel_id=1, source_target_pairs={{0,1},{1,2},{2,3},{3,4},{4,5},{5,6},{6,7},{7,8},{8,9},{9,10},{10,1... | collective-permute-start | bytes 1179656 | tf_op jit(solution)/shard_map/ppermute | solution.py:97
  76.2 1.9 %collective-permute-start.7 = (f32[2,384,128]{2,1,0:T(8,128)S(1)}, f32[2,384,128]{2,1,0:T(8,128)}, u32[]{:S(2)}, u32[]{:S(2)}) collective-permute-start(f32[2,384,128]{2,1,0:T(8,128)S(1)} %get-tuple-element.6), channel_id=1, source_target_pairs={{1,0},{2,1},{3,2},{4,3},{5,4},{6,5},{7,6},{8,7},{9,8},{10,9},{11,1... | collective-permute-start | bytes 1179656 | tf_op jit(solution)/shard_map/ppermute | solution.py:97
  78.1 0.1 multiply_reduce_fusion
  78.2 0.7 reduce_max.9
  79.6 0.1 broadcast_and_fusion
  79.7 1.5 %collective-permute-done.6 = f32[2,384,128]{2,1,0:T(8,128)S(1)} collective-permute-done((f32[2,384,128]{2,1,0:T(8,128)}, f32[2,384,128]{2,1,0:T(8,128)S(1)}, u32[]{:S(2)}, u32[]{:S(2)}) %collective-permute-start.6) | collective-permute-done | bytes 393248 | tf_op jit(solution)/shard_map/ppermute | solution.py:97
  81.2 0.7 copy-done.4
  81.9 4.7 %collective-permute-done.7 = f32[2,384,128]{2,1,0:T(8,128)} collective-permute-done((f32[2,384,128]{2,1,0:T(8,128)S(1)}, f32[2,384,128]{2,1,0:T(8,128)}, u32[]{:S(2)}, u32[]{:S(2)}) %collective-permute-start.7) | collective-permute-done | bytes 393248 | tf_op jit(solution)/shard_map/ppermute | solution.py:97
  86.6 2.6 %add_select_fusion = f32[2,384,384]{2,1,0:T(8,128)S(1)} fusion(f32[2,384,128]{2,1,0:T(8,128)} %collective-permute-done.7, f32[2,384,128]{2,1,0:T(8,128)} %copy-done.4, f32[]{:T(128)S(6)} %add.205, pred[384,384]{1,0:T(8,128)(4,1)S(1)} %broadcast_and_fusion, s32[]{:T(128)S(6)} %select_n.52, s32[]{:T(128)S(6)} %select_n.53, f32[2,128,256]{2,1,0:T(8,128)S(1)} %slice.112, ...), kind=kLoop, calls=%fused_computation.9 | loop fusion | flops 2654208 | bytes 4341788 | tf_op jit(solution)/shard_map/jit(_where)/select_n | solution.py:182
  89.2 1.0 constant_dynamic-slice_fusion.window_ref
  90.2 5.3 %shard_map.47 = f32[2,256,256]{2,1,0:T(8,128)} custom-call(f32[2,256,256]{2,1,0:T(8,128)} %constant_dynamic-slice_fusion.window_ref, f32[2,3,256,256]{3,2,1,0:T(8,128)} %probe_ref.3, f32[256,256]{1,0:T(8,128)} %bitcast.21, bf16[256,256]{1,0:T(8,128)(2,1)} %get-tuple-element.28.table_re_ref, bf16[256,256]{1,0:T(8,128)(2,1)} %get-tuple-element.27.table_im_ref), custom_call_target="tpu_custom_call" | custom-call | tf_op jit(solution)/shard_map/pallas_call | solution.py:86
  95.4 1.5 %pad_dynamic-slice_fusion.1 = (f32[2,384,64]{2,1,0:T(8,128)S(1)}, f32[2,384,64]{2,1,0:T(8,128)S(1)}) fusion(s32[]{:T(128)S(6)} %select_n.48, s32[]{:T(128)S(6)} %add.212, f32[2,256,256]{2,1,0:T(8,128)} %shard_map.47, s32[]{:T(128)S(6)} %select_n.49), kind=kLoop, calls=%fused_computation.1 | loop fusion | bytes 917516 | tf_op jit(solution)/shard_map/slice | solution.py:107
  96.9 1.9 %collective-permute-start.8 = (f32[2,384,64]{2,1,0:T(8,128)S(1)}, f32[2,384,64]{2,1,0:T(8,128)S(1)}, u32[]{:S(2)}, u32[]{:S(2)}) collective-permute-start(f32[2,384,64]{2,1,0:T(8,128)S(1)} %get-tuple-element.11), channel_id=1, source_target_pairs={{0,1},{1,2},{2,3},{3,4},{4,5},{5,6},{6,7},{7,8},{8,9},{9,10},{10,1... | collective-permute-start | bytes 589832 | tf_op jit(solution)/shard_map/ppermute | solution.py:97
  98.9 2.4 %collective-permute-start.9 = (f32[2,384,64]{2,1,0:T(8,128)S(1)}, f32[2,384,64]{2,1,0:T(8,128)S(1)}, u32[]{:S(2)}, u32[]{:S(2)}) collective-permute-start(f32[2,384,64]{2,1,0:T(8,128)S(1)} %get-tuple-element.12), channel_id=1, source_target_pairs={{1,0},{2,1},{3,2},{4,3},{5,4},{6,5},{7,6},{8,7},{9,8},{10,9},{11,1... | collective-permute-start | bytes 589832 | tf_op jit(solution)/shard_map/ppermute | solution.py:97
  101.3 2.3 %collective-permute-done.8 = f32[2,384,64]{2,1,0:T(8,128)S(1)} collective-permute-done((f32[2,384,64]{2,1,0:T(8,128)S(1)}, f32[2,384,64]{2,1,0:T(8,128)S(1)}, u32[]{:S(2)}, u32[]{:S(2)}) %collective-permute-start.8) | collective-permute-done | bytes 196640 | tf_op jit(solution)/shard_map/ppermute | solution.py:97
  103.6 5.6 %collective-permute-done.9 = f32[2,384,64]{2,1,0:T(8,128)S(1)} collective-permute-done((f32[2,384,64]{2,1,0:T(8,128)S(1)}, f32[2,384,64]{2,1,0:T(8,128)S(1)}, u32[]{:S(2)}, u32[]{:S(2)}) %collective-permute-start.9) | collective-permute-done | bytes 196640 | tf_op jit(solution)/shard_map/ppermute | solution.py:97
  109.2 0.4 fusion.3
  109.6 1.9 %collective-permute-start.10 = (f32[2,64,256]{2,1,0:T(8,128)S(1)}, f32[2,64,256]{2,1,0:T(8,128)S(1)}, u32[]{:S(2)}, u32[]{:S(2)}) collective-permute-start(f32[2,64,256]{2,1,0:T(8,128)S(1)} %get-tuple-element.7), channel_id=1, source_target_pairs={{0,32},{32,64},{64,96},{96,128},{128,160},{160,192},{192,224},{224... | collective-permute-start | bytes 393224 | tf_op jit(solution)/shard_map/ppermute | solution.py:97
  111.6 7.6 %collective-permute-start.11 = (f32[2,64,256]{2,1,0:T(8,128)S(1)}, f32[2,64,256]{2,1,0:T(8,128)S(1)}, u32[]{:S(2)}, u32[]{:S(2)}) collective-permute-start(f32[2,64,256]{2,1,0:T(8,128)S(1)} %get-tuple-element.8), channel_id=1, source_target_pairs={{32,0},{64,32},{96,64},{128,96},{160,128},{192,160},{224,192},{256... | collective-permute-start | bytes 393224 | tf_op jit(solution)/shard_map/ppermute | solution.py:97
  119.1 1.9 %collective-permute-done.10 = f32[2,64,256]{2,1,0:T(8,128)S(1)} collective-permute-done((f32[2,64,256]{2,1,0:T(8,128)S(1)}, f32[2,64,256]{2,1,0:T(8,128)S(1)}, u32[]{:S(2)}, u32[]{:S(2)}) %collective-permute-start.10) | collective-permute-done | bytes 131104 | tf_op jit(solution)/shard_map/ppermute | solution.py:97
  121.1 2.7 %collective-permute-done.11 = f32[2,64,256]{2,1,0:T(8,128)S(1)} collective-permute-done((f32[2,64,256]{2,1,0:T(8,128)S(1)}, f32[2,64,256]{2,1,0:T(8,128)S(1)}, u32[]{:S(2)}, u32[]{:S(2)}) %collective-permute-start.11) | collective-permute-done | bytes 131104 | tf_op jit(solution)/shard_map/ppermute | solution.py:97
  123.8 1.0 fusion.6
  (19 shorter events, 0.1 us)
Async XLA Ops:
  1.0 23.8 %collective-permute-start = (f32[2,64,256]{2,1,0:T(8,128)S(1)}, f32[2,64,256]{2,1,0:T(8,128)S(1)}, u32[]{:S(2)}, u32[]{:S(2)}) collective-permute-start(f32[2,64,256]{2,1,0:T(8,128)S(1)} %get-tuple-element.15), channel_id=1, source_target_pairs={{0,32},{32,64},{64,96},{96,128},{128,160},{160,192},{192,224},{224... | collective-permute-start | bytes 393224 | tf_op jit(solution)/shard_map/ppermute | solution.py:97
  5.9 18.9 %collective-permute-start.1 = (f32[2,64,256]{2,1,0:T(8,128)S(1)}, f32[2,64,256]{2,1,0:T(8,128)S(1)}, u32[]{:S(2)}, u32[]{:S(2)}) collective-permute-start(f32[2,64,256]{2,1,0:T(8,128)S(1)} %get-tuple-element.16), channel_id=1, source_target_pairs={{32,0},{64,32},{96,64},{128,96},{160,128},{192,160},{224,192},{256... | collective-permute-start | bytes 393224 | tf_op jit(solution)/shard_map/ppermute | solution.py:97
  25.9 6.9 %copy-start.5 = (s32[1,1,1,2]{3,2,1,0:T(1,128)S(1)}, s32[1,1,1,2]{3,2,1,0:T(1,128)}, u32[]{:S(2)}) copy-start(s32[1,1,1,2]{3,2,1,0:T(1,128)} %param.6) | copy-start | bytes 28
  26.0 14.3 %collective-permute-start.2 = (f32[2,384,64]{2,1,0:T(8,128)S(1)}, f32[2,384,64]{2,1,0:T(8,128)S(1)}, u32[]{:S(2)}, u32[]{:S(2)}) collective-permute-start(f32[2,384,64]{2,1,0:T(8,128)S(1)} %get-tuple-element.9), channel_id=1, source_target_pairs={{0,1},{1,2},{2,3},{3,4},{4,5},{5,6},{6,7},{7,8},{8,9},{9,10},{10,1... | collective-permute-start | bytes 589832 | tf_op jit(solution)/shard_map/ppermute | solution.py:97
  30.8 10.3 %collective-permute-start.3 = (f32[2,384,64]{2,1,0:T(8,128)S(1)}, f32[2,384,64]{2,1,0:T(8,128)S(1)}, u32[]{:S(2)}, u32[]{:S(2)}) collective-permute-start(f32[2,384,64]{2,1,0:T(8,128)S(1)} %get-tuple-element.10), channel_id=1, source_target_pairs={{1,0},{2,1},{3,2},{4,3},{5,4},{6,5},{7,6},{8,7},{9,8},{10,9},{11,1... | collective-permute-start | bytes 589832 | tf_op jit(solution)/shard_map/ppermute | solution.py:97
  41.1 0.8 copy-start.3
  49.2 22.2 %copy-start.1 = (f32[2,256,256]{2,1,0:T(8,128)S(1)}, f32[2,256,256]{2,1,0:T(8,128)}, u32[]{:S(2)}) copy-start(f32[2,256,256]{2,1,0:T(8,128)} %shard_map.46) | copy-start | bytes 1572868
  49.3 18.3 %collective-permute-start.5 = (f32[2,136,256]{2,1,0:T(8,128)S(1)}, f32[2,136,256]{2,1,0:T(8,128)S(1)}, u32[]{:S(2)}, u32[]{:S(2)}) collective-permute-start(f32[2,136,256]{2,1,0:T(8,128)S(1)} %get-tuple-element.21), channel_id=1, source_target_pairs={{0,32},{32,64},{64,96},{96,128},{128,160},{160,192},{192,224},{224... | collective-permute-start | bytes 835592 | tf_op jit(solution)/shard_map/ppermute | solution.py:97
  51.4 17.5 %collective-permute-start.4 = (f32[2,136,256]{2,1,0:T(8,128)S(1)}, f32[2,136,256]{2,1,0:T(8,128)S(1)}, u32[]{:S(2)}, u32[]{:S(2)}) collective-permute-start(f32[2,136,256]{2,1,0:T(8,128)S(1)} %get-tuple-element.22), channel_id=1, source_target_pairs={{32,0},{64,32},{96,64},{128,96},{160,128},{192,160},{224,192},{256... | collective-permute-start | bytes 835592 | tf_op jit(solution)/shard_map/ppermute | solution.py:97
  72.4 5.7 %copy-start = (f32[2,3,256,256]{3,2,1,0:T(8,128)S(1)}, f32[2,3,256,256]{3,2,1,0:T(8,128)}, u32[]{:S(2)}) copy-start(f32[2,3,256,256]{3,2,1,0:T(8,128)} %probe_ref.3) | copy-start | bytes 4718596
  73.2 8.0 %collective-permute-start.6 = (f32[2,384,128]{2,1,0:T(8,128)}, f32[2,384,128]{2,1,0:T(8,128)S(1)}, u32[]{:S(2)}, u32[]{:S(2)}) collective-permute-start(f32[2,384,128]{2,1,0:T(8,128)} %get-tuple-element.5), channel_id=1, source_target_pairs={{0,1},{1,2},{2,3},{3,4},{4,5},{5,6},{6,7},{7,8},{8,9},{9,10},{10,1... | collective-permute-start | bytes 1179656 | tf_op jit(solution)/shard_map/ppermute | solution.py:97
  76.2 10.4 %collective-permute-start.7 = (f32[2,384,128]{2,1,0:T(8,128)S(1)}, f32[2,384,128]{2,1,0:T(8,128)}, u32[]{:S(2)}, u32[]{:S(2)}) collective-permute-start(f32[2,384,128]{2,1,0:T(8,128)S(1)} %get-tuple-element.6), channel_id=1, source_target_pairs={{1,0},{2,1},{3,2},{4,3},{5,4},{6,5},{7,6},{8,7},{9,8},{10,9},{11,1... | collective-permute-start | bytes 1179656 | tf_op jit(solution)/shard_map/ppermute | solution.py:97
  81.2 0.7 copy-start.4
  95.4 13.7 %copy-start.2 = (f32[2,256,256]{2,1,0:T(8,128)S(1)}, f32[2,256,256]{2,1,0:T(8,128)}, u32[]{:S(2)}) copy-start(f32[2,256,256]{2,1,0:T(8,128)} %shard_map.47) | copy-start | bytes 1572868
  96.9 6.6 %collective-permute-start.8 = (f32[2,384,64]{2,1,0:T(8,128)S(1)}, f32[2,384,64]{2,1,0:T(8,128)S(1)}, u32[]{:S(2)}, u32[]{:S(2)}) collective-permute-start(f32[2,384,64]{2,1,0:T(8,128)S(1)} %get-tuple-element.11), channel_id=1, source_target_pairs={{0,1},{1,2},{2,3},{3,4},{4,5},{5,6},{6,7},{7,8},{8,9},{9,10},{10,1... | collective-permute-start | bytes 589832 | tf_op jit(solution)/shard_map/ppermute | solution.py:97
  98.9 10.3 %collective-permute-start.9 = (f32[2,384,64]{2,1,0:T(8,128)S(1)}, f32[2,384,64]{2,1,0:T(8,128)S(1)}, u32[]{:S(2)}, u32[]{:S(2)}) collective-permute-start(f32[2,384,64]{2,1,0:T(8,128)S(1)} %get-tuple-element.12), channel_id=1, source_target_pairs={{1,0},{2,1},{3,2},{4,3},{5,4},{6,5},{7,6},{8,7},{9,8},{10,9},{11,1... | collective-permute-start | bytes 589832 | tf_op jit(solution)/shard_map/ppermute | solution.py:97
  109.6 11.4 %collective-permute-start.10 = (f32[2,64,256]{2,1,0:T(8,128)S(1)}, f32[2,64,256]{2,1,0:T(8,128)S(1)}, u32[]{:S(2)}, u32[]{:S(2)}) collective-permute-start(f32[2,64,256]{2,1,0:T(8,128)S(1)} %get-tuple-element.7), channel_id=1, source_target_pairs={{0,32},{32,64},{64,96},{96,128},{128,160},{160,192},{192,224},{224... | collective-permute-start | bytes 393224 | tf_op jit(solution)/shard_map/ppermute | solution.py:97
  111.6 12.2 %collective-permute-start.11 = (f32[2,64,256]{2,1,0:T(8,128)S(1)}, f32[2,64,256]{2,1,0:T(8,128)S(1)}, u32[]{:S(2)}, u32[]{:S(2)}) collective-permute-start(f32[2,64,256]{2,1,0:T(8,128)S(1)} %get-tuple-element.8), channel_id=1, source_target_pairs={{32,0},{64,32},{96,64},{128,96},{160,128},{192,160},{224,192},{256... | collective-permute-start | bytes 393224 | tf_op jit(solution)/shard_map/ppermute | solution.py:97

commit v7 on v6

--- a/solution.py
+++ b/solution.py
@@ -117,10 +117,8 @@
 def rows_from_neighbors(change, offset, tile_size, extent):
     reach = 2 * M
     size = change.shape[1]
-    tag = jnp.broadcast_to(
-        jnp.stack([offset[0], offset[1]] + [offset[0]] * 6).astype(jnp.float32)[None, :, None],
-        (2, 8, change.shape[2]),
-    )
+    tag_rows = lax.broadcasted_iota(jnp.int32, (2, 8, change.shape[2]), 1)
+    tag = jnp.where(tag_rows == 1, offset[1], offset[0]).astype(jnp.float32)
     to_low = jnp.concatenate([change[:, :reach], tag], axis=1)
     to_high = jnp.concatenate([change[:, size - reach :], tag], axis=1)
     from_high = from_neighbor(to_low, "row", 1)

time: 126 us -> 129 us (1.024)
  the two profiles are of different devices: /device:TPU:87 before, /device:TPU:71 now
where the time goes in v7:
time: 129 us; the launch traced here: 128 us
  starting transfers between devices  57.3 us (44%)
  waiting for transfers between devices  28.8 us (22%)
  other arithmetic  11.6 us (9%)
  local copies, waits for them, and re-layouts  11.4 us (9%)
  Pallas kernels  10.5 us (8%)
  between operations  8.56 us (7%)
    ppermute x12, starting transfers between devices, from_neighbor(): return lax.ppermute(x, axis, pairs)  57.3 us
    ppermute x12, waiting for transfers between devices, from_neighbor(): return lax.ppermute(x, axis, pairs)  28.8 us
    pallas_call x2, Pallas kernels, pattern_gradient(): pl.pallas_call(gradient_kernel, out_shape=jax.ShapeDtypeStruct((2, rows,...  10.5 us
    slice x5, local copies, waits for them, and re-layouts, neighbor_sum(): piece = lax.slice_in_dim(frame, low - shift, high - shift, axis=dim)  3.46 us
    add x3, other arithmetic, neighbor_sum(): total = piece if total is None else total + piece  2.99 us
    select_n x1, other arithmetic, on_device(): extended = jnp.where(mask[None], extended + total / peak_power, 0.0)  2.58 us
  transfers between devices with their start and end apart: 12, of which 9 were waited for; matrix products, arithmetic and copies ran while one was open for 6% of the time, Pallas kernels for 0%

profile of v7, /device:TPU:71, one launch (start us, length us, event | category | flops | bytes accessed | tf_op | source)
XLA Modules:
  0.0 128.2 jit_solution(13425409957826420844)
XLA Ops:
  0.0 1.0 fusion.24
  1.0 4.9 %collective-permute-start = (f32[2,64,256]{2,1,0:T(8,128)S(1)}, f32[2,64,256]{2,1,0:T(8,128)S(1)}, u32[]{:S(2)}, u32[]{:S(2)}) collective-permute-start(f32[2,64,256]{2,1,0:T(8,128)S(1)} %get-tuple-element.15), channel_id=1, source_target_pairs={{0,32},{32,64},{64,96},{96,128},{128,160},{160,192},{192,224},{224... | collective-permute-start | bytes 393224 | tf_op jit(solution)/shard_map/ppermute | solution.py:97
  5.9 13.6 %collective-permute-start.1 = (f32[2,64,256]{2,1,0:T(8,128)S(1)}, f32[2,64,256]{2,1,0:T(8,128)S(1)}, u32[]{:S(2)}, u32[]{:S(2)}) collective-permute-start(f32[2,64,256]{2,1,0:T(8,128)S(1)} %get-tuple-element.16), channel_id=1, source_target_pairs={{32,0},{64,32},{96,64},{128,96},{160,128},{192,160},{224,192},{256... | collective-permute-start | bytes 393224 | tf_op jit(solution)/shard_map/ppermute | solution.py:97
  19.5 1.3 %fusion.28 = (s32[1,1]{1,0:T(1,128)}, s32[1,1]{1,0:T(1,128)}) fusion(s32[1,2]{1,0:T(1,128)} %bitcast.22), kind=kLoop, calls=%fused_computation.52 | loop fusion | bytes 16 | tf_op jit(solution)/shard_map/slice | solution.py:167
  23.4 1.3 %fusion.27 = (s32[1,1,1,1]{3,2,1,0:T(1,128)}, s32[1,1,1,1]{3,2,1,0:T(1,128)}) fusion(s32[1,1,1,2]{3,2,1,0:T(1,128)} %param.6), kind=kLoop, calls=%fused_computation.51 | loop fusion | bytes 16 | tf_op jit(solution)/shard_map/slice | solution.py:121
  24.7 1.1 pad_add_fusion.1
  25.8 0.2 fusion.22
  26.0 5.5 %collective-permute-start.2 = (f32[2,384,64]{2,1,0:T(8,128)S(1)}, f32[2,384,64]{2,1,0:T(8,128)S(1)}, u32[]{:S(2)}, u32[]{:S(2)}) collective-permute-start(f32[2,384,64]{2,1,0:T(8,128)S(1)} %get-tuple-element.9), channel_id=1, source_target_pairs={{0,1},{1,2},{2,3},{3,4},{4,5},{5,6},{6,7},{7,8},{8,9},{9,10},{10,1... | collective-permute-start | bytes 589832 | tf_op jit(solution)/shard_map/ppermute | solution.py:97
  31.5 1.9 %collective-permute-start.3 = (f32[2,384,64]{2,1,0:T(8,128)S(1)}, f32[2,384,64]{2,1,0:T(8,128)S(1)}, u32[]{:S(2)}, u32[]{:S(2)}) collective-permute-start(f32[2,384,64]{2,1,0:T(8,128)S(1)} %get-tuple-element.10), channel_id=1, source_target_pairs={{1,0},{2,1},{3,2},{4,3},{5,4},{6,5},{7,6},{8,7},{9,8},{10,9},{11,1... | collective-permute-start | bytes 589832 | tf_op jit(solution)/shard_map/ppermute | solution.py:97
  33.4 1.3 fusion.19
  34.7 1.8 %multiply_convert_fusion = (bf16[256,256]{1,0:T(8,128)(2,1)}, bf16[256,256]{1,0:T(8,128)(2,1)}) fusion(), kind=kLoop, calls=%fused_computation.27 | loop fusion | flops 1245184 | bytes 262144 | tf_op jit(solution)/shard_map/convert_element_type | solution.py:26
  36.5 5.3 %collective-permute-done.3 = f32[2,384,64]{2,1,0:T(8,128)S(1)} collective-permute-done((f32[2,384,64]{2,1,0:T(8,128)S(1)}, f32[2,384,64]{2,1,0:T(8,128)S(1)}, u32[]{:S(2)}, u32[]{:S(2)}) %collective-permute-start.3) | collective-permute-done | bytes 196640 | tf_op jit(solution)/shard_map/ppermute | solution.py:97
  41.8 0.5 pad_add_fusion
  42.3 0.3 copy-done.3
  42.6 1.0 constant_dynamic-slice_fusion.1.window_ref
  43.6 5.2 %shard_map.46 = f32[2,256,256]{2,1,0:T(8,128)} custom-call(f32[2,256,256]{2,1,0:T(8,128)} %constant_dynamic-slice_fusion.1.window_ref, f32[2,3,256,256]{3,2,1,0:T(8,128)} %probe_ref.3, f32[256,256]{1,0:T(8,128)} %bitcast.20, bf16[256,256]{1,0:T(8,128)(2,1)} %get-tuple-element.28.table_re_ref, bf16[256,256]{1,0:T(8,128)(2,1)} %get-tuple-element.27.table_im_ref), custom_call_target="tpu_custom_call" | custom-call | tf_op jit(solution)/shard_map/pallas_call | solution.py:86
  48.8 1.1 fusion.23
  49.9 0.1 pad_maximum_fusion.1
  50.0 2.1 %collective-permute-start.5 = (f32[2,136,256]{2,1,0:T(8,128)S(1)}, f32[2,136,256]{2,1,0:T(8,128)S(1)}, u32[]{:S(2)}, u32[]{:S(2)}) collective-permute-start(f32[2,136,256]{2,1,0:T(8,128)S(1)} %get-tuple-element.21), channel_id=1, source_target_pairs={{0,32},{32,64},{64,96},{96,128},{128,160},{160,192},{192,224},{224... | collective-permute-start | bytes 835592 | tf_op jit(solution)/shard_map/ppermute | solution.py:97
  52.1 8.3 %collective-permute-start.4 = (f32[2,136,256]{2,1,0:T(8,128)S(1)}, f32[2,136,256]{2,1,0:T(8,128)S(1)}, u32[]{:S(2)}, u32[]{:S(2)}) collective-permute-start(f32[2,136,256]{2,1,0:T(8,128)S(1)} %get-tuple-element.22), channel_id=1, source_target_pairs={{32,0},{64,32},{96,64},{128,96},{160,128},{192,160},{224,192},{256... | collective-permute-start | bytes 835592 | tf_op jit(solution)/shard_map/ppermute | solution.py:97
  63.0 4.3 %collective-permute-done.5 = f32[2,136,256]{2,1,0:T(8,128)S(1)} collective-permute-done((f32[2,136,256]{2,1,0:T(8,128)S(1)}, f32[2,136,256]{2,1,0:T(8,128)S(1)}, u32[]{:S(2)}, u32[]{:S(2)}) %collective-permute-start.5) | collective-permute-done | bytes 278560 | tf_op jit(solution)/shard_map/ppermute | solution.py:97
  67.3 0.5 fusion.25
  68.5 1.1 collective-permute-done.4
  69.6 0.6 fusion.26
  72.2 1.0 fusion
  73.2 0.8 fusion.20
  74.0 4.5 %collective-permute-start.6 = (f32[2,384,128]{2,1,0:T(8,128)}, f32[2,384,128]{2,1,0:T(8,128)S(1)}, u32[]{:S(2)}, u32[]{:S(2)}) collective-permute-start(f32[2,384,128]{2,1,0:T(8,128)} %get-tuple-element.5), channel_id=1, source_target_pairs={{0,1},{1,2},{2,3},{3,4},{4,5},{5,6},{6,7},{7,8},{8,9},{9,10},{10,1... | collective-permute-start | bytes 1179656 | tf_op jit(solution)/shard_map/ppermute | solution.py:97
  78.6 1.9 %collective-permute-start.7 = (f32[2,384,128]{2,1,0:T(8,128)S(1)}, f32[2,384,128]{2,1,0:T(8,128)}, u32[]{:S(2)}, u32[]{:S(2)}) collective-permute-start(f32[2,384,128]{2,1,0:T(8,128)S(1)} %get-tuple-element.6), channel_id=1, source_target_pairs={{1,0},{2,1},{3,2},{4,3},{5,4},{6,5},{7,6},{8,7},{9,8},{10,9},{11,1... | collective-permute-start | bytes 1179656 | tf_op jit(solution)/shard_map/ppermute | solution.py:97
  80.5 0.1 multiply_reduce_fusion
  80.6 0.6 reduce_max.9
  81.9 0.1 broadcast_and_fusion
  82.0 1.6 %collective-permute-done.6 = f32[2,384,128]{2,1,0:T(8,128)S(1)} collective-permute-done((f32[2,384,128]{2,1,0:T(8,128)}, f32[2,384,128]{2,1,0:T(8,128)S(1)}, u32[]{:S(2)}, u32[]{:S(2)}) %collective-permute-start.6) | collective-permute-done | bytes 393248 | tf_op jit(solution)/shard_map/ppermute | solution.py:97
  83.6 0.7 copy-done.4
  84.3 4.7 %collective-permute-done.7 = f32[2,384,128]{2,1,0:T(8,128)} collective-permute-done((f32[2,384,128]{2,1,0:T(8,128)S(1)}, f32[2,384,128]{2,1,0:T(8,128)}, u32[]{:S(2)}, u32[]{:S(2)}) %collective-permute-start.7) | collective-permute-done | bytes 393248 | tf_op jit(solution)/shard_map/ppermute | solution.py:97
  89.0 2.6 %add_select_fusion = f32[2,384,384]{2,1,0:T(8,128)S(1)} fusion(f32[2,384,128]{2,1,0:T(8,128)} %collective-permute-done.7, f32[2,384,128]{2,1,0:T(8,128)} %copy-done.4, f32[]{:T(128)S(6)} %add.205, pred[384,384]{1,0:T(8,128)(4,1)S(1)} %broadcast_and_fusion, s32[]{:T(128)S(6)} %select_n.58, s32[]{:T(128)S(6)} %select_n.59, f32[2,128,256]{2,1,0:T(8,128)S(1)} %slice.111, ...), kind=kLoop, calls=%fused_computation.9 | loop fusion | flops 2654208 | bytes 4341788 | tf_op jit(solution)/shard_map/jit(_where)/select_n | solution.py:180
  91.6 1.0 constant_dynamic-slice_fusion.window_ref
  92.6 5.3 %shard_map.47 = f32[2,256,256]{2,1,0:T(8,128)} custom-call(f32[2,256,256]{2,1,0:T(8,128)} %constant_dynamic-slice_fusion.window_ref, f32[2,3,256,256]{3,2,1,0:T(8,128)} %probe_ref.3, f32[256,256]{1,0:T(8,128)} %bitcast.21, bf16[256,256]{1,0:T(8,128)(2,1)} %get-tuple-element.28.table_re_ref, bf16[256,256]{1,0:T(8,128)(2,1)} %get-tuple-element.27.table_im_ref), custom_call_target="tpu_custom_call" | custom-call | tf_op jit(solution)/shard_map/pallas_call | solution.py:86
  97.9 1.5 %pad_dynamic-slice_fusion.1 = (f32[2,384,64]{2,1,0:T(8,128)S(1)}, f32[2,384,64]{2,1,0:T(8,128)S(1)}) fusion(s32[]{:T(128)S(6)} %select_n.53, s32[]{:T(128)S(6)} %add.212, f32[2,256,256]{2,1,0:T(8,128)} %shard_map.47, s32[]{:T(128)S(6)} %select_n.54), kind=kLoop, calls=%fused_computation.1 | loop fusion | bytes 917516 | tf_op jit(solution)/shard_map/slice | solution.py:107
  99.4 1.9 %collective-permute-start.8 = (f32[2,384,64]{2,1,0:T(8,128)S(1)}, f32[2,384,64]{2,1,0:T(8,128)S(1)}, u32[]{:S(2)}, u32[]{:S(2)}) collective-permute-start(f32[2,384,64]{2,1,0:T(8,128)S(1)} %get-tuple-element.11), channel_id=1, source_target_pairs={{0,1},{1,2},{2,3},{3,4},{4,5},{5,6},{6,7},{7,8},{8,9},{9,10},{10,1... | collective-permute-start | bytes 589832 | tf_op jit(solution)/shard_map/ppermute | solution.py:97
  101.3 2.4 %collective-permute-start.9 = (f32[2,384,64]{2,1,0:T(8,128)S(1)}, f32[2,384,64]{2,1,0:T(8,128)}, u32[]{:S(2)}, u32[]{:S(2)}) collective-permute-start(f32[2,384,64]{2,1,0:T(8,128)S(1)} %get-tuple-element.12), channel_id=1, source_target_pairs={{1,0},{2,1},{3,2},{4,3},{5,4},{6,5},{7,6},{8,7},{9,8},{10,9},{11,1... | collective-permute-start | bytes 589832 | tf_op jit(solution)/shard_map/ppermute | solution.py:97
  103.7 2.3 %collective-permute-done.8 = f32[2,384,64]{2,1,0:T(8,128)S(1)} collective-permute-done((f32[2,384,64]{2,1,0:T(8,128)S(1)}, f32[2,384,64]{2,1,0:T(8,128)S(1)}, u32[]{:S(2)}, u32[]{:S(2)}) %collective-permute-start.8) | collective-permute-done | bytes 196640 | tf_op jit(solution)/shard_map/ppermute | solution.py:97
  106.0 5.7 %collective-permute-done.9 = f32[2,384,64]{2,1,0:T(8,128)} collective-permute-done((f32[2,384,64]{2,1,0:T(8,128)S(1)}, f32[2,384,64]{2,1,0:T(8,128)}, u32[]{:S(2)}, u32[]{:S(2)}) %collective-permute-start.9) | collective-permute-done | bytes 196640 | tf_op jit(solution)/shard_map/ppermute | solution.py:97
  111.7 1.4 %fusion.3 = f32[2,384,256]{2,1,0:T(8,128)S(1)} fusion(s32[]{:T(128)S(6)} %select_n.53, s32[]{:T(128)S(6)} %add.213, f32[2,256,256]{2,1,0:T(8,128)S(1)} %copy-done.2, f32[2,384,64]{2,1,0:T(8,128)} %collective-permute-done.9, f32[2,384,64]{2,1,0:T(8,128)S(1)} %collective-permute-done.8), kind=kLoop, calls=%fused_computation.12 | loop fusion | flops 393216 | bytes 1703944 | tf_op jit(solution)/shard_map/add | solution.py:113
  113.1 1.9 %collective-permute-start.10 = (f32[2,64,256]{2,1,0:T(8,128)S(1)}, f32[2,64,256]{2,1,0:T(8,128)S(1)}, u32[]{:S(2)}, u32[]{:S(2)}) collective-permute-start(f32[2,64,256]{2,1,0:T(8,128)S(1)} %get-tuple-element.7), channel_id=1, source_target_pairs={{0,32},{32,64},{64,96},{96,128},{128,160},{160,192},{192,224},{224... | collective-permute-start | bytes 393224 | tf_op jit(solution)/shard_map/ppermute | solution.py:97
  115.1 8.3 %collective-permute-start.11 = (f32[2,64,256]{2,1,0:T(8,128)S(1)}, f32[2,64,256]{2,1,0:T(8,128)S(1)}, u32[]{:S(2)}, u32[]{:S(2)}) collective-permute-start(f32[2,64,256]{2,1,0:T(8,128)S(1)} %get-tuple-element.8), channel_id=1, source_target_pairs={{32,0},{64,32},{96,64},{128,96},{160,128},{192,160},{224,192},{256... | collective-permute-start | bytes 393224 | tf_op jit(solution)/shard_map/ppermute | solution.py:97
  123.4 0.4 collective-permute-done.10
  123.8 3.4 %collective-permute-done.11 = f32[2,64,256]{2,1,0:T(8,128)S(1)} collective-permute-done((f32[2,64,256]{2,1,0:T(8,128)S(1)}, f32[2,64,256]{2,1,0:T(8,128)S(1)}, u32[]{:S(2)}, u32[]{:S(2)}) %collective-permute-start.11) | collective-permute-done | bytes 131104 | tf_op jit(solution)/shard_map/ppermute | solution.py:97
  127.2 1.0 fusion.6
  (16 shorter events, 0.1 us)
Async XLA Ops:
  1.0 23.7 %collective-permute-start = (f32[2,64,256]{2,1,0:T(8,128)S(1)}, f32[2,64,256]{2,1,0:T(8,128)S(1)}, u32[]{:S(2)}, u32[]{:S(2)}) collective-permute-start(f32[2,64,256]{2,1,0:T(8,128)S(1)} %get-tuple-element.15), channel_id=1, source_target_pairs={{0,32},{32,64},{64,96},{96,128},{128,160},{160,192},{192,224},{224... | collective-permute-start | bytes 393224 | tf_op jit(solution)/shard_map/ppermute | solution.py:97
  5.9 18.8 %collective-permute-start.1 = (f32[2,64,256]{2,1,0:T(8,128)S(1)}, f32[2,64,256]{2,1,0:T(8,128)S(1)}, u32[]{:S(2)}, u32[]{:S(2)}) collective-permute-start(f32[2,64,256]{2,1,0:T(8,128)S(1)} %get-tuple-element.16), channel_id=1, source_target_pairs={{32,0},{64,32},{96,64},{128,96},{160,128},{192,160},{224,192},{256... | collective-permute-start | bytes 393224 | tf_op jit(solution)/shard_map/ppermute | solution.py:97
  26.0 10.5 %collective-permute-start.2 = (f32[2,384,64]{2,1,0:T(8,128)S(1)}, f32[2,384,64]{2,1,0:T(8,128)S(1)}, u32[]{:S(2)}, u32[]{:S(2)}) collective-permute-start(f32[2,384,64]{2,1,0:T(8,128)S(1)} %get-tuple-element.9), channel_id=1, source_target_pairs={{0,1},{1,2},{2,3},{3,4},{4,5},{5,6},{6,7},{7,8},{8,9},{9,10},{10,1... | collective-permute-start | bytes 589832 | tf_op jit(solution)/shard_map/ppermute | solution.py:97
  31.5 10.3 %collective-permute-start.3 = (f32[2,384,64]{2,1,0:T(8,128)S(1)}, f32[2,384,64]{2,1,0:T(8,128)S(1)}, u32[]{:S(2)}, u32[]{:S(2)}) collective-permute-start(f32[2,384,64]{2,1,0:T(8,128)S(1)} %get-tuple-element.10), channel_id=1, source_target_pairs={{1,0},{2,1},{3,2},{4,3},{5,4},{6,5},{7,6},{8,7},{9,8},{10,9},{11,1... | collective-permute-start | bytes 589832 | tf_op jit(solution)/shard_map/ppermute | solution.py:97
  41.8 0.8 copy-start.3
  49.9 22.4 %copy-start.1 = (f32[2,256,256]{2,1,0:T(8,128)S(1)}, f32[2,256,256]{2,1,0:T(8,128)}, u32[]{:S(2)}) copy-start(f32[2,256,256]{2,1,0:T(8,128)} %shard_map.46) | copy-start | bytes 1572868
  50.0 17.3 %collective-permute-start.5 = (f32[2,136,256]{2,1,0:T(8,128)S(1)}, f32[2,136,256]{2,1,0:T(8,128)S(1)}, u32[]{:S(2)}, u32[]{:S(2)}) collective-permute-start(f32[2,136,256]{2,1,0:T(8,128)S(1)} %get-tuple-element.21), channel_id=1, source_target_pairs={{0,32},{32,64},{64,96},{96,128},{128,160},{160,192},{192,224},{224... | collective-permute-start | bytes 835592 | tf_op jit(solution)/shard_map/ppermute | solution.py:97
  52.1 17.5 %collective-permute-start.4 = (f32[2,136,256]{2,1,0:T(8,128)S(1)}, f32[2,136,256]{2,1,0:T(8,128)S(1)}, u32[]{:S(2)}, u32[]{:S(2)}) collective-permute-start(f32[2,136,256]{2,1,0:T(8,128)S(1)} %get-tuple-element.22), channel_id=1, source_target_pairs={{32,0},{64,32},{96,64},{128,96},{160,128},{192,160},{224,192},{256... | collective-permute-start | bytes 835592 | tf_op jit(solution)/shard_map/ppermute | solution.py:97
  73.2 7.3 %copy-start = (f32[2,3,256,256]{3,2,1,0:T(8,128)S(1)}, f32[2,3,256,256]{3,2,1,0:T(8,128)}, u32[]{:S(2)}) copy-start(f32[2,3,256,256]{3,2,1,0:T(8,128)} %probe_ref.3) | copy-start | bytes 4718596
  74.0 9.5 %collective-permute-start.6 = (f32[2,384,128]{2,1,0:T(8,128)}, f32[2,384,128]{2,1,0:T(8,128)S(1)}, u32[]{:S(2)}, u32[]{:S(2)}) collective-permute-start(f32[2,384,128]{2,1,0:T(8,128)} %get-tuple-element.5), channel_id=1, source_target_pairs={{0,1},{1,2},{2,3},{3,4},{4,5},{5,6},{6,7},{7,8},{8,9},{9,10},{10,1... | collective-permute-start | bytes 1179656 | tf_op jit(solution)/shard_map/ppermute | solution.py:97
  78.6 10.4 %collective-permute-start.7 = (f32[2,384,128]{2,1,0:T(8,128)S(1)}, f32[2,384,128]{2,1,0:T(8,128)}, u32[]{:S(2)}, u32[]{:S(2)}) collective-permute-start(f32[2,384,128]{2,1,0:T(8,128)S(1)} %get-tuple-element.6), channel_id=1, source_target_pairs={{1,0},{2,1},{3,2},{4,3},{5,4},{6,5},{7,6},{8,7},{9,8},{10,9},{11,1... | collective-permute-start | bytes 1179656 | tf_op jit(solution)/shard_map/ppermute | solution.py:97
  83.6 0.7 copy-start.4
  97.9 13.8 %copy-start.2 = (f32[2,256,256]{2,1,0:T(8,128)S(1)}, f32[2,256,256]{2,1,0:T(8,128)}, u32[]{:S(2)}) copy-start(f32[2,256,256]{2,1,0:T(8,128)} %shard_map.47) | copy-start | bytes 1572868
  99.4 6.6 %collective-permute-start.8 = (f32[2,384,64]{2,1,0:T(8,128)S(1)}, f32[2,384,64]{2,1,0:T(8,128)S(1)}, u32[]{:S(2)}, u32[]{:S(2)}) collective-permute-start(f32[2,384,64]{2,1,0:T(8,128)S(1)} %get-tuple-element.11), channel_id=1, source_target_pairs={{0,1},{1,2},{2,3},{3,4},{4,5},{5,6},{6,7},{7,8},{8,9},{9,10},{10,1... | collective-permute-start | bytes 589832 | tf_op jit(solution)/shard_map/ppermute | solution.py:97
  101.3 10.4 %collective-permute-start.9 = (f32[2,384,64]{2,1,0:T(8,128)S(1)}, f32[2,384,64]{2,1,0:T(8,128)}, u32[]{:S(2)}, u32[]{:S(2)}) collective-permute-start(f32[2,384,64]{2,1,0:T(8,128)S(1)} %get-tuple-element.12), channel_id=1, source_target_pairs={{1,0},{2,1},{3,2},{4,3},{5,4},{6,5},{7,6},{8,7},{9,8},{10,9},{11,1... | collective-permute-start | bytes 589832 | tf_op jit(solution)/shard_map/ppermute | solution.py:97
  113.1 10.7 %collective-permute-start.10 = (f32[2,64,256]{2,1,0:T(8,128)S(1)}, f32[2,64,256]{2,1,0:T(8,128)S(1)}, u32[]{:S(2)}, u32[]{:S(2)}) collective-permute-start(f32[2,64,256]{2,1,0:T(8,128)S(1)} %get-tuple-element.7), channel_id=1, source_target_pairs={{0,32},{32,64},{64,96},{96,128},{128,160},{160,192},{192,224},{224... | collective-permute-start | bytes 393224 | tf_op jit(solution)/shard_map/ppermute | solution.py:97
  115.1 12.1 %collective-permute-start.11 = (f32[2,64,256]{2,1,0:T(8,128)S(1)}, f32[2,64,256]{2,1,0:T(8,128)S(1)}, u32[]{:S(2)}, u32[]{:S(2)}) collective-permute-start(f32[2,64,256]{2,1,0:T(8,128)S(1)} %get-tuple-element.8), channel_id=1, source_target_pairs={{32,0},{64,32},{96,64},{128,96},{160,128},{192,160},{224,192},{256... | collective-permute-start | bytes 393224 | tf_op jit(solution)/shard_map/ppermute | solution.py:97

commit v8 on v6

--- a/solution.py
+++ b/solution.py
@@ -114,8 +114,7 @@
     return total
 
 
-def rows_from_neighbors(change, offset, tile_size, extent):
-    reach = 2 * M
+def rows_from_neighbors(change, offset, tile_size, reach, dst_origin, dst_size, extent):
     size = change.shape[1]
     tag = jnp.broadcast_to(
         jnp.stack([offset[0], offset[1]] + [offset[0]] * 6).astype(jnp.float32)[None, :, None],
@@ -126,21 +125,22 @@
     from_high = from_neighbor(to_low, "row", 1)
     from_low = from_neighbor(to_high, "row", -1)
     place = extent - W
+    least = -M
+    most = tile_size - W + M
     total = None
-    for got, low_side in ((from_high, False), (from_low, True)):
+    for got, base in (
+        (from_high, M + tile_size - dst_origin),
+        (from_low, M + size - reach - tile_size - dst_origin),
+    ):
         strip = got[:, :reach]
         row_at = got[0, reach, 0].astype(jnp.int32)
         col_at = got[0, reach + 1, 0].astype(jnp.int32)
-        if low_side:
-            top = row_at + M + size - reach - tile_size
-            widths = (0, extent)
-        else:
-            top = row_at + M + tile_size
-            widths = (extent, 0)
-        padded = jnp.pad(strip, ((0, 0), widths, (place, place)))
-        start = widths[0] - top
+        above = max(0, base + most)
+        below = max(0, dst_size - reach - (base + least))
+        padded = jnp.pad(strip, ((0, 0), (above, below), (place, place)))
+        start = above - (row_at + base)
         piece = lax.dynamic_slice(
-            padded, (jnp.zeros((), jnp.int32), start, place - M - col_at), (2, extent, extent)
+            padded, (jnp.zeros((), jnp.int32), start, place - M - col_at), (2, dst_size, extent)
         )
         total = piece if total is None else total + piece
     return total
@@ -176,13 +176,15 @@
         padded = jnp.pad(change, ((0, 0), (place, place), (place, place)))
         gathered = lax.dynamic_slice(padded, spread, (2, extent, extent))
         if update + 1 < ITERS:
-            total = gathered + rows_from_neighbors(change, offsets[0], tile_size, extent)
+            total = gathered + rows_from_neighbors(change, offsets[0], tile_size, 2 * M, 0, extent, extent)
             total = neighbor_sum(total, "col", 2, tile_size, 0, 0, extent)
             mask = inside_mask(extent, tile_size)
             extended = jnp.where(mask[None], extended + total / peak_power, 0.0)
         else:
-            total = neighbor_sum(gathered, "col", 2, tile_size, 0, M, tile_size)
-            total = neighbor_sum(total, "row", 1, tile_size, 0, M, tile_size)
+            total = gathered[:, M : M + tile_size] + rows_from_neighbors(
+                change, offsets[0], tile_size, M, M, tile_size, extent
+            )
+            total = neighbor_sum(total, "col", 2, tile_size, 0, M, tile_size)
             current = extended[:, M : M + tile_size, M : M + tile_size] + total / peak_power
     return current
 

time: 126 us -> 129 us (1.024)
  the two profiles are of different devices: /device:TPU:87 before, /device:TPU:71 now
where the time goes in v8:
time: 129 us; the launch traced here: 128 us
  starting transfers between devices  57.1 us (44%)
  waiting for transfers between devices  23.3 us (18%)
  local copies, waits for them, and re-layouts  16.4 us (13%)
  between operations  11.3 us (9%)
  Pallas kernels  10.5 us (8%)
  other arithmetic  9.81 us (8%)
    ppermute x12, starting transfers between devices, from_neighbor(): return lax.ppermute(x, axis, pairs)  57.1 us
    ppermute x12, waiting for transfers between devices, from_neighbor(): return lax.ppermute(x, axis, pairs)  23.3 us
    pallas_call x2, Pallas kernels, pattern_gradient(): pl.pallas_call(gradient_kernel, out_shape=jax.ShapeDtypeStruct((2, rows,...  10.5 us
    another operation x1, local copies, waits for them, and re-layouts, rows_from_neighbors(): jnp.stack([offset[0], offset[1]] + [offset[0]] * 6).astype(jnp.float32)  4.69 us
    select_n x1, other arithmetic, on_device(): extended = jnp.where(mask[None], extended + total / peak_power, 0.0)  2.58 us
  transfers between devices with their start and end apart: 12, of which 8 were waited for; matrix products, arithmetic and copies ran while one was open for 8% of the time, Pallas kernels for 0%

profile of v8, /device:TPU:71, one launch (start us, length us, event | category | flops | bytes accessed | tf_op | source)
XLA Modules:
  0.0 128.5 jit_solution(16103708250786408825)
XLA Ops:
  0.0 1.0 fusion.24
  1.0 4.9 %collective-permute-start = (f32[2,64,256]{2,1,0:T(8,128)S(1)}, f32[2,64,256]{2,1,0:T(8,128)S(1)}, u32[]{:S(2)}, u32[]{:S(2)}) collective-permute-start(f32[2,64,256]{2,1,0:T(8,128)S(1)} %get-tuple-element.15), channel_id=1, source_target_pairs={{0,32},{32,64},{64,96},{96,128},{128,160},{160,192},{192,224},{224... | collective-permute-start | bytes 393224 | tf_op jit(solution)/shard_map/ppermute | solution.py:97
  5.9 13.6 %collective-permute-start.1 = (f32[2,64,256]{2,1,0:T(8,128)S(1)}, f32[2,64,256]{2,1,0:T(8,128)S(1)}, u32[]{:S(2)}, u32[]{:S(2)}) collective-permute-start(f32[2,64,256]{2,1,0:T(8,128)S(1)} %get-tuple-element.16), channel_id=1, source_target_pairs={{32,0},{64,32},{96,64},{128,96},{160,128},{192,160},{224,192},{256... | collective-permute-start | bytes 393224 | tf_op jit(solution)/shard_map/ppermute | solution.py:97
  19.5 1.4 %fusion.29 = (s32[1,1]{1,0:T(1,128)}, s32[1,1]{1,0:T(1,128)}) fusion(s32[1,2]{1,0:T(1,128)} %bitcast.30), kind=kLoop, calls=%fused_computation.54 | loop fusion | bytes 16 | tf_op jit(solution)/shard_map/slice | solution.py:169
  23.6 1.1 pad_add_fusion.1
  24.7 0.2 fusion.21
  24.8 6.7 %collective-permute-start.2 = (f32[2,384,64]{2,1,0:T(8,128)S(1)}, f32[2,384,64]{2,1,0:T(8,128)S(1)}, u32[]{:S(2)}, u32[]{:S(2)}) collective-permute-start(f32[2,384,64]{2,1,0:T(8,128)S(1)} %get-tuple-element.9), channel_id=1, source_target_pairs={{0,1},{1,2},{2,3},{3,4},{4,5},{5,6},{6,7},{7,8},{8,9},{9,10},{10,1... | collective-permute-start | bytes 589832 | tf_op jit(solution)/shard_map/ppermute | solution.py:97
  31.5 1.9 %collective-permute-start.3 = (f32[2,384,64]{2,1,0:T(8,128)S(1)}, f32[2,384,64]{2,1,0:T(8,128)S(1)}, u32[]{:S(2)}, u32[]{:S(2)}) collective-permute-start(f32[2,384,64]{2,1,0:T(8,128)S(1)} %get-tuple-element.10), channel_id=1, source_target_pairs={{1,0},{2,1},{3,2},{4,3},{5,4},{6,5},{7,6},{8,7},{9,8},{10,9},{11,1... | collective-permute-start | bytes 589832 | tf_op jit(solution)/shard_map/ppermute | solution.py:97
  33.4 0.6 fusion.30
  34.0 4.7 %stack.10 = s32[8]{0:T(128)S(1)} concatenate(s32[1]{0:T(128)} %bitcast.10, s32[1]{0:T(128)} %bitcast.11, s32[1]{0:T(128)} %bitcast.10, s32[1]{0:T(128)} %bitcast.10, s32[1]{0:T(128)} %bitcast.10, s32[1]{0:T(128)} %bitcast.10, s32[1]{0:T(128)} %bitcast.10, s32[1]{0:T(128)} %bitcast.10), dimensions={0} | concatenate | bytes 64 | tf_op jit(solution)/shard_map/stack | solution.py:120
  38.7 1.8 %multiply_convert_fusion = (bf16[256,256]{1,0:T(8,128)(2,1)}, bf16[256,256]{1,0:T(8,128)(2,1)}) fusion(), kind=kLoop, calls=%fused_computation.27 | loop fusion | flops 1245184 | bytes 262144 | tf_op jit(solution)/shard_map/convert_element_type | solution.py:26
  40.5 1.3 %collective-permute-done.3 = f32[2,384,64]{2,1,0:T(8,128)S(1)} collective-permute-done((f32[2,384,64]{2,1,0:T(8,128)S(1)}, f32[2,384,64]{2,1,0:T(8,128)S(1)}, u32[]{:S(2)}, u32[]{:S(2)}) %collective-permute-start.3) | collective-permute-done | bytes 196640 | tf_op jit(solution)/shard_map/ppermute | solution.py:97
  41.8 0.5 pad_add_fusion
  42.3 0.3 copy-done.3
  42.6 1.0 constant_dynamic-slice_fusion.1.window_ref
  43.5 5.2 %shard_map.46 = f32[2,256,256]{2,1,0:T(8,128)} custom-call(f32[2,256,256]{2,1,0:T(8,128)} %constant_dynamic-slice_fusion.1.window_ref, f32[2,3,256,256]{3,2,1,0:T(8,128)} %probe_ref.3, f32[256,256]{1,0:T(8,128)} %bitcast.28, bf16[256,256]{1,0:T(8,128)(2,1)} %get-tuple-element.34.table_re_ref, bf16[256,256]{1,0:T(8,128)(2,1)} %get-tuple-element.33.table_im_ref), custom_call_target="tpu_custom_call" | custom-call | tf_op jit(solution)/shard_map/pallas_call | solution.py:86
  48.8 1.1 fusion.23
  50.0 2.1 %collective-permute-start.5 = (f32[2,136,256]{2,1,0:T(8,128)S(1)}, f32[2,136,256]{2,1,0:T(8,128)S(1)}, u32[]{:S(2)}, u32[]{:S(2)}) collective-permute-start(f32[2,136,256]{2,1,0:T(8,128)S(1)} %get-tuple-element.27), channel_id=1, source_target_pairs={{0,32},{32,64},{64,96},{96,128},{128,160},{160,192},{192,224},{224... | collective-permute-start | bytes 835592 | tf_op jit(solution)/shard_map/ppermute | solution.py:97
  52.0 8.3 %collective-permute-start.4 = (f32[2,136,256]{2,1,0:T(8,128)S(1)}, f32[2,136,256]{2,1,0:T(8,128)S(1)}, u32[]{:S(2)}, u32[]{:S(2)}) collective-permute-start(f32[2,136,256]{2,1,0:T(8,128)S(1)} %get-tuple-element.28), channel_id=1, source_target_pairs={{32,0},{64,32},{96,64},{128,96},{160,128},{192,160},{224,192},{256... | collective-permute-start | bytes 835592 | tf_op jit(solution)/shard_map/ppermute | solution.py:97
  63.0 5.4 %collective-permute-done.5 = f32[2,136,256]{2,1,0:T(8,128)S(1)} collective-permute-done((f32[2,136,256]{2,1,0:T(8,128)S(1)}, f32[2,136,256]{2,1,0:T(8,128)S(1)}, u32[]{:S(2)}, u32[]{:S(2)}) %collective-permute-start.5) | collective-permute-done | bytes 278560 | tf_op jit(solution)/shard_map/ppermute | solution.py:97
  68.4 0.6 fusion.25
  69.6 1.0 collective-permute-done.4
  70.7 0.6 fusion.26
  73.3 1.0 fusion
  74.3 0.9 fusion.19
  75.3 2.3 %collective-permute-start.6 = (f32[2,384,128]{2,1,0:T(8,128)}, f32[2,384,128]{2,1,0:T(8,128)S(1)}, u32[]{:S(2)}, u32[]{:S(2)}) collective-permute-start(f32[2,384,128]{2,1,0:T(8,128)} %get-tuple-element.5), channel_id=1, source_target_pairs={{0,1},{1,2},{2,3},{3,4},{4,5},{5,6},{6,7},{7,8},{8,9},{9,10},{10,1... | collective-permute-start | bytes 1179656 | tf_op jit(solution)/shard_map/ppermute | solution.py:97
  77.6 2.0 %collective-permute-start.7 = (f32[2,384,128]{2,1,0:T(8,128)}, f32[2,384,128]{2,1,0:T(8,128)}, u32[]{:S(2)}, u32[]{:S(2)}) collective-permute-start(f32[2,384,128]{2,1,0:T(8,128)} %get-tuple-element.6), channel_id=1, source_target_pairs={{1,0},{2,1},{3,2},{4,3},{5,4},{6,5},{7,6},{8,7},{9,8},{10,9},{11,1... | collective-permute-start | bytes 1179656 | tf_op jit(solution)/shard_map/ppermute | solution.py:97
  79.7 0.6 reduce_max.9
  80.9 0.1 broadcast_and_fusion
  81.1 1.5 %collective-permute-done.6 = f32[2,384,128]{2,1,0:T(8,128)S(1)} collective-permute-done((f32[2,384,128]{2,1,0:T(8,128)}, f32[2,384,128]{2,1,0:T(8,128)S(1)}, u32[]{:S(2)}, u32[]{:S(2)}) %collective-permute-start.6) | collective-permute-done | bytes 393248 | tf_op jit(solution)/shard_map/ppermute | solution.py:97
  82.6 0.7 copy-done.4
  83.3 4.9 %collective-permute-done.7 = f32[2,384,128]{2,1,0:T(8,128)} collective-permute-done((f32[2,384,128]{2,1,0:T(8,128)}, f32[2,384,128]{2,1,0:T(8,128)}, u32[]{:S(2)}, u32[]{:S(2)}) %collective-permute-start.7) | collective-permute-done | bytes 393248 | tf_op jit(solution)/shard_map/ppermute | solution.py:97
  88.2 2.6 %add_select_fusion = f32[2,384,384]{2,1,0:T(8,128)S(1)} fusion(f32[2,384,128]{2,1,0:T(8,128)} %collective-permute-done.7, f32[2,384,128]{2,1,0:T(8,128)} %copy-done.4, f32[]{:T(128)S(6)} %add.228, pred[384,384]{1,0:T(8,128)(4,1)S(1)} %broadcast_and_fusion, s32[]{:T(128)S(6)} %select_n.64, s32[]{:T(128)S(6)} %select_n.65, f32[2,128,256]{2,1,0:T(8,128)S(1)} %slice.139, ...), kind=kLoop, calls=%fused_computation.9 | loop fusion | flops 2654208 | bytes 4341788 | tf_op jit(solution)/shard_map/jit(_where)/select_n | solution.py:182
  90.8 1.0 constant_dynamic-slice_fusion.window_ref
  91.8 5.2 %shard_map.47 = f32[2,256,256]{2,1,0:T(8,128)} custom-call(f32[2,256,256]{2,1,0:T(8,128)} %constant_dynamic-slice_fusion.window_ref, f32[2,3,256,256]{3,2,1,0:T(8,128)} %probe_ref.3, f32[256,256]{1,0:T(8,128)} %bitcast.29, bf16[256,256]{1,0:T(8,128)(2,1)} %get-tuple-element.34.table_re_ref, bf16[256,256]{1,0:T(8,128)(2,1)} %get-tuple-element.33.table_im_ref), custom_call_target="tpu_custom_call" | custom-call | tf_op jit(solution)/shard_map/pallas_call | solution.py:86
  97.0 1.0 fusion.22
  98.1 1.9 %collective-permute-start.9 = (f32[2,72,256]{2,1,0:T(8,128)S(1)}, f32[2,72,256]{2,1,0:T(8,128)S(1)}, u32[]{:S(2)}, u32[]{:S(2)}) collective-permute-start(f32[2,72,256]{2,1,0:T(8,128)S(1)} %get-tuple-element.25), channel_id=1, source_target_pairs={{0,32},{32,64},{64,96},{96,128},{128,160},{160,192},{192,224},{224... | collective-permute-start | bytes 442376 | tf_op jit(solution)/shard_map/ppermute | solution.py:97
  100.0 8.3 %collective-permute-start.8 = (f32[2,72,256]{2,1,0:T(8,128)S(1)}, f32[2,72,256]{2,1,0:T(8,128)S(1)}, u32[]{:S(2)}, u32[]{:S(2)}) collective-permute-start(f32[2,72,256]{2,1,0:T(8,128)S(1)} %get-tuple-element.26), channel_id=1, source_target_pairs={{32,0},{64,32},{96,64},{128,96},{160,128},{192,160},{224,192},{256... | collective-permute-start | bytes 442376 | tf_op jit(solution)/shard_map/ppermute | solution.py:97
  108.4 2.3 %collective-permute-done.9 = f32[2,72,256]{2,1,0:T(8,128)S(1)} collective-permute-done((f32[2,72,256]{2,1,0:T(8,128)S(1)}, f32[2,72,256]{2,1,0:T(8,128)S(1)}, u32[]{:S(2)}, u32[]{:S(2)}) %collective-permute-start.9) | collective-permute-done | bytes 147488 | tf_op jit(solution)/shard_map/ppermute | solution.py:97
  110.6 0.5 fusion.27
  112.5 0.5 fusion.28
  114.4 0.7 fusion.3
  115.1 0.1 fusion.20
  115.2 3.1 %collective-permute-start.10 = (f32[2,256,64]{2,1,0:T(8,128)S(1)}, f32[2,256,64]{2,1,0:T(8,128)S(1)}, u32[]{:S(2)}, u32[]{:S(2)}) collective-permute-start(f32[2,256,64]{2,1,0:T(8,128)S(1)} %get-tuple-element.7), channel_id=1, source_target_pairs={{0,1},{1,2},{2,3},{3,4},{4,5},{5,6},{6,7},{7,8},{8,9},{9,10},{10,1... | collective-permute-start | bytes 393224 | tf_op jit(solution)/shard_map/ppermute | solution.py:97
  118.4 1.9 %collective-permute-start.11 = (f32[2,256,64]{2,1,0:T(8,128)S(1)}, f32[2,256,64]{2,1,0:T(8,128)S(1)}, u32[]{:S(2)}, u32[]{:S(2)}) collective-permute-start(f32[2,256,64]{2,1,0:T(8,128)S(1)} %get-tuple-element.8), channel_id=1, source_target_pairs={{1,0},{2,1},{3,2},{4,3},{5,4},{6,5},{7,6},{8,7},{9,8},{10,9},{11,1... | collective-permute-start | bytes 393224 | tf_op jit(solution)/shard_map/ppermute | solution.py:97
  120.3 1.4 %collective-permute-done.10 = f32[2,256,64]{2,1,0:T(8,128)S(1)} collective-permute-done((f32[2,256,64]{2,1,0:T(8,128)S(1)}, f32[2,256,64]{2,1,0:T(8,128)S(1)}, u32[]{:S(2)}, u32[]{:S(2)}) %collective-permute-start.10) | collective-permute-done | bytes 131104 | tf_op jit(solution)/shard_map/ppermute | solution.py:97
  121.7 5.6 %collective-permute-done.11 = f32[2,256,64]{2,1,0:T(8,128)S(1)} collective-permute-done((f32[2,256,64]{2,1,0:T(8,128)S(1)}, f32[2,256,64]{2,1,0:T(8,128)S(1)}, u32[]{:S(2)}, u32[]{:S(2)}) %collective-permute-start.11) | collective-permute-done | bytes 131104 | tf_op jit(solution)/shard_map/ppermute | solution.py:97
  127.3 1.2 fusion.6
  (24 shorter events, 0.4 us)
Async XLA Ops:
  1.0 22.5 %collective-permute-start = (f32[2,64,256]{2,1,0:T(8,128)S(1)}, f32[2,64,256]{2,1,0:T(8,128)S(1)}, u32[]{:S(2)}, u32[]{:S(2)}) collective-permute-start(f32[2,64,256]{2,1,0:T(8,128)S(1)} %get-tuple-element.15), channel_id=1, source_target_pairs={{0,32},{32,64},{64,96},{96,128},{128,160},{160,192},{192,224},{224... | collective-permute-start | bytes 393224 | tf_op jit(solution)/shard_map/ppermute | solution.py:97
  5.9 17.6 %collective-permute-start.1 = (f32[2,64,256]{2,1,0:T(8,128)S(1)}, f32[2,64,256]{2,1,0:T(8,128)S(1)}, u32[]{:S(2)}, u32[]{:S(2)}) collective-permute-start(f32[2,64,256]{2,1,0:T(8,128)S(1)} %get-tuple-element.16), channel_id=1, source_target_pairs={{32,0},{64,32},{96,64},{128,96},{160,128},{192,160},{224,192},{256... | collective-permute-start | bytes 393224 | tf_op jit(solution)/shard_map/ppermute | solution.py:97
  24.7 8.8 %copy-start.5 = (s32[1,1,1,2]{3,2,1,0:T(1,128)S(1)}, s32[1,1,1,2]{3,2,1,0:T(1,128)}, u32[]{:S(2)}) copy-start(s32[1,1,1,2]{3,2,1,0:T(1,128)} %param.6) | copy-start | bytes 28
  24.8 15.7 %collective-permute-start.2 = (f32[2,384,64]{2,1,0:T(8,128)S(1)}, f32[2,384,64]{2,1,0:T(8,128)S(1)}, u32[]{:S(2)}, u32[]{:S(2)}) collective-permute-start(f32[2,384,64]{2,1,0:T(8,128)S(1)} %get-tuple-element.9), channel_id=1, source_target_pairs={{0,1},{1,2},{2,3},{3,4},{4,5},{5,6},{6,7},{7,8},{8,9},{9,10},{10,1... | collective-permute-start | bytes 589832 | tf_op jit(solution)/shard_map/ppermute | solution.py:97
  31.5 10.3 %collective-permute-start.3 = (f32[2,384,64]{2,1,0:T(8,128)S(1)}, f32[2,384,64]{2,1,0:T(8,128)S(1)}, u32[]{:S(2)}, u32[]{:S(2)}) collective-permute-start(f32[2,384,64]{2,1,0:T(8,128)S(1)} %get-tuple-element.10), channel_id=1, source_target_pairs={{1,0},{2,1},{3,2},{4,3},{5,4},{6,5},{7,6},{8,7},{9,8},{10,9},{11,1... | collective-permute-start | bytes 589832 | tf_op jit(solution)/shard_map/ppermute | solution.py:97
  41.8 0.7 copy-start.3
  49.9 23.5 %copy-start.1 = (f32[2,256,256]{2,1,0:T(8,128)S(1)}, f32[2,256,256]{2,1,0:T(8,128)}, u32[]{:S(2)}) copy-start(f32[2,256,256]{2,1,0:T(8,128)} %shard_map.46) | copy-start | bytes 1572868
  50.0 18.4 %collective-permute-start.5 = (f32[2,136,256]{2,1,0:T(8,128)S(1)}, f32[2,136,256]{2,1,0:T(8,128)S(1)}, u32[]{:S(2)}, u32[]{:S(2)}) collective-permute-start(f32[2,136,256]{2,1,0:T(8,128)S(1)} %get-tuple-element.27), channel_id=1, source_target_pairs={{0,32},{32,64},{64,96},{96,128},{128,160},{160,192},{192,224},{224... | collective-permute-start | bytes 835592 | tf_op jit(solution)/shard_map/ppermute | solution.py:97
  52.0 18.6 %collective-permute-start.4 = (f32[2,136,256]{2,1,0:T(8,128)S(1)}, f32[2,136,256]{2,1,0:T(8,128)S(1)}, u32[]{:S(2)}, u32[]{:S(2)}) collective-permute-start(f32[2,136,256]{2,1,0:T(8,128)S(1)} %get-tuple-element.28), channel_id=1, source_target_pairs={{32,0},{64,32},{96,64},{128,96},{160,128},{192,160},{224,192},{256... | collective-permute-start | bytes 835592 | tf_op jit(solution)/shard_map/ppermute | solution.py:97
  74.3 5.3 %copy-start = (f32[2,3,256,256]{3,2,1,0:T(8,128)S(1)}, f32[2,3,256,256]{3,2,1,0:T(8,128)}, u32[]{:S(2)}) copy-start(f32[2,3,256,256]{3,2,1,0:T(8,128)} %probe_ref.3) | copy-start | bytes 4718596
  75.3 7.3 %collective-permute-start.6 = (f32[2,384,128]{2,1,0:T(8,128)}, f32[2,384,128]{2,1,0:T(8,128)S(1)}, u32[]{:S(2)}, u32[]{:S(2)}) collective-permute-start(f32[2,384,128]{2,1,0:T(8,128)} %get-tuple-element.5), channel_id=1, source_target_pairs={{0,1},{1,2},{2,3},{3,4},{4,5},{5,6},{6,7},{7,8},{8,9},{9,10},{10,1... | collective-permute-start | bytes 1179656 | tf_op jit(solution)/shard_map/ppermute | solution.py:97
  77.6 10.6 %collective-permute-start.7 = (f32[2,384,128]{2,1,0:T(8,128)}, f32[2,384,128]{2,1,0:T(8,128)}, u32[]{:S(2)}, u32[]{:S(2)}) collective-permute-start(f32[2,384,128]{2,1,0:T(8,128)} %get-tuple-element.6), channel_id=1, source_target_pairs={{1,0},{2,1},{3,2},{4,3},{5,4},{6,5},{7,6},{8,7},{9,8},{10,9},{11,1... | collective-permute-start | bytes 1179656 | tf_op jit(solution)/shard_map/ppermute | solution.py:97
  82.6 0.7 copy-start.4
  97.0 17.3 %copy-start.2 = (f32[2,256,256]{2,1,0:T(8,128)S(1)}, f32[2,256,256]{2,1,0:T(8,128)}, u32[]{:S(2)}) copy-start(f32[2,256,256]{2,1,0:T(8,128)} %shard_map.47) | copy-start | bytes 1572868
  98.1 12.5 %collective-permute-start.9 = (f32[2,72,256]{2,1,0:T(8,128)S(1)}, f32[2,72,256]{2,1,0:T(8,128)S(1)}, u32[]{:S(2)}, u32[]{:S(2)}) collective-permute-start(f32[2,72,256]{2,1,0:T(8,128)S(1)} %get-tuple-element.25), channel_id=1, source_target_pairs={{0,32},{32,64},{64,96},{96,128},{128,160},{160,192},{192,224},{224... | collective-permute-start | bytes 442376 | tf_op jit(solution)/shard_map/ppermute | solution.py:97
  100.0 12.4 %collective-permute-start.8 = (f32[2,72,256]{2,1,0:T(8,128)S(1)}, f32[2,72,256]{2,1,0:T(8,128)S(1)}, u32[]{:S(2)}, u32[]{:S(2)}) collective-permute-start(f32[2,72,256]{2,1,0:T(8,128)S(1)} %get-tuple-element.26), channel_id=1, source_target_pairs={{32,0},{64,32},{96,64},{128,96},{160,128},{192,160},{224,192},{256... | collective-permute-start | bytes 442376 | tf_op jit(solution)/shard_map/ppermute | solution.py:97
  115.2 6.4 %collective-permute-start.10 = (f32[2,256,64]{2,1,0:T(8,128)S(1)}, f32[2,256,64]{2,1,0:T(8,128)S(1)}, u32[]{:S(2)}, u32[]{:S(2)}) collective-permute-start(f32[2,256,64]{2,1,0:T(8,128)S(1)} %get-tuple-element.7), channel_id=1, source_target_pairs={{0,1},{1,2},{2,3},{3,4},{4,5},{5,6},{6,7},{7,8},{8,9},{9,10},{10,1... | collective-permute-start | bytes 393224 | tf_op jit(solution)/shard_map/ppermute | solution.py:97
  118.4 8.9 %collective-permute-start.11 = (f32[2,256,64]{2,1,0:T(8,128)S(1)}, f32[2,256,64]{2,1,0:T(8,128)S(1)}, u32[]{:S(2)}, u32[]{:S(2)}) collective-permute-start(f32[2,256,64]{2,1,0:T(8,128)S(1)} %get-tuple-element.8), channel_id=1, source_target_pairs={{1,0},{2,1},{3,2},{4,3},{5,4},{6,5},{7,6},{8,7},{9,8},{10,9},{11,1... | collective-permute-start | bytes 393224 | tf_op jit(solution)/shard_map/ppermute | solution.py:97

commit v9 on v6

--- a/solution.py
+++ b/solution.py
@@ -170,20 +170,30 @@
     spread = (zero, place - M - offsets[0, 0], place - M - offsets[0, 1])
     extended = neighbor_sum(object_planes, "row", 1, tile_size, M, 0, extent)
     extended = neighbor_sum(extended, "col", 2, tile_size, M, 0, extent)
+    mask = inside_mask(extent, tile_size)
+    grown = None
     for update in range(ITERS):
         window = lax.dynamic_slice(extended, corner, (2, W, W))
+        if grown is not None:
+            inside = lax.dynamic_slice(mask, corner[1:], (W, W))
+            step = lax.dynamic_slice(grown, corner, (2, W, W))
+            window = jnp.where(inside[None], window + step, 0.0)
         change = pattern_gradient(window, measured[0], probe_modes, table_re, table_im)
         padded = jnp.pad(change, ((0, 0), (place, place), (place, place)))
         gathered = lax.dynamic_slice(padded, spread, (2, extent, extent))
         if update + 1 < ITERS:
+            if grown is not None:
+                extended = jnp.where(mask[None], extended + grown, 0.0)
             total = gathered + rows_from_neighbors(change, offsets[0], tile_size, extent)
             total = neighbor_sum(total, "col", 2, tile_size, 0, 0, extent)
-            mask = inside_mask(extent, tile_size)
-            extended = jnp.where(mask[None], extended + total / peak_power, 0.0)
+            grown = total / peak_power
         else:
             total = neighbor_sum(gathered, "col", 2, tile_size, 0, M, tile_size)
             total = neighbor_sum(total, "row", 1, tile_size, 0, M, tile_size)
-            current = extended[:, M : M + tile_size, M : M + tile_size] + total / peak_power
+            current = extended[:, M : M + tile_size, M : M + tile_size]
+            if grown is not None:
+                current = current + grown[:, M : M + tile_size, M : M + tile_size]
+            current = current + total / peak_power
     return current
 
 

time: 126 us -> 132 us (1.048)
  the two profiles are of different devices: /device:TPU:87 before, /device:TPU:71 now
where the time goes in v9:
time: 132 us
  starting transfers between devices  56.6 us (43%)
  waiting for transfers between devices  25.6 us (19%)
  local copies, waits for them, and re-layouts  18 us (14%)
  other arithmetic  12.7 us (10%)
  Pallas kernels  10.5 us (8%)
  between operations  8.18 us (6%)
    ppermute x12, starting transfers between devices, from_neighbor(): return lax.ppermute(x, axis, pairs)  56.6 us
    ppermute x12, waiting for transfers between devices, from_neighbor(): return lax.ppermute(x, axis, pairs)  25.6 us
    pallas_call x2, Pallas kernels, pattern_gradient(): pl.pallas_call(gradient_kernel, out_shape=jax.ShapeDtypeStruct((2, rows,...  10.5 us
    another operation x1, local copies, waits for them, and re-layouts, rows_from_neighbors(): jnp.stack([offset[0], offset[1]] + [offset[0]] * 6).astype(jnp.float32)  5.19 us
    slice x5, local copies, waits for them, and re-layouts, neighbor_sum(): piece = lax.slice_in_dim(frame, low - shift, high - shift, axis=dim)  3.44 us
    add x3, other arithmetic, neighbor_sum(): total = piece if total is None else total + piece  3.12 us
  transfers between devices with their start and end apart: 12, of which 9 were waited for; matrix products, arithmetic and copies ran while one was open for 10% of the time, Pallas kernels for 0%

profile of v9, /device:TPU:71, one launch (start us, length us, event | category | flops | bytes accessed | tf_op | source)
XLA Modules:
  0.0 131.6 jit_solution(12888549825819804521)
XLA Ops:
  0.0 1.0 fusion.23
  1.0 4.9 %collective-permute-start = (f32[2,64,256]{2,1,0:T(8,128)S(1)}, f32[2,64,256]{2,1,0:T(8,128)S(1)}, u32[]{:S(2)}, u32[]{:S(2)}) collective-permute-start(f32[2,64,256]{2,1,0:T(8,128)S(1)} %get-tuple-element.15), channel_id=1, source_target_pairs={{0,32},{32,64},{64,96},{96,128},{128,160},{160,192},{192,224},{224... | collective-permute-start | bytes 393224 | tf_op jit(solution)/shard_map/ppermute | solution.py:97
  5.9 13.6 %collective-permute-start.1 = (f32[2,64,256]{2,1,0:T(8,128)S(1)}, f32[2,64,256]{2,1,0:T(8,128)S(1)}, u32[]{:S(2)}, u32[]{:S(2)}) collective-permute-start(f32[2,64,256]{2,1,0:T(8,128)S(1)} %get-tuple-element.16), channel_id=1, source_target_pairs={{32,0},{64,32},{96,64},{128,96},{160,128},{192,160},{224,192},{256... | collective-permute-start | bytes 393224 | tf_op jit(solution)/shard_map/ppermute | solution.py:97
  19.5 1.3 fusion.27
  23.2 1.1 pad_add_fusion.1
  24.4 0.2 fusion.21
  24.5 7.0 %collective-permute-start.2 = (f32[2,384,64]{2,1,0:T(8,128)S(1)}, f32[2,384,64]{2,1,0:T(8,128)S(1)}, u32[]{:S(2)}, u32[]{:S(2)}) collective-permute-start(f32[2,384,64]{2,1,0:T(8,128)S(1)} %get-tuple-element.9), channel_id=1, source_target_pairs={{0,1},{1,2},{2,3},{3,4},{4,5},{5,6},{6,7},{7,8},{8,9},{9,10},{10,1... | collective-permute-start | bytes 589832 | tf_op jit(solution)/shard_map/ppermute | solution.py:97
  31.5 1.9 %collective-permute-start.3 = (f32[2,384,64]{2,1,0:T(8,128)S(1)}, f32[2,384,64]{2,1,0:T(8,128)S(1)}, u32[]{:S(2)}, u32[]{:S(2)}) collective-permute-start(f32[2,384,64]{2,1,0:T(8,128)S(1)} %get-tuple-element.10), channel_id=1, source_target_pairs={{1,0},{2,1},{3,2},{4,3},{5,4},{6,5},{7,6},{8,7},{9,8},{10,9},{11,1... | collective-permute-start | bytes 589832 | tf_op jit(solution)/shard_map/ppermute | solution.py:97
  33.4 0.7 fusion.26
  34.1 5.2 %stack.9 = s32[8]{0:T(128)S(1)} concatenate(s32[1]{0:T(128)} %bitcast.10, s32[1]{0:T(128)} %bitcast.11, s32[1]{0:T(128)} %bitcast.10, s32[1]{0:T(128)} %bitcast.10, s32[1]{0:T(128)} %bitcast.10, s32[1]{0:T(128)} %bitcast.10, s32[1]{0:T(128)} %bitcast.10, s32[1]{0:T(128)} %bitcast.10), dimensions={0} | concatenate | bytes 64 | tf_op jit(solution)/shard_map/stack | solution.py:121
  39.3 0.6 pad.82.clone
  39.9 1.7 %multiply_convert_fusion = (bf16[256,256]{1,0:T(8,128)(2,1)}, bf16[256,256]{1,0:T(8,128)(2,1)}) fusion(), kind=kLoop, calls=%fused_computation.28 | loop fusion | flops 1245184 | bytes 262144 | tf_op jit(solution)/shard_map/convert_element_type | solution.py:26
  41.6 0.2 collective-permute-done.3
  41.8 0.5 pad_add_fusion
  42.3 1.0 constant_dynamic-slice_fusion.window_ref
  43.3 5.2 %shard_map.46 = f32[2,256,256]{2,1,0:T(8,128)} custom-call(f32[2,256,256]{2,1,0:T(8,128)} %constant_dynamic-slice_fusion.window_ref, f32[2,3,256,256]{3,2,1,0:T(8,128)} %probe_ref.3, f32[256,256]{1,0:T(8,128)} %bitcast.20, bf16[256,256]{1,0:T(8,128)(2,1)} %get-tuple-element.28.table_re_ref, bf16[256,256]{1,0:T(8,128)(2,1)} %get-tuple-element.27.table_im_ref), custom_call_target="tpu_custom_call" | custom-call | tf_op jit(solution)/shard_map/pallas_call | solution.py:86
  48.5 1.2 fusion.22
  49.7 0.8 pad_maximum_fusion.1
  50.5 1.9 %collective-permute-start.5 = (f32[2,136,256]{2,1,0:T(8,128)}, f32[2,136,256]{2,1,0:T(8,128)}, u32[]{:S(2)}, u32[]{:S(2)}) collective-permute-start(f32[2,136,256]{2,1,0:T(8,128)} %get-tuple-element.21), channel_id=1, source_target_pairs={{0,32},{32,64},{64,96},{96,128},{128,160},{160,192},{192,224},{224... | collective-permute-start | bytes 835592 | tf_op jit(solution)/shard_map/ppermute | solution.py:97
  54.9 8.5 %collective-permute-start.4 = (f32[2,136,256]{2,1,0:T(8,128)S(1)}, f32[2,136,256]{2,1,0:T(8,128)S(1)}, u32[]{:S(2)}, u32[]{:S(2)}) collective-permute-start(f32[2,136,256]{2,1,0:T(8,128)S(1)} %get-tuple-element.22), channel_id=1, source_target_pairs={{32,0},{64,32},{96,64},{128,96},{160,128},{192,160},{224,192},{256... | collective-permute-start | bytes 835592 | tf_op jit(solution)/shard_map/ppermute | solution.py:97
  63.4 0.8 multiply_reduce_fusion
  64.2 6.0 %collective-permute-done.5 = f32[2,136,256]{2,1,0:T(8,128)} collective-permute-done((f32[2,136,256]{2,1,0:T(8,128)}, f32[2,136,256]{2,1,0:T(8,128)}, u32[]{:S(2)}, u32[]{:S(2)}) %collective-permute-start.5) | collective-permute-done | bytes 278560 | tf_op jit(solution)/shard_map/ppermute | solution.py:97
  70.2 1.3 fusion.24
  72.1 2.4 %collective-permute-done.4 = f32[2,136,256]{2,1,0:T(8,128)S(1)} collective-permute-done((f32[2,136,256]{2,1,0:T(8,128)S(1)}, f32[2,136,256]{2,1,0:T(8,128)S(1)}, u32[]{:S(2)}, u32[]{:S(2)}) %collective-permute-start.4) | collective-permute-done | bytes 278560 | tf_op jit(solution)/shard_map/ppermute | solution.py:97
  74.6 0.7 copy-done.4
  75.3 0.6 fusion.25
  77.6 1.0 slice.113
  78.6 1.0 slice.117
  79.6 1.0 fusion
  80.6 2.3 %collective-permute-start.6 = (f32[2,384,128]{2,1,0:T(8,128)S(1)}, f32[2,384,128]{2,1,0:T(8,128)}, u32[]{:S(2)}, u32[]{:S(2)}) collective-permute-start(f32[2,384,128]{2,1,0:T(8,128)S(1)} %get-tuple-element.5), channel_id=1, source_target_pairs={{0,1},{1,2},{2,3},{3,4},{4,5},{5,6},{6,7},{7,8},{8,9},{9,10},{10,1... | collective-permute-start | bytes 1179656 | tf_op jit(solution)/shard_map/ppermute | solution.py:97
  83.0 2.0 %collective-permute-start.7 = (f32[2,384,128]{2,1,0:T(8,128)S(1)}, f32[2,384,128]{2,1,0:T(8,128)}, u32[]{:S(2)}, u32[]{:S(2)}) collective-permute-start(f32[2,384,128]{2,1,0:T(8,128)S(1)} %get-tuple-element.6), channel_id=1, source_target_pairs={{1,0},{2,1},{3,2},{4,3},{5,4},{6,5},{7,6},{8,7},{9,8},{10,9},{11,1... | collective-permute-start | bytes 1179656 | tf_op jit(solution)/shard_map/ppermute | solution.py:97
  85.0 0.7 reduce_max.9
  86.6 1.0 collective-permute-done.6
  87.7 5.7 %collective-permute-done.7 = f32[2,384,128]{2,1,0:T(8,128)} collective-permute-done((f32[2,384,128]{2,1,0:T(8,128)S(1)}, f32[2,384,128]{2,1,0:T(8,128)}, u32[]{:S(2)}, u32[]{:S(2)}) %collective-permute-start.7) | collective-permute-done | bytes 393248 | tf_op jit(solution)/shard_map/ppermute | solution.py:97
  93.4 2.1 %add_divide_fusion = f32[2,384,384]{2,1,0:T(8,128)S(1)} fusion(f32[2,384,128]{2,1,0:T(8,128)} %collective-permute-done.7, f32[2,384,128]{2,1,0:T(8,128)} %collective-permute-done.6, f32[]{:T(128)S(6)} %add.212, s32[]{:T(128)S(6)} %select_n.56, s32[]{:T(128)S(6)} %select_n.57, f32[2,128,256]{2,1,0:T(8,128)S(1)} %slice.117, s32[]{:T(128)S(6)} %select_n.54, ...), kind=kLoop, calls=%fused_computation.9 | loop fusion | flops 1474560 | bytes 3014684 | tf_op jit(solution)/shard_map/div | solution.py:189
  95.5 1.1 add_select_fusion.window_ref
  96.6 5.3 %shard_map.47 = f32[2,256,256]{2,1,0:T(8,128)} custom-call(f32[2,256,256]{2,1,0:T(8,128)} %add_select_fusion.window_ref, f32[2,3,256,256]{3,2,1,0:T(8,128)} %probe_ref.3, f32[256,256]{1,0:T(8,128)} %bitcast.21, bf16[256,256]{1,0:T(8,128)(2,1)} %get-tuple-element.28.table_re_ref, bf16[256,256]{1,0:T(8,128)(2,1)} %get-tuple-element.27.table_im_ref), custom_call_target="tpu_custom_call" | custom-call | tf_op jit(solution)/shard_map/pallas_call | solution.py:86
  101.9 2.2 %pad_dynamic-slice_fusion.1 = (f32[2,384,64]{2,1,0:T(8,128)}, f32[2,384,64]{2,1,0:T(8,128)S(1)}) fusion(s32[]{:T(128)S(6)} %select_n.52, s32[]{:T(128)S(6)} %add.220, f32[2,256,256]{2,1,0:T(8,128)} %shard_map.47, s32[]{:T(128)S(6)} %select_n.53), kind=kLoop, calls=%fused_computation.1 | loop fusion | bytes 917516 | tf_op jit(solution)/shard_map/slice | solution.py:107
  104.1 1.9 %collective-permute-start.8 = (f32[2,384,64]{2,1,0:T(8,128)}, f32[2,384,64]{2,1,0:T(8,128)}, u32[]{:S(2)}, u32[]{:S(2)}) collective-permute-start(f32[2,384,64]{2,1,0:T(8,128)} %get-tuple-element.11), channel_id=1, source_target_pairs={{0,1},{1,2},{2,3},{3,4},{4,5},{5,6},{6,7},{7,8},{8,9},{9,10},{10,1... | collective-permute-start | bytes 589832 | tf_op jit(solution)/shard_map/ppermute | solution.py:97
  106.0 2.4 %collective-permute-start.9 = (f32[2,384,64]{2,1,0:T(8,128)S(1)}, f32[2,384,64]{2,1,0:T(8,128)}, u32[]{:S(2)}, u32[]{:S(2)}) collective-permute-start(f32[2,384,64]{2,1,0:T(8,128)S(1)} %get-tuple-element.12), channel_id=1, source_target_pairs={{1,0},{2,1},{3,2},{4,3},{5,4},{6,5},{7,6},{8,7},{9,8},{10,9},{11,1... | collective-permute-start | bytes 589832 | tf_op jit(solution)/shard_map/ppermute | solution.py:97
  108.4 2.6 %collective-permute-done.8 = f32[2,384,64]{2,1,0:T(8,128)} collective-permute-done((f32[2,384,64]{2,1,0:T(8,128)}, f32[2,384,64]{2,1,0:T(8,128)}, u32[]{:S(2)}, u32[]{:S(2)}) %collective-permute-start.8) | collective-permute-done | bytes 196640 | tf_op jit(solution)/shard_map/ppermute | solution.py:97
  111.0 5.4 %collective-permute-done.9 = f32[2,384,64]{2,1,0:T(8,128)} collective-permute-done((f32[2,384,64]{2,1,0:T(8,128)S(1)}, f32[2,384,64]{2,1,0:T(8,128)}, u32[]{:S(2)}, u32[]{:S(2)}) %collective-permute-start.9) | collective-permute-done | bytes 196640 | tf_op jit(solution)/shard_map/ppermute | solution.py:97
  116.4 1.5 %fusion.3 = f32[2,384,256]{2,1,0:T(8,128)S(1)} fusion(s32[]{:T(128)S(6)} %select_n.52, s32[]{:T(128)S(6)} %add.221, f32[2,256,256]{2,1,0:T(8,128)S(1)} %copy-done.2, f32[2,384,64]{2,1,0:T(8,128)} %collective-permute-done.9, f32[2,384,64]{2,1,0:T(8,128)} %collective-permute-done.8), kind=kLoop, calls=%fused_computation.12 | loop fusion | flops 393216 | bytes 1703944 | tf_op jit(solution)/shard_map/add | solution.py:113
  118.0 1.9 %collective-permute-start.10 = (f32[2,64,256]{2,1,0:T(8,128)S(1)}, f32[2,64,256]{2,1,0:T(8,128)S(1)}, u32[]{:S(2)}, u32[]{:S(2)}) collective-permute-start(f32[2,64,256]{2,1,0:T(8,128)S(1)} %get-tuple-element.7), channel_id=1, source_target_pairs={{0,32},{32,64},{64,96},{96,128},{128,160},{160,192},{192,224},{224... | collective-permute-start | bytes 393224 | tf_op jit(solution)/shard_map/ppermute | solution.py:97
  119.9 8.3 %collective-permute-start.11 = (f32[2,64,256]{2,1,0:T(8,128)S(1)}, f32[2,64,256]{2,1,0:T(8,128)S(1)}, u32[]{:S(2)}, u32[]{:S(2)}) collective-permute-start(f32[2,64,256]{2,1,0:T(8,128)S(1)} %get-tuple-element.8), channel_id=1, source_target_pairs={{32,0},{64,32},{96,64},{128,96},{160,128},{192,160},{224,192},{256... | collective-permute-start | bytes 393224 | tf_op jit(solution)/shard_map/ppermute | solution.py:97
  128.3 0.4 collective-permute-done.10
  128.7 1.8 %collective-permute-done.11 = f32[2,64,256]{2,1,0:T(8,128)S(1)} collective-permute-done((f32[2,64,256]{2,1,0:T(8,128)S(1)}, f32[2,64,256]{2,1,0:T(8,128)S(1)}, u32[]{:S(2)}, u32[]{:S(2)}) %collective-permute-start.11) | collective-permute-done | bytes 131104 | tf_op jit(solution)/shard_map/ppermute | solution.py:97
  130.4 1.1 fusion.6
  (24 shorter events, 0.4 us)
Async XLA Ops:
  1.0 22.2 %collective-permute-start = (f32[2,64,256]{2,1,0:T(8,128)S(1)}, f32[2,64,256]{2,1,0:T(8,128)S(1)}, u32[]{:S(2)}, u32[]{:S(2)}) collective-permute-start(f32[2,64,256]{2,1,0:T(8,128)S(1)} %get-tuple-element.15), channel_id=1, source_target_pairs={{0,32},{32,64},{64,96},{96,128},{128,160},{160,192},{192,224},{224... | collective-permute-start | bytes 393224 | tf_op jit(solution)/shard_map/ppermute | solution.py:97
  5.9 17.3 %collective-permute-start.1 = (f32[2,64,256]{2,1,0:T(8,128)S(1)}, f32[2,64,256]{2,1,0:T(8,128)S(1)}, u32[]{:S(2)}, u32[]{:S(2)}) collective-permute-start(f32[2,64,256]{2,1,0:T(8,128)S(1)} %get-tuple-element.16), channel_id=1, source_target_pairs={{32,0},{64,32},{96,64},{128,96},{160,128},{192,160},{224,192},{256... | collective-permute-start | bytes 393224 | tf_op jit(solution)/shard_map/ppermute | solution.py:97
  24.3 9.1 %copy-start.5 = (s32[1,1,1,2]{3,2,1,0:T(1,128)S(1)}, s32[1,1,1,2]{3,2,1,0:T(1,128)}, u32[]{:S(2)}) copy-start(s32[1,1,1,2]{3,2,1,0:T(1,128)} %param.6) | copy-start | bytes 28
  24.5 17.1 %collective-permute-start.2 = (f32[2,384,64]{2,1,0:T(8,128)S(1)}, f32[2,384,64]{2,1,0:T(8,128)S(1)}, u32[]{:S(2)}, u32[]{:S(2)}) collective-permute-start(f32[2,384,64]{2,1,0:T(8,128)S(1)} %get-tuple-element.9), channel_id=1, source_target_pairs={{0,1},{1,2},{2,3},{3,4},{4,5},{5,6},{6,7},{7,8},{8,9},{9,10},{10,1... | collective-permute-start | bytes 589832 | tf_op jit(solution)/shard_map/ppermute | solution.py:97
  31.5 10.3 %collective-permute-start.3 = (f32[2,384,64]{2,1,0:T(8,128)S(1)}, f32[2,384,64]{2,1,0:T(8,128)S(1)}, u32[]{:S(2)}, u32[]{:S(2)}) collective-permute-start(f32[2,384,64]{2,1,0:T(8,128)S(1)} %get-tuple-element.10), channel_id=1, source_target_pairs={{1,0},{2,1},{3,2},{4,3},{5,4},{6,5},{7,6},{8,7},{9,8},{10,9},{11,1... | collective-permute-start | bytes 589832 | tf_op jit(solution)/shard_map/ppermute | solution.py:97
  43.3 6.4 %copy-start.6 = (f32[136]{0:T(256)S(1)}, f32[136]{0:T(256)}, u32[]{:S(2)}) copy-start(f32[136]{0:T(256)} %pad.82.clone) | copy-start | bytes 1636
  48.5 14.8 %copy-start = (f32[2,3,256,256]{3,2,1,0:T(8,128)S(1)}, f32[2,3,256,256]{3,2,1,0:T(8,128)}, u32[]{:S(2)}) copy-start(f32[2,3,256,256]{3,2,1,0:T(8,128)} %probe_ref.3) | copy-start | bytes 4718596
  50.5 19.7 %collective-permute-start.5 = (f32[2,136,256]{2,1,0:T(8,128)}, f32[2,136,256]{2,1,0:T(8,128)}, u32[]{:S(2)}, u32[]{:S(2)}) collective-permute-start(f32[2,136,256]{2,1,0:T(8,128)} %get-tuple-element.21), channel_id=1, source_target_pairs={{0,32},{32,64},{64,96},{96,128},{128,160},{160,192},{192,224},{224... | collective-permute-start | bytes 835592 | tf_op jit(solution)/shard_map/ppermute | solution.py:97
  54.9 24.7 %copy-start.1 = (f32[2,256,256]{2,1,0:T(8,128)S(1)}, f32[2,256,256]{2,1,0:T(8,128)}, u32[]{:S(2)}) copy-start(f32[2,256,256]{2,1,0:T(8,128)} %shard_map.46) | copy-start | bytes 1572868
  54.9 19.7 %collective-permute-start.4 = (f32[2,136,256]{2,1,0:T(8,128)S(1)}, f32[2,136,256]{2,1,0:T(8,128)S(1)}, u32[]{:S(2)}, u32[]{:S(2)}) collective-permute-start(f32[2,136,256]{2,1,0:T(8,128)S(1)} %get-tuple-element.22), channel_id=1, source_target_pairs={{32,0},{64,32},{96,64},{128,96},{160,128},{192,160},{224,192},{256... | collective-permute-start | bytes 835592 | tf_op jit(solution)/shard_map/ppermute | solution.py:97
  74.6 0.7 copy-start.4
  80.6 4.4 %copy-start.3 = (f32[256,256]{1,0:T(8,128)S(1)}, f32[256,256]{1,0:T(8,128)}, u32[]{:S(2)}) copy-start(f32[256,256]{1,0:T(8,128)} %multiply_reduce_fusion) | copy-start | bytes 786436
  80.6 7.0 %collective-permute-start.6 = (f32[2,384,128]{2,1,0:T(8,128)S(1)}, f32[2,384,128]{2,1,0:T(8,128)}, u32[]{:S(2)}, u32[]{:S(2)}) collective-permute-start(f32[2,384,128]{2,1,0:T(8,128)S(1)} %get-tuple-element.5), channel_id=1, source_target_pairs={{0,1},{1,2},{2,3},{3,4},{4,5},{5,6},{6,7},{7,8},{8,9},{9,10},{10,1... | collective-permute-start | bytes 1179656 | tf_op jit(solution)/shard_map/ppermute | solution.py:97
  83.0 10.4 %collective-permute-start.7 = (f32[2,384,128]{2,1,0:T(8,128)S(1)}, f32[2,384,128]{2,1,0:T(8,128)}, u32[]{:S(2)}, u32[]{:S(2)}) collective-permute-start(f32[2,384,128]{2,1,0:T(8,128)S(1)} %get-tuple-element.6), channel_id=1, source_target_pairs={{1,0},{2,1},{3,2},{4,3},{5,4},{6,5},{7,6},{8,7},{9,8},{10,9},{11,1... | collective-permute-start | bytes 1179656 | tf_op jit(solution)/shard_map/ppermute | solution.py:97
  101.9 14.6 %copy-start.2 = (f32[2,256,256]{2,1,0:T(8,128)S(1)}, f32[2,256,256]{2,1,0:T(8,128)}, u32[]{:S(2)}) copy-start(f32[2,256,256]{2,1,0:T(8,128)} %shard_map.47) | copy-start | bytes 1572868
  104.1 6.9 %collective-permute-start.8 = (f32[2,384,64]{2,1,0:T(8,128)}, f32[2,384,64]{2,1,0:T(8,128)}, u32[]{:S(2)}, u32[]{:S(2)}) collective-permute-start(f32[2,384,64]{2,1,0:T(8,128)} %get-tuple-element.11), channel_id=1, source_target_pairs={{0,1},{1,2},{2,3},{3,4},{4,5},{5,6},{6,7},{7,8},{8,9},{9,10},{10,1... | collective-permute-start | bytes 589832 | tf_op jit(solution)/shard_map/ppermute | solution.py:97
  106.0 10.4 %collective-permute-start.9 = (f32[2,384,64]{2,1,0:T(8,128)S(1)}, f32[2,384,64]{2,1,0:T(8,128)}, u32[]{:S(2)}, u32[]{:S(2)}) collective-permute-start(f32[2,384,64]{2,1,0:T(8,128)S(1)} %get-tuple-element.12), channel_id=1, source_target_pairs={{1,0},{2,1},{3,2},{4,3},{5,4},{6,5},{7,6},{8,7},{9,8},{10,9},{11,1... | collective-permute-start | bytes 589832 | tf_op jit(solution)/shard_map/ppermute | solution.py:97
  118.0 10.7 %collective-permute-start.10 = (f32[2,64,256]{2,1,0:T(8,128)S(1)}, f32[2,64,256]{2,1,0:T(8,128)S(1)}, u32[]{:S(2)}, u32[]{:S(2)}) collective-permute-start(f32[2,64,256]{2,1,0:T(8,128)S(1)} %get-tuple-element.7), channel_id=1, source_target_pairs={{0,32},{32,64},{64,96},{96,128},{128,160},{160,192},{192,224},{224... | collective-permute-start | bytes 393224 | tf_op jit(solution)/shard_map/ppermute | solution.py:97
  119.9 10.5 %collective-permute-start.11 = (f32[2,64,256]{2,1,0:T(8,128)S(1)}, f32[2,64,256]{2,1,0:T(8,128)S(1)}, u32[]{:S(2)}, u32[]{:S(2)}) collective-permute-start(f32[2,64,256]{2,1,0:T(8,128)S(1)} %get-tuple-element.8), channel_id=1, source_target_pairs={{32,0},{64,32},{96,64},{128,96},{160,128},{192,160},{224,192},{256... | collective-permute-start | bytes 393224 | tf_op jit(solution)/shard_map/ppermute | solution.py:97

commit v10 on v7

--- a/solution.py
+++ b/solution.py
@@ -114,21 +114,27 @@
     return total
 
 
-def rows_from_neighbors(change, offset, tile_size, extent):
+def first_rows(object_planes, tag):
+    size = object_planes.shape[1]
+    to_low = jnp.concatenate([object_planes[:, :M], tag], axis=1)
+    to_high = jnp.concatenate([object_planes[:, size - M :], tag], axis=1)
+    from_high = from_neighbor(to_low, "row", 1)
+    from_low = from_neighbor(to_high, "row", -1)
+    rows = jnp.concatenate([from_low[:, :M], object_planes, from_high[:, :M]], axis=1)
+    return rows, from_high[:, M:], from_low[:, M:]
+
+
+def rows_from_neighbors(change, tags, tile_size, extent):
     reach = 2 * M
     size = change.shape[1]
-    tag_rows = lax.broadcasted_iota(jnp.int32, (2, 8, change.shape[2]), 1)
-    tag = jnp.where(tag_rows == 1, offset[1], offset[0]).astype(jnp.float32)
-    to_low = jnp.concatenate([change[:, :reach], tag], axis=1)
-    to_high = jnp.concatenate([change[:, size - reach :], tag], axis=1)
-    from_high = from_neighbor(to_low, "row", 1)
-    from_low = from_neighbor(to_high, "row", -1)
+    high_tag, low_tag = tags
+    from_high = from_neighbor(change[:, :reach], "row", 1)
+    from_low = from_neighbor(change[:, size - reach :], "row", -1)
     place = extent - W
     total = None
-    for got, low_side in ((from_high, False), (from_low, True)):
-        strip = got[:, :reach]
-        row_at = got[0, reach, 0].astype(jnp.int32)
-        col_at = got[0, reach + 1, 0].astype(jnp.int32)
+    for strip, tag, low_side in ((from_high, high_tag, False), (from_low, low_tag, True)):
+        row_at = tag[0, 0, 0].astype(jnp.int32)
+        col_at = tag[0, 1, 0].astype(jnp.int32)
         if low_side:
             top = row_at + M + size - reach - tile_size
             widths = (0, extent)
@@ -166,7 +172,9 @@
     zero = jnp.zeros((), jnp.int32)
     corner = (zero, offsets[0, 0] + M, offsets[0, 1] + M)
     spread = (zero, place - M - offsets[0, 0], place - M - offsets[0, 1])
-    extended = neighbor_sum(object_planes, "row", 1, tile_size, M, 0, extent)
+    tag = offsets[:1].astype(jnp.float32).reshape(1, 2, 1)
+    tag = jnp.pad(jnp.broadcast_to(tag, (2, 2, object_planes.shape[2])), ((0, 0), (0, 6), (0, 0)))
+    extended, high_tag, low_tag = first_rows(object_planes, tag)
     extended = neighbor_sum(extended, "col", 2, tile_size, M, 0, extent)
     for update in range(ITERS):
         window = lax.dynamic_slice(extended, corner, (2, W, W))
@@ -174,7 +182,7 @@
         padded = jnp.pad(change, ((0, 0), (place, place), (place, place)))
         gathered = lax.dynamic_slice(padded, spread, (2, extent, extent))
         if update + 1 < ITERS:
-            total = gathered + rows_from_neighbors(change, offsets[0], tile_size, extent)
+            total = gathered + rows_from_neighbors(change, (high_tag, low_tag), tile_size, extent)
             total = neighbor_sum(total, "col", 2, tile_size, 0, 0, extent)
             mask = inside_mask(extent, tile_size)
             extended = jnp.where(mask[None], extended + total / peak_power, 0.0)

time: 129 us -> 127 us (0.984)
  the two profiles are of different devices: /device:TPU:71 before, /device:TPU:112 now
where the time goes in v10:
time: 127 us
  starting transfers between devices  62.9 us (50%)
  waiting for transfers between devices  26.6 us (21%)
  Pallas kernels  10.5 us (8%)
  local copies, waits for them, and re-layouts  9.11 us (7%)
  other arithmetic  9 us (7%)
  between operations  8.57 us (7%)
    ppermute x12, starting transfers between devices, from_neighbor(): return lax.ppermute(x, axis, pairs)  62.9 us
    ppermute x12, waiting for transfers between devices, from_neighbor(): return lax.ppermute(x, axis, pairs)  26.6 us
    pallas_call x2, Pallas kernels, pattern_gradient(): pl.pallas_call(gradient_kernel, out_shape=jax.ShapeDtypeStruct((2, rows,...  10.5 us
  transfers between devices with their start and end apart: 12, of which 9 were waited for; matrix products, arithmetic and copies ran while one was open for 4% of the time, Pallas kernels for 0%

profile of v10, /device:TPU:112, one launch (start us, length us, event | category | flops | bytes accessed | tf_op | source)
XLA Modules:
  0.0 126.7 jit_solution(16260042417444193449)
XLA Ops:
  0.0 1.0 fusion.23
  1.1 0.7 convert_bitcast_fusion
  1.7 0.1 compare_select_fusion
  1.8 0.1 pad_maximum_fusion.1
  1.9 5.2 %collective-permute-start = (f32[2,72,256]{2,1,0:T(8,128)S(1)}, f32[2,72,256]{2,1,0:T(8,128)S(1)}, u32[]{:S(2)}, u32[]{:S(2)}) collective-permute-start(f32[2,72,256]{2,1,0:T(8,128)S(1)} %get-tuple-element.21), channel_id=1, source_target_pairs={{0,32},{32,64},{64,96},{96,128},{128,160},{160,192},{192,224},{224... | collective-permute-start | bytes 442376 | tf_op jit(solution)/shard_map/ppermute | solution.py:97
  7.1 15.4 %collective-permute-start.1 = (f32[2,72,256]{2,1,0:T(8,128)S(1)}, f32[2,72,256]{2,1,0:T(8,128)S(1)}, u32[]{:S(2)}, u32[]{:S(2)}) collective-permute-start(f32[2,72,256]{2,1,0:T(8,128)S(1)} %get-tuple-element.22), channel_id=1, source_target_pairs={{32,0},{64,32},{96,64},{128,96},{160,128},{192,160},{224,192},{256... | collective-permute-start | bytes 442376 | tf_op jit(solution)/shard_map/ppermute | solution.py:97
  22.5 4.4 %collective-permute-done = f32[2,72,256]{2,1,0:T(8,128)S(1)} collective-permute-done((f32[2,72,256]{2,1,0:T(8,128)S(1)}, f32[2,72,256]{2,1,0:T(8,128)S(1)}, u32[]{:S(2)}, u32[]{:S(2)}) %collective-permute-start) | collective-permute-done | bytes 147488 | tf_op jit(solution)/shard_map/ppermute | solution.py:97
  27.0 0.1 pad_maximum_fusion
  27.0 0.2 fusion.21
  27.2 1.9 %collective-permute-start.2 = (f32[2,384,64]{2,1,0:T(8,128)S(1)}, f32[2,384,64]{2,1,0:T(8,128)S(1)}, u32[]{:S(2)}, u32[]{:S(2)}) collective-permute-start(f32[2,384,64]{2,1,0:T(8,128)S(1)} %get-tuple-element.9), channel_id=1, source_target_pairs={{0,1},{1,2},{2,3},{3,4},{4,5},{5,6},{6,7},{7,8},{8,9},{9,10},{10,1... | collective-permute-start | bytes 589832 | tf_op jit(solution)/shard_map/ppermute | solution.py:97
  29.1 6.6 %collective-permute-start.3 = (f32[2,384,64]{2,1,0:T(8,128)S(1)}, f32[2,384,64]{2,1,0:T(8,128)S(1)}, u32[]{:S(2)}, u32[]{:S(2)}) collective-permute-start(f32[2,384,64]{2,1,0:T(8,128)S(1)} %get-tuple-element.10), channel_id=1, source_target_pairs={{1,0},{2,1},{3,2},{4,3},{5,4},{6,5},{7,6},{8,7},{9,8},{10,9},{11,1... | collective-permute-start | bytes 589832 | tf_op jit(solution)/shard_map/ppermute | solution.py:97
  35.8 0.6 fusion.26
  38.9 1.8 %multiply_convert_fusion = (bf16[256,256]{1,0:T(8,128)(2,1)}, bf16[256,256]{1,0:T(8,128)(2,1)}) fusion(), kind=kLoop, calls=%fused_computation.25 | loop fusion | flops 1245184 | bytes 262144 | tf_op jit(solution)/shard_map/convert_element_type | solution.py:26
  40.7 0.4 collective-permute-done.3
  41.0 0.5 pad_add_fusion
  41.5 1.0 constant_dynamic-slice_fusion.1.window_ref
  42.5 5.3 %shard_map.46 = f32[2,256,256]{2,1,0:T(8,128)} custom-call(f32[2,256,256]{2,1,0:T(8,128)} %constant_dynamic-slice_fusion.1.window_ref, f32[2,3,256,256]{3,2,1,0:T(8,128)} %probe_ref.3, f32[256,256]{1,0:T(8,128)} %bitcast.20, bf16[256,256]{1,0:T(8,128)(2,1)} %get-tuple-element.26.table_re_ref, bf16[256,256]{1,0:T(8,128)(2,1)} %get-tuple-element.25.table_im_ref), custom_call_target="tpu_custom_call" | custom-call | tf_op jit(solution)/shard_map/pallas_call | solution.py:86
  47.8 1.1 fusion.22
  48.9 7.4 %collective-permute-start.4 = (f32[2,128,256]{2,1,0:T(8,128)S(1)}, f32[2,128,256]{2,1,0:T(8,128)S(1)}, u32[]{:S(2)}, u32[]{:S(2)}) collective-permute-start(f32[2,128,256]{2,1,0:T(8,128)S(1)} %get-tuple-element.14), channel_id=1, source_target_pairs={{32,0},{64,32},{96,64},{128,96},{160,128},{192,160},{224,192},{256... | collective-permute-start | bytes 786440 | tf_op jit(solution)/shard_map/ppermute | solution.py:97
  56.3 1.9 %collective-permute-start.5 = (f32[2,128,256]{2,1,0:T(8,128)S(1)}, f32[2,128,256]{2,1,0:T(8,128)S(1)}, u32[]{:S(2)}, u32[]{:S(2)}) collective-permute-start(f32[2,128,256]{2,1,0:T(8,128)S(1)} %get-tuple-element.13), channel_id=1, source_target_pairs={{0,32},{32,64},{64,96},{96,128},{128,160},{160,192},{192,224},{224... | collective-permute-start | bytes 786440 | tf_op jit(solution)/shard_map/ppermute | solution.py:97
  60.7 0.5 fusion.25
  61.9 0.6 fusion.24
  64.4 11.2 %collective-permute-done.5 = f32[2,128,256]{2,1,0:T(8,128)S(1)} collective-permute-done((f32[2,128,256]{2,1,0:T(8,128)S(1)}, f32[2,128,256]{2,1,0:T(8,128)S(1)}, u32[]{:S(2)}, u32[]{:S(2)}) %collective-permute-start.5) | collective-permute-done | bytes 262176 | tf_op jit(solution)/shard_map/ppermute | solution.py:97
  75.6 1.0 fusion
  76.6 0.0 copy-start
  76.6 0.8 fusion.19
  77.4 1.9 %collective-permute-start.6 = (f32[2,384,128]{2,1,0:T(8,128)}, f32[2,384,128]{2,1,0:T(8,128)S(1)}, u32[]{:S(2)}, u32[]{:S(2)}) collective-permute-start(f32[2,384,128]{2,1,0:T(8,128)} %get-tuple-element.5), channel_id=1, source_target_pairs={{0,1},{1,2},{2,3},{3,4},{4,5},{5,6},{6,7},{7,8},{8,9},{9,10},{10,1... | collective-permute-start | bytes 1179656 | tf_op jit(solution)/shard_map/ppermute | solution.py:97
  79.3 5.8 %collective-permute-start.7 = (f32[2,384,128]{2,1,0:T(8,128)S(1)}, f32[2,384,128]{2,1,0:T(8,128)}, u32[]{:S(2)}, u32[]{:S(2)}) collective-permute-start(f32[2,384,128]{2,1,0:T(8,128)S(1)} %get-tuple-element.6), channel_id=1, source_target_pairs={{1,0},{2,1},{3,2},{4,3},{5,4},{6,5},{7,6},{8,7},{9,8},{10,9},{11,1... | collective-permute-start | bytes 1179656 | tf_op jit(solution)/shard_map/ppermute | solution.py:97
  85.1 0.1 multiply_reduce_fusion
  85.2 0.7 reduce_max.9
  86.7 0.1 broadcast_and_fusion
  86.8 2.0 %collective-permute-done.6 = f32[2,384,128]{2,1,0:T(8,128)S(1)} collective-permute-done((f32[2,384,128]{2,1,0:T(8,128)}, f32[2,384,128]{2,1,0:T(8,128)S(1)}, u32[]{:S(2)}, u32[]{:S(2)}) %collective-permute-start.6) | collective-permute-done | bytes 393248 | tf_op jit(solution)/shard_map/ppermute | solution.py:97
  88.8 0.7 copy-done.5
  89.6 0.8 collective-permute-done.7
  90.4 2.5 %add_select_fusion = f32[2,384,384]{2,1,0:T(8,128)S(1)} fusion(f32[2,384,128]{2,1,0:T(8,128)} %collective-permute-done.7, f32[2,384,128]{2,1,0:T(8,128)} %copy-done.5, f32[]{:T(128)S(6)} %add.193, pred[384,384]{1,0:T(8,128)(4,1)S(1)} %broadcast_and_fusion, s32[]{:T(128)S(6)} %select_n.52, s32[]{:T(128)S(6)} %select_n.53, f32[2,128,256]{2,1,0:T(8,128)} %copy-done.4, ...), kind=kLoop, calls=%fused_computation.9 | loop fusion | flops 2654208 | bytes 4341788 | tf_op jit(solution)/shard_map/jit(_where)/select_n | solution.py:188
  92.9 1.0 constant_dynamic-slice_fusion.window_ref
  93.9 5.3 %shard_map.47 = f32[2,256,256]{2,1,0:T(8,128)} custom-call(f32[2,256,256]{2,1,0:T(8,128)} %constant_dynamic-slice_fusion.window_ref, f32[2,3,256,256]{3,2,1,0:T(8,128)} %probe_ref.3, f32[256,256]{1,0:T(8,128)} %bitcast.21, bf16[256,256]{1,0:T(8,128)(2,1)} %get-tuple-element.26.table_re_ref, bf16[256,256]{1,0:T(8,128)(2,1)} %get-tuple-element.25.table_im_ref), custom_call_target="tpu_custom_call" | custom-call | tf_op jit(solution)/shard_map/pallas_call | solution.py:86
  99.1 1.4 %pad_dynamic-slice_fusion.1 = (f32[2,384,64]{2,1,0:T(8,128)S(1)}, f32[2,384,64]{2,1,0:T(8,128)S(1)}) fusion(s32[]{:T(128)S(6)} %select_n.48, s32[]{:T(128)S(6)} %add.200, f32[2,256,256]{2,1,0:T(8,128)} %shard_map.47, s32[]{:T(128)S(6)} %select_n.49), kind=kLoop, calls=%fused_computation.1 | loop fusion | bytes 917516 | tf_op jit(solution)/shard_map/slice | solution.py:107
  100.6 1.9 %collective-permute-start.8 = (f32[2,384,64]{2,1,0:T(8,128)S(1)}, f32[2,384,64]{2,1,0:T(8,128)S(1)}, u32[]{:S(2)}, u32[]{:S(2)}) collective-permute-start(f32[2,384,64]{2,1,0:T(8,128)S(1)} %get-tuple-element.11), channel_id=1, source_target_pairs={{0,1},{1,2},{2,3},{3,4},{4,5},{5,6},{6,7},{7,8},{8,9},{9,10},{10,1... | collective-permute-start | bytes 589832 | tf_op jit(solution)/shard_map/ppermute | solution.py:97
  102.5 6.1 %collective-permute-start.9 = (f32[2,384,64]{2,1,0:T(8,128)S(1)}, f32[2,384,64]{2,1,0:T(8,128)S(1)}, u32[]{:S(2)}, u32[]{:S(2)}) collective-permute-start(f32[2,384,64]{2,1,0:T(8,128)S(1)} %get-tuple-element.12), channel_id=1, source_target_pairs={{1,0},{2,1},{3,2},{4,3},{5,4},{6,5},{7,6},{8,7},{9,8},{10,9},{11,1... | collective-permute-start | bytes 589832 | tf_op jit(solution)/shard_map/ppermute | solution.py:97
  108.6 3.5 %collective-permute-done.8 = f32[2,384,64]{2,1,0:T(8,128)S(1)} collective-permute-done((f32[2,384,64]{2,1,0:T(8,128)S(1)}, f32[2,384,64]{2,1,0:T(8,128)S(1)}, u32[]{:S(2)}, u32[]{:S(2)}) %collective-permute-start.8) | collective-permute-done | bytes 196640 | tf_op jit(solution)/shard_map/ppermute | solution.py:97
  112.1 1.8 %collective-permute-done.9 = f32[2,384,64]{2,1,0:T(8,128)S(1)} collective-permute-done((f32[2,384,64]{2,1,0:T(8,128)S(1)}, f32[2,384,64]{2,1,0:T(8,128)S(1)}, u32[]{:S(2)}, u32[]{:S(2)}) %collective-permute-start.9) | collective-permute-done | bytes 196640 | tf_op jit(solution)/shard_map/ppermute | solution.py:97
  113.9 0.4 fusion.3
  114.3 1.9 %collective-permute-start.10 = (f32[2,64,256]{2,1,0:T(8,128)S(1)}, f32[2,64,256]{2,1,0:T(8,128)S(1)}, u32[]{:S(2)}, u32[]{:S(2)}) collective-permute-start(f32[2,64,256]{2,1,0:T(8,128)S(1)} %get-tuple-element.7), channel_id=1, source_target_pairs={{0,32},{32,64},{64,96},{96,128},{128,160},{160,192},{192,224},{224... | collective-permute-start | bytes 393224 | tf_op jit(solution)/shard_map/ppermute | solution.py:97
  116.3 6.9 %collective-permute-start.11 = (f32[2,64,256]{2,1,0:T(8,128)S(1)}, f32[2,64,256]{2,1,0:T(8,128)S(1)}, u32[]{:S(2)}, u32[]{:S(2)}) collective-permute-start(f32[2,64,256]{2,1,0:T(8,128)S(1)} %get-tuple-element.8), channel_id=1, source_target_pairs={{32,0},{64,32},{96,64},{128,96},{160,128},{192,160},{224,192},{256... | collective-permute-start | bytes 393224 | tf_op jit(solution)/shard_map/ppermute | solution.py:97
  123.2 1.0 collective-permute-done.10
  124.2 1.5 %collective-permute-done.11 = f32[2,64,256]{2,1,0:T(8,128)S(1)} collective-permute-done((f32[2,64,256]{2,1,0:T(8,128)S(1)}, f32[2,64,256]{2,1,0:T(8,128)S(1)}, u32[]{:S(2)}, u32[]{:S(2)}) %collective-permute-start.11) | collective-permute-done | bytes 131104 | tf_op jit(solution)/shard_map/ppermute | solution.py:97
  125.7 1.0 fusion.6
  (19 shorter events, 0.1 us)
Async XLA Ops:
  0.0 26.9 %copy-start.3 = (f32[2,256,256]{2,1,0:T(8,128)S(1)}, f32[2,256,256]{2,1,0:T(8,128)}, u32[]{:S(2)}) copy-start(f32[2,256,256]{2,1,0:T(8,128)} %param.4) | copy-start | bytes 1572868
  1.9 25.0 %collective-permute-start = (f32[2,72,256]{2,1,0:T(8,128)S(1)}, f32[2,72,256]{2,1,0:T(8,128)S(1)}, u32[]{:S(2)}, u32[]{:S(2)}) collective-permute-start(f32[2,72,256]{2,1,0:T(8,128)S(1)} %get-tuple-element.21), channel_id=1, source_target_pairs={{0,32},{32,64},{64,96},{96,128},{128,160},{160,192},{192,224},{224... | collective-permute-start | bytes 442376 | tf_op jit(solution)/shard_map/ppermute | solution.py:97
  7.1 19.8 %collective-permute-start.1 = (f32[2,72,256]{2,1,0:T(8,128)S(1)}, f32[2,72,256]{2,1,0:T(8,128)S(1)}, u32[]{:S(2)}, u32[]{:S(2)}) collective-permute-start(f32[2,72,256]{2,1,0:T(8,128)S(1)} %get-tuple-element.22), channel_id=1, source_target_pairs={{32,0},{64,32},{96,64},{128,96},{160,128},{192,160},{224,192},{256... | collective-permute-start | bytes 442376 | tf_op jit(solution)/shard_map/ppermute | solution.py:97
  27.0 8.8 %copy-start.6 = (s32[1,1,1,2]{3,2,1,0:T(1,128)S(1)}, s32[1,1,1,2]{3,2,1,0:T(1,128)}, u32[]{:S(2)}) copy-start(s32[1,1,1,2]{3,2,1,0:T(1,128)} %param.6) | copy-start | bytes 28
  27.2 13.5 %collective-permute-start.2 = (f32[2,384,64]{2,1,0:T(8,128)S(1)}, f32[2,384,64]{2,1,0:T(8,128)S(1)}, u32[]{:S(2)}, u32[]{:S(2)}) collective-permute-start(f32[2,384,64]{2,1,0:T(8,128)S(1)} %get-tuple-element.9), channel_id=1, source_target_pairs={{0,1},{1,2},{2,3},{3,4},{4,5},{5,6},{6,7},{7,8},{8,9},{9,10},{10,1... | collective-permute-start | bytes 589832 | tf_op jit(solution)/shard_map/ppermute | solution.py:97
  29.1 11.9 %collective-permute-start.3 = (f32[2,384,64]{2,1,0:T(8,128)S(1)}, f32[2,384,64]{2,1,0:T(8,128)S(1)}, u32[]{:S(2)}, u32[]{:S(2)}) collective-permute-start(f32[2,384,64]{2,1,0:T(8,128)S(1)} %get-tuple-element.10), channel_id=1, source_target_pairs={{1,0},{2,1},{3,2},{4,3},{5,4},{6,5},{7,6},{8,7},{9,8},{10,9},{11,1... | collective-permute-start | bytes 589832 | tf_op jit(solution)/shard_map/ppermute | solution.py:97
  47.8 27.8 %copy-start.1 = (f32[2,256,256]{2,1,0:T(8,128)S(1)}, f32[2,256,256]{2,1,0:T(8,128)}, u32[]{:S(2)}) copy-start(f32[2,256,256]{2,1,0:T(8,128)} %shard_map.46) | copy-start | bytes 1572868
  48.9 15.5 %collective-permute-start.4 = (f32[2,128,256]{2,1,0:T(8,128)S(1)}, f32[2,128,256]{2,1,0:T(8,128)S(1)}, u32[]{:S(2)}, u32[]{:S(2)}) collective-permute-start(f32[2,128,256]{2,1,0:T(8,128)S(1)} %get-tuple-element.14), channel_id=1, source_target_pairs={{32,0},{64,32},{96,64},{128,96},{160,128},{192,160},{224,192},{256... | collective-permute-start | bytes 786440 | tf_op jit(solution)/shard_map/ppermute | solution.py:97
  56.3 19.3 %collective-permute-start.5 = (f32[2,128,256]{2,1,0:T(8,128)S(1)}, f32[2,128,256]{2,1,0:T(8,128)S(1)}, u32[]{:S(2)}, u32[]{:S(2)}) collective-permute-start(f32[2,128,256]{2,1,0:T(8,128)S(1)} %get-tuple-element.13), channel_id=1, source_target_pairs={{0,32},{32,64},{64,96},{96,128},{128,160},{160,192},{192,224},{224... | collective-permute-start | bytes 786440 | tf_op jit(solution)/shard_map/ppermute | solution.py:97
  75.6 1.8 %copy-start.4 = (f32[2,128,256]{2,1,0:T(8,128)}, f32[2,128,256]{2,1,0:T(8,128)S(1)}, u32[]{:S(2)}) copy-start(f32[2,128,256]{2,1,0:T(8,128)S(1)} %collective-permute-done.5) | copy-start | bytes 786436
  76.6 8.5 %copy-start = (f32[2,3,256,256]{3,2,1,0:T(8,128)S(1)}, f32[2,3,256,256]{3,2,1,0:T(8,128)}, u32[]{:S(2)}) copy-start(f32[2,3,256,256]{3,2,1,0:T(8,128)} %probe_ref.3) | copy-start | bytes 4718596
  77.4 11.4 %collective-permute-start.6 = (f32[2,384,128]{2,1,0:T(8,128)}, f32[2,384,128]{2,1,0:T(8,128)S(1)}, u32[]{:S(2)}, u32[]{:S(2)}) collective-permute-start(f32[2,384,128]{2,1,0:T(8,128)} %get-tuple-element.5), channel_id=1, source_target_pairs={{0,1},{1,2},{2,3},{3,4},{4,5},{5,6},{6,7},{7,8},{8,9},{9,10},{10,1... | collective-permute-start | bytes 1179656 | tf_op jit(solution)/shard_map/ppermute | solution.py:97
  79.3 11.0 %collective-permute-start.7 = (f32[2,384,128]{2,1,0:T(8,128)S(1)}, f32[2,384,128]{2,1,0:T(8,128)}, u32[]{:S(2)}, u32[]{:S(2)}) collective-permute-start(f32[2,384,128]{2,1,0:T(8,128)S(1)} %get-tuple-element.6), channel_id=1, source_target_pairs={{1,0},{2,1},{3,2},{4,3},{5,4},{6,5},{7,6},{8,7},{9,8},{10,9},{11,1... | collective-permute-start | bytes 1179656 | tf_op jit(solution)/shard_map/ppermute | solution.py:97
  88.8 0.7 copy-start.5
  99.1 14.8 %copy-start.2 = (f32[2,256,256]{2,1,0:T(8,128)S(1)}, f32[2,256,256]{2,1,0:T(8,128)}, u32[]{:S(2)}) copy-start(f32[2,256,256]{2,1,0:T(8,128)} %shard_map.47) | copy-start | bytes 1572868
  100.6 11.5 %collective-permute-start.8 = (f32[2,384,64]{2,1,0:T(8,128)S(1)}, f32[2,384,64]{2,1,0:T(8,128)S(1)}, u32[]{:S(2)}, u32[]{:S(2)}) collective-permute-start(f32[2,384,64]{2,1,0:T(8,128)S(1)} %get-tuple-element.11), channel_id=1, source_target_pairs={{0,1},{1,2},{2,3},{3,4},{4,5},{5,6},{6,7},{7,8},{8,9},{9,10},{10,1... | collective-permute-start | bytes 589832 | tf_op jit(solution)/shard_map/ppermute | solution.py:97
  102.5 11.4 %collective-permute-start.9 = (f32[2,384,64]{2,1,0:T(8,128)S(1)}, f32[2,384,64]{2,1,0:T(8,128)S(1)}, u32[]{:S(2)}, u32[]{:S(2)}) collective-permute-start(f32[2,384,64]{2,1,0:T(8,128)S(1)} %get-tuple-element.12), channel_id=1, source_target_pairs={{1,0},{2,1},{3,2},{4,3},{5,4},{6,5},{7,6},{8,7},{9,8},{10,9},{11,1... | collective-permute-start | bytes 589832 | tf_op jit(solution)/shard_map/ppermute | solution.py:97
  114.3 9.9 %collective-permute-start.10 = (f32[2,64,256]{2,1,0:T(8,128)S(1)}, f32[2,64,256]{2,1,0:T(8,128)S(1)}, u32[]{:S(2)}, u32[]{:S(2)}) collective-permute-start(f32[2,64,256]{2,1,0:T(8,128)S(1)} %get-tuple-element.7), channel_id=1, source_target_pairs={{0,32},{32,64},{64,96},{96,128},{128,160},{160,192},{192,224},{224... | collective-permute-start | bytes 393224 | tf_op jit(solution)/shard_map/ppermute | solution.py:97
  116.3 9.4 %collective-permute-start.11 = (f32[2,64,256]{2,1,0:T(8,128)S(1)}, f32[2,64,256]{2,1,0:T(8,128)S(1)}, u32[]{:S(2)}, u32[]{:S(2)}) collective-permute-start(f32[2,64,256]{2,1,0:T(8,128)S(1)} %get-tuple-element.8), channel_id=1, source_target_pairs={{32,0},{64,32},{96,64},{128,96},{160,128},{192,160},{224,192},{256... | collective-permute-start | bytes 393224 | tf_op jit(solution)/shard_map/ppermute | solution.py:97

commit v11 on v6

--- a/solution.py
+++ b/solution.py
@@ -181,8 +181,8 @@
             mask = inside_mask(extent, tile_size)
             extended = jnp.where(mask[None], extended + total / peak_power, 0.0)
         else:
-            total = neighbor_sum(gathered, "col", 2, tile_size, 0, M, tile_size)
-            total = neighbor_sum(total, "row", 1, tile_size, 0, M, tile_size)
+            total = neighbor_sum(gathered, "row", 1, tile_size, 0, M, tile_size)
+            total = neighbor_sum(total, "col", 2, tile_size, 0, M, tile_size)
             current = extended[:, M : M + tile_size, M : M + tile_size] + total / peak_power
     return current
 

time: 126 us -> 128 us (1.016)
  waiting for transfers between devices: 25.9 us -> 27.6 us
    ppermute x12, waiting for transfers between devices: 25.9 us -> 27.6 us  [from_neighbor(): return lax.ppermute(x, axis, pairs)]
where the time goes in v11:
time: 128 us; the launch traced here: 127 us
  starting transfers between devices  55.2 us (43%)
  waiting for transfers between devices  27.6 us (22%)
  local copies, waits for them, and re-layouts  15.6 us (12%)
  Pallas kernels  10.5 us (8%)
  other arithmetic  9.5 us (7%)
  between operations  8.57 us (7%)
    ppermute x12, starting transfers between devices, from_neighbor(): return lax.ppermute(x, axis, pairs)  55.2 us
    ppermute x12, waiting for transfers between devices, from_neighbor(): return lax.ppermute(x, axis, pairs)  27.6 us
    pallas_call x2, Pallas kernels, pattern_gradient(): pl.pallas_call(gradient_kernel, out_shape=jax.ShapeDtypeStruct((2, rows,...  10.5 us
    another operation x1, local copies, waits for them, and re-layouts, rows_from_neighbors(): jnp.stack([offset[0], offset[1]] + [offset[0]] * 6).astype(jnp.float32)  5.19 us
    slice x5, local copies, waits for them, and re-layouts, neighbor_sum(): piece = lax.slice_in_dim(frame, low - shift, high - shift, axis=dim)  3.12 us
    select_n x1, other arithmetic, on_device(): extended = jnp.where(mask[None], extended + total / peak_power, 0.0)  2.58 us
  transfers between devices with their start and end apart: 12, of which 9 were waited for; matrix products, arithmetic and copies ran while one was open for 8% of the time, Pallas kernels for 0%

profile of v11, /device:TPU:87, one launch (start us, length us, event | category | flops | bytes accessed | tf_op | source)
XLA Modules:
  0.0 126.9 jit_solution(17499780439311201590)
XLA Ops:
  0.0 1.0 fusion.23
  1.0 4.9 %collective-permute-start = (f32[2,64,256]{2,1,0:T(8,128)S(1)}, f32[2,64,256]{2,1,0:T(8,128)S(1)}, u32[]{:S(2)}, u32[]{:S(2)}) collective-permute-start(f32[2,64,256]{2,1,0:T(8,128)S(1)} %get-tuple-element.15), channel_id=1, source_target_pairs={{0,32},{32,64},{64,96},{96,128},{128,160},{160,192},{192,224},{224... | collective-permute-start | bytes 393224 | tf_op jit(solution)/shard_map/ppermute | solution.py:97
  5.9 14.5 %collective-permute-start.1 = (f32[2,64,256]{2,1,0:T(8,128)S(1)}, f32[2,64,256]{2,1,0:T(8,128)S(1)}, u32[]{:S(2)}, u32[]{:S(2)}) collective-permute-start(f32[2,64,256]{2,1,0:T(8,128)S(1)} %get-tuple-element.16), channel_id=1, source_target_pairs={{32,0},{64,32},{96,64},{128,96},{160,128},{192,160},{224,192},{256... | collective-permute-start | bytes 393224 | tf_op jit(solution)/shard_map/ppermute | solution.py:97
  20.4 1.3 %fusion.27 = (s32[1,1]{1,0:T(1,128)}, s32[1,1]{1,0:T(1,128)}) fusion(s32[1,2]{1,0:T(1,128)} %bitcast.22), kind=kLoop, calls=%fused_computation.50 | loop fusion | bytes 16 | tf_op jit(solution)/shard_map/slice | solution.py:169
  24.3 0.5 collective-permute-done
  24.8 1.1 pad_add_fusion.1
  25.9 0.2 fusion.21
  26.0 4.7 %collective-permute-start.2 = (f32[2,384,64]{2,1,0:T(8,128)S(1)}, f32[2,384,64]{2,1,0:T(8,128)S(1)}, u32[]{:S(2)}, u32[]{:S(2)}) collective-permute-start(f32[2,384,64]{2,1,0:T(8,128)S(1)} %get-tuple-element.9), channel_id=1, source_target_pairs={{0,1},{1,2},{2,3},{3,4},{4,5},{5,6},{6,7},{7,8},{8,9},{9,10},{10,1... | collective-permute-start | bytes 589832 | tf_op jit(solution)/shard_map/ppermute | solution.py:97
  30.8 1.9 %collective-permute-start.3 = (f32[2,384,64]{2,1,0:T(8,128)S(1)}, f32[2,384,64]{2,1,0:T(8,128)S(1)}, u32[]{:S(2)}, u32[]{:S(2)}) collective-permute-start(f32[2,384,64]{2,1,0:T(8,128)S(1)} %get-tuple-element.10), channel_id=1, source_target_pairs={{1,0},{2,1},{3,2},{4,3},{5,4},{6,5},{7,6},{8,7},{9,8},{10,9},{11,1... | collective-permute-start | bytes 589832 | tf_op jit(solution)/shard_map/ppermute | solution.py:97
  32.7 0.7 fusion.26
  33.4 5.2 %stack.9 = s32[8]{0:T(128)S(1)} concatenate(s32[1]{0:T(128)} %bitcast.10, s32[1]{0:T(128)} %bitcast.11, s32[1]{0:T(128)} %bitcast.10, s32[1]{0:T(128)} %bitcast.10, s32[1]{0:T(128)} %bitcast.10, s32[1]{0:T(128)} %bitcast.10, s32[1]{0:T(128)} %bitcast.10, s32[1]{0:T(128)} %bitcast.10), dimensions={0} | concatenate | bytes 64 | tf_op jit(solution)/shard_map/stack | solution.py:121
  38.6 1.8 %multiply_convert_fusion = (bf16[256,256]{1,0:T(8,128)(2,1)}, bf16[256,256]{1,0:T(8,128)(2,1)}) fusion(), kind=kLoop, calls=%fused_computation.27 | loop fusion | flops 1245184 | bytes 262144 | tf_op jit(solution)/shard_map/convert_element_type | solution.py:26
  40.3 0.7 collective-permute-done.3
  41.1 0.5 pad_add_fusion
  41.6 0.3 copy-done.3
  41.9 1.0 constant_dynamic-slice_fusion.1.window_ref
  42.9 5.2 %shard_map.46 = f32[2,256,256]{2,1,0:T(8,128)} custom-call(f32[2,256,256]{2,1,0:T(8,128)} %constant_dynamic-slice_fusion.1.window_ref, f32[2,3,256,256]{3,2,1,0:T(8,128)} %probe_ref.3, f32[256,256]{1,0:T(8,128)} %bitcast.20, bf16[256,256]{1,0:T(8,128)(2,1)} %get-tuple-element.28.table_re_ref, bf16[256,256]{1,0:T(8,128)(2,1)} %get-tuple-element.27.table_im_ref), custom_call_target="tpu_custom_call" | custom-call | tf_op jit(solution)/shard_map/pallas_call | solution.py:86
  48.1 1.1 fusion.22
  49.3 2.1 %collective-permute-start.5 = (f32[2,136,256]{2,1,0:T(8,128)S(1)}, f32[2,136,256]{2,1,0:T(8,128)S(1)}, u32[]{:S(2)}, u32[]{:S(2)}) collective-permute-start(f32[2,136,256]{2,1,0:T(8,128)S(1)} %get-tuple-element.21), channel_id=1, source_target_pairs={{0,32},{32,64},{64,96},{96,128},{128,160},{160,192},{192,224},{224... | collective-permute-start | bytes 835592 | tf_op jit(solution)/shard_map/ppermute | solution.py:97
  51.3 7.6 %collective-permute-start.4 = (f32[2,136,256]{2,1,0:T(8,128)S(1)}, f32[2,136,256]{2,1,0:T(8,128)S(1)}, u32[]{:S(2)}, u32[]{:S(2)}) collective-permute-start(f32[2,136,256]{2,1,0:T(8,128)S(1)} %get-tuple-element.22), channel_id=1, source_target_pairs={{32,0},{64,32},{96,64},{128,96},{160,128},{192,160},{224,192},{256... | collective-permute-start | bytes 835592 | tf_op jit(solution)/shard_map/ppermute | solution.py:97
  61.5 6.1 %collective-permute-done.5 = f32[2,136,256]{2,1,0:T(8,128)S(1)} collective-permute-done((f32[2,136,256]{2,1,0:T(8,128)S(1)}, f32[2,136,256]{2,1,0:T(8,128)S(1)}, u32[]{:S(2)}, u32[]{:S(2)}) %collective-permute-start.5) | collective-permute-done | bytes 278560 | tf_op jit(solution)/shard_map/ppermute | solution.py:97
  67.6 0.6 fusion.24
  68.9 0.5 fusion.25
  71.4 1.0 fusion
  72.4 0.8 fusion.19
  73.2 2.9 %collective-permute-start.6 = (f32[2,384,128]{2,1,0:T(8,128)}, f32[2,384,128]{2,1,0:T(8,128)S(1)}, u32[]{:S(2)}, u32[]{:S(2)}) collective-permute-start(f32[2,384,128]{2,1,0:T(8,128)} %get-tuple-element.5), channel_id=1, source_target_pairs={{0,1},{1,2},{2,3},{3,4},{4,5},{5,6},{6,7},{7,8},{8,9},{9,10},{10,1... | collective-permute-start | bytes 1179656 | tf_op jit(solution)/shard_map/ppermute | solution.py:97
  76.1 1.9 %collective-permute-start.7 = (f32[2,384,128]{2,1,0:T(8,128)S(1)}, f32[2,384,128]{2,1,0:T(8,128)}, u32[]{:S(2)}, u32[]{:S(2)}) collective-permute-start(f32[2,384,128]{2,1,0:T(8,128)S(1)} %get-tuple-element.6), channel_id=1, source_target_pairs={{1,0},{2,1},{3,2},{4,3},{5,4},{6,5},{7,6},{8,7},{9,8},{10,9},{11,1... | collective-permute-start | bytes 1179656 | tf_op jit(solution)/shard_map/ppermute | solution.py:97
  78.1 0.1 multiply_reduce_fusion
  78.2 0.7 reduce_max.9
  79.5 0.1 broadcast_and_fusion
  79.7 1.5 %collective-permute-done.6 = f32[2,384,128]{2,1,0:T(8,128)S(1)} collective-permute-done((f32[2,384,128]{2,1,0:T(8,128)}, f32[2,384,128]{2,1,0:T(8,128)S(1)}, u32[]{:S(2)}, u32[]{:S(2)}) %collective-permute-start.6) | collective-permute-done | bytes 393248 | tf_op jit(solution)/shard_map/ppermute | solution.py:97
  81.1 0.7 copy-done.4
  81.9 4.7 %collective-permute-done.7 = f32[2,384,128]{2,1,0:T(8,128)} collective-permute-done((f32[2,384,128]{2,1,0:T(8,128)S(1)}, f32[2,384,128]{2,1,0:T(8,128)}, u32[]{:S(2)}, u32[]{:S(2)}) %collective-permute-start.7) | collective-permute-done | bytes 393248 | tf_op jit(solution)/shard_map/ppermute | solution.py:97
  86.5 2.6 %add_select_fusion = f32[2,384,384]{2,1,0:T(8,128)S(1)} fusion(f32[2,384,128]{2,1,0:T(8,128)} %collective-permute-done.7, f32[2,384,128]{2,1,0:T(8,128)} %copy-done.4, f32[]{:T(128)S(6)} %add.205, pred[384,384]{1,0:T(8,128)(4,1)S(1)} %broadcast_and_fusion, s32[]{:T(128)S(6)} %select_n.52, s32[]{:T(128)S(6)} %select_n.53, f32[2,128,256]{2,1,0:T(8,128)S(1)} %slice.112, ...), kind=kLoop, calls=%fused_computation.9 | loop fusion | flops 2654208 | bytes 4341788 | tf_op jit(solution)/shard_map/jit(_where)/select_n | solution.py:182
  89.1 1.0 constant_dynamic-slice_fusion.window_ref
  90.1 5.3 %shard_map.47 = f32[2,256,256]{2,1,0:T(8,128)} custom-call(f32[2,256,256]{2,1,0:T(8,128)} %constant_dynamic-slice_fusion.window_ref, f32[2,3,256,256]{3,2,1,0:T(8,128)} %probe_ref.3, f32[256,256]{1,0:T(8,128)} %bitcast.21, bf16[256,256]{1,0:T(8,128)(2,1)} %get-tuple-element.28.table_re_ref, bf16[256,256]{1,0:T(8,128)(2,1)} %get-tuple-element.27.table_im_ref), custom_call_target="tpu_custom_call" | custom-call | tf_op jit(solution)/shard_map/pallas_call | solution.py:86
  95.4 1.0 pad_dynamic-slice_fusion.1
  96.4 1.9 %collective-permute-start.8 = (f32[2,64,384]{2,1,0:T(8,128)S(1)}, f32[2,64,384]{2,1,0:T(8,128)S(1)}, u32[]{:S(2)}, u32[]{:S(2)}) collective-permute-start(f32[2,64,384]{2,1,0:T(8,128)S(1)} %get-tuple-element.11), channel_id=1, source_target_pairs={{0,32},{32,64},{64,96},{96,128},{128,160},{160,192},{192,224},{224... | collective-permute-start | bytes 589832 | tf_op jit(solution)/shard_map/ppermute | solution.py:97
  98.4 7.6 %collective-permute-start.9 = (f32[2,64,384]{2,1,0:T(8,128)S(1)}, f32[2,64,384]{2,1,0:T(8,128)S(1)}, u32[]{:S(2)}, u32[]{:S(2)}) collective-permute-start(f32[2,64,384]{2,1,0:T(8,128)S(1)} %get-tuple-element.12), channel_id=1, source_target_pairs={{32,0},{64,32},{96,64},{128,96},{160,128},{192,160},{224,192},{256... | collective-permute-start | bytes 589832 | tf_op jit(solution)/shard_map/ppermute | solution.py:97
  106.0 3.6 %collective-permute-done.8 = f32[2,64,384]{2,1,0:T(8,128)S(1)} collective-permute-done((f32[2,64,384]{2,1,0:T(8,128)S(1)}, f32[2,64,384]{2,1,0:T(8,128)S(1)}, u32[]{:S(2)}, u32[]{:S(2)}) %collective-permute-start.8) | collective-permute-done | bytes 196640 | tf_op jit(solution)/shard_map/ppermute | solution.py:97
  109.5 3.6 %collective-permute-done.9 = f32[2,64,384]{2,1,0:T(8,128)S(1)} collective-permute-done((f32[2,64,384]{2,1,0:T(8,128)S(1)}, f32[2,64,384]{2,1,0:T(8,128)S(1)}, u32[]{:S(2)}, u32[]{:S(2)}) %collective-permute-start.9) | collective-permute-done | bytes 196640 | tf_op jit(solution)/shard_map/ppermute | solution.py:97
  113.1 0.3 fusion.3
  113.5 0.1 fusion.20
  113.6 3.2 %collective-permute-start.10 = (f32[2,256,64]{2,1,0:T(8,128)S(1)}, f32[2,256,64]{2,1,0:T(8,128)S(1)}, u32[]{:S(2)}, u32[]{:S(2)}) collective-permute-start(f32[2,256,64]{2,1,0:T(8,128)S(1)} %get-tuple-element.7), channel_id=1, source_target_pairs={{0,1},{1,2},{2,3},{3,4},{4,5},{5,6},{6,7},{7,8},{8,9},{9,10},{10,1... | collective-permute-start | bytes 393224 | tf_op jit(solution)/shard_map/ppermute | solution.py:97
  116.8 1.9 %collective-permute-start.11 = (f32[2,256,64]{2,1,0:T(8,128)S(1)}, f32[2,256,64]{2,1,0:T(8,128)S(1)}, u32[]{:S(2)}, u32[]{:S(2)}) collective-permute-start(f32[2,256,64]{2,1,0:T(8,128)S(1)} %get-tuple-element.8), channel_id=1, source_target_pairs={{1,0},{2,1},{3,2},{4,3},{5,4},{6,5},{7,6},{8,7},{9,8},{10,9},{11,1... | collective-permute-start | bytes 393224 | tf_op jit(solution)/shard_map/ppermute | solution.py:97
  118.7 1.4 %collective-permute-done.10 = f32[2,256,64]{2,1,0:T(8,128)S(1)} collective-permute-done((f32[2,256,64]{2,1,0:T(8,128)S(1)}, f32[2,256,64]{2,1,0:T(8,128)S(1)}, u32[]{:S(2)}, u32[]{:S(2)}) %collective-permute-start.10) | collective-permute-done | bytes 131104 | tf_op jit(solution)/shard_map/ppermute | solution.py:97
  120.1 5.6 %collective-permute-done.11 = f32[2,256,64]{2,1,0:T(8,128)S(1)} collective-permute-done((f32[2,256,64]{2,1,0:T(8,128)S(1)}, f32[2,256,64]{2,1,0:T(8,128)S(1)}, u32[]{:S(2)}, u32[]{:S(2)}) %collective-permute-start.11) | collective-permute-done | bytes 131104 | tf_op jit(solution)/shard_map/ppermute | solution.py:97
  125.7 1.2 fusion.6
  (19 shorter events, 0.2 us)
Async XLA Ops:
  1.0 23.8 %collective-permute-start = (f32[2,64,256]{2,1,0:T(8,128)S(1)}, f32[2,64,256]{2,1,0:T(8,128)S(1)}, u32[]{:S(2)}, u32[]{:S(2)}) collective-permute-start(f32[2,64,256]{2,1,0:T(8,128)S(1)} %get-tuple-element.15), channel_id=1, source_target_pairs={{0,32},{32,64},{64,96},{96,128},{128,160},{160,192},{192,224},{224... | collective-permute-start | bytes 393224 | tf_op jit(solution)/shard_map/ppermute | solution.py:97
  5.9 18.9 %collective-permute-start.1 = (f32[2,64,256]{2,1,0:T(8,128)S(1)}, f32[2,64,256]{2,1,0:T(8,128)S(1)}, u32[]{:S(2)}, u32[]{:S(2)}) collective-permute-start(f32[2,64,256]{2,1,0:T(8,128)S(1)} %get-tuple-element.16), channel_id=1, source_target_pairs={{32,0},{64,32},{96,64},{128,96},{160,128},{192,160},{224,192},{256... | collective-permute-start | bytes 393224 | tf_op jit(solution)/shard_map/ppermute | solution.py:97
  25.9 6.9 %copy-start.5 = (s32[1,1,1,2]{3,2,1,0:T(1,128)S(1)}, s32[1,1,1,2]{3,2,1,0:T(1,128)}, u32[]{:S(2)}) copy-start(s32[1,1,1,2]{3,2,1,0:T(1,128)} %param.6) | copy-start | bytes 28
  26.0 14.3 %collective-permute-start.2 = (f32[2,384,64]{2,1,0:T(8,128)S(1)}, f32[2,384,64]{2,1,0:T(8,128)S(1)}, u32[]{:S(2)}, u32[]{:S(2)}) collective-permute-start(f32[2,384,64]{2,1,0:T(8,128)S(1)} %get-tuple-element.9), channel_id=1, source_target_pairs={{0,1},{1,2},{2,3},{3,4},{4,5},{5,6},{6,7},{7,8},{8,9},{9,10},{10,1... | collective-permute-start | bytes 589832 | tf_op jit(solution)/shard_map/ppermute | solution.py:97
  30.8 10.3 %collective-permute-start.3 = (f32[2,384,64]{2,1,0:T(8,128)S(1)}, f32[2,384,64]{2,1,0:T(8,128)S(1)}, u32[]{:S(2)}, u32[]{:S(2)}) collective-permute-start(f32[2,384,64]{2,1,0:T(8,128)S(1)} %get-tuple-element.10), channel_id=1, source_target_pairs={{1,0},{2,1},{3,2},{4,3},{5,4},{6,5},{7,6},{8,7},{9,8},{10,9},{11,1... | collective-permute-start | bytes 589832 | tf_op jit(solution)/shard_map/ppermute | solution.py:97
  41.1 0.8 copy-start.3
  49.2 22.2 %copy-start.1 = (f32[2,256,256]{2,1,0:T(8,128)S(1)}, f32[2,256,256]{2,1,0:T(8,128)}, u32[]{:S(2)}) copy-start(f32[2,256,256]{2,1,0:T(8,128)} %shard_map.46) | copy-start | bytes 1572868
  49.3 18.3 %collective-permute-start.5 = (f32[2,136,256]{2,1,0:T(8,128)S(1)}, f32[2,136,256]{2,1,0:T(8,128)S(1)}, u32[]{:S(2)}, u32[]{:S(2)}) collective-permute-start(f32[2,136,256]{2,1,0:T(8,128)S(1)} %get-tuple-element.21), channel_id=1, source_target_pairs={{0,32},{32,64},{64,96},{96,128},{128,160},{160,192},{192,224},{224... | collective-permute-start | bytes 835592 | tf_op jit(solution)/shard_map/ppermute | solution.py:97
  51.3 17.5 %collective-permute-start.4 = (f32[2,136,256]{2,1,0:T(8,128)S(1)}, f32[2,136,256]{2,1,0:T(8,128)S(1)}, u32[]{:S(2)}, u32[]{:S(2)}) collective-permute-start(f32[2,136,256]{2,1,0:T(8,128)S(1)} %get-tuple-element.22), channel_id=1, source_target_pairs={{32,0},{64,32},{96,64},{128,96},{160,128},{192,160},{224,192},{256... | collective-permute-start | bytes 835592 | tf_op jit(solution)/shard_map/ppermute | solution.py:97
  72.4 5.7 %copy-start = (f32[2,3,256,256]{3,2,1,0:T(8,128)S(1)}, f32[2,3,256,256]{3,2,1,0:T(8,128)}, u32[]{:S(2)}) copy-start(f32[2,3,256,256]{3,2,1,0:T(8,128)} %probe_ref.3) | copy-start | bytes 4718596
  73.2 7.9 %collective-permute-start.6 = (f32[2,384,128]{2,1,0:T(8,128)}, f32[2,384,128]{2,1,0:T(8,128)S(1)}, u32[]{:S(2)}, u32[]{:S(2)}) collective-permute-start(f32[2,384,128]{2,1,0:T(8,128)} %get-tuple-element.5), channel_id=1, source_target_pairs={{0,1},{1,2},{2,3},{3,4},{4,5},{5,6},{6,7},{7,8},{8,9},{9,10},{10,1... | collective-permute-start | bytes 1179656 | tf_op jit(solution)/shard_map/ppermute | solution.py:97
  76.1 10.4 %collective-permute-start.7 = (f32[2,384,128]{2,1,0:T(8,128)S(1)}, f32[2,384,128]{2,1,0:T(8,128)}, u32[]{:S(2)}, u32[]{:S(2)}) collective-permute-start(f32[2,384,128]{2,1,0:T(8,128)S(1)} %get-tuple-element.6), channel_id=1, source_target_pairs={{1,0},{2,1},{3,2},{4,3},{5,4},{6,5},{7,6},{8,7},{9,8},{10,9},{11,1... | collective-permute-start | bytes 1179656 | tf_op jit(solution)/shard_map/ppermute | solution.py:97
  81.1 0.7 copy-start.4
  95.4 17.7 %copy-start.2 = (f32[2,256,256]{2,1,0:T(8,128)S(1)}, f32[2,256,256]{2,1,0:T(8,128)}, u32[]{:S(2)}) copy-start(f32[2,256,256]{2,1,0:T(8,128)} %shard_map.47) | copy-start | bytes 1572868
  96.4 13.1 %collective-permute-start.8 = (f32[2,64,384]{2,1,0:T(8,128)S(1)}, f32[2,64,384]{2,1,0:T(8,128)S(1)}, u32[]{:S(2)}, u32[]{:S(2)}) collective-permute-start(f32[2,64,384]{2,1,0:T(8,128)S(1)} %get-tuple-element.11), channel_id=1, source_target_pairs={{0,32},{32,64},{64,96},{96,128},{128,160},{160,192},{192,224},{224... | collective-permute-start | bytes 589832 | tf_op jit(solution)/shard_map/ppermute | solution.py:97
  98.4 14.7 %collective-permute-start.9 = (f32[2,64,384]{2,1,0:T(8,128)S(1)}, f32[2,64,384]{2,1,0:T(8,128)S(1)}, u32[]{:S(2)}, u32[]{:S(2)}) collective-permute-start(f32[2,64,384]{2,1,0:T(8,128)S(1)} %get-tuple-element.12), channel_id=1, source_target_pairs={{32,0},{64,32},{96,64},{128,96},{160,128},{192,160},{224,192},{256... | collective-permute-start | bytes 589832 | tf_op jit(solution)/shard_map/ppermute | solution.py:97
  113.6 6.5 %collective-permute-start.10 = (f32[2,256,64]{2,1,0:T(8,128)S(1)}, f32[2,256,64]{2,1,0:T(8,128)S(1)}, u32[]{:S(2)}, u32[]{:S(2)}) collective-permute-start(f32[2,256,64]{2,1,0:T(8,128)S(1)} %get-tuple-element.7), channel_id=1, source_target_pairs={{0,1},{1,2},{2,3},{3,4},{4,5},{5,6},{6,7},{7,8},{8,9},{9,10},{10,1... | collective-permute-start | bytes 393224 | tf_op jit(solution)/shard_map/ppermute | solution.py:97
  116.8 8.9 %collective-permute-start.11 = (f32[2,256,64]{2,1,0:T(8,128)S(1)}, f32[2,256,64]{2,1,0:T(8,128)S(1)}, u32[]{:S(2)}, u32[]{:S(2)}) collective-permute-start(f32[2,256,64]{2,1,0:T(8,128)S(1)} %get-tuple-element.8), channel_id=1, source_target_pairs={{1,0},{2,1},{3,2},{4,3},{5,4},{6,5},{7,6},{8,7},{9,8},{10,9},{11,1... | collective-permute-start | bytes 393224 | tf_op jit(solution)/shard_map/ppermute | solution.py:97

commit v12 on v6

--- a/solution.py
+++ b/solution.py
@@ -30,7 +30,8 @@
 INTERPRET = False
 
 
-def gradient_kernel(window_ref, probe_ref, measured_ref, table_re_ref, table_im_ref, out_ref, spectrum_ref):
+def gradient_kernel(window_ref, probe_ref, measured_ref, table_re_ref, table_im_ref, out_ref, spectrum_ref,
+                    exit_ref):
     modes = probe_ref.shape[1]
     table_re = table_re_ref[...]
     table_im = table_im_ref[...]
@@ -48,6 +49,8 @@
     power = None
     for k in range(modes):
         exit_re, exit_im = exit_wave(k)
+        exit_ref[0, k] = exit_re
+        exit_ref[1, k] = exit_im
         exit_re = exit_re.astype(jnp.bfloat16)
         exit_im = exit_im.astype(jnp.bfloat16)
         half_re = (product(table_re, exit_re) - product(table_im, exit_im)).astype(jnp.bfloat16)
@@ -68,9 +71,8 @@
         back_im = (product(table_re, fixed_im) - product(table_im, fixed_re)).astype(jnp.bfloat16)
         revised_re = product(back_re, table_re) + product(back_im, table_im)
         revised_im = product(back_im, table_re) - product(back_re, table_im)
-        exit_re, exit_im = exit_wave(k)
-        residue_re = revised_re - exit_re
-        residue_im = revised_im - exit_im
+        residue_re = revised_re - exit_ref[0, k]
+        residue_im = revised_im - exit_ref[1, k]
         probe_re = probe_ref[0, k]
         probe_im = probe_ref[1, k]
         part_re = probe_re * residue_re + probe_im * residue_im
@@ -86,7 +88,7 @@
     return pl.pallas_call(
         gradient_kernel,
         out_shape=jax.ShapeDtypeStruct((2, rows, cols), jnp.float32),
-        scratch_shapes=[pltpu.VMEM((2, modes, rows, cols), jnp.float32)],
+        scratch_shapes=[pltpu.VMEM((2, modes, rows, cols), jnp.float32)] * 2,
         interpret=INTERPRET,
     )(window, probe_modes, measured, table_re, table_im)
 

time: 126 us -> 125 us (level)
  no operation moved by 1% of the time
where the time goes in v12:
time: 125 us
  starting transfers between devices  54.3 us (43%)
  waiting for transfers between devices  26 us (21%)
  local copies, waits for them, and re-layouts  15.9 us (13%)
  Pallas kernels  10.4 us (8%)
  other arithmetic  9.39 us (8%)
  between operations  8.57 us (7%)
    ppermute x12, starting transfers between devices, from_neighbor(): return lax.ppermute(x, axis, pairs)  54.3 us
    ppermute x12, waiting for transfers between devices, from_neighbor(): return lax.ppermute(x, axis, pairs)  26 us
    pallas_call x2, Pallas kernels, pattern_gradient(): pl.pallas_call(gradient_kernel, out_shape=jax.ShapeDtypeStruct((2, rows,...  10.4 us
    another operation x1, local copies, waits for them, and re-layouts, rows_from_neighbors(): jnp.stack([offset[0], offset[1]] + [offset[0]] * 6).astype(jnp.float32)  5.19 us
    slice x5, local copies, waits for them, and re-layouts, neighbor_sum(): piece = lax.slice_in_dim(frame, low - shift, high - shift, axis=dim)  3.39 us
    select_n x1, other arithmetic, on_device(): extended = jnp.where(mask[None], extended + total / peak_power, 0.0)  2.59 us
  transfers between devices with their start and end apart: 12, of which 9 were waited for; matrix products, arithmetic and copies ran while one was open for 8% of the time, Pallas kernels for 0%

profile of v12, /device:TPU:87, one launch (start us, length us, event | category | flops | bytes accessed | tf_op | source)
XLA Modules:
  0.0 124.5 jit_solution(7920914743935178187)
XLA Ops:
  0.0 1.0 fusion.23
  1.0 4.9 %collective-permute-start = (f32[2,64,256]{2,1,0:T(8,128)S(1)}, f32[2,64,256]{2,1,0:T(8,128)S(1)}, u32[]{:S(2)}, u32[]{:S(2)}) collective-permute-start(f32[2,64,256]{2,1,0:T(8,128)S(1)} %get-tuple-element.15), channel_id=1, source_target_pairs={{0,32},{32,64},{64,96},{96,128},{128,160},{160,192},{192,224},{224... | collective-permute-start | bytes 393224 | tf_op jit(solution)/shard_map/ppermute | solution.py:99
  5.9 14.5 %collective-permute-start.1 = (f32[2,64,256]{2,1,0:T(8,128)S(1)}, f32[2,64,256]{2,1,0:T(8,128)S(1)}, u32[]{:S(2)}, u32[]{:S(2)}) collective-permute-start(f32[2,64,256]{2,1,0:T(8,128)S(1)} %get-tuple-element.16), channel_id=1, source_target_pairs={{32,0},{64,32},{96,64},{128,96},{160,128},{192,160},{224,192},{256... | collective-permute-start | bytes 393224 | tf_op jit(solution)/shard_map/ppermute | solution.py:99
  20.4 1.4 %fusion.27 = (s32[1,1]{1,0:T(1,128)}, s32[1,1]{1,0:T(1,128)}) fusion(s32[1,2]{1,0:T(1,128)} %bitcast.22), kind=kLoop, calls=%fused_computation.50 | loop fusion | bytes 16 | tf_op jit(solution)/shard_map/slice | solution.py:171
  24.3 0.4 collective-permute-done
  24.8 1.1 pad_add_fusion.1
  25.9 0.2 fusion.21
  26.0 4.8 %collective-permute-start.2 = (f32[2,384,64]{2,1,0:T(8,128)S(1)}, f32[2,384,64]{2,1,0:T(8,128)S(1)}, u32[]{:S(2)}, u32[]{:S(2)}) collective-permute-start(f32[2,384,64]{2,1,0:T(8,128)S(1)} %get-tuple-element.9), channel_id=1, source_target_pairs={{0,1},{1,2},{2,3},{3,4},{4,5},{5,6},{6,7},{7,8},{8,9},{9,10},{10,1... | collective-permute-start | bytes 589832 | tf_op jit(solution)/shard_map/ppermute | solution.py:99
  30.8 1.9 %collective-permute-start.3 = (f32[2,384,64]{2,1,0:T(8,128)S(1)}, f32[2,384,64]{2,1,0:T(8,128)S(1)}, u32[]{:S(2)}, u32[]{:S(2)}) collective-permute-start(f32[2,384,64]{2,1,0:T(8,128)S(1)} %get-tuple-element.10), channel_id=1, source_target_pairs={{1,0},{2,1},{3,2},{4,3},{5,4},{6,5},{7,6},{8,7},{9,8},{10,9},{11,1... | collective-permute-start | bytes 589832 | tf_op jit(solution)/shard_map/ppermute | solution.py:99
  32.7 0.7 fusion.26
  33.4 5.2 %stack.9 = s32[8]{0:T(128)S(1)} concatenate(s32[1]{0:T(128)} %bitcast.10, s32[1]{0:T(128)} %bitcast.11, s32[1]{0:T(128)} %bitcast.10, s32[1]{0:T(128)} %bitcast.10, s32[1]{0:T(128)} %bitcast.10, s32[1]{0:T(128)} %bitcast.10, s32[1]{0:T(128)} %bitcast.10, s32[1]{0:T(128)} %bitcast.10), dimensions={0} | concatenate | bytes 64 | tf_op jit(solution)/shard_map/stack | solution.py:123
  38.6 1.8 %multiply_convert_fusion = (bf16[256,256]{1,0:T(8,128)(2,1)}, bf16[256,256]{1,0:T(8,128)(2,1)}) fusion(), kind=kLoop, calls=%fused_computation.27 | loop fusion | flops 1245184 | bytes 262144 | tf_op jit(solution)/shard_map/convert_element_type | solution.py:26
  40.4 0.7 collective-permute-done.3
  41.1 0.5 pad_add_fusion
  41.6 0.3 copy-done.3
  41.9 1.0 constant_dynamic-slice_fusion.1.window_ref
  42.9 5.2 %shard_map.46 = f32[2,256,256]{2,1,0:T(8,128)} custom-call(f32[2,256,256]{2,1,0:T(8,128)} %constant_dynamic-slice_fusion.1.window_ref, f32[2,3,256,256]{3,2,1,0:T(8,128)} %probe_ref.3, f32[256,256]{1,0:T(8,128)} %bitcast.20, bf16[256,256]{1,0:T(8,128)(2,1)} %get-tuple-element.28.table_re_ref, bf16[256,256]{1,0:T(8,128)(2,1)} %get-tuple-element.27.table_im_ref), custom_call_target="tpu_custom_call" | custom-call | tf_op jit(solution)/shard_map/pallas_call | solution.py:88
  48.1 1.1 fusion.22
  49.1 0.1 pad_maximum_fusion.1
  49.2 2.1 %collective-permute-start.5 = (f32[2,136,256]{2,1,0:T(8,128)S(1)}, f32[2,136,256]{2,1,0:T(8,128)S(1)}, u32[]{:S(2)}, u32[]{:S(2)}) collective-permute-start(f32[2,136,256]{2,1,0:T(8,128)S(1)} %get-tuple-element.21), channel_id=1, source_target_pairs={{0,32},{32,64},{64,96},{96,128},{128,160},{160,192},{192,224},{224... | collective-permute-start | bytes 835592 | tf_op jit(solution)/shard_map/ppermute | solution.py:99
  51.3 7.6 %collective-permute-start.4 = (f32[2,136,256]{2,1,0:T(8,128)S(1)}, f32[2,136,256]{2,1,0:T(8,128)S(1)}, u32[]{:S(2)}, u32[]{:S(2)}) collective-permute-start(f32[2,136,256]{2,1,0:T(8,128)S(1)} %get-tuple-element.22), channel_id=1, source_target_pairs={{32,0},{64,32},{96,64},{128,96},{160,128},{192,160},{224,192},{256... | collective-permute-start | bytes 835592 | tf_op jit(solution)/shard_map/ppermute | solution.py:99
  61.4 6.2 %collective-permute-done.5 = f32[2,136,256]{2,1,0:T(8,128)S(1)} collective-permute-done((f32[2,136,256]{2,1,0:T(8,128)S(1)}, f32[2,136,256]{2,1,0:T(8,128)S(1)}, u32[]{:S(2)}, u32[]{:S(2)}) %collective-permute-start.5) | collective-permute-done | bytes 278560 | tf_op jit(solution)/shard_map/ppermute | solution.py:99
  67.6 0.6 fusion.24
  68.8 0.5 fusion.25
  71.4 1.0 fusion
  72.4 0.8 fusion.19
  73.2 2.9 %collective-permute-start.6 = (f32[2,384,128]{2,1,0:T(8,128)}, f32[2,384,128]{2,1,0:T(8,128)S(1)}, u32[]{:S(2)}, u32[]{:S(2)}) collective-permute-start(f32[2,384,128]{2,1,0:T(8,128)} %get-tuple-element.5), channel_id=1, source_target_pairs={{0,1},{1,2},{2,3},{3,4},{4,5},{5,6},{6,7},{7,8},{8,9},{9,10},{10,1... | collective-permute-start | bytes 1179656 | tf_op jit(solution)/shard_map/ppermute | solution.py:99
  76.1 1.9 %collective-permute-start.7 = (f32[2,384,128]{2,1,0:T(8,128)S(1)}, f32[2,384,128]{2,1,0:T(8,128)}, u32[]{:S(2)}, u32[]{:S(2)}) collective-permute-start(f32[2,384,128]{2,1,0:T(8,128)S(1)} %get-tuple-element.6), channel_id=1, source_target_pairs={{1,0},{2,1},{3,2},{4,3},{5,4},{6,5},{7,6},{8,7},{9,8},{10,9},{11,1... | collective-permute-start | bytes 1179656 | tf_op jit(solution)/shard_map/ppermute | solution.py:99
  78.0 0.1 multiply_reduce_fusion
  78.1 0.7 reduce_max.9
  79.5 0.1 broadcast_and_fusion
  79.6 1.5 %collective-permute-done.6 = f32[2,384,128]{2,1,0:T(8,128)S(1)} collective-permute-done((f32[2,384,128]{2,1,0:T(8,128)}, f32[2,384,128]{2,1,0:T(8,128)S(1)}, u32[]{:S(2)}, u32[]{:S(2)}) %collective-permute-start.6) | collective-permute-done | bytes 393248 | tf_op jit(solution)/shard_map/ppermute | solution.py:99
  81.1 0.7 copy-done.4
  81.8 4.7 %collective-permute-done.7 = f32[2,384,128]{2,1,0:T(8,128)} collective-permute-done((f32[2,384,128]{2,1,0:T(8,128)S(1)}, f32[2,384,128]{2,1,0:T(8,128)}, u32[]{:S(2)}, u32[]{:S(2)}) %collective-permute-start.7) | collective-permute-done | bytes 393248 | tf_op jit(solution)/shard_map/ppermute | solution.py:99
  86.5 2.6 %add_select_fusion = f32[2,384,384]{2,1,0:T(8,128)S(1)} fusion(f32[2,384,128]{2,1,0:T(8,128)} %collective-permute-done.7, f32[2,384,128]{2,1,0:T(8,128)} %copy-done.4, f32[]{:T(128)S(6)} %add.205, pred[384,384]{1,0:T(8,128)(4,1)S(1)} %broadcast_and_fusion, s32[]{:T(128)S(6)} %select_n.52, s32[]{:T(128)S(6)} %select_n.53, f32[2,128,256]{2,1,0:T(8,128)S(1)} %slice.112, ...), kind=kLoop, calls=%fused_computation.9 | loop fusion | flops 2654208 | bytes 4341788 | tf_op jit(solution)/shard_map/jit(_where)/select_n | solution.py:184
  89.1 1.0 constant_dynamic-slice_fusion.window_ref
  90.1 5.2 %shard_map.47 = f32[2,256,256]{2,1,0:T(8,128)} custom-call(f32[2,256,256]{2,1,0:T(8,128)} %constant_dynamic-slice_fusion.window_ref, f32[2,3,256,256]{3,2,1,0:T(8,128)} %probe_ref.3, f32[256,256]{1,0:T(8,128)} %bitcast.21, bf16[256,256]{1,0:T(8,128)(2,1)} %get-tuple-element.28.table_re_ref, bf16[256,256]{1,0:T(8,128)(2,1)} %get-tuple-element.27.table_im_ref), custom_call_target="tpu_custom_call" | custom-call | tf_op jit(solution)/shard_map/pallas_call | solution.py:88
  95.3 1.4 %pad_dynamic-slice_fusion.1 = (f32[2,384,64]{2,1,0:T(8,128)S(1)}, f32[2,384,64]{2,1,0:T(8,128)S(1)}) fusion(s32[]{:T(128)S(6)} %select_n.48, s32[]{:T(128)S(6)} %add.212, f32[2,256,256]{2,1,0:T(8,128)} %shard_map.47, s32[]{:T(128)S(6)} %select_n.49), kind=kLoop, calls=%fused_computation.1 | loop fusion | bytes 917516 | tf_op jit(solution)/shard_map/slice | solution.py:109
  96.7 1.9 %collective-permute-start.8 = (f32[2,384,64]{2,1,0:T(8,128)S(1)}, f32[2,384,64]{2,1,0:T(8,128)S(1)}, u32[]{:S(2)}, u32[]{:S(2)}) collective-permute-start(f32[2,384,64]{2,1,0:T(8,128)S(1)} %get-tuple-element.11), channel_id=1, source_target_pairs={{0,1},{1,2},{2,3},{3,4},{4,5},{5,6},{6,7},{7,8},{8,9},{9,10},{10,1... | collective-permute-start | bytes 589832 | tf_op jit(solution)/shard_map/ppermute | solution.py:99
  98.6 2.4 %collective-permute-start.9 = (f32[2,384,64]{2,1,0:T(8,128)S(1)}, f32[2,384,64]{2,1,0:T(8,128)S(1)}, u32[]{:S(2)}, u32[]{:S(2)}) collective-permute-start(f32[2,384,64]{2,1,0:T(8,128)S(1)} %get-tuple-element.12), channel_id=1, source_target_pairs={{1,0},{2,1},{3,2},{4,3},{5,4},{6,5},{7,6},{8,7},{9,8},{10,9},{11,1... | collective-permute-start | bytes 589832 | tf_op jit(solution)/shard_map/ppermute | solution.py:99
  101.0 2.3 %collective-permute-done.8 = f32[2,384,64]{2,1,0:T(8,128)S(1)} collective-permute-done((f32[2,384,64]{2,1,0:T(8,128)S(1)}, f32[2,384,64]{2,1,0:T(8,128)S(1)}, u32[]{:S(2)}, u32[]{:S(2)}) %collective-permute-start.8) | collective-permute-done | bytes 196640 | tf_op jit(solution)/shard_map/ppermute | solution.py:99
  103.3 5.6 %collective-permute-done.9 = f32[2,384,64]{2,1,0:T(8,128)S(1)} collective-permute-done((f32[2,384,64]{2,1,0:T(8,128)S(1)}, f32[2,384,64]{2,1,0:T(8,128)S(1)}, u32[]{:S(2)}, u32[]{:S(2)}) %collective-permute-start.9) | collective-permute-done | bytes 196640 | tf_op jit(solution)/shard_map/ppermute | solution.py:99
  108.9 0.4 fusion.3
  109.4 1.9 %collective-permute-start.10 = (f32[2,64,256]{2,1,0:T(8,128)S(1)}, f32[2,64,256]{2,1,0:T(8,128)S(1)}, u32[]{:S(2)}, u32[]{:S(2)}) collective-permute-start(f32[2,64,256]{2,1,0:T(8,128)S(1)} %get-tuple-element.7), channel_id=1, source_target_pairs={{0,32},{32,64},{64,96},{96,128},{128,160},{160,192},{192,224},{224... | collective-permute-start | bytes 393224 | tf_op jit(solution)/shard_map/ppermute | solution.py:99
  111.3 7.6 %collective-permute-start.11 = (f32[2,64,256]{2,1,0:T(8,128)S(1)}, f32[2,64,256]{2,1,0:T(8,128)S(1)}, u32[]{:S(2)}, u32[]{:S(2)}) collective-permute-start(f32[2,64,256]{2,1,0:T(8,128)S(1)} %get-tuple-element.8), channel_id=1, source_target_pairs={{32,0},{64,32},{96,64},{128,96},{160,128},{192,160},{224,192},{256... | collective-permute-start | bytes 393224 | tf_op jit(solution)/shard_map/ppermute | solution.py:99
  118.9 1.9 %collective-permute-done.10 = f32[2,64,256]{2,1,0:T(8,128)S(1)} collective-permute-done((f32[2,64,256]{2,1,0:T(8,128)S(1)}, f32[2,64,256]{2,1,0:T(8,128)S(1)}, u32[]{:S(2)}, u32[]{:S(2)}) %collective-permute-start.10) | collective-permute-done | bytes 131104 | tf_op jit(solution)/shard_map/ppermute | solution.py:99
  120.8 2.7 %collective-permute-done.11 = f32[2,64,256]{2,1,0:T(8,128)S(1)} collective-permute-done((f32[2,64,256]{2,1,0:T(8,128)S(1)}, f32[2,64,256]{2,1,0:T(8,128)S(1)}, u32[]{:S(2)}, u32[]{:S(2)}) %collective-permute-start.11) | collective-permute-done | bytes 131104 | tf_op jit(solution)/shard_map/ppermute | solution.py:99
  123.5 1.0 fusion.6
  (19 shorter events, 0.1 us)
Async XLA Ops:
  1.0 23.8 %collective-permute-start = (f32[2,64,256]{2,1,0:T(8,128)S(1)}, f32[2,64,256]{2,1,0:T(8,128)S(1)}, u32[]{:S(2)}, u32[]{:S(2)}) collective-permute-start(f32[2,64,256]{2,1,0:T(8,128)S(1)} %get-tuple-element.15), channel_id=1, source_target_pairs={{0,32},{32,64},{64,96},{96,128},{128,160},{160,192},{192,224},{224... | collective-permute-start | bytes 393224 | tf_op jit(solution)/shard_map/ppermute | solution.py:99
  5.9 18.9 %collective-permute-start.1 = (f32[2,64,256]{2,1,0:T(8,128)S(1)}, f32[2,64,256]{2,1,0:T(8,128)S(1)}, u32[]{:S(2)}, u32[]{:S(2)}) collective-permute-start(f32[2,64,256]{2,1,0:T(8,128)S(1)} %get-tuple-element.16), channel_id=1, source_target_pairs={{32,0},{64,32},{96,64},{128,96},{160,128},{192,160},{224,192},{256... | collective-permute-start | bytes 393224 | tf_op jit(solution)/shard_map/ppermute | solution.py:99
  25.9 6.9 %copy-start.5 = (s32[1,1,1,2]{3,2,1,0:T(1,128)S(1)}, s32[1,1,1,2]{3,2,1,0:T(1,128)}, u32[]{:S(2)}) copy-start(s32[1,1,1,2]{3,2,1,0:T(1,128)} %param.6) | copy-start | bytes 28
  26.0 14.3 %collective-permute-start.2 = (f32[2,384,64]{2,1,0:T(8,128)S(1)}, f32[2,384,64]{2,1,0:T(8,128)S(1)}, u32[]{:S(2)}, u32[]{:S(2)}) collective-permute-start(f32[2,384,64]{2,1,0:T(8,128)S(1)} %get-tuple-element.9), channel_id=1, source_target_pairs={{0,1},{1,2},{2,3},{3,4},{4,5},{5,6},{6,7},{7,8},{8,9},{9,10},{10,1... | collective-permute-start | bytes 589832 | tf_op jit(solution)/shard_map/ppermute | solution.py:99
  30.8 10.3 %collective-permute-start.3 = (f32[2,384,64]{2,1,0:T(8,128)S(1)}, f32[2,384,64]{2,1,0:T(8,128)S(1)}, u32[]{:S(2)}, u32[]{:S(2)}) collective-permute-start(f32[2,384,64]{2,1,0:T(8,128)S(1)} %get-tuple-element.10), channel_id=1, source_target_pairs={{1,0},{2,1},{3,2},{4,3},{5,4},{6,5},{7,6},{8,7},{9,8},{10,9},{11,1... | collective-permute-start | bytes 589832 | tf_op jit(solution)/shard_map/ppermute | solution.py:99
  41.1 0.8 copy-start.3
  49.1 22.2 %copy-start.1 = (f32[2,256,256]{2,1,0:T(8,128)S(1)}, f32[2,256,256]{2,1,0:T(8,128)}, u32[]{:S(2)}) copy-start(f32[2,256,256]{2,1,0:T(8,128)} %shard_map.46) | copy-start | bytes 1572868
  49.2 18.4 %collective-permute-start.5 = (f32[2,136,256]{2,1,0:T(8,128)S(1)}, f32[2,136,256]{2,1,0:T(8,128)S(1)}, u32[]{:S(2)}, u32[]{:S(2)}) collective-permute-start(f32[2,136,256]{2,1,0:T(8,128)S(1)} %get-tuple-element.21), channel_id=1, source_target_pairs={{0,32},{32,64},{64,96},{96,128},{128,160},{160,192},{192,224},{224... | collective-permute-start | bytes 835592 | tf_op jit(solution)/shard_map/ppermute | solution.py:99
  51.3 17.5 %collective-permute-start.4 = (f32[2,136,256]{2,1,0:T(8,128)S(1)}, f32[2,136,256]{2,1,0:T(8,128)S(1)}, u32[]{:S(2)}, u32[]{:S(2)}) collective-permute-start(f32[2,136,256]{2,1,0:T(8,128)S(1)} %get-tuple-element.22), channel_id=1, source_target_pairs={{32,0},{64,32},{96,64},{128,96},{160,128},{192,160},{224,192},{256... | collective-permute-start | bytes 835592 | tf_op jit(solution)/shard_map/ppermute | solution.py:99
  72.4 5.6 %copy-start = (f32[2,3,256,256]{3,2,1,0:T(8,128)S(1)}, f32[2,3,256,256]{3,2,1,0:T(8,128)}, u32[]{:S(2)}) copy-start(f32[2,3,256,256]{3,2,1,0:T(8,128)} %probe_ref.3) | copy-start | bytes 4718596
  73.2 7.9 %collective-permute-start.6 = (f32[2,384,128]{2,1,0:T(8,128)}, f32[2,384,128]{2,1,0:T(8,128)S(1)}, u32[]{:S(2)}, u32[]{:S(2)}) collective-permute-start(f32[2,384,128]{2,1,0:T(8,128)} %get-tuple-element.5), channel_id=1, source_target_pairs={{0,1},{1,2},{2,3},{3,4},{4,5},{5,6},{6,7},{7,8},{8,9},{9,10},{10,1... | collective-permute-start | bytes 1179656 | tf_op jit(solution)/shard_map/ppermute | solution.py:99
  76.1 10.4 %collective-permute-start.7 = (f32[2,384,128]{2,1,0:T(8,128)S(1)}, f32[2,384,128]{2,1,0:T(8,128)}, u32[]{:S(2)}, u32[]{:S(2)}) collective-permute-start(f32[2,384,128]{2,1,0:T(8,128)S(1)} %get-tuple-element.6), channel_id=1, source_target_pairs={{1,0},{2,1},{3,2},{4,3},{5,4},{6,5},{7,6},{8,7},{9,8},{10,9},{11,1... | collective-permute-start | bytes 1179656 | tf_op jit(solution)/shard_map/ppermute | solution.py:99
  81.1 0.7 copy-start.4
  95.3 13.7 %copy-start.2 = (f32[2,256,256]{2,1,0:T(8,128)S(1)}, f32[2,256,256]{2,1,0:T(8,128)}, u32[]{:S(2)}) copy-start(f32[2,256,256]{2,1,0:T(8,128)} %shard_map.47) | copy-start | bytes 1572868
  96.7 6.6 %collective-permute-start.8 = (f32[2,384,64]{2,1,0:T(8,128)S(1)}, f32[2,384,64]{2,1,0:T(8,128)S(1)}, u32[]{:S(2)}, u32[]{:S(2)}) collective-permute-start(f32[2,384,64]{2,1,0:T(8,128)S(1)} %get-tuple-element.11), channel_id=1, source_target_pairs={{0,1},{1,2},{2,3},{3,4},{4,5},{5,6},{6,7},{7,8},{8,9},{9,10},{10,1... | collective-permute-start | bytes 589832 | tf_op jit(solution)/shard_map/ppermute | solution.py:99
  98.6 10.3 %collective-permute-start.9 = (f32[2,384,64]{2,1,0:T(8,128)S(1)}, f32[2,384,64]{2,1,0:T(8,128)S(1)}, u32[]{:S(2)}, u32[]{:S(2)}) collective-permute-start(f32[2,384,64]{2,1,0:T(8,128)S(1)} %get-tuple-element.12), channel_id=1, source_target_pairs={{1,0},{2,1},{3,2},{4,3},{5,4},{6,5},{7,6},{8,7},{9,8},{10,9},{11,1... | collective-permute-start | bytes 589832 | tf_op jit(solution)/shard_map/ppermute | solution.py:99
  109.4 11.4 %collective-permute-start.10 = (f32[2,64,256]{2,1,0:T(8,128)S(1)}, f32[2,64,256]{2,1,0:T(8,128)S(1)}, u32[]{:S(2)}, u32[]{:S(2)}) collective-permute-start(f32[2,64,256]{2,1,0:T(8,128)S(1)} %get-tuple-element.7), channel_id=1, source_target_pairs={{0,32},{32,64},{64,96},{96,128},{128,160},{160,192},{192,224},{224... | collective-permute-start | bytes 393224 | tf_op jit(solution)/shard_map/ppermute | solution.py:99
  111.3 12.2 %collective-permute-start.11 = (f32[2,64,256]{2,1,0:T(8,128)S(1)}, f32[2,64,256]{2,1,0:T(8,128)S(1)}, u32[]{:S(2)}, u32[]{:S(2)}) collective-permute-start(f32[2,64,256]{2,1,0:T(8,128)S(1)} %get-tuple-element.8), channel_id=1, source_target_pairs={{32,0},{64,32},{96,64},{128,96},{160,128},{192,160},{224,192},{256... | collective-permute-start | bytes 393224 | tf_op jit(solution)/shard_map/ppermute | solution.py:99

commit v13 on v12

--- a/solution.py
+++ b/solution.py
@@ -148,6 +148,13 @@
     return total
 
 
+def first_rows(object_planes):
+    size = object_planes.shape[1]
+    from_high = from_neighbor(object_planes[:, :M], "row", 1)
+    from_low = from_neighbor(object_planes[:, size - M :], "row", -1)
+    return jnp.concatenate([from_low, object_planes, from_high], axis=1)
+
+
 def inside_mask(extent, tile_size):
     rows = lax.axis_size("row")
     cols = lax.axis_size("col")
@@ -170,7 +177,7 @@
     zero = jnp.zeros((), jnp.int32)
     corner = (zero, offsets[0, 0] + M, offsets[0, 1] + M)
     spread = (zero, place - M - offsets[0, 0], place - M - offsets[0, 1])
-    extended = neighbor_sum(object_planes, "row", 1, tile_size, M, 0, extent)
+    extended = first_rows(object_planes)
     extended = neighbor_sum(extended, "col", 2, tile_size, M, 0, extent)
     for update in range(ITERS):
         window = lax.dynamic_slice(extended, corner, (2, W, W))

time: 125 us -> 127 us (1.016)
  the two profiles are of different devices: /device:TPU:87 before, /device:TPU:71 now
where the time goes in v13:
time: 127 us; the launch traced here: 126 us
  starting transfers between devices  55.5 us (44%)
  waiting for transfers between devices  25.4 us (20%)
  local copies, waits for them, and re-layouts  17 us (13%)
  Pallas kernels  10.4 us (8%)
  other arithmetic  9.29 us (7%)
  between operations  8.59 us (7%)
    ppermute x12, starting transfers between devices, from_neighbor(): return lax.ppermute(x, axis, pairs)  55.5 us
    ppermute x12, waiting for transfers between devices, from_neighbor(): return lax.ppermute(x, axis, pairs)  25.4 us
    pallas_call x2, Pallas kernels, pattern_gradient(): pl.pallas_call(gradient_kernel, out_shape=jax.ShapeDtypeStruct((2, rows,...  10.4 us
    another operation x1, local copies, waits for them, and re-layouts, rows_from_neighbors(): jnp.stack([offset[0], offset[1]] + [offset[0]] * 6).astype(jnp.float32)  5.19 us
    select_n x1, other arithmetic, on_device(): extended = jnp.where(mask[None], extended + total / peak_power, 0.0)  2.59 us
  transfers between devices with their start and end apart: 12, of which 9 were waited for; matrix products, arithmetic and copies ran while one was open for 9% of the time, Pallas kernels for 0%

profile of v13, /device:TPU:71, one launch (start us, length us, event | category | flops | bytes accessed | tf_op | source)
XLA Modules:
  0.0 126.2 jit_solution(15429890438376488725)
XLA Ops:
  0.0 1.0 fusion.23
  1.0 4.9 %collective-permute-start = (f32[2,64,256]{2,1,0:T(8,128)S(1)}, f32[2,64,256]{2,1,0:T(8,128)S(1)}, u32[]{:S(2)}, u32[]{:S(2)}) collective-permute-start(f32[2,64,256]{2,1,0:T(8,128)S(1)} %get-tuple-element.16), channel_id=1, source_target_pairs={{0,32},{32,64},{64,96},{96,128},{128,160},{160,192},{192,224},{224... | collective-permute-start | bytes 393224 | tf_op jit(solution)/shard_map/ppermute | solution.py:99
  5.9 13.6 %collective-permute-start.1 = (f32[2,64,256]{2,1,0:T(8,128)S(1)}, f32[2,64,256]{2,1,0:T(8,128)S(1)}, u32[]{:S(2)}, u32[]{:S(2)}) collective-permute-start(f32[2,64,256]{2,1,0:T(8,128)S(1)} %get-tuple-element.15), channel_id=1, source_target_pairs={{32,0},{64,32},{96,64},{128,96},{160,128},{192,160},{224,192},{256... | collective-permute-start | bytes 393224 | tf_op jit(solution)/shard_map/ppermute | solution.py:99
  19.5 1.4 %fusion.27 = (s32[1,1]{1,0:T(1,128)}, s32[1,1]{1,0:T(1,128)}) fusion(s32[1,2]{1,0:T(1,128)} %bitcast.22), kind=kLoop, calls=%fused_computation.52 | loop fusion | bytes 16 | tf_op jit(solution)/shard_map/slice | solution.py:178
  23.5 1.1 constant_dynamic-update-slice_fusion.1
  24.6 0.2 fusion.21
  24.7 5.7 %collective-permute-start.2 = (f32[2,384,64]{2,1,0:T(8,128)S(1)}, f32[2,384,64]{2,1,0:T(8,128)S(1)}, u32[]{:S(2)}, u32[]{:S(2)}) collective-permute-start(f32[2,384,64]{2,1,0:T(8,128)S(1)} %get-tuple-element.9), channel_id=1, source_target_pairs={{0,1},{1,2},{2,3},{3,4},{4,5},{5,6},{6,7},{7,8},{8,9},{9,10},{10,1... | collective-permute-start | bytes 589832 | tf_op jit(solution)/shard_map/ppermute | solution.py:99
  30.4 1.9 %collective-permute-start.3 = (f32[2,384,64]{2,1,0:T(8,128)S(1)}, f32[2,384,64]{2,1,0:T(8,128)S(1)}, u32[]{:S(2)}, u32[]{:S(2)}) collective-permute-start(f32[2,384,64]{2,1,0:T(8,128)S(1)} %get-tuple-element.10), channel_id=1, source_target_pairs={{1,0},{2,1},{3,2},{4,3},{5,4},{6,5},{7,6},{8,7},{9,8},{10,9},{11,1... | collective-permute-start | bytes 589832 | tf_op jit(solution)/shard_map/ppermute | solution.py:99
  32.4 0.7 fusion.26
  33.0 5.2 %stack.9 = s32[8]{0:T(128)S(1)} concatenate(s32[1]{0:T(128)} %bitcast.10, s32[1]{0:T(128)} %bitcast.11, s32[1]{0:T(128)} %bitcast.10, s32[1]{0:T(128)} %bitcast.10, s32[1]{0:T(128)} %bitcast.10, s32[1]{0:T(128)} %bitcast.10, s32[1]{0:T(128)} %bitcast.10, s32[1]{0:T(128)} %bitcast.10), dimensions={0} | concatenate | bytes 64 | tf_op jit(solution)/shard_map/stack | solution.py:123
  38.2 1.8 %multiply_convert_fusion = (bf16[256,256]{1,0:T(8,128)(2,1)}, bf16[256,256]{1,0:T(8,128)(2,1)}) fusion(), kind=kLoop, calls=%fused_computation.26 | loop fusion | flops 1245184 | bytes 262144 | tf_op jit(solution)/shard_map/convert_element_type | solution.py:26
  40.0 0.7 collective-permute-done.3
  40.7 0.5 pad_add_fusion
  41.2 0.3 copy-done.3
  41.5 1.0 constant_dynamic-slice_fusion.1.window_ref
  42.5 5.2 %shard_map.46 = f32[2,256,256]{2,1,0:T(8,128)} custom-call(f32[2,256,256]{2,1,0:T(8,128)} %constant_dynamic-slice_fusion.1.window_ref, f32[2,3,256,256]{3,2,1,0:T(8,128)} %probe_ref.3, f32[256,256]{1,0:T(8,128)} %bitcast.20, bf16[256,256]{1,0:T(8,128)(2,1)} %get-tuple-element.28.table_re_ref, bf16[256,256]{1,0:T(8,128)(2,1)} %get-tuple-element.27.table_im_ref), custom_call_target="tpu_custom_call" | custom-call | tf_op jit(solution)/shard_map/pallas_call | solution.py:88
  47.7 1.1 fusion.22
  48.7 0.1 pad_maximum_fusion.1
  48.9 2.1 %collective-permute-start.5 = (f32[2,136,256]{2,1,0:T(8,128)S(1)}, f32[2,136,256]{2,1,0:T(8,128)S(1)}, u32[]{:S(2)}, u32[]{:S(2)}) collective-permute-start(f32[2,136,256]{2,1,0:T(8,128)S(1)} %get-tuple-element.21), channel_id=1, source_target_pairs={{0,32},{32,64},{64,96},{96,128},{128,160},{160,192},{192,224},{224... | collective-permute-start | bytes 835592 | tf_op jit(solution)/shard_map/ppermute | solution.py:99
  50.9 8.3 %collective-permute-start.4 = (f32[2,136,256]{2,1,0:T(8,128)S(1)}, f32[2,136,256]{2,1,0:T(8,128)S(1)}, u32[]{:S(2)}, u32[]{:S(2)}) collective-permute-start(f32[2,136,256]{2,1,0:T(8,128)S(1)} %get-tuple-element.22), channel_id=1, source_target_pairs={{32,0},{64,32},{96,64},{128,96},{160,128},{192,160},{224,192},{256... | collective-permute-start | bytes 835592 | tf_op jit(solution)/shard_map/ppermute | solution.py:99
  61.8 6.8 %collective-permute-done.5 = f32[2,136,256]{2,1,0:T(8,128)S(1)} collective-permute-done((f32[2,136,256]{2,1,0:T(8,128)S(1)}, f32[2,136,256]{2,1,0:T(8,128)S(1)}, u32[]{:S(2)}, u32[]{:S(2)}) %collective-permute-start.5) | collective-permute-done | bytes 278560 | tf_op jit(solution)/shard_map/ppermute | solution.py:99
  68.6 0.6 fusion.24
  69.8 1.0 collective-permute-done.4
  70.8 0.5 fusion.25
  73.3 1.0 fusion
  74.3 0.8 fusion.19
  75.1 2.5 %collective-permute-start.6 = (f32[2,384,128]{2,1,0:T(8,128)}, f32[2,384,128]{2,1,0:T(8,128)S(1)}, u32[]{:S(2)}, u32[]{:S(2)}) collective-permute-start(f32[2,384,128]{2,1,0:T(8,128)} %get-tuple-element.5), channel_id=1, source_target_pairs={{0,1},{1,2},{2,3},{3,4},{4,5},{5,6},{6,7},{7,8},{8,9},{9,10},{10,1... | collective-permute-start | bytes 1179656 | tf_op jit(solution)/shard_map/ppermute | solution.py:99
  77.6 1.9 %collective-permute-start.7 = (f32[2,384,128]{2,1,0:T(8,128)S(1)}, f32[2,384,128]{2,1,0:T(8,128)}, u32[]{:S(2)}, u32[]{:S(2)}) collective-permute-start(f32[2,384,128]{2,1,0:T(8,128)S(1)} %get-tuple-element.6), channel_id=1, source_target_pairs={{1,0},{2,1},{3,2},{4,3},{5,4},{6,5},{7,6},{8,7},{9,8},{10,9},{11,1... | collective-permute-start | bytes 1179656 | tf_op jit(solution)/shard_map/ppermute | solution.py:99
  79.6 0.1 multiply_reduce_fusion
  79.7 0.7 reduce_max.9
  81.1 0.1 broadcast_and_fusion
  81.2 1.5 %collective-permute-done.6 = f32[2,384,128]{2,1,0:T(8,128)S(1)} collective-permute-done((f32[2,384,128]{2,1,0:T(8,128)}, f32[2,384,128]{2,1,0:T(8,128)S(1)}, u32[]{:S(2)}, u32[]{:S(2)}) %collective-permute-start.6) | collective-permute-done | bytes 393248 | tf_op jit(solution)/shard_map/ppermute | solution.py:99
  82.7 0.7 copy-done.4
  83.4 4.7 %collective-permute-done.7 = f32[2,384,128]{2,1,0:T(8,128)} collective-permute-done((f32[2,384,128]{2,1,0:T(8,128)S(1)}, f32[2,384,128]{2,1,0:T(8,128)}, u32[]{:S(2)}, u32[]{:S(2)}) %collective-permute-start.7) | collective-permute-done | bytes 393248 | tf_op jit(solution)/shard_map/ppermute | solution.py:99
  88.1 2.6 %add_select_fusion = f32[2,384,384]{2,1,0:T(8,128)S(1)} fusion(f32[2,384,128]{2,1,0:T(8,128)} %collective-permute-done.7, f32[2,384,128]{2,1,0:T(8,128)} %copy-done.4, f32[]{:T(128)S(6)} %add.191, pred[384,384]{1,0:T(8,128)(4,1)S(1)} %broadcast_and_fusion, s32[]{:T(128)S(6)} %select_n.52, s32[]{:T(128)S(6)} %select_n.53, f32[2,128,256]{2,1,0:T(8,128)S(1)} %slice.112, ...), kind=kLoop, calls=%fused_computation.9 | loop fusion | flops 2654208 | bytes 4341788 | tf_op jit(solution)/shard_map/jit(_where)/select_n | solution.py:191
  90.7 1.0 constant_dynamic-slice_fusion.window_ref
  91.7 5.2 %shard_map.47 = f32[2,256,256]{2,1,0:T(8,128)} custom-call(f32[2,256,256]{2,1,0:T(8,128)} %constant_dynamic-slice_fusion.window_ref, f32[2,3,256,256]{3,2,1,0:T(8,128)} %probe_ref.3, f32[256,256]{1,0:T(8,128)} %bitcast.21, bf16[256,256]{1,0:T(8,128)(2,1)} %get-tuple-element.28.table_re_ref, bf16[256,256]{1,0:T(8,128)(2,1)} %get-tuple-element.27.table_im_ref), custom_call_target="tpu_custom_call" | custom-call | tf_op jit(solution)/shard_map/pallas_call | solution.py:88
  96.8 1.4 %pad_dynamic-slice_fusion.1 = (f32[2,384,64]{2,1,0:T(8,128)S(1)}, f32[2,384,64]{2,1,0:T(8,128)S(1)}) fusion(s32[]{:T(128)S(6)} %select_n.48, s32[]{:T(128)S(6)} %add.198, f32[2,256,256]{2,1,0:T(8,128)} %shard_map.47, s32[]{:T(128)S(6)} %select_n.49), kind=kLoop, calls=%fused_computation.1 | loop fusion | bytes 917516 | tf_op jit(solution)/shard_map/slice | solution.py:109
  98.3 1.9 %collective-permute-start.8 = (f32[2,384,64]{2,1,0:T(8,128)S(1)}, f32[2,384,64]{2,1,0:T(8,128)S(1)}, u32[]{:S(2)}, u32[]{:S(2)}) collective-permute-start(f32[2,384,64]{2,1,0:T(8,128)S(1)} %get-tuple-element.11), channel_id=1, source_target_pairs={{0,1},{1,2},{2,3},{3,4},{4,5},{5,6},{6,7},{7,8},{8,9},{9,10},{10,1... | collective-permute-start | bytes 589832 | tf_op jit(solution)/shard_map/ppermute | solution.py:99
  100.2 2.4 %collective-permute-start.9 = (f32[2,384,64]{2,1,0:T(8,128)S(1)}, f32[2,384,64]{2,1,0:T(8,128)}, u32[]{:S(2)}, u32[]{:S(2)}) collective-permute-start(f32[2,384,64]{2,1,0:T(8,128)S(1)} %get-tuple-element.12), channel_id=1, source_target_pairs={{1,0},{2,1},{3,2},{4,3},{5,4},{6,5},{7,6},{8,7},{9,8},{10,9},{11,1... | collective-permute-start | bytes 589832 | tf_op jit(solution)/shard_map/ppermute | solution.py:99
  102.6 2.3 %collective-permute-done.8 = f32[2,384,64]{2,1,0:T(8,128)S(1)} collective-permute-done((f32[2,384,64]{2,1,0:T(8,128)S(1)}, f32[2,384,64]{2,1,0:T(8,128)S(1)}, u32[]{:S(2)}, u32[]{:S(2)}) %collective-permute-start.8) | collective-permute-done | bytes 196640 | tf_op jit(solution)/shard_map/ppermute | solution.py:99
  104.9 5.7 %collective-permute-done.9 = f32[2,384,64]{2,1,0:T(8,128)} collective-permute-done((f32[2,384,64]{2,1,0:T(8,128)S(1)}, f32[2,384,64]{2,1,0:T(8,128)}, u32[]{:S(2)}, u32[]{:S(2)}) %collective-permute-start.9) | collective-permute-done | bytes 196640 | tf_op jit(solution)/shard_map/ppermute | solution.py:99
  110.6 1.4 %fusion.3 = f32[2,384,256]{2,1,0:T(8,128)S(1)} fusion(s32[]{:T(128)S(6)} %select_n.48, s32[]{:T(128)S(6)} %add.199, f32[2,256,256]{2,1,0:T(8,128)S(1)} %copy-done.2, f32[2,384,64]{2,1,0:T(8,128)} %collective-permute-done.9, f32[2,384,64]{2,1,0:T(8,128)S(1)} %collective-permute-done.8), kind=kLoop, calls=%fused_computation.12 | loop fusion | flops 393216 | bytes 1703944 | tf_op jit(solution)/shard_map/add | solution.py:115
  112.1 1.9 %collective-permute-start.10 = (f32[2,64,256]{2,1,0:T(8,128)S(1)}, f32[2,64,256]{2,1,0:T(8,128)S(1)}, u32[]{:S(2)}, u32[]{:S(2)}) collective-permute-start(f32[2,64,256]{2,1,0:T(8,128)S(1)} %get-tuple-element.7), channel_id=1, source_target_pairs={{0,32},{32,64},{64,96},{96,128},{128,160},{160,192},{192,224},{224... | collective-permute-start | bytes 393224 | tf_op jit(solution)/shard_map/ppermute | solution.py:99
  114.0 8.4 %collective-permute-start.11 = (f32[2,64,256]{2,1,0:T(8,128)S(1)}, f32[2,64,256]{2,1,0:T(8,128)S(1)}, u32[]{:S(2)}, u32[]{:S(2)}) collective-permute-start(f32[2,64,256]{2,1,0:T(8,128)S(1)} %get-tuple-element.8), channel_id=1, source_target_pairs={{32,0},{64,32},{96,64},{128,96},{160,128},{192,160},{224,192},{256... | collective-permute-start | bytes 393224 | tf_op jit(solution)/shard_map/ppermute | solution.py:99
  122.4 0.4 collective-permute-done.10
  122.8 2.4 %collective-permute-done.11 = f32[2,64,256]{2,1,0:T(8,128)S(1)} collective-permute-done((f32[2,64,256]{2,1,0:T(8,128)S(1)}, f32[2,64,256]{2,1,0:T(8,128)S(1)}, u32[]{:S(2)}, u32[]{:S(2)}) %collective-permute-start.11) | collective-permute-done | bytes 131104 | tf_op jit(solution)/shard_map/ppermute | solution.py:99
  125.2 1.0 fusion.6
  (21 shorter events, 0.1 us)
Async XLA Ops:
  1.0 22.4 %collective-permute-start = (f32[2,64,256]{2,1,0:T(8,128)S(1)}, f32[2,64,256]{2,1,0:T(8,128)S(1)}, u32[]{:S(2)}, u32[]{:S(2)}) collective-permute-start(f32[2,64,256]{2,1,0:T(8,128)S(1)} %get-tuple-element.16), channel_id=1, source_target_pairs={{0,32},{32,64},{64,96},{96,128},{128,160},{160,192},{192,224},{224... | collective-permute-start | bytes 393224 | tf_op jit(solution)/shard_map/ppermute | solution.py:99
  5.9 18.6 %collective-permute-start.1 = (f32[2,64,256]{2,1,0:T(8,128)S(1)}, f32[2,64,256]{2,1,0:T(8,128)S(1)}, u32[]{:S(2)}, u32[]{:S(2)}) collective-permute-start(f32[2,64,256]{2,1,0:T(8,128)S(1)} %get-tuple-element.15), channel_id=1, source_target_pairs={{32,0},{64,32},{96,64},{128,96},{160,128},{192,160},{224,192},{256... | collective-permute-start | bytes 393224 | tf_op jit(solution)/shard_map/ppermute | solution.py:99
  24.5 7.8 %copy-start.5 = (s32[1,1,1,2]{3,2,1,0:T(1,128)S(1)}, s32[1,1,1,2]{3,2,1,0:T(1,128)}, u32[]{:S(2)}) copy-start(s32[1,1,1,2]{3,2,1,0:T(1,128)} %param.6) | copy-start | bytes 28
  24.7 15.2 %collective-permute-start.2 = (f32[2,384,64]{2,1,0:T(8,128)S(1)}, f32[2,384,64]{2,1,0:T(8,128)S(1)}, u32[]{:S(2)}, u32[]{:S(2)}) collective-permute-start(f32[2,384,64]{2,1,0:T(8,128)S(1)} %get-tuple-element.9), channel_id=1, source_target_pairs={{0,1},{1,2},{2,3},{3,4},{4,5},{5,6},{6,7},{7,8},{8,9},{9,10},{10,1... | collective-permute-start | bytes 589832 | tf_op jit(solution)/shard_map/ppermute | solution.py:99
  30.4 10.3 %collective-permute-start.3 = (f32[2,384,64]{2,1,0:T(8,128)S(1)}, f32[2,384,64]{2,1,0:T(8,128)S(1)}, u32[]{:S(2)}, u32[]{:S(2)}) collective-permute-start(f32[2,384,64]{2,1,0:T(8,128)S(1)} %get-tuple-element.10), channel_id=1, source_target_pairs={{1,0},{2,1},{3,2},{4,3},{5,4},{6,5},{7,6},{8,7},{9,8},{10,9},{11,1... | collective-permute-start | bytes 589832 | tf_op jit(solution)/shard_map/ppermute | solution.py:99
  40.7 0.8 copy-start.3
  48.7 24.6 %copy-start.1 = (f32[2,256,256]{2,1,0:T(8,128)S(1)}, f32[2,256,256]{2,1,0:T(8,128)}, u32[]{:S(2)}) copy-start(f32[2,256,256]{2,1,0:T(8,128)} %shard_map.46) | copy-start | bytes 1572868
  48.9 19.7 %collective-permute-start.5 = (f32[2,136,256]{2,1,0:T(8,128)S(1)}, f32[2,136,256]{2,1,0:T(8,128)S(1)}, u32[]{:S(2)}, u32[]{:S(2)}) collective-permute-start(f32[2,136,256]{2,1,0:T(8,128)S(1)} %get-tuple-element.21), channel_id=1, source_target_pairs={{0,32},{32,64},{64,96},{96,128},{128,160},{160,192},{192,224},{224... | collective-permute-start | bytes 835592 | tf_op jit(solution)/shard_map/ppermute | solution.py:99
  50.9 19.9 %collective-permute-start.4 = (f32[2,136,256]{2,1,0:T(8,128)S(1)}, f32[2,136,256]{2,1,0:T(8,128)S(1)}, u32[]{:S(2)}, u32[]{:S(2)}) collective-permute-start(f32[2,136,256]{2,1,0:T(8,128)S(1)} %get-tuple-element.22), channel_id=1, source_target_pairs={{32,0},{64,32},{96,64},{128,96},{160,128},{192,160},{224,192},{256... | collective-permute-start | bytes 835592 | tf_op jit(solution)/shard_map/ppermute | solution.py:99
  74.3 5.3 %copy-start = (f32[2,3,256,256]{3,2,1,0:T(8,128)S(1)}, f32[2,3,256,256]{3,2,1,0:T(8,128)}, u32[]{:S(2)}) copy-start(f32[2,3,256,256]{3,2,1,0:T(8,128)} %probe_ref.3) | copy-start | bytes 4718596
  75.1 7.5 %collective-permute-start.6 = (f32[2,384,128]{2,1,0:T(8,128)}, f32[2,384,128]{2,1,0:T(8,128)S(1)}, u32[]{:S(2)}, u32[]{:S(2)}) collective-permute-start(f32[2,384,128]{2,1,0:T(8,128)} %get-tuple-element.5), channel_id=1, source_target_pairs={{0,1},{1,2},{2,3},{3,4},{4,5},{5,6},{6,7},{7,8},{8,9},{9,10},{10,1... | collective-permute-start | bytes 1179656 | tf_op jit(solution)/shard_map/ppermute | solution.py:99
  77.6 10.4 %collective-permute-start.7 = (f32[2,384,128]{2,1,0:T(8,128)S(1)}, f32[2,384,128]{2,1,0:T(8,128)}, u32[]{:S(2)}, u32[]{:S(2)}) collective-permute-start(f32[2,384,128]{2,1,0:T(8,128)S(1)} %get-tuple-element.6), channel_id=1, source_target_pairs={{1,0},{2,1},{3,2},{4,3},{5,4},{6,5},{7,6},{8,7},{9,8},{10,9},{11,1... | collective-permute-start | bytes 1179656 | tf_op jit(solution)/shard_map/ppermute | solution.py:99
  82.7 0.7 copy-start.4
  96.8 13.8 %copy-start.2 = (f32[2,256,256]{2,1,0:T(8,128)S(1)}, f32[2,256,256]{2,1,0:T(8,128)}, u32[]{:S(2)}) copy-start(f32[2,256,256]{2,1,0:T(8,128)} %shard_map.47) | copy-start | bytes 1572868
  98.3 6.6 %collective-permute-start.8 = (f32[2,384,64]{2,1,0:T(8,128)S(1)}, f32[2,384,64]{2,1,0:T(8,128)S(1)}, u32[]{:S(2)}, u32[]{:S(2)}) collective-permute-start(f32[2,384,64]{2,1,0:T(8,128)S(1)} %get-tuple-element.11), channel_id=1, source_target_pairs={{0,1},{1,2},{2,3},{3,4},{4,5},{5,6},{6,7},{7,8},{8,9},{9,10},{10,1... | collective-permute-start | bytes 589832 | tf_op jit(solution)/shard_map/ppermute | solution.py:99
  100.2 10.4 %collective-permute-start.9 = (f32[2,384,64]{2,1,0:T(8,128)S(1)}, f32[2,384,64]{2,1,0:T(8,128)}, u32[]{:S(2)}, u32[]{:S(2)}) collective-permute-start(f32[2,384,64]{2,1,0:T(8,128)S(1)} %get-tuple-element.12), channel_id=1, source_target_pairs={{1,0},{2,1},{3,2},{4,3},{5,4},{6,5},{7,6},{8,7},{9,8},{10,9},{11,1... | collective-permute-start | bytes 589832 | tf_op jit(solution)/shard_map/ppermute | solution.py:99
  112.1 10.7 %collective-permute-start.10 = (f32[2,64,256]{2,1,0:T(8,128)S(1)}, f32[2,64,256]{2,1,0:T(8,128)S(1)}, u32[]{:S(2)}, u32[]{:S(2)}) collective-permute-start(f32[2,64,256]{2,1,0:T(8,128)S(1)} %get-tuple-element.7), channel_id=1, source_target_pairs={{0,32},{32,64},{64,96},{96,128},{128,160},{160,192},{192,224},{224... | collective-permute-start | bytes 393224 | tf_op jit(solution)/shard_map/ppermute | solution.py:99
  114.0 11.2 %collective-permute-start.11 = (f32[2,64,256]{2,1,0:T(8,128)S(1)}, f32[2,64,256]{2,1,0:T(8,128)S(1)}, u32[]{:S(2)}, u32[]{:S(2)}) collective-permute-start(f32[2,64,256]{2,1,0:T(8,128)S(1)} %get-tuple-element.8), channel_id=1, source_target_pairs={{32,0},{64,32},{96,64},{128,96},{160,128},{192,160},{224,192},{256... | collective-permute-start | bytes 393224 | tf_op jit(solution)/shard_map/ppermute | solution.py:99

commit v14 on v12

--- a/solution.py
+++ b/solution.py
@@ -30,9 +30,16 @@
 INTERPRET = False
 
 
-def gradient_kernel(window_ref, probe_ref, measured_ref, table_re_ref, table_im_ref, out_ref, spectrum_ref,
-                    exit_ref):
+def gradient_kernel(window_ref, probe_hbm, measured_ref, table_re_ref, table_im_ref, out_ref, spectrum_ref,
+                    exit_ref, probe_ref, arrived):
     modes = probe_ref.shape[1]
+    copies = [
+        [pltpu.make_async_copy(probe_hbm.at[p, k], probe_ref.at[p, k], arrived.at[p, k]) for p in range(2)]
+        for k in range(modes)
+    ]
+    for pair in copies:
+        for copy in pair:
+            copy.start()
     table_re = table_re_ref[...]
     table_im = table_im_ref[...]
 
@@ -48,6 +55,8 @@
 
     power = None
     for k in range(modes):
+        for copy in copies[k]:
+            copy.wait()
         exit_re, exit_im = exit_wave(k)
         exit_ref[0, k] = exit_re
         exit_ref[1, k] = exit_im
@@ -88,7 +97,15 @@
     return pl.pallas_call(
         gradient_kernel,
         out_shape=jax.ShapeDtypeStruct((2, rows, cols), jnp.float32),
-        scratch_shapes=[pltpu.VMEM((2, modes, rows, cols), jnp.float32)] * 2,
+        in_specs=[
+            pl.BlockSpec(memory_space=pltpu.VMEM),
+            pl.BlockSpec(memory_space=pl.ANY),
+            pl.BlockSpec(memory_space=pltpu.VMEM),
+            pl.BlockSpec(memory_space=pltpu.VMEM),
+            pl.BlockSpec(memory_space=pltpu.VMEM),
+        ],
+        scratch_shapes=[pltpu.VMEM((2, modes, rows, cols), jnp.float32)] * 3
+        + [pltpu.SemaphoreType.DMA((2, modes))],
         interpret=INTERPRET,
     )(window, probe_modes, measured, table_re, table_im)
 

time: 125 us -> 128 us (1.024)
  Pallas kernels: 10.4 us -> 12.5 us
    pallas_call x2, Pallas kernels: 10.4 us -> 12.5 us  [pattern_gradient(): pl.pallas_call(gradient_kernel, out_shape=jax.ShapeDtypeStruct((2, rows,...]
where the time goes in v14:
time: 128 us; the launch traced here: 127 us
  starting transfers between devices  54.3 us (42%)
  waiting for transfers between devices  26 us (20%)
  local copies, waits for them, and re-layouts  15.9 us (12%)
  Pallas kernels  12.5 us (10%)
  other arithmetic  9.38 us (7%)
  between operations  8.59 us (7%)
    ppermute x12, starting transfers between devices, from_neighbor(): return lax.ppermute(x, axis, pairs)  54.3 us
    ppermute x12, waiting for transfers between devices, from_neighbor(): return lax.ppermute(x, axis, pairs)  26 us
    pallas_call x2, Pallas kernels, pattern_gradient(): pl.pallas_call(gradient_kernel, out_shape=jax.ShapeDtypeStruct((2, rows,...  12.5 us
    another operation x1, local copies, waits for them, and re-layouts, rows_from_neighbors(): jnp.stack([offset[0], offset[1]] + [offset[0]] * 6).astype(jnp.float32)  5.19 us
    slice x5, local copies, waits for them, and re-layouts, neighbor_sum(): piece = lax.slice_in_dim(frame, low - shift, high - shift, axis=dim)  3.41 us
    select_n x1, other arithmetic, on_device(): extended = jnp.where(mask[None], extended + total / peak_power, 0.0)  2.59 us
  transfers between devices with their start and end apart: 12, of which 9 were waited for; matrix products, arithmetic and copies ran while one was open for 8% of the time, Pallas kernels for 0%

profile of v14, /device:TPU:87, one launch (start us, length us, event | category | flops | bytes accessed | tf_op | source)
XLA Modules:
  0.0 126.7 jit_solution(4996704469917257018)
XLA Ops:
  0.0 1.0 fusion.23
  1.0 4.9 %collective-permute-start = (f32[2,64,256]{2,1,0:T(8,128)S(1)}, f32[2,64,256]{2,1,0:T(8,128)S(1)}, u32[]{:S(2)}, u32[]{:S(2)}) collective-permute-start(f32[2,64,256]{2,1,0:T(8,128)S(1)} %get-tuple-element.15), channel_id=1, source_target_pairs={{0,32},{32,64},{64,96},{96,128},{128,160},{160,192},{192,224},{224... | collective-permute-start | bytes 393224 | tf_op jit(solution)/shard_map/ppermute | solution.py:116
  5.9 14.5 %collective-permute-start.1 = (f32[2,64,256]{2,1,0:T(8,128)S(1)}, f32[2,64,256]{2,1,0:T(8,128)S(1)}, u32[]{:S(2)}, u32[]{:S(2)}) collective-permute-start(f32[2,64,256]{2,1,0:T(8,128)S(1)} %get-tuple-element.16), channel_id=1, source_target_pairs={{32,0},{64,32},{96,64},{128,96},{160,128},{192,160},{224,192},{256... | collective-permute-start | bytes 393224 | tf_op jit(solution)/shard_map/ppermute | solution.py:116
  20.4 1.4 %fusion.27 = (s32[1,1]{1,0:T(1,128)}, s32[1,1]{1,0:T(1,128)}) fusion(s32[1,2]{1,0:T(1,128)} %bitcast.22), kind=kLoop, calls=%fused_computation.50 | loop fusion | bytes 16 | tf_op jit(solution)/shard_map/slice | solution.py:188
  24.3 0.4 collective-permute-done
  24.8 1.1 pad_add_fusion.1
  25.9 0.2 fusion.21
  26.0 4.8 %collective-permute-start.2 = (f32[2,384,64]{2,1,0:T(8,128)S(1)}, f32[2,384,64]{2,1,0:T(8,128)S(1)}, u32[]{:S(2)}, u32[]{:S(2)}) collective-permute-start(f32[2,384,64]{2,1,0:T(8,128)S(1)} %get-tuple-element.9), channel_id=1, source_target_pairs={{0,1},{1,2},{2,3},{3,4},{4,5},{5,6},{6,7},{7,8},{8,9},{9,10},{10,1... | collective-permute-start | bytes 589832 | tf_op jit(solution)/shard_map/ppermute | solution.py:116
  30.8 1.9 %collective-permute-start.3 = (f32[2,384,64]{2,1,0:T(8,128)S(1)}, f32[2,384,64]{2,1,0:T(8,128)S(1)}, u32[]{:S(2)}, u32[]{:S(2)}) collective-permute-start(f32[2,384,64]{2,1,0:T(8,128)S(1)} %get-tuple-element.10), channel_id=1, source_target_pairs={{1,0},{2,1},{3,2},{4,3},{5,4},{6,5},{7,6},{8,7},{9,8},{10,9},{11,1... | collective-permute-start | bytes 589832 | tf_op jit(solution)/shard_map/ppermute | solution.py:116
  32.7 0.7 fusion.26
  33.4 5.2 %stack.9 = s32[8]{0:T(128)S(1)} concatenate(s32[1]{0:T(128)} %bitcast.10, s32[1]{0:T(128)} %bitcast.11, s32[1]{0:T(128)} %bitcast.10, s32[1]{0:T(128)} %bitcast.10, s32[1]{0:T(128)} %bitcast.10, s32[1]{0:T(128)} %bitcast.10, s32[1]{0:T(128)} %bitcast.10, s32[1]{0:T(128)} %bitcast.10), dimensions={0} | concatenate | bytes 64 | tf_op jit(solution)/shard_map/stack | solution.py:140
  38.6 1.8 %multiply_convert_fusion = (bf16[256,256]{1,0:T(8,128)(2,1)}, bf16[256,256]{1,0:T(8,128)(2,1)}) fusion(), kind=kLoop, calls=%fused_computation.27 | loop fusion | flops 1245184 | bytes 262144 | tf_op jit(solution)/shard_map/convert_element_type | solution.py:26
  40.4 0.7 collective-permute-done.3
  41.1 0.5 pad_add_fusion
  41.6 0.3 copy-done.3
  41.9 1.0 constant_dynamic-slice_fusion.1.window_ref
  42.9 6.2 %shard_map.46 = f32[2,256,256]{2,1,0:T(8,128)} custom-call(f32[2,256,256]{2,1,0:T(8,128)} %constant_dynamic-slice_fusion.1.window_ref, f32[2,3,256,256]{3,2,1,0:T(8,128)} %probe_hbm.3, f32[256,256]{1,0:T(8,128)} %bitcast.20, bf16[256,256]{1,0:T(8,128)(2,1)} %get-tuple-element.28.table_re_ref, bf16[256,256]{1,0:T(8,128)(2,1)} %get-tuple-element.27.table_im_ref), custom_call_target="tpu_custom_call" | custom-call | tf_op jit(solution)/shard_map/pallas_call | solution.py:97
  49.1 1.1 fusion.22
  50.2 0.1 pad_maximum_fusion.1
  50.3 2.1 %collective-permute-start.5 = (f32[2,136,256]{2,1,0:T(8,128)S(1)}, f32[2,136,256]{2,1,0:T(8,128)S(1)}, u32[]{:S(2)}, u32[]{:S(2)}) collective-permute-start(f32[2,136,256]{2,1,0:T(8,128)S(1)} %get-tuple-element.21), channel_id=1, source_target_pairs={{0,32},{32,64},{64,96},{96,128},{128,160},{160,192},{192,224},{224... | collective-permute-start | bytes 835592 | tf_op jit(solution)/shard_map/ppermute | solution.py:116
  52.4 7.6 %collective-permute-start.4 = (f32[2,136,256]{2,1,0:T(8,128)S(1)}, f32[2,136,256]{2,1,0:T(8,128)S(1)}, u32[]{:S(2)}, u32[]{:S(2)}) collective-permute-start(f32[2,136,256]{2,1,0:T(8,128)S(1)} %get-tuple-element.22), channel_id=1, source_target_pairs={{32,0},{64,32},{96,64},{128,96},{160,128},{192,160},{224,192},{256... | collective-permute-start | bytes 835592 | tf_op jit(solution)/shard_map/ppermute | solution.py:116
  62.5 6.2 %collective-permute-done.5 = f32[2,136,256]{2,1,0:T(8,128)S(1)} collective-permute-done((f32[2,136,256]{2,1,0:T(8,128)S(1)}, f32[2,136,256]{2,1,0:T(8,128)S(1)}, u32[]{:S(2)}, u32[]{:S(2)}) %collective-permute-start.5) | collective-permute-done | bytes 278560 | tf_op jit(solution)/shard_map/ppermute | solution.py:116
  68.7 0.6 fusion.24
  69.9 0.5 fusion.25
  72.4 1.0 fusion
  73.5 0.8 fusion.19
  74.3 2.9 %collective-permute-start.6 = (f32[2,384,128]{2,1,0:T(8,128)}, f32[2,384,128]{2,1,0:T(8,128)S(1)}, u32[]{:S(2)}, u32[]{:S(2)}) collective-permute-start(f32[2,384,128]{2,1,0:T(8,128)} %get-tuple-element.5), channel_id=1, source_target_pairs={{0,1},{1,2},{2,3},{3,4},{4,5},{5,6},{6,7},{7,8},{8,9},{9,10},{10,1... | collective-permute-start | bytes 1179656 | tf_op jit(solution)/shard_map/ppermute | solution.py:116
  77.1 1.9 %collective-permute-start.7 = (f32[2,384,128]{2,1,0:T(8,128)S(1)}, f32[2,384,128]{2,1,0:T(8,128)}, u32[]{:S(2)}, u32[]{:S(2)}) collective-permute-start(f32[2,384,128]{2,1,0:T(8,128)S(1)} %get-tuple-element.6), channel_id=1, source_target_pairs={{1,0},{2,1},{3,2},{4,3},{5,4},{6,5},{7,6},{8,7},{9,8},{10,9},{11,1... | collective-permute-start | bytes 1179656 | tf_op jit(solution)/shard_map/ppermute | solution.py:116
  79.1 0.1 multiply_reduce_fusion
  79.2 0.7 reduce_max.9
  80.6 0.1 broadcast_and_fusion
  80.7 1.5 %collective-permute-done.6 = f32[2,384,128]{2,1,0:T(8,128)S(1)} collective-permute-done((f32[2,384,128]{2,1,0:T(8,128)}, f32[2,384,128]{2,1,0:T(8,128)S(1)}, u32[]{:S(2)}, u32[]{:S(2)}) %collective-permute-start.6) | collective-permute-done | bytes 393248 | tf_op jit(solution)/shard_map/ppermute | solution.py:116
  82.2 0.7 copy-done.4
  82.9 4.7 %collective-permute-done.7 = f32[2,384,128]{2,1,0:T(8,128)} collective-permute-done((f32[2,384,128]{2,1,0:T(8,128)S(1)}, f32[2,384,128]{2,1,0:T(8,128)}, u32[]{:S(2)}, u32[]{:S(2)}) %collective-permute-start.7) | collective-permute-done | bytes 393248 | tf_op jit(solution)/shard_map/ppermute | solution.py:116
  87.6 2.6 %add_select_fusion = f32[2,384,384]{2,1,0:T(8,128)S(1)} fusion(f32[2,384,128]{2,1,0:T(8,128)} %collective-permute-done.7, f32[2,384,128]{2,1,0:T(8,128)} %copy-done.4, f32[]{:T(128)S(6)} %add.205, pred[384,384]{1,0:T(8,128)(4,1)S(1)} %broadcast_and_fusion, s32[]{:T(128)S(6)} %select_n.52, s32[]{:T(128)S(6)} %select_n.53, f32[2,128,256]{2,1,0:T(8,128)S(1)} %slice.112, ...), kind=kLoop, calls=%fused_computation.9 | loop fusion | flops 2654208 | bytes 4341788 | tf_op jit(solution)/shard_map/jit(_where)/select_n | solution.py:201
  90.1 1.0 constant_dynamic-slice_fusion.window_ref
  91.2 6.3 %shard_map.47 = f32[2,256,256]{2,1,0:T(8,128)} custom-call(f32[2,256,256]{2,1,0:T(8,128)} %constant_dynamic-slice_fusion.window_ref, f32[2,3,256,256]{3,2,1,0:T(8,128)} %probe_hbm.3, f32[256,256]{1,0:T(8,128)} %bitcast.21, bf16[256,256]{1,0:T(8,128)(2,1)} %get-tuple-element.28.table_re_ref, bf16[256,256]{1,0:T(8,128)(2,1)} %get-tuple-element.27.table_im_ref), custom_call_target="tpu_custom_call" | custom-call | tf_op jit(solution)/shard_map/pallas_call | solution.py:97
  97.4 1.4 %pad_dynamic-slice_fusion.1 = (f32[2,384,64]{2,1,0:T(8,128)S(1)}, f32[2,384,64]{2,1,0:T(8,128)S(1)}) fusion(s32[]{:T(128)S(6)} %select_n.48, s32[]{:T(128)S(6)} %add.212, f32[2,256,256]{2,1,0:T(8,128)} %shard_map.47, s32[]{:T(128)S(6)} %select_n.49), kind=kLoop, calls=%fused_computation.1 | loop fusion | bytes 917516 | tf_op jit(solution)/shard_map/slice | solution.py:126
  98.9 1.9 %collective-permute-start.8 = (f32[2,384,64]{2,1,0:T(8,128)S(1)}, f32[2,384,64]{2,1,0:T(8,128)S(1)}, u32[]{:S(2)}, u32[]{:S(2)}) collective-permute-start(f32[2,384,64]{2,1,0:T(8,128)S(1)} %get-tuple-element.11), channel_id=1, source_target_pairs={{0,1},{1,2},{2,3},{3,4},{4,5},{5,6},{6,7},{7,8},{8,9},{9,10},{10,1... | collective-permute-start | bytes 589832 | tf_op jit(solution)/shard_map/ppermute | solution.py:116
  100.8 2.4 %collective-permute-start.9 = (f32[2,384,64]{2,1,0:T(8,128)S(1)}, f32[2,384,64]{2,1,0:T(8,128)S(1)}, u32[]{:S(2)}, u32[]{:S(2)}) collective-permute-start(f32[2,384,64]{2,1,0:T(8,128)S(1)} %get-tuple-element.12), channel_id=1, source_target_pairs={{1,0},{2,1},{3,2},{4,3},{5,4},{6,5},{7,6},{8,7},{9,8},{10,9},{11,1... | collective-permute-start | bytes 589832 | tf_op jit(solution)/shard_map/ppermute | solution.py:116
  103.2 2.3 %collective-permute-done.8 = f32[2,384,64]{2,1,0:T(8,128)S(1)} collective-permute-done((f32[2,384,64]{2,1,0:T(8,128)S(1)}, f32[2,384,64]{2,1,0:T(8,128)S(1)}, u32[]{:S(2)}, u32[]{:S(2)}) %collective-permute-start.8) | collective-permute-done | bytes 196640 | tf_op jit(solution)/shard_map/ppermute | solution.py:116
  105.5 5.6 %collective-permute-done.9 = f32[2,384,64]{2,1,0:T(8,128)S(1)} collective-permute-done((f32[2,384,64]{2,1,0:T(8,128)S(1)}, f32[2,384,64]{2,1,0:T(8,128)S(1)}, u32[]{:S(2)}, u32[]{:S(2)}) %collective-permute-start.9) | collective-permute-done | bytes 196640 | tf_op jit(solution)/shard_map/ppermute | solution.py:116
  111.1 0.4 fusion.3
  111.6 1.9 %collective-permute-start.10 = (f32[2,64,256]{2,1,0:T(8,128)S(1)}, f32[2,64,256]{2,1,0:T(8,128)S(1)}, u32[]{:S(2)}, u32[]{:S(2)}) collective-permute-start(f32[2,64,256]{2,1,0:T(8,128)S(1)} %get-tuple-element.7), channel_id=1, source_target_pairs={{0,32},{32,64},{64,96},{96,128},{128,160},{160,192},{192,224},{224... | collective-permute-start | bytes 393224 | tf_op jit(solution)/shard_map/ppermute | solution.py:116
  113.5 7.6 %collective-permute-start.11 = (f32[2,64,256]{2,1,0:T(8,128)S(1)}, f32[2,64,256]{2,1,0:T(8,128)S(1)}, u32[]{:S(2)}, u32[]{:S(2)}) collective-permute-start(f32[2,64,256]{2,1,0:T(8,128)S(1)} %get-tuple-element.8), channel_id=1, source_target_pairs={{32,0},{64,32},{96,64},{128,96},{160,128},{192,160},{224,192},{256... | collective-permute-start | bytes 393224 | tf_op jit(solution)/shard_map/ppermute | solution.py:116
  121.1 1.9 %collective-permute-done.10 = f32[2,64,256]{2,1,0:T(8,128)S(1)} collective-permute-done((f32[2,64,256]{2,1,0:T(8,128)S(1)}, f32[2,64,256]{2,1,0:T(8,128)S(1)}, u32[]{:S(2)}, u32[]{:S(2)}) %collective-permute-start.10) | collective-permute-done | bytes 131104 | tf_op jit(solution)/shard_map/ppermute | solution.py:116
  123.0 2.7 %collective-permute-done.11 = f32[2,64,256]{2,1,0:T(8,128)S(1)} collective-permute-done((f32[2,64,256]{2,1,0:T(8,128)S(1)}, f32[2,64,256]{2,1,0:T(8,128)S(1)}, u32[]{:S(2)}, u32[]{:S(2)}) %collective-permute-start.11) | collective-permute-done | bytes 131104 | tf_op jit(solution)/shard_map/ppermute | solution.py:116
  125.7 1.0 fusion.6
  (19 shorter events, 0.1 us)
Async XLA Ops:
  1.0 23.8 %collective-permute-start = (f32[2,64,256]{2,1,0:T(8,128)S(1)}, f32[2,64,256]{2,1,0:T(8,128)S(1)}, u32[]{:S(2)}, u32[]{:S(2)}) collective-permute-start(f32[2,64,256]{2,1,0:T(8,128)S(1)} %get-tuple-element.15), channel_id=1, source_target_pairs={{0,32},{32,64},{64,96},{96,128},{128,160},{160,192},{192,224},{224... | collective-permute-start | bytes 393224 | tf_op jit(solution)/shard_map/ppermute | solution.py:116
  5.9 18.9 %collective-permute-start.1 = (f32[2,64,256]{2,1,0:T(8,128)S(1)}, f32[2,64,256]{2,1,0:T(8,128)S(1)}, u32[]{:S(2)}, u32[]{:S(2)}) collective-permute-start(f32[2,64,256]{2,1,0:T(8,128)S(1)} %get-tuple-element.16), channel_id=1, source_target_pairs={{32,0},{64,32},{96,64},{128,96},{160,128},{192,160},{224,192},{256... | collective-permute-start | bytes 393224 | tf_op jit(solution)/shard_map/ppermute | solution.py:116
  25.9 6.9 %copy-start.5 = (s32[1,1,1,2]{3,2,1,0:T(1,128)S(1)}, s32[1,1,1,2]{3,2,1,0:T(1,128)}, u32[]{:S(2)}) copy-start(s32[1,1,1,2]{3,2,1,0:T(1,128)} %param.6) | copy-start | bytes 28
  26.0 14.3 %collective-permute-start.2 = (f32[2,384,64]{2,1,0:T(8,128)S(1)}, f32[2,384,64]{2,1,0:T(8,128)S(1)}, u32[]{:S(2)}, u32[]{:S(2)}) collective-permute-start(f32[2,384,64]{2,1,0:T(8,128)S(1)} %get-tuple-element.9), channel_id=1, source_target_pairs={{0,1},{1,2},{2,3},{3,4},{4,5},{5,6},{6,7},{7,8},{8,9},{9,10},{10,1... | collective-permute-start | bytes 589832 | tf_op jit(solution)/shard_map/ppermute | solution.py:116
  30.8 10.3 %collective-permute-start.3 = (f32[2,384,64]{2,1,0:T(8,128)S(1)}, f32[2,384,64]{2,1,0:T(8,128)S(1)}, u32[]{:S(2)}, u32[]{:S(2)}) collective-permute-start(f32[2,384,64]{2,1,0:T(8,128)S(1)} %get-tuple-element.10), channel_id=1, source_target_pairs={{1,0},{2,1},{3,2},{4,3},{5,4},{6,5},{7,6},{8,7},{9,8},{10,9},{11,1... | collective-permute-start | bytes 589832 | tf_op jit(solution)/shard_map/ppermute | solution.py:116
  41.1 0.8 copy-start.3
  50.2 22.2 %copy-start.1 = (f32[2,256,256]{2,1,0:T(8,128)S(1)}, f32[2,256,256]{2,1,0:T(8,128)}, u32[]{:S(2)}) copy-start(f32[2,256,256]{2,1,0:T(8,128)} %shard_map.46) | copy-start | bytes 1572868
  50.3 18.3 %collective-permute-start.5 = (f32[2,136,256]{2,1,0:T(8,128)S(1)}, f32[2,136,256]{2,1,0:T(8,128)S(1)}, u32[]{:S(2)}, u32[]{:S(2)}) collective-permute-start(f32[2,136,256]{2,1,0:T(8,128)S(1)} %get-tuple-element.21), channel_id=1, source_target_pairs={{0,32},{32,64},{64,96},{96,128},{128,160},{160,192},{192,224},{224... | collective-permute-start | bytes 835592 | tf_op jit(solution)/shard_map/ppermute | solution.py:116
  52.4 17.5 %collective-permute-start.4 = (f32[2,136,256]{2,1,0:T(8,128)S(1)}, f32[2,136,256]{2,1,0:T(8,128)S(1)}, u32[]{:S(2)}, u32[]{:S(2)}) collective-permute-start(f32[2,136,256]{2,1,0:T(8,128)S(1)} %get-tuple-element.22), channel_id=1, source_target_pairs={{32,0},{64,32},{96,64},{128,96},{160,128},{192,160},{224,192},{256... | collective-permute-start | bytes 835592 | tf_op jit(solution)/shard_map/ppermute | solution.py:116
  73.4 5.6 %copy-start = (f32[2,3,256,256]{3,2,1,0:T(8,128)S(1)}, f32[2,3,256,256]{3,2,1,0:T(8,128)}, u32[]{:S(2)}) copy-start(f32[2,3,256,256]{3,2,1,0:T(8,128)} %probe_hbm.3) | copy-start | bytes 4718596
  74.3 7.9 %collective-permute-start.6 = (f32[2,384,128]{2,1,0:T(8,128)}, f32[2,384,128]{2,1,0:T(8,128)S(1)}, u32[]{:S(2)}, u32[]{:S(2)}) collective-permute-start(f32[2,384,128]{2,1,0:T(8,128)} %get-tuple-element.5), channel_id=1, source_target_pairs={{0,1},{1,2},{2,3},{3,4},{4,5},{5,6},{6,7},{7,8},{8,9},{9,10},{10,1... | collective-permute-start | bytes 1179656 | tf_op jit(solution)/shard_map/ppermute | solution.py:116
  77.1 10.4 %collective-permute-start.7 = (f32[2,384,128]{2,1,0:T(8,128)S(1)}, f32[2,384,128]{2,1,0:T(8,128)}, u32[]{:S(2)}, u32[]{:S(2)}) collective-permute-start(f32[2,384,128]{2,1,0:T(8,128)S(1)} %get-tuple-element.6), channel_id=1, source_target_pairs={{1,0},{2,1},{3,2},{4,3},{5,4},{6,5},{7,6},{8,7},{9,8},{10,9},{11,1... | collective-permute-start | bytes 1179656 | tf_op jit(solution)/shard_map/ppermute | solution.py:116
  82.2 0.7 copy-start.4
  97.4 13.7 %copy-start.2 = (f32[2,256,256]{2,1,0:T(8,128)S(1)}, f32[2,256,256]{2,1,0:T(8,128)}, u32[]{:S(2)}) copy-start(f32[2,256,256]{2,1,0:T(8,128)} %shard_map.47) | copy-start | bytes 1572868
  98.9 6.6 %collective-permute-start.8 = (f32[2,384,64]{2,1,0:T(8,128)S(1)}, f32[2,384,64]{2,1,0:T(8,128)S(1)}, u32[]{:S(2)}, u32[]{:S(2)}) collective-permute-start(f32[2,384,64]{2,1,0:T(8,128)S(1)} %get-tuple-element.11), channel_id=1, source_target_pairs={{0,1},{1,2},{2,3},{3,4},{4,5},{5,6},{6,7},{7,8},{8,9},{9,10},{10,1... | collective-permute-start | bytes 589832 | tf_op jit(solution)/shard_map/ppermute | solution.py:116
  100.8 10.3 %collective-permute-start.9 = (f32[2,384,64]{2,1,0:T(8,128)S(1)}, f32[2,384,64]{2,1,0:T(8,128)S(1)}, u32[]{:S(2)}, u32[]{:S(2)}) collective-permute-start(f32[2,384,64]{2,1,0:T(8,128)S(1)} %get-tuple-element.12), channel_id=1, source_target_pairs={{1,0},{2,1},{3,2},{4,3},{5,4},{6,5},{7,6},{8,7},{9,8},{10,9},{11,1... | collective-permute-start | bytes 589832 | tf_op jit(solution)/shard_map/ppermute | solution.py:116
  111.6 11.4 %collective-permute-start.10 = (f32[2,64,256]{2,1,0:T(8,128)S(1)}, f32[2,64,256]{2,1,0:T(8,128)S(1)}, u32[]{:S(2)}, u32[]{:S(2)}) collective-permute-start(f32[2,64,256]{2,1,0:T(8,128)S(1)} %get-tuple-element.7), channel_id=1, source_target_pairs={{0,32},{32,64},{64,96},{96,128},{128,160},{160,192},{192,224},{224... | collective-permute-start | bytes 393224 | tf_op jit(solution)/shard_map/ppermute | solution.py:116
  113.5 12.2 %collective-permute-start.11 = (f32[2,64,256]{2,1,0:T(8,128)S(1)}, f32[2,64,256]{2,1,0:T(8,128)S(1)}, u32[]{:S(2)}, u32[]{:S(2)}) collective-permute-start(f32[2,64,256]{2,1,0:T(8,128)S(1)} %get-tuple-element.8), channel_id=1, source_target_pairs={{32,0},{64,32},{96,64},{128,96},{160,128},{192,160},{224,192},{256... | collective-permute-start | bytes 393224 | tf_op jit(solution)/shard_map/ppermute | solution.py:116

commit v15 on v10

--- a/solution.py
+++ b/solution.py
@@ -30,7 +30,8 @@
 INTERPRET = False
 
 
-def gradient_kernel(window_ref, probe_ref, measured_ref, table_re_ref, table_im_ref, out_ref, spectrum_ref):
+def gradient_kernel(window_ref, probe_ref, measured_ref, table_re_ref, table_im_ref, out_ref, spectrum_ref,
+                    exit_ref):
     modes = probe_ref.shape[1]
     table_re = table_re_ref[...]
     table_im = table_im_ref[...]
@@ -48,6 +49,8 @@
     power = None
     for k in range(modes):
         exit_re, exit_im = exit_wave(k)
+        exit_ref[0, k] = exit_re
+        exit_ref[1, k] = exit_im
         exit_re = exit_re.astype(jnp.bfloat16)
         exit_im = exit_im.astype(jnp.bfloat16)
         half_re = (product(table_re, exit_re) - product(table_im, exit_im)).astype(jnp.bfloat16)
@@ -68,9 +71,8 @@
         back_im = (product(table_re, fixed_im) - product(table_im, fixed_re)).astype(jnp.bfloat16)
         revised_re = product(back_re, table_re) + product(back_im, table_im)
         revised_im = product(back_im, table_re) - product(back_re, table_im)
-        exit_re, exit_im = exit_wave(k)
-        residue_re = revised_re - exit_re
-        residue_im = revised_im - exit_im
+        residue_re = revised_re - exit_ref[0, k]
+        residue_im = revised_im - exit_ref[1, k]
         probe_re = probe_ref[0, k]
         probe_im = probe_ref[1, k]
         part_re = probe_re * residue_re + probe_im * residue_im
@@ -86,7 +88,7 @@
     return pl.pallas_call(
         gradient_kernel,
         out_shape=jax.ShapeDtypeStruct((2, rows, cols), jnp.float32),
-        scratch_shapes=[pltpu.VMEM((2, modes, rows, cols), jnp.float32)],
+        scratch_shapes=[pltpu.VMEM((2, modes, rows, cols), jnp.float32)] * 2,
         interpret=INTERPRET,
     )(window, probe_modes, measured, table_re, table_im)
 

time: 127 us -> 127 us (level)
  no operation moved by 1% of the time
where the time goes in v15:
time: 127 us
  starting transfers between devices  63 us (50%)
  waiting for transfers between devices  26.6 us (21%)
  Pallas kernels  10.3 us (8%)
  local copies, waits for them, and re-layouts  9.11 us (7%)
  other arithmetic  9.01 us (7%)
  between operations  8.57 us (7%)
    ppermute x12, starting transfers between devices, from_neighbor(): return lax.ppermute(x, axis, pairs)  63 us
    ppermute x12, waiting for transfers between devices, from_neighbor(): return lax.ppermute(x, axis, pairs)  26.6 us
    pallas_call x2, Pallas kernels, pattern_gradient(): pl.pallas_call(gradient_kernel, out_shape=jax.ShapeDtypeStruct((2, rows,...  10.3 us
  transfers between devices with their start and end apart: 12, of which 9 were waited for; matrix products, arithmetic and copies ran while one was open for 4% of the time, Pallas kernels for 0%

profile of v15, /device:TPU:112, one launch (start us, length us, event | category | flops | bytes accessed | tf_op | source)
XLA Modules:
  0.0 126.5 jit_solution(8525786519351525823)
XLA Ops:
  0.0 1.0 fusion.23
  1.1 0.7 convert_bitcast_fusion
  1.7 0.1 compare_select_fusion
  1.8 0.1 pad_maximum_fusion.1
  1.9 5.2 %collective-permute-start = (f32[2,72,256]{2,1,0:T(8,128)S(1)}, f32[2,72,256]{2,1,0:T(8,128)S(1)}, u32[]{:S(2)}, u32[]{:S(2)}) collective-permute-start(f32[2,72,256]{2,1,0:T(8,128)S(1)} %get-tuple-element.21), channel_id=1, source_target_pairs={{0,32},{32,64},{64,96},{96,128},{128,160},{160,192},{192,224},{224... | collective-permute-start | bytes 442376 | tf_op jit(solution)/shard_map/ppermute | solution.py:99
  7.1 15.4 %collective-permute-start.1 = (f32[2,72,256]{2,1,0:T(8,128)S(1)}, f32[2,72,256]{2,1,0:T(8,128)S(1)}, u32[]{:S(2)}, u32[]{:S(2)}) collective-permute-start(f32[2,72,256]{2,1,0:T(8,128)S(1)} %get-tuple-element.22), channel_id=1, source_target_pairs={{32,0},{64,32},{96,64},{128,96},{160,128},{192,160},{224,192},{256... | collective-permute-start | bytes 442376 | tf_op jit(solution)/shard_map/ppermute | solution.py:99
  22.5 4.4 %collective-permute-done = f32[2,72,256]{2,1,0:T(8,128)S(1)} collective-permute-done((f32[2,72,256]{2,1,0:T(8,128)S(1)}, f32[2,72,256]{2,1,0:T(8,128)S(1)}, u32[]{:S(2)}, u32[]{:S(2)}) %collective-permute-start) | collective-permute-done | bytes 147488 | tf_op jit(solution)/shard_map/ppermute | solution.py:99
  27.0 0.1 pad_maximum_fusion
  27.0 0.2 fusion.21
  27.2 1.9 %collective-permute-start.2 = (f32[2,384,64]{2,1,0:T(8,128)S(1)}, f32[2,384,64]{2,1,0:T(8,128)S(1)}, u32[]{:S(2)}, u32[]{:S(2)}) collective-permute-start(f32[2,384,64]{2,1,0:T(8,128)S(1)} %get-tuple-element.9), channel_id=1, source_target_pairs={{0,1},{1,2},{2,3},{3,4},{4,5},{5,6},{6,7},{7,8},{8,9},{9,10},{10,1... | collective-permute-start | bytes 589832 | tf_op jit(solution)/shard_map/ppermute | solution.py:99
  29.1 6.6 %collective-permute-start.3 = (f32[2,384,64]{2,1,0:T(8,128)S(1)}, f32[2,384,64]{2,1,0:T(8,128)S(1)}, u32[]{:S(2)}, u32[]{:S(2)}) collective-permute-start(f32[2,384,64]{2,1,0:T(8,128)S(1)} %get-tuple-element.10), channel_id=1, source_target_pairs={{1,0},{2,1},{3,2},{4,3},{5,4},{6,5},{7,6},{8,7},{9,8},{10,9},{11,1... | collective-permute-start | bytes 589832 | tf_op jit(solution)/shard_map/ppermute | solution.py:99
  35.8 0.6 fusion.26
  38.9 1.8 %multiply_convert_fusion = (bf16[256,256]{1,0:T(8,128)(2,1)}, bf16[256,256]{1,0:T(8,128)(2,1)}) fusion(), kind=kLoop, calls=%fused_computation.25 | loop fusion | flops 1245184 | bytes 262144 | tf_op jit(solution)/shard_map/convert_element_type | solution.py:26
  40.7 0.4 collective-permute-done.3
  41.0 0.5 pad_add_fusion
  41.5 1.0 constant_dynamic-slice_fusion.1.window_ref
  42.5 5.2 %shard_map.46 = f32[2,256,256]{2,1,0:T(8,128)} custom-call(f32[2,256,256]{2,1,0:T(8,128)} %constant_dynamic-slice_fusion.1.window_ref, f32[2,3,256,256]{3,2,1,0:T(8,128)} %probe_ref.3, f32[256,256]{1,0:T(8,128)} %bitcast.20, bf16[256,256]{1,0:T(8,128)(2,1)} %get-tuple-element.26.table_re_ref, bf16[256,256]{1,0:T(8,128)(2,1)} %get-tuple-element.25.table_im_ref), custom_call_target="tpu_custom_call" | custom-call | tf_op jit(solution)/shard_map/pallas_call | solution.py:88
  47.7 1.1 fusion.22
  48.8 7.4 %collective-permute-start.4 = (f32[2,128,256]{2,1,0:T(8,128)S(1)}, f32[2,128,256]{2,1,0:T(8,128)S(1)}, u32[]{:S(2)}, u32[]{:S(2)}) collective-permute-start(f32[2,128,256]{2,1,0:T(8,128)S(1)} %get-tuple-element.14), channel_id=1, source_target_pairs={{32,0},{64,32},{96,64},{128,96},{160,128},{192,160},{224,192},{256... | collective-permute-start | bytes 786440 | tf_op jit(solution)/shard_map/ppermute | solution.py:99
  56.2 1.9 %collective-permute-start.5 = (f32[2,128,256]{2,1,0:T(8,128)S(1)}, f32[2,128,256]{2,1,0:T(8,128)S(1)}, u32[]{:S(2)}, u32[]{:S(2)}) collective-permute-start(f32[2,128,256]{2,1,0:T(8,128)S(1)} %get-tuple-element.13), channel_id=1, source_target_pairs={{0,32},{32,64},{64,96},{96,128},{128,160},{160,192},{192,224},{224... | collective-permute-start | bytes 786440 | tf_op jit(solution)/shard_map/ppermute | solution.py:99
  60.7 0.5 fusion.25
  61.9 0.6 fusion.24
  64.4 11.1 %collective-permute-done.5 = f32[2,128,256]{2,1,0:T(8,128)S(1)} collective-permute-done((f32[2,128,256]{2,1,0:T(8,128)S(1)}, f32[2,128,256]{2,1,0:T(8,128)S(1)}, u32[]{:S(2)}, u32[]{:S(2)}) %collective-permute-start.5) | collective-permute-done | bytes 262176 | tf_op jit(solution)/shard_map/ppermute | solution.py:99
  75.5 1.0 fusion
  76.5 0.0 copy-start
  76.5 0.8 fusion.19
  77.3 1.9 %collective-permute-start.6 = (f32[2,384,128]{2,1,0:T(8,128)}, f32[2,384,128]{2,1,0:T(8,128)S(1)}, u32[]{:S(2)}, u32[]{:S(2)}) collective-permute-start(f32[2,384,128]{2,1,0:T(8,128)} %get-tuple-element.5), channel_id=1, source_target_pairs={{0,1},{1,2},{2,3},{3,4},{4,5},{5,6},{6,7},{7,8},{8,9},{9,10},{10,1... | collective-permute-start | bytes 1179656 | tf_op jit(solution)/shard_map/ppermute | solution.py:99
  79.3 5.8 %collective-permute-start.7 = (f32[2,384,128]{2,1,0:T(8,128)S(1)}, f32[2,384,128]{2,1,0:T(8,128)}, u32[]{:S(2)}, u32[]{:S(2)}) collective-permute-start(f32[2,384,128]{2,1,0:T(8,128)S(1)} %get-tuple-element.6), channel_id=1, source_target_pairs={{1,0},{2,1},{3,2},{4,3},{5,4},{6,5},{7,6},{8,7},{9,8},{10,9},{11,1... | collective-permute-start | bytes 1179656 | tf_op jit(solution)/shard_map/ppermute | solution.py:99
  85.0 0.1 multiply_reduce_fusion
  85.2 0.7 reduce_max.9
  86.6 0.1 broadcast_and_fusion
  86.7 2.0 %collective-permute-done.6 = f32[2,384,128]{2,1,0:T(8,128)S(1)} collective-permute-done((f32[2,384,128]{2,1,0:T(8,128)}, f32[2,384,128]{2,1,0:T(8,128)S(1)}, u32[]{:S(2)}, u32[]{:S(2)}) %collective-permute-start.6) | collective-permute-done | bytes 393248 | tf_op jit(solution)/shard_map/ppermute | solution.py:99
  88.8 0.7 copy-done.5
  89.5 0.8 collective-permute-done.7
  90.3 2.5 %add_select_fusion = f32[2,384,384]{2,1,0:T(8,128)S(1)} fusion(f32[2,384,128]{2,1,0:T(8,128)} %collective-permute-done.7, f32[2,384,128]{2,1,0:T(8,128)} %copy-done.5, f32[]{:T(128)S(6)} %add.193, pred[384,384]{1,0:T(8,128)(4,1)S(1)} %broadcast_and_fusion, s32[]{:T(128)S(6)} %select_n.52, s32[]{:T(128)S(6)} %select_n.53, f32[2,128,256]{2,1,0:T(8,128)} %copy-done.4, ...), kind=kLoop, calls=%fused_computation.9 | loop fusion | flops 2654208 | bytes 4341788 | tf_op jit(solution)/shard_map/jit(_where)/select_n | solution.py:190
  92.8 1.0 constant_dynamic-slice_fusion.window_ref
  93.8 5.2 %shard_map.47 = f32[2,256,256]{2,1,0:T(8,128)} custom-call(f32[2,256,256]{2,1,0:T(8,128)} %constant_dynamic-slice_fusion.window_ref, f32[2,3,256,256]{3,2,1,0:T(8,128)} %probe_ref.3, f32[256,256]{1,0:T(8,128)} %bitcast.21, bf16[256,256]{1,0:T(8,128)(2,1)} %get-tuple-element.26.table_re_ref, bf16[256,256]{1,0:T(8,128)(2,1)} %get-tuple-element.25.table_im_ref), custom_call_target="tpu_custom_call" | custom-call | tf_op jit(solution)/shard_map/pallas_call | solution.py:88
  99.0 1.4 %pad_dynamic-slice_fusion.1 = (f32[2,384,64]{2,1,0:T(8,128)S(1)}, f32[2,384,64]{2,1,0:T(8,128)S(1)}) fusion(s32[]{:T(128)S(6)} %select_n.48, s32[]{:T(128)S(6)} %add.200, f32[2,256,256]{2,1,0:T(8,128)} %shard_map.47, s32[]{:T(128)S(6)} %select_n.49), kind=kLoop, calls=%fused_computation.1 | loop fusion | bytes 917516 | tf_op jit(solution)/shard_map/slice | solution.py:109
  100.4 1.9 %collective-permute-start.8 = (f32[2,384,64]{2,1,0:T(8,128)S(1)}, f32[2,384,64]{2,1,0:T(8,128)S(1)}, u32[]{:S(2)}, u32[]{:S(2)}) collective-permute-start(f32[2,384,64]{2,1,0:T(8,128)S(1)} %get-tuple-element.11), channel_id=1, source_target_pairs={{0,1},{1,2},{2,3},{3,4},{4,5},{5,6},{6,7},{7,8},{8,9},{9,10},{10,1... | collective-permute-start | bytes 589832 | tf_op jit(solution)/shard_map/ppermute | solution.py:99
  102.3 6.1 %collective-permute-start.9 = (f32[2,384,64]{2,1,0:T(8,128)S(1)}, f32[2,384,64]{2,1,0:T(8,128)S(1)}, u32[]{:S(2)}, u32[]{:S(2)}) collective-permute-start(f32[2,384,64]{2,1,0:T(8,128)S(1)} %get-tuple-element.12), channel_id=1, source_target_pairs={{1,0},{2,1},{3,2},{4,3},{5,4},{6,5},{7,6},{8,7},{9,8},{10,9},{11,1... | collective-permute-start | bytes 589832 | tf_op jit(solution)/shard_map/ppermute | solution.py:99
  108.4 3.5 %collective-permute-done.8 = f32[2,384,64]{2,1,0:T(8,128)S(1)} collective-permute-done((f32[2,384,64]{2,1,0:T(8,128)S(1)}, f32[2,384,64]{2,1,0:T(8,128)S(1)}, u32[]{:S(2)}, u32[]{:S(2)}) %collective-permute-start.8) | collective-permute-done | bytes 196640 | tf_op jit(solution)/shard_map/ppermute | solution.py:99
  111.9 1.8 %collective-permute-done.9 = f32[2,384,64]{2,1,0:T(8,128)S(1)} collective-permute-done((f32[2,384,64]{2,1,0:T(8,128)S(1)}, f32[2,384,64]{2,1,0:T(8,128)S(1)}, u32[]{:S(2)}, u32[]{:S(2)}) %collective-permute-start.9) | collective-permute-done | bytes 196640 | tf_op jit(solution)/shard_map/ppermute | solution.py:99
  113.7 0.4 fusion.3
  114.2 1.9 %collective-permute-start.10 = (f32[2,64,256]{2,1,0:T(8,128)S(1)}, f32[2,64,256]{2,1,0:T(8,128)S(1)}, u32[]{:S(2)}, u32[]{:S(2)}) collective-permute-start(f32[2,64,256]{2,1,0:T(8,128)S(1)} %get-tuple-element.7), channel_id=1, source_target_pairs={{0,32},{32,64},{64,96},{96,128},{128,160},{160,192},{192,224},{224... | collective-permute-start | bytes 393224 | tf_op jit(solution)/shard_map/ppermute | solution.py:99
  116.1 6.9 %collective-permute-start.11 = (f32[2,64,256]{2,1,0:T(8,128)S(1)}, f32[2,64,256]{2,1,0:T(8,128)S(1)}, u32[]{:S(2)}, u32[]{:S(2)}) collective-permute-start(f32[2,64,256]{2,1,0:T(8,128)S(1)} %get-tuple-element.8), channel_id=1, source_target_pairs={{32,0},{64,32},{96,64},{128,96},{160,128},{192,160},{224,192},{256... | collective-permute-start | bytes 393224 | tf_op jit(solution)/shard_map/ppermute | solution.py:99
  123.1 1.0 collective-permute-done.10
  124.1 1.5 %collective-permute-done.11 = f32[2,64,256]{2,1,0:T(8,128)S(1)} collective-permute-done((f32[2,64,256]{2,1,0:T(8,128)S(1)}, f32[2,64,256]{2,1,0:T(8,128)S(1)}, u32[]{:S(2)}, u32[]{:S(2)}) %collective-permute-start.11) | collective-permute-done | bytes 131104 | tf_op jit(solution)/shard_map/ppermute | solution.py:99
  125.6 1.0 fusion.6
  (19 shorter events, 0.1 us)
Async XLA Ops:
  0.0 26.9 %copy-start.3 = (f32[2,256,256]{2,1,0:T(8,128)S(1)}, f32[2,256,256]{2,1,0:T(8,128)}, u32[]{:S(2)}) copy-start(f32[2,256,256]{2,1,0:T(8,128)} %param.4) | copy-start | bytes 1572868
  1.9 25.0 %collective-permute-start = (f32[2,72,256]{2,1,0:T(8,128)S(1)}, f32[2,72,256]{2,1,0:T(8,128)S(1)}, u32[]{:S(2)}, u32[]{:S(2)}) collective-permute-start(f32[2,72,256]{2,1,0:T(8,128)S(1)} %get-tuple-element.21), channel_id=1, source_target_pairs={{0,32},{32,64},{64,96},{96,128},{128,160},{160,192},{192,224},{224... | collective-permute-start | bytes 442376 | tf_op jit(solution)/shard_map/ppermute | solution.py:99
  7.1 19.8 %collective-permute-start.1 = (f32[2,72,256]{2,1,0:T(8,128)S(1)}, f32[2,72,256]{2,1,0:T(8,128)S(1)}, u32[]{:S(2)}, u32[]{:S(2)}) collective-permute-start(f32[2,72,256]{2,1,0:T(8,128)S(1)} %get-tuple-element.22), channel_id=1, source_target_pairs={{32,0},{64,32},{96,64},{128,96},{160,128},{192,160},{224,192},{256... | collective-permute-start | bytes 442376 | tf_op jit(solution)/shard_map/ppermute | solution.py:99
  27.0 8.8 %copy-start.6 = (s32[1,1,1,2]{3,2,1,0:T(1,128)S(1)}, s32[1,1,1,2]{3,2,1,0:T(1,128)}, u32[]{:S(2)}) copy-start(s32[1,1,1,2]{3,2,1,0:T(1,128)} %param.6) | copy-start | bytes 28
  27.2 13.5 %collective-permute-start.2 = (f32[2,384,64]{2,1,0:T(8,128)S(1)}, f32[2,384,64]{2,1,0:T(8,128)S(1)}, u32[]{:S(2)}, u32[]{:S(2)}) collective-permute-start(f32[2,384,64]{2,1,0:T(8,128)S(1)} %get-tuple-element.9), channel_id=1, source_target_pairs={{0,1},{1,2},{2,3},{3,4},{4,5},{5,6},{6,7},{7,8},{8,9},{9,10},{10,1... | collective-permute-start | bytes 589832 | tf_op jit(solution)/shard_map/ppermute | solution.py:99
  29.1 11.9 %collective-permute-start.3 = (f32[2,384,64]{2,1,0:T(8,128)S(1)}, f32[2,384,64]{2,1,0:T(8,128)S(1)}, u32[]{:S(2)}, u32[]{:S(2)}) collective-permute-start(f32[2,384,64]{2,1,0:T(8,128)S(1)} %get-tuple-element.10), channel_id=1, source_target_pairs={{1,0},{2,1},{3,2},{4,3},{5,4},{6,5},{7,6},{8,7},{9,8},{10,9},{11,1... | collective-permute-start | bytes 589832 | tf_op jit(solution)/shard_map/ppermute | solution.py:99
  47.7 27.8 %copy-start.1 = (f32[2,256,256]{2,1,0:T(8,128)S(1)}, f32[2,256,256]{2,1,0:T(8,128)}, u32[]{:S(2)}) copy-start(f32[2,256,256]{2,1,0:T(8,128)} %shard_map.46) | copy-start | bytes 1572868
  48.8 15.6 %collective-permute-start.4 = (f32[2,128,256]{2,1,0:T(8,128)S(1)}, f32[2,128,256]{2,1,0:T(8,128)S(1)}, u32[]{:S(2)}, u32[]{:S(2)}) collective-permute-start(f32[2,128,256]{2,1,0:T(8,128)S(1)} %get-tuple-element.14), channel_id=1, source_target_pairs={{32,0},{64,32},{96,64},{128,96},{160,128},{192,160},{224,192},{256... | collective-permute-start | bytes 786440 | tf_op jit(solution)/shard_map/ppermute | solution.py:99
  56.2 19.3 %collective-permute-start.5 = (f32[2,128,256]{2,1,0:T(8,128)S(1)}, f32[2,128,256]{2,1,0:T(8,128)S(1)}, u32[]{:S(2)}, u32[]{:S(2)}) collective-permute-start(f32[2,128,256]{2,1,0:T(8,128)S(1)} %get-tuple-element.13), channel_id=1, source_target_pairs={{0,32},{32,64},{64,96},{96,128},{128,160},{160,192},{192,224},{224... | collective-permute-start | bytes 786440 | tf_op jit(solution)/shard_map/ppermute | solution.py:99
  75.5 1.8 %copy-start.4 = (f32[2,128,256]{2,1,0:T(8,128)}, f32[2,128,256]{2,1,0:T(8,128)S(1)}, u32[]{:S(2)}) copy-start(f32[2,128,256]{2,1,0:T(8,128)S(1)} %collective-permute-done.5) | copy-start | bytes 786436
  76.5 8.5 %copy-start = (f32[2,3,256,256]{3,2,1,0:T(8,128)S(1)}, f32[2,3,256,256]{3,2,1,0:T(8,128)}, u32[]{:S(2)}) copy-start(f32[2,3,256,256]{3,2,1,0:T(8,128)} %probe_ref.3) | copy-start | bytes 4718596
  77.3 11.4 %collective-permute-start.6 = (f32[2,384,128]{2,1,0:T(8,128)}, f32[2,384,128]{2,1,0:T(8,128)S(1)}, u32[]{:S(2)}, u32[]{:S(2)}) collective-permute-start(f32[2,384,128]{2,1,0:T(8,128)} %get-tuple-element.5), channel_id=1, source_target_pairs={{0,1},{1,2},{2,3},{3,4},{4,5},{5,6},{6,7},{7,8},{8,9},{9,10},{10,1... | collective-permute-start | bytes 1179656 | tf_op jit(solution)/shard_map/ppermute | solution.py:99
  79.3 11.0 %collective-permute-start.7 = (f32[2,384,128]{2,1,0:T(8,128)S(1)}, f32[2,384,128]{2,1,0:T(8,128)}, u32[]{:S(2)}, u32[]{:S(2)}) collective-permute-start(f32[2,384,128]{2,1,0:T(8,128)S(1)} %get-tuple-element.6), channel_id=1, source_target_pairs={{1,0},{2,1},{3,2},{4,3},{5,4},{6,5},{7,6},{8,7},{9,8},{10,9},{11,1... | collective-permute-start | bytes 1179656 | tf_op jit(solution)/shard_map/ppermute | solution.py:99
  88.8 0.7 copy-start.5
  99.0 14.8 %copy-start.2 = (f32[2,256,256]{2,1,0:T(8,128)S(1)}, f32[2,256,256]{2,1,0:T(8,128)}, u32[]{:S(2)}) copy-start(f32[2,256,256]{2,1,0:T(8,128)} %shard_map.47) | copy-start | bytes 1572868
  100.4 11.5 %collective-permute-start.8 = (f32[2,384,64]{2,1,0:T(8,128)S(1)}, f32[2,384,64]{2,1,0:T(8,128)S(1)}, u32[]{:S(2)}, u32[]{:S(2)}) collective-permute-start(f32[2,384,64]{2,1,0:T(8,128)S(1)} %get-tuple-element.11), channel_id=1, source_target_pairs={{0,1},{1,2},{2,3},{3,4},{4,5},{5,6},{6,7},{7,8},{8,9},{9,10},{10,1... | collective-permute-start | bytes 589832 | tf_op jit(solution)/shard_map/ppermute | solution.py:99
  102.3 11.4 %collective-permute-start.9 = (f32[2,384,64]{2,1,0:T(8,128)S(1)}, f32[2,384,64]{2,1,0:T(8,128)S(1)}, u32[]{:S(2)}, u32[]{:S(2)}) collective-permute-start(f32[2,384,64]{2,1,0:T(8,128)S(1)} %get-tuple-element.12), channel_id=1, source_target_pairs={{1,0},{2,1},{3,2},{4,3},{5,4},{6,5},{7,6},{8,7},{9,8},{10,9},{11,1... | collective-permute-start | bytes 589832 | tf_op jit(solution)/shard_map/ppermute | solution.py:99
  114.2 9.9 %collective-permute-start.10 = (f32[2,64,256]{2,1,0:T(8,128)S(1)}, f32[2,64,256]{2,1,0:T(8,128)S(1)}, u32[]{:S(2)}, u32[]{:S(2)}) collective-permute-start(f32[2,64,256]{2,1,0:T(8,128)S(1)} %get-tuple-element.7), channel_id=1, source_target_pairs={{0,32},{32,64},{64,96},{96,128},{128,160},{160,192},{192,224},{224... | collective-permute-start | bytes 393224 | tf_op jit(solution)/shard_map/ppermute | solution.py:99
  116.1 9.4 %collective-permute-start.11 = (f32[2,64,256]{2,1,0:T(8,128)S(1)}, f32[2,64,256]{2,1,0:T(8,128)S(1)}, u32[]{:S(2)}, u32[]{:S(2)}) collective-permute-start(f32[2,64,256]{2,1,0:T(8,128)S(1)} %get-tuple-element.8), channel_id=1, source_target_pairs={{32,0},{64,32},{96,64},{128,96},{160,128},{192,160},{224,192},{256... | collective-permute-start | bytes 393224 | tf_op jit(solution)/shard_map/ppermute | solution.py:99

commit v16 on v6

--- a/solution.py
+++ b/solution.py
@@ -168,8 +168,8 @@
     zero = jnp.zeros((), jnp.int32)
     corner = (zero, offsets[0, 0] + M, offsets[0, 1] + M)
     spread = (zero, place - M - offsets[0, 0], place - M - offsets[0, 1])
-    extended = neighbor_sum(object_planes, "row", 1, tile_size, M, 0, extent)
-    extended = neighbor_sum(extended, "col", 2, tile_size, M, 0, extent)
+    extended = neighbor_sum(object_planes, "col", 2, tile_size, M, 0, extent)
+    extended = neighbor_sum(extended, "row", 1, tile_size, M, 0, extent)
     for update in range(ITERS):
         window = lax.dynamic_slice(extended, corner, (2, W, W))
         change = pattern_gradient(window, measured[0], probe_modes, table_re, table_im)

time: 126 us -> 126 us (level)
  other arithmetic: 9.38 us -> 7.76 us
  waiting for transfers between devices: 25.9 us -> 27.3 us
    ppermute x12, waiting for transfers between devices: 25.9 us -> 27.3 us  [from_neighbor(): return lax.ppermute(x, axis, pairs)]
  transfers between devices with their start and end apart: 12 -> 12, of which waited for: 9 -> 8; matrix products, arithmetic and copies ran while one was open for 8% -> 8% of each run, Pallas kernels for 0% -> 0%
where the time goes in v16:
time: 126 us; the launch traced here: 124 us
  starting transfers between devices  54.7 us (43%)
  waiting for transfers between devices  27.3 us (22%)
  local copies, waits for them, and re-layouts  15.7 us (12%)
  Pallas kernels  10.5 us (8%)
  between operations  8.48 us (7%)
  other arithmetic  7.76 us (6%)
    ppermute x12, starting transfers between devices, from_neighbor(): return lax.ppermute(x, axis, pairs)  54.7 us
    ppermute x12, waiting for transfers between devices, from_neighbor(): return lax.ppermute(x, axis, pairs)  27.3 us
    pallas_call x2, Pallas kernels, pattern_gradient(): pl.pallas_call(gradient_kernel, out_shape=jax.ShapeDtypeStruct((2, rows,...  10.5 us
    another operation x1, local copies, waits for them, and re-layouts, rows_from_neighbors(): jnp.stack([offset[0], offset[1]] + [offset[0]] * 6).astype(jnp.float32)  5.19 us
    slice x5, local copies, waits for them, and re-layouts, neighbor_sum(): piece = lax.slice_in_dim(frame, low - shift, high - shift, axis=dim)  3.48 us
  transfers between devices with their start and end apart: 12, of which 8 were waited for; matrix products, arithmetic and copies ran while one was open for 8% of the time, Pallas kernels for 0%

profile of v16, /device:TPU:87, one launch (start us, length us, event | category | flops | bytes accessed | tf_op | source)
XLA Modules:
  0.0 124.4 jit_solution(12344355340042228333)
XLA Ops:
  0.0 1.2 fusion.23
  1.2 4.9 %collective-permute-start = (f32[2,256,64]{2,1,0:T(8,128)S(1)}, f32[2,256,64]{2,1,0:T(8,128)S(1)}, u32[]{:S(2)}, u32[]{:S(2)}) collective-permute-start(f32[2,256,64]{2,1,0:T(8,128)S(1)} %get-tuple-element.15), channel_id=1, source_target_pairs={{0,1},{1,2},{2,3},{3,4},{4,5},{5,6},{6,7},{7,8},{8,9},{9,10},{10,1... | collective-permute-start | bytes 393224 | tf_op jit(solution)/shard_map/ppermute | solution.py:97
  6.1 1.9 %collective-permute-start.1 = (f32[2,256,64]{2,1,0:T(8,128)S(1)}, f32[2,256,64]{2,1,0:T(8,128)S(1)}, u32[]{:S(2)}, u32[]{:S(2)}) collective-permute-start(f32[2,256,64]{2,1,0:T(8,128)S(1)} %get-tuple-element.16), channel_id=1, source_target_pairs={{1,0},{2,1},{3,2},{4,3},{5,4},{6,5},{7,6},{8,7},{9,8},{10,9},{11,1... | collective-permute-start | bytes 393224 | tf_op jit(solution)/shard_map/ppermute | solution.py:97
  8.0 1.3 %fusion.27 = (s32[1,1]{1,0:T(1,128)}, s32[1,1]{1,0:T(1,128)}) fusion(s32[1,2]{1,0:T(1,128)} %bitcast.22), kind=kLoop, calls=%fused_computation.50 | loop fusion | bytes 16 | tf_op jit(solution)/shard_map/slice | solution.py:169
  11.9 0.0 copy-start.5
  11.9 3.1 %collective-permute-done.1 = f32[2,256,64]{2,1,0:T(8,128)S(1)} collective-permute-done((f32[2,256,64]{2,1,0:T(8,128)S(1)}, f32[2,256,64]{2,1,0:T(8,128)S(1)}, u32[]{:S(2)}, u32[]{:S(2)}) %collective-permute-start.1) | collective-permute-done | bytes 131104 | tf_op jit(solution)/shard_map/ppermute | solution.py:97
  15.0 0.3 pad_add_fusion.1
  15.4 4.9 %collective-permute-start.2 = (f32[2,64,384]{2,1,0:T(8,128)S(1)}, f32[2,64,384]{2,1,0:T(8,128)S(1)}, u32[]{:S(2)}, u32[]{:S(2)}) collective-permute-start(f32[2,64,384]{2,1,0:T(8,128)S(1)} %get-tuple-element.9), channel_id=1, source_target_pairs={{0,32},{32,64},{64,96},{96,128},{128,160},{160,192},{192,224},{224... | collective-permute-start | bytes 589832 | tf_op jit(solution)/shard_map/ppermute | solution.py:97
  20.3 14.5 %collective-permute-start.3 = (f32[2,64,384]{2,1,0:T(8,128)S(1)}, f32[2,64,384]{2,1,0:T(8,128)S(1)}, u32[]{:S(2)}, u32[]{:S(2)}) collective-permute-start(f32[2,64,384]{2,1,0:T(8,128)S(1)} %get-tuple-element.10), channel_id=1, source_target_pairs={{32,0},{64,32},{96,64},{128,96},{160,128},{192,160},{224,192},{256... | collective-permute-start | bytes 589832 | tf_op jit(solution)/shard_map/ppermute | solution.py:97
  34.8 0.7 fusion.26
  35.5 5.2 %stack.9 = s32[8]{0:T(128)S(1)} concatenate(s32[1]{0:T(128)} %bitcast.10, s32[1]{0:T(128)} %bitcast.11, s32[1]{0:T(128)} %bitcast.10, s32[1]{0:T(128)} %bitcast.10, s32[1]{0:T(128)} %bitcast.10, s32[1]{0:T(128)} %bitcast.10, s32[1]{0:T(128)} %bitcast.10, s32[1]{0:T(128)} %bitcast.10), dimensions={0} | concatenate | bytes 64 | tf_op jit(solution)/shard_map/stack | solution.py:121
  40.7 1.7 %multiply_convert_fusion = (bf16[256,256]{1,0:T(8,128)(2,1)}, bf16[256,256]{1,0:T(8,128)(2,1)}) fusion(), kind=kLoop, calls=%fused_computation.27 | loop fusion | flops 1245184 | bytes 262144 | tf_op jit(solution)/shard_map/convert_element_type | solution.py:26
  42.4 0.0 collective-permute-done.3
  42.4 0.1 pad_add_fusion
  42.5 1.0 constant_dynamic-slice_fusion.1.window_ref
  43.5 5.3 %shard_map.46 = f32[2,256,256]{2,1,0:T(8,128)} custom-call(f32[2,256,256]{2,1,0:T(8,128)} %constant_dynamic-slice_fusion.1.window_ref, f32[2,3,256,256]{3,2,1,0:T(8,128)} %probe_ref.3, f32[256,256]{1,0:T(8,128)} %bitcast.20, bf16[256,256]{1,0:T(8,128)(2,1)} %get-tuple-element.28.table_re_ref, bf16[256,256]{1,0:T(8,128)(2,1)} %get-tuple-element.27.table_im_ref), custom_call_target="tpu_custom_call" | custom-call | tf_op jit(solution)/shard_map/pallas_call | solution.py:86
  48.8 1.1 fusion.22
  49.9 0.1 pad_maximum_fusion.1
  50.0 2.1 %collective-permute-start.5 = (f32[2,136,256]{2,1,0:T(8,128)S(1)}, f32[2,136,256]{2,1,0:T(8,128)S(1)}, u32[]{:S(2)}, u32[]{:S(2)}) collective-permute-start(f32[2,136,256]{2,1,0:T(8,128)S(1)} %get-tuple-element.21), channel_id=1, source_target_pairs={{0,32},{32,64},{64,96},{96,128},{128,160},{160,192},{192,224},{224... | collective-permute-start | bytes 835592 | tf_op jit(solution)/shard_map/ppermute | solution.py:97
  52.1 7.6 %collective-permute-start.4 = (f32[2,136,256]{2,1,0:T(8,128)S(1)}, f32[2,136,256]{2,1,0:T(8,128)S(1)}, u32[]{:S(2)}, u32[]{:S(2)}) collective-permute-start(f32[2,136,256]{2,1,0:T(8,128)S(1)} %get-tuple-element.22), channel_id=1, source_target_pairs={{32,0},{64,32},{96,64},{128,96},{160,128},{192,160},{224,192},{256... | collective-permute-start | bytes 835592 | tf_op jit(solution)/shard_map/ppermute | solution.py:97
  62.1 5.5 %collective-permute-done.5 = f32[2,136,256]{2,1,0:T(8,128)S(1)} collective-permute-done((f32[2,136,256]{2,1,0:T(8,128)S(1)}, f32[2,136,256]{2,1,0:T(8,128)S(1)}, u32[]{:S(2)}, u32[]{:S(2)}) %collective-permute-start.5) | collective-permute-done | bytes 278560 | tf_op jit(solution)/shard_map/ppermute | solution.py:97
  67.6 0.6 fusion.24
  68.9 0.5 fusion.25
  71.4 1.0 fusion
  72.4 0.0 copy-start
  72.4 0.8 fusion.19
  73.2 3.1 %collective-permute-start.6 = (f32[2,384,128]{2,1,0:T(8,128)}, f32[2,384,128]{2,1,0:T(8,128)S(1)}, u32[]{:S(2)}, u32[]{:S(2)}) collective-permute-start(f32[2,384,128]{2,1,0:T(8,128)} %get-tuple-element.5), channel_id=1, source_target_pairs={{0,1},{1,2},{2,3},{3,4},{4,5},{5,6},{6,7},{7,8},{8,9},{9,10},{10,1... | collective-permute-start | bytes 1179656 | tf_op jit(solution)/shard_map/ppermute | solution.py:97
  76.4 1.9 %collective-permute-start.7 = (f32[2,384,128]{2,1,0:T(8,128)S(1)}, f32[2,384,128]{2,1,0:T(8,128)}, u32[]{:S(2)}, u32[]{:S(2)}) collective-permute-start(f32[2,384,128]{2,1,0:T(8,128)S(1)} %get-tuple-element.6), channel_id=1, source_target_pairs={{1,0},{2,1},{3,2},{4,3},{5,4},{6,5},{7,6},{8,7},{9,8},{10,9},{11,1... | collective-permute-start | bytes 1179656 | tf_op jit(solution)/shard_map/ppermute | solution.py:97
  78.3 0.1 multiply_reduce_fusion
  78.4 0.7 reduce_max.9
  79.8 0.1 broadcast_and_fusion
  79.9 1.5 %collective-permute-done.6 = f32[2,384,128]{2,1,0:T(8,128)S(1)} collective-permute-done((f32[2,384,128]{2,1,0:T(8,128)}, f32[2,384,128]{2,1,0:T(8,128)S(1)}, u32[]{:S(2)}, u32[]{:S(2)}) %collective-permute-start.6) | collective-permute-done | bytes 393248 | tf_op jit(solution)/shard_map/ppermute | solution.py:97
  81.4 0.7 copy-done.4
  82.1 4.7 %collective-permute-done.7 = f32[2,384,128]{2,1,0:T(8,128)} collective-permute-done((f32[2,384,128]{2,1,0:T(8,128)S(1)}, f32[2,384,128]{2,1,0:T(8,128)}, u32[]{:S(2)}, u32[]{:S(2)}) %collective-permute-start.7) | collective-permute-done | bytes 393248 | tf_op jit(solution)/shard_map/ppermute | solution.py:97
  86.8 2.1 %add_select_fusion = f32[2,384,384]{2,1,0:T(8,128)S(1)} fusion(f32[2,384,128]{2,1,0:T(8,128)} %collective-permute-done.7, f32[2,384,128]{2,1,0:T(8,128)} %copy-done.4, f32[]{:T(128)S(6)} %add.205, pred[384,384]{1,0:T(8,128)(4,1)S(1)} %broadcast_and_fusion, f32[2,64,384]{2,1,0:T(8,128)S(1)} %collective-permute-done.3, f32[2,256,384]{2,1,0:T(8,128)S(1)} %pad_add_fusion.1, ...), kind=kLoop, calls=%fused_computation.9 | loop fusion | flops 2654208 | bytes 4341788 | tf_op jit(solution)/shard_map/jit(_where)/select_n | solution.py:182
  88.9 1.0 constant_dynamic-slice_fusion.window_ref
  89.9 5.2 %shard_map.47 = f32[2,256,256]{2,1,0:T(8,128)} custom-call(f32[2,256,256]{2,1,0:T(8,128)} %constant_dynamic-slice_fusion.window_ref, f32[2,3,256,256]{3,2,1,0:T(8,128)} %probe_ref.3, f32[256,256]{1,0:T(8,128)} %bitcast.21, bf16[256,256]{1,0:T(8,128)(2,1)} %get-tuple-element.28.table_re_ref, bf16[256,256]{1,0:T(8,128)(2,1)} %get-tuple-element.27.table_im_ref), custom_call_target="tpu_custom_call" | custom-call | tf_op jit(solution)/shard_map/pallas_call | solution.py:86
  95.1 1.4 %pad_dynamic-slice_fusion.1 = (f32[2,384,64]{2,1,0:T(8,128)S(1)}, f32[2,384,64]{2,1,0:T(8,128)S(1)}) fusion(s32[]{:T(128)S(6)} %select_n.48, s32[]{:T(128)S(6)} %add.212, f32[2,256,256]{2,1,0:T(8,128)} %shard_map.47, s32[]{:T(128)S(6)} %select_n.49), kind=kLoop, calls=%fused_computation.1 | loop fusion | bytes 917516 | tf_op jit(solution)/shard_map/slice | solution.py:107
  96.6 1.9 %collective-permute-start.8 = (f32[2,384,64]{2,1,0:T(8,128)S(1)}, f32[2,384,64]{2,1,0:T(8,128)S(1)}, u32[]{:S(2)}, u32[]{:S(2)}) collective-permute-start(f32[2,384,64]{2,1,0:T(8,128)S(1)} %get-tuple-element.11), channel_id=1, source_target_pairs={{0,1},{1,2},{2,3},{3,4},{4,5},{5,6},{6,7},{7,8},{8,9},{9,10},{10,1... | collective-permute-start | bytes 589832 | tf_op jit(solution)/shard_map/ppermute | solution.py:97
  98.5 2.4 %collective-permute-start.9 = (f32[2,384,64]{2,1,0:T(8,128)S(1)}, f32[2,384,64]{2,1,0:T(8,128)S(1)}, u32[]{:S(2)}, u32[]{:S(2)}) collective-permute-start(f32[2,384,64]{2,1,0:T(8,128)S(1)} %get-tuple-element.12), channel_id=1, source_target_pairs={{1,0},{2,1},{3,2},{4,3},{5,4},{6,5},{7,6},{8,7},{9,8},{10,9},{11,1... | collective-permute-start | bytes 589832 | tf_op jit(solution)/shard_map/ppermute | solution.py:97
  100.9 2.3 %collective-permute-done.8 = f32[2,384,64]{2,1,0:T(8,128)S(1)} collective-permute-done((f32[2,384,64]{2,1,0:T(8,128)S(1)}, f32[2,384,64]{2,1,0:T(8,128)S(1)}, u32[]{:S(2)}, u32[]{:S(2)}) %collective-permute-start.8) | collective-permute-done | bytes 196640 | tf_op jit(solution)/shard_map/ppermute | solution.py:97
  103.2 5.6 %collective-permute-done.9 = f32[2,384,64]{2,1,0:T(8,128)S(1)} collective-permute-done((f32[2,384,64]{2,1,0:T(8,128)S(1)}, f32[2,384,64]{2,1,0:T(8,128)S(1)}, u32[]{:S(2)}, u32[]{:S(2)}) %collective-permute-start.9) | collective-permute-done | bytes 196640 | tf_op jit(solution)/shard_map/ppermute | solution.py:97
  108.8 0.4 fusion.3
  109.2 1.9 %collective-permute-start.10 = (f32[2,64,256]{2,1,0:T(8,128)S(1)}, f32[2,64,256]{2,1,0:T(8,128)S(1)}, u32[]{:S(2)}, u32[]{:S(2)}) collective-permute-start(f32[2,64,256]{2,1,0:T(8,128)S(1)} %get-tuple-element.7), channel_id=1, source_target_pairs={{0,32},{32,64},{64,96},{96,128},{128,160},{160,192},{192,224},{224... | collective-permute-start | bytes 393224 | tf_op jit(solution)/shard_map/ppermute | solution.py:97
  111.2 7.6 %collective-permute-start.11 = (f32[2,64,256]{2,1,0:T(8,128)S(1)}, f32[2,64,256]{2,1,0:T(8,128)S(1)}, u32[]{:S(2)}, u32[]{:S(2)}) collective-permute-start(f32[2,64,256]{2,1,0:T(8,128)S(1)} %get-tuple-element.8), channel_id=1, source_target_pairs={{32,0},{64,32},{96,64},{128,96},{160,128},{192,160},{224,192},{256... | collective-permute-start | bytes 393224 | tf_op jit(solution)/shard_map/ppermute | solution.py:97
  118.8 3.2 %collective-permute-done.10 = f32[2,64,256]{2,1,0:T(8,128)S(1)} collective-permute-done((f32[2,64,256]{2,1,0:T(8,128)S(1)}, f32[2,64,256]{2,1,0:T(8,128)S(1)}, u32[]{:S(2)}, u32[]{:S(2)}) %collective-permute-start.10) | collective-permute-done | bytes 131104 | tf_op jit(solution)/shard_map/ppermute | solution.py:97
  122.0 1.4 %collective-permute-done.11 = f32[2,64,256]{2,1,0:T(8,128)S(1)} collective-permute-done((f32[2,64,256]{2,1,0:T(8,128)S(1)}, f32[2,64,256]{2,1,0:T(8,128)S(1)}, u32[]{:S(2)}, u32[]{:S(2)}) %collective-permute-start.11) | collective-permute-done | bytes 131104 | tf_op jit(solution)/shard_map/ppermute | solution.py:97
  123.4 1.0 fusion.6
  (19 shorter events, 0.1 us)
Async XLA Ops:
  0.0 15.0 %copy-start.3 = (f32[2,256,256]{2,1,0:T(8,128)S(1)}, f32[2,256,256]{2,1,0:T(8,128)}, u32[]{:S(2)}) copy-start(f32[2,256,256]{2,1,0:T(8,128)} %param.4) | copy-start | bytes 1572868
  1.2 10.7 %collective-permute-start = (f32[2,256,64]{2,1,0:T(8,128)S(1)}, f32[2,256,64]{2,1,0:T(8,128)S(1)}, u32[]{:S(2)}, u32[]{:S(2)}) collective-permute-start(f32[2,256,64]{2,1,0:T(8,128)S(1)} %get-tuple-element.15), channel_id=1, source_target_pairs={{0,1},{1,2},{2,3},{3,4},{4,5},{5,6},{6,7},{7,8},{8,9},{9,10},{10,1... | collective-permute-start | bytes 393224 | tf_op jit(solution)/shard_map/ppermute | solution.py:97
  6.1 8.9 %collective-permute-start.1 = (f32[2,256,64]{2,1,0:T(8,128)S(1)}, f32[2,256,64]{2,1,0:T(8,128)S(1)}, u32[]{:S(2)}, u32[]{:S(2)}) collective-permute-start(f32[2,256,64]{2,1,0:T(8,128)S(1)} %get-tuple-element.16), channel_id=1, source_target_pairs={{1,0},{2,1},{3,2},{4,3},{5,4},{6,5},{7,6},{8,7},{9,8},{10,9},{11,1... | collective-permute-start | bytes 393224 | tf_op jit(solution)/shard_map/ppermute | solution.py:97
  11.9 22.9 %copy-start.5 = (s32[1,1,1,2]{3,2,1,0:T(1,128)S(1)}, s32[1,1,1,2]{3,2,1,0:T(1,128)}, u32[]{:S(2)}) copy-start(s32[1,1,1,2]{3,2,1,0:T(1,128)} %param.6) | copy-start | bytes 28
  15.4 27.0 %collective-permute-start.2 = (f32[2,64,384]{2,1,0:T(8,128)S(1)}, f32[2,64,384]{2,1,0:T(8,128)S(1)}, u32[]{:S(2)}, u32[]{:S(2)}) collective-permute-start(f32[2,64,384]{2,1,0:T(8,128)S(1)} %get-tuple-element.9), channel_id=1, source_target_pairs={{0,32},{32,64},{64,96},{96,128},{128,160},{160,192},{192,224},{224... | collective-permute-start | bytes 589832 | tf_op jit(solution)/shard_map/ppermute | solution.py:97
  20.3 22.1 %collective-permute-start.3 = (f32[2,64,384]{2,1,0:T(8,128)S(1)}, f32[2,64,384]{2,1,0:T(8,128)S(1)}, u32[]{:S(2)}, u32[]{:S(2)}) collective-permute-start(f32[2,64,384]{2,1,0:T(8,128)S(1)} %get-tuple-element.10), channel_id=1, source_target_pairs={{32,0},{64,32},{96,64},{128,96},{160,128},{192,160},{224,192},{256... | collective-permute-start | bytes 589832 | tf_op jit(solution)/shard_map/ppermute | solution.py:97
  49.9 21.5 %copy-start.1 = (f32[2,256,256]{2,1,0:T(8,128)S(1)}, f32[2,256,256]{2,1,0:T(8,128)}, u32[]{:S(2)}) copy-start(f32[2,256,256]{2,1,0:T(8,128)} %shard_map.46) | copy-start | bytes 1572868
  50.0 17.6 %collective-permute-start.5 = (f32[2,136,256]{2,1,0:T(8,128)S(1)}, f32[2,136,256]{2,1,0:T(8,128)S(1)}, u32[]{:S(2)}, u32[]{:S(2)}) collective-permute-start(f32[2,136,256]{2,1,0:T(8,128)S(1)} %get-tuple-element.21), channel_id=1, source_target_pairs={{0,32},{32,64},{64,96},{96,128},{128,160},{160,192},{192,224},{224... | collective-permute-start | bytes 835592 | tf_op jit(solution)/shard_map/ppermute | solution.py:97
  52.1 16.8 %collective-permute-start.4 = (f32[2,136,256]{2,1,0:T(8,128)S(1)}, f32[2,136,256]{2,1,0:T(8,128)S(1)}, u32[]{:S(2)}, u32[]{:S(2)}) collective-permute-start(f32[2,136,256]{2,1,0:T(8,128)S(1)} %get-tuple-element.22), channel_id=1, source_target_pairs={{32,0},{64,32},{96,64},{128,96},{160,128},{192,160},{224,192},{256... | collective-permute-start | bytes 835592 | tf_op jit(solution)/shard_map/ppermute | solution.py:97
  72.4 5.9 %copy-start = (f32[2,3,256,256]{3,2,1,0:T(8,128)S(1)}, f32[2,3,256,256]{3,2,1,0:T(8,128)}, u32[]{:S(2)}) copy-start(f32[2,3,256,256]{3,2,1,0:T(8,128)} %probe_ref.3) | copy-start | bytes 4718596
  73.2 8.1 %collective-permute-start.6 = (f32[2,384,128]{2,1,0:T(8,128)}, f32[2,384,128]{2,1,0:T(8,128)S(1)}, u32[]{:S(2)}, u32[]{:S(2)}) collective-permute-start(f32[2,384,128]{2,1,0:T(8,128)} %get-tuple-element.5), channel_id=1, source_target_pairs={{0,1},{1,2},{2,3},{3,4},{4,5},{5,6},{6,7},{7,8},{8,9},{9,10},{10,1... | collective-permute-start | bytes 1179656 | tf_op jit(solution)/shard_map/ppermute | solution.py:97
  76.4 10.4 %collective-permute-start.7 = (f32[2,384,128]{2,1,0:T(8,128)S(1)}, f32[2,384,128]{2,1,0:T(8,128)}, u32[]{:S(2)}, u32[]{:S(2)}) collective-permute-start(f32[2,384,128]{2,1,0:T(8,128)S(1)} %get-tuple-element.6), channel_id=1, source_target_pairs={{1,0},{2,1},{3,2},{4,3},{5,4},{6,5},{7,6},{8,7},{9,8},{10,9},{11,1... | collective-permute-start | bytes 1179656 | tf_op jit(solution)/shard_map/ppermute | solution.py:97
  81.4 0.7 copy-start.4
  95.1 13.7 %copy-start.2 = (f32[2,256,256]{2,1,0:T(8,128)S(1)}, f32[2,256,256]{2,1,0:T(8,128)}, u32[]{:S(2)}) copy-start(f32[2,256,256]{2,1,0:T(8,128)} %shard_map.47) | copy-start | bytes 1572868
  96.6 6.6 %collective-permute-start.8 = (f32[2,384,64]{2,1,0:T(8,128)S(1)}, f32[2,384,64]{2,1,0:T(8,128)S(1)}, u32[]{:S(2)}, u32[]{:S(2)}) collective-permute-start(f32[2,384,64]{2,1,0:T(8,128)S(1)} %get-tuple-element.11), channel_id=1, source_target_pairs={{0,1},{1,2},{2,3},{3,4},{4,5},{5,6},{6,7},{7,8},{8,9},{9,10},{10,1... | collective-permute-start | bytes 589832 | tf_op jit(solution)/shard_map/ppermute | solution.py:97
  98.5 10.3 %collective-permute-start.9 = (f32[2,384,64]{2,1,0:T(8,128)S(1)}, f32[2,384,64]{2,1,0:T(8,128)S(1)}, u32[]{:S(2)}, u32[]{:S(2)}) collective-permute-start(f32[2,384,64]{2,1,0:T(8,128)S(1)} %get-tuple-element.12), channel_id=1, source_target_pairs={{1,0},{2,1},{3,2},{4,3},{5,4},{6,5},{7,6},{8,7},{9,8},{10,9},{11,1... | collective-permute-start | bytes 589832 | tf_op jit(solution)/shard_map/ppermute | solution.py:97
  109.2 12.7 %collective-permute-start.10 = (f32[2,64,256]{2,1,0:T(8,128)S(1)}, f32[2,64,256]{2,1,0:T(8,128)S(1)}, u32[]{:S(2)}, u32[]{:S(2)}) collective-permute-start(f32[2,64,256]{2,1,0:T(8,128)S(1)} %get-tuple-element.7), channel_id=1, source_target_pairs={{0,32},{32,64},{64,96},{96,128},{128,160},{160,192},{192,224},{224... | collective-permute-start | bytes 393224 | tf_op jit(solution)/shard_map/ppermute | solution.py:97
  111.2 12.2 %collective-permute-start.11 = (f32[2,64,256]{2,1,0:T(8,128)S(1)}, f32[2,64,256]{2,1,0:T(8,128)S(1)}, u32[]{:S(2)}, u32[]{:S(2)}) collective-permute-start(f32[2,64,256]{2,1,0:T(8,128)S(1)} %get-tuple-element.8), channel_id=1, source_target_pairs={{32,0},{64,32},{96,64},{128,96},{160,128},{192,160},{224,192},{256... | collective-permute-start | bytes 393224 | tf_op jit(solution)/shard_map/ppermute | solution.py:97
